TPU v7x, 256 devices: a whole 4x4x8 slice. The times are simulated.
256 devices in a mesh: fsdp: 16 (over x, y), seq: 16 (over z, core).
Axes of the slice: x: 4, y: 4, z: 8, core: 2. Of those that a mesh axis runs over, the one named last changes fastest.
Arguments:
- tokens: bfloat16 [65536, 2048], P(('fsdp', 'seq')), may hold values from -6 to 6
- seq_lengths: int32 [16, 4], P('fsdp'), may hold values from 1 to 2048, 4096 in all within a row
- in_weight: bfloat16 [2048, 6144], P(None, 'fsdp'), may hold values from -0.125 to 0.125
- short_filter: float32 [7, 6144], replicated, may hold values from -2.5 to 2.5
- long_filter: bfloat16 [128, 128], replicated, may hold values from -0.5 to 0.5
- out_weight: bfloat16 [2048, 2048], replicated, may hold values from -0.125 to 0.125
Outputs:
- mixed: bfloat16 [65536, 2048], P(('fsdp', 'seq'))
Inputs may be any that keep to these rules, and one draw needn't show every extreme that they name: `seq_lengths`: in each pack the 4 lengths sum to 4096 and the longest is exactly 2048.
All inputs are finite; a program needn't handle non-finite values.
Results may differ from a plain program's by a relative error of at most 0.0073.
Values may be sent and summed in bfloat16 or wider, within the bound.
No kernel may reach another device: no remote copies, remote signals or barrier semaphores. Data moves between devices by JAX's collectives and lax.ppermute only.
A program may use at most 128 MiB of HBM per device.

v0:
```python
import jax
import jax.numpy as jnp
from jax import lax
from jax.sharding import PartitionSpec as P


def from_behind(block, axis, distance):
    devices = range(lax.axis_size(axis))
    route = [(i - distance, i) for i in devices if i - distance in devices]
    return lax.ppermute(block, axis, route)


def positions(row_ids, seq_starts):
    seq_begin = jnp.max(
        jnp.where(seq_starts[None, :] <= row_ids[:, None], seq_starts[None, :], 0), axis=1
    )
    return row_ids - seq_begin


def featurize(extended, position, taps):
    width = taps.shape[0]
    rows = position.shape[0]
    total = jnp.zeros((rows, extended.shape[1]), jnp.float32)
    for tap_index in range(width):
        part = extended[width - 1 - tap_index : width - 1 - tap_index + rows].astype(jnp.float32)
        total = total + taps[tap_index] * jnp.where((position >= tap_index)[:, None], part, 0.0)
    return total


def tap_table(tap_ids, long_filter):
    filter_len = long_filter.shape[0]
    one_hot = (
        tap_ids[:, :, None] == jnp.arange(filter_len, dtype=jnp.int32)[None, None, :]
    ).astype(jnp.bfloat16)
    return jnp.einsum(
        "ijt,tg->ijg", one_hot, long_filter, preferred_element_type=jnp.float32
    ).astype(jnp.bfloat16)


def local(tokens, seq_lengths, in_weight, short_filter, long_filter, out_weight):
    row_count, channels = tokens.shape
    width = short_filter.shape[0]
    filter_len, group_count = long_filter.shape
    projected = jnp.dot(
        tokens,
        lax.all_gather(in_weight, "fsdp", axis=1, tiled=True),
        preferred_element_type=jnp.float32,
    ).astype(jnp.bfloat16)
    lengths_row = seq_lengths[0]
    seq_starts = jnp.cumsum(lengths_row) - lengths_row
    first_global = lax.axis_index("seq") * row_count
    row_ids = first_global + jnp.arange(row_count, dtype=jnp.int32)
    position = positions(row_ids, seq_starts)
    prev_tail = from_behind(projected[row_count - (width - 1) :], "seq", 1)
    extended = jnp.concatenate([prev_tail, projected], axis=0)
    featured = featurize(extended, position, short_filter)
    queries = featured[:, :channels]
    mixed_in = (featured[:, channels : 2 * channels] * featured[:, 2 * channels :]).astype(
        jnp.bfloat16
    )
    conv_tail = from_behind(mixed_in[row_count - (filter_len - 1) :], "seq", 1)
    window_all = jnp.concatenate([conv_tail, mixed_in], axis=0)
    out_rows = jnp.arange(filter_len, dtype=jnp.int32)[:, None]
    cur_tap = out_rows - jnp.arange(filter_len, dtype=jnp.int32)[None, :]
    prev_tap = out_rows + (filter_len - 1) - jnp.arange(filter_len - 1, dtype=jnp.int32)[None, :]
    cur_table = tap_table(cur_tap, long_filter)
    prev_table = tap_table(prev_tap, long_filter)
    per_group = channels // group_count
    pieces = []
    for block_id in range(row_count // filter_len):
        first_row = block_id * filter_len
        block_pos = position[first_row : first_row + filter_len]
        cur_kernel = jnp.where((cur_tap <= block_pos[:, None])[:, :, None], cur_table, 0.0)
        prev_kernel = jnp.where((prev_tap <= block_pos[:, None])[:, :, None], prev_table, 0.0)
        prev_src = window_all[first_row : first_row + filter_len - 1].reshape(
            filter_len - 1, group_count, per_group
        )
        cur_src = window_all[first_row + filter_len - 1 : first_row + 2 * filter_len - 1].reshape(
            filter_len, group_count, per_group
        )
        block_out = jnp.einsum(
            "ijg,jgc->igc", cur_kernel, cur_src, preferred_element_type=jnp.float32
        )
        block_out = block_out + jnp.einsum(
            "ijg,jgc->igc", prev_kernel, prev_src, preferred_element_type=jnp.float32
        )
        pieces.append(block_out.reshape(filter_len, channels))
    filtered = jnp.concatenate(pieces, axis=0)
    gated_out = (queries * filtered).astype(jnp.bfloat16)
    result = tokens.astype(jnp.float32) + jnp.dot(
        gated_out, out_weight, preferred_element_type=jnp.float32
    )
    return result.astype(jnp.bfloat16)


def solution(mesh):
    in_specs = (P(("fsdp", "seq"), None), P("fsdp", None), P(None, "fsdp"), P(), P(), P())
    out_specs = P(("fsdp", "seq"), None)
    return jax.shard_map(local, mesh=mesh, in_specs=in_specs, out_specs=out_specs, check_vma=False)
```

profile of v0, /device:TPU:1, one launch (start us, length us, event | category | flops | bytes accessed | tf_op | source)
XLA Modules:
  0.0 275.3 jit_solution(17743482276146317237)
XLA Ops:
  6.5 0.7 all-gather.2.cloned.1.call-update
  7.3 0.8 reduce-window_clone.1
  8.1 0.7 subtract_bitcast_fusion
  8.8 0.1 select_reduce_fusion
  8.9 0.1 fusion.15
  9.1 8.8 %broadcast_select_fusion.3 = (bf16[128,127,128]{2,0,1:T(8,128)(2,1)}, bf16[128,127,128]{2,0,1:T(8,128)(2,1)}) fusion(pred[128,127]{0,1:T(8,128)(4,1)S(1)} %get-tuple-element.30, pred[128,127]{0,1:T(8,128)(4,1)S(1)} %get-tuple-element.31, bf16[128,128]{1,0:T(8,128)(2,1)S(1)} %copy-done, s32[128,127]{0,1:T(8,128)S(1)} %iota_subtract_fusion), kind=kOutput, calls=%fused_computation.16 | convolution fusion | flops 540999680 | bytes 8453376 | tf_op jit(solution)/shard_map/ijt,tg->ijg/dot_general | solution.py:35
  17.9 10.4 %broadcast_select_fusion.1 = (bf16[128,128,128]{2,1,0:T(8,128)(2,1)}, bf16[128,128,128]{2,1,0:T(8,128)(2,1)}) fusion(pred[128,128]{1,0:T(8,128)(4,1)S(1)} %get-tuple-element.33, pred[128,128]{1,0:T(8,128)(4,1)S(1)} %get-tuple-element.32, bf16[128,128]{1,0:T(8,128)(2,1)S(1)} %copy-done, s32[128,128]{1,0:T(8,128)S(1)} %iota_subtract_fusion.1), kind=kOutput, calls=%fused_computation.13 | convolution fusion | flops 545259520 | bytes 8519680 | tf_op jit(solution)/shard_map/ijt,tg->ijg/dot_general | solution.py:35
  28.3 0.1 fusion.26
  28.4 153.1 %all-gather.2.cloned.1.call-done = bf16[2048,6144]{1,0:T(8,128)(2,1)} async-done(((bf16[2048,384]{1,0:T(8,128)(2,1)}), bf16[2048,6144]{1,0:T(8,128)(2,1)}) %all-gather.2.cloned.1.call-update) | async-done | bytes 25165840 | tf_op jit(solution)/shard_map/all_gather | solution.py:46
  181.5 11.9 %convolution_convert_fusion = bf16[256,6144]{1,0:T(8,128)(2,1)S(1)} fusion(bf16[256,2048]{1,0:T(8,128)(2,1)} %param.6, bf16[2048,6144]{1,0:T(8,128)(2,1)} %all-gather.2.cloned.1.call-done), kind=kOutput, calls=%fused_computation.9 | convolution fusion | flops 6444023808 | bytes 29360128 | tf_op jit(solution)/shard_map/dot_general | solution.py:44
  193.4 4.6 %collective-permute-start = (bf16[6,6144]{1,0:T(8,128)(2,1)S(1)}, bf16[6,6144]{1,0:T(8,128)(2,1)S(1)}, u32[]{:S(2)}, u32[]{:S(2)}) collective-permute-start(bf16[6,6144]{1,0:T(8,128)(2,1)S(1)} %slice.92), channel_id=1, source_target_pairs={{0,1},{1,2},{2,3},{3,4},{4,5},{5,6},{6,7},{7,8},{8,9},{9,10},{10,1... | collective-permute-start | bytes 221192 | tf_op jit(solution)/shard_map/ppermute | solution.py:10
  198.1 6.7 %copy.32 = bf16[128,128,128]{1,0,2:T(8,128)(2,1)} copy(bf16[128,128,128]{2,1,0:T(8,128)(2,1)} %get-tuple-element.8) | data formatting | bytes 8388608 | tf_op jit(solution)/shard_map/jit(_where)/select_n | solution.py:73
  204.7 7.2 %copy.34 = bf16[128,127,128]{1,0,2:T(8,128)(2,1)} copy(bf16[128,127,128]{2,0,1:T(8,128)(2,1)} %get-tuple-element.10) | data formatting | bytes 8323072 | tf_op jit(solution)/shard_map/jit(_where)/select_n | solution.py:74
  211.9 6.7 %copy.28 = bf16[128,128,128]{1,0,2:T(8,128)(2,1)} copy(bf16[128,128,128]{2,1,0:T(8,128)(2,1)} %get-tuple-element.7) | data formatting | bytes 8388608 | tf_op jit(solution)/shard_map/jit(_where)/select_n | solution.py:73
  218.6 7.2 %copy.30 = bf16[128,127,128]{1,0,2:T(8,128)(2,1)} copy(bf16[128,127,128]{2,0,1:T(8,128)(2,1)} %get-tuple-element.9) | data formatting | bytes 8323072 | tf_op jit(solution)/shard_map/jit(_where)/select_n | solution.py:74
  225.8 9.8 %multiply_add_fusion = f32[256,6144]{1,0:T(8,128)S(1)} fusion(bf16[256,6144]{1,0:T(8,128)(2,1)S(1)} %convolution_convert_fusion, bf16[6,6144]{1,0:T(8,128)(2,1)S(1)} %collective-permute-done, f32[6144]{0:T(1024)S(1)} %bitcast.52, f32[6144]{0:T(1024)S(1)} %bitcast.53, f32[6144]{0:T(1024)S(1)} %bitcast.48, f32[6144]{0:T(1024)S(1)} %bitcast.49, ...), kind=kLoop, calls=%fused_computation.10 | loop fusion | flops 70778880 | bytes 9684736 | tf_op jit(solution)/shard_map/add | solution.py:26
  235.7 2.6 copy-done.2
  238.3 0.3 fusion.12
  238.6 0.1 fusion.25
  238.6 1.1 fusion.24
  239.7 0.3 copy.31
  240.0 0.3 copy.33
  240.3 2.4 collective-permute-start.1
  242.6 4.5 %fusion.29 = f32[128,16,128]{2,1,0:T(8,128)S(1)} fusion(bf16[128,128,16]{0,2,1:T(8,128)(2,1)S(1)} %bitcast.44, bf16[128,128,128]{1,0,2:T(8,128)(2,1)} %copy.32), kind=kOutput, calls=%fused_computation.62 | convolution fusion | flops 67108864 | bytes 5767168 | tf_op jit(solution)/shard_map/ijg,jgc->igc/dot_general | solution.py:81
  247.1 2.3 convolution_add_fusion.1
  249.4 1.4 copy.36
  250.7 0.3 copy.27
  251.0 4.5 %fusion.28 = f32[128,16,128]{2,1,0:T(8,128)S(1)} fusion(bf16[128,128,16]{0,2,1:T(8,128)(2,1)S(1)} %bitcast.46, bf16[128,128,128]{1,0,2:T(8,128)(2,1)} %copy.28), kind=kOutput, calls=%fused_computation.61 | convolution fusion | flops 67108864 | bytes 5767168 | tf_op jit(solution)/shard_map/ijg,jgc->igc/dot_general | solution.py:81
  255.5 0.3 copy.29
  255.8 4.4 %convolution_add_fusion.2 = f32[128,16,128]{2,1,0:T(8,128)S(1)} fusion(f32[128,16,128]{2,1,0:T(8,128)S(1)} %fusion.28, bf16[127,128,16]{0,2,1:T(8,128)(2,1)S(1)} %bitcast.45, bf16[128,127,128]{1,0,2:T(8,128)(2,1)} %copy.30), kind=kOutput, calls=%fused_computation.35 | convolution fusion | flops 66846720 | bytes 6778880 | tf_op jit(solution)/shard_map/ijg,jgc->igc/dot_general | solution.py:84
  260.2 0.4 copy.35
  260.6 7.9 %fusion.11 = bf16[256,2048]{1,0:T(8,128)(2,1)} fusion(bf16[2048,2048]{1,0:T(8,128)(2,1)} %param.11, bf16[256,2048]{1,0:T(8,128)(2,1)} %param.6, f32[256,6144]{1,0:T(8,128)} %copy-done.2, f32[128,2048]{1,0:T(8,128)} %copy.36, f32[128,2048]{1,0:T(8,128)S(1)} %copy.35), kind=kOutput, calls=%fused_computation.29 | convolution fusion | flops 2150629376 | bytes 14680064 | tf_op jit(solution)/shard_map/dot_general | solution.py:90
  (21 shorter events, 0.1 us)
Async XLA Ops:
  6.5 2.5 copy-start
  6.5 175.0 %all-gather.2.cloned.1.call-start = ((), (), s32[]{:S(2)}) async-start(), calls=%async_computation | async-start | bytes 26738688 | tf_op jit(solution)/shard_map/all_gather | solution.py:46
  17.9 10.4 %copy-start.4 = (f32[7,6144]{1,0:T(8,128)S(1)}, f32[7,6144]{1,0:T(8,128)}, u32[]{:S(2)}) copy-start(f32[7,6144]{1,0:T(8,128)} %param.9) | copy-start | bytes 516100
  193.4 32.4 %collective-permute-start = (bf16[6,6144]{1,0:T(8,128)(2,1)S(1)}, bf16[6,6144]{1,0:T(8,128)(2,1)S(1)}, u32[]{:S(2)}, u32[]{:S(2)}) collective-permute-start(bf16[6,6144]{1,0:T(8,128)(2,1)S(1)} %slice.92), channel_id=1, source_target_pairs={{0,1},{1,2},{2,3},{3,4},{4,5},{5,6},{6,7},{7,8},{8,9},{9,10},{10,1... | collective-permute-start | bytes 221192 | tf_op jit(solution)/shard_map/ppermute | solution.py:10
  235.7 2.6 copy-start.2
  240.3 6.8 %copy-start.3 = (bf16[128,127,128]{1,0,2:T(8,128)(2,1)S(1)}, bf16[128,127,128]{1,0,2:T(8,128)(2,1)}, u32[]{:S(2)}) copy-start(bf16[128,127,128]{1,0,2:T(8,128)(2,1)} %copy.34) | copy-start | bytes 12484612
  240.3 15.2 %collective-permute-start.1 = (bf16[127,2048]{1,0:T(8,128)(2,1)}, bf16[127,2048]{1,0:T(8,128)(2,1)S(1)}, u32[]{:S(2)}, u32[]{:S(2)}) collective-permute-start(bf16[127,2048]{1,0:T(8,128)(2,1)} %get-tuple-element.11), channel_id=1, source_target_pairs={{0,1},{1,2},{2,3},{3,4},{4,5},{5,6},{6,7},{7,8},{8,9},{9,10},{10,1... | collective-permute-start | bytes 1560584 | tf_op jit(solution)/shard_map/ppermute | solution.py:10
  260.6 7.9 %copy-start.1 = (bf16[128,128]{1,0:T(8,128)(2,1)S(1)}, bf16[128,128]{1,0:T(8,128)(2,1)}, u32[]{:S(2)}) copy-start(bf16[128,128]{1,0:T(8,128)(2,1)} %param.10) | copy-start | bytes 98308
Sparse Core Ops, SparseCore 0:
  9.8 171.6 all-gather.1
where the time goes:
time: 276 us; the launch traced here: 275 us
  waiting for transfers between devices  154 us (56%)
  matrix products  54.6 us (20%)
  local copies, waits for them, and re-layouts  34.5 us (12%)
  between operations  13.6 us (5%)
  other arithmetic  11.8 us (4%)
  starting transfers between devices  6.97 us (3%)
    all_gather x1, waiting for transfers between devices, local(): lax.all_gather(in_weight, 'fsdp', axis=1, tiled=True)  153 us
    dot_general x2, matrix products, tap_table(): jnp.einsum('ijt,tg->ijg', one_hot, long_filter, preferred_element_type=jn...  19.2 us
    select_n x2, local copies, waits for them, and re-layouts, local(): jnp.where((prev_tap <= block_pos[:, None])[:, :, None], prev_table, 0.0)  14.4 us
    select_n x2, local copies, waits for them, and re-layouts, local(): jnp.where((cur_tap <= block_pos[:, None])[:, :, None], cur_table, 0.0)  13.4 us
    dot_general x1, matrix products, local(): jnp.dot(tokens, lax.all_gather(in_weight, 'fsdp', axis=1, tiled=True), pr...  11.9 us
    add x1, other arithmetic, featurize(): total + taps[tap_index] * jnp.where((position >= tap_index)[:, None], par...  9.84 us
    dot_general x2, matrix products, local(): jnp.einsum('ijg,jgc->igc', cur_kernel, cur_src, preferred_element_type=jn...  8.91 us
    dot_general x1, matrix products, local(): jnp.dot(gated_out, out_weight, preferred_element_type=jnp.float32)  7.87 us
  transfers between devices with their start and end apart: 3, of which 1 were waited for; matrix products, arithmetic and copies ran while one was open for 22% of the time, Pallas kernels for 0%

commit v1 on v0

v1 whole, which is shorter than its diff:
```python
import jax
import jax.numpy as jnp
from jax import lax
from jax.sharding import PartitionSpec as P

LANE = 128


def positions(row_ids, seq_starts):
    seq_begin = jnp.max(
        jnp.where(seq_starts[None, :] <= row_ids[:, None], seq_starts[None, :], 0), axis=1
    )
    return row_ids - seq_begin


def tap_table(tap_ids, long_filter):
    filter_len = long_filter.shape[0]
    one_hot = (
        tap_ids[:, :, None] == jnp.arange(filter_len, dtype=jnp.int32)[None, None, :]
    ).astype(jnp.bfloat16)
    return jnp.einsum(
        "ijt,tg->gij", one_hot, long_filter, preferred_element_type=jnp.float32
    ).astype(jnp.bfloat16)


def local(tokens, seq_lengths, in_weight, short_filter, long_filter, out_weight):
    rows, channels = tokens.shape
    width = short_filter.shape[0]
    filter_len, group_count = long_filter.shape
    per_group = channels // group_count
    n_seq = lax.axis_size("seq")
    s = lax.axis_index("seq")
    core = s % 2
    half = LANE // 2
    n_lblk = channels // LANE
    tail = filter_len + 8
    ext_rows = tail + 2 * rows

    sib_perm = [(i, i ^ 1) for i in range(n_seq)]
    sib_tokens = lax.ppermute(tokens, "seq", sib_perm)
    first = jnp.where(core == 0, tokens, sib_tokens)
    second = jnp.where(core == 0, sib_tokens, tokens)
    tail_src = tokens[rows - tail :]
    to_even = [(i - 1, i) for i in range(2, n_seq, 2)]
    to_odd = [(i - 2, i) for i in range(3, n_seq, 2)]
    tail_a = lax.ppermute(tail_src, "seq", to_even)
    tail_b = lax.ppermute(tail_src, "seq", to_odd)
    tail_tok = jnp.where(core == 0, tail_a, tail_b)
    ext_tokens = jnp.concatenate([tail_tok, first, second], axis=0)

    lengths_row = seq_lengths[0]
    seq_starts = jnp.cumsum(lengths_row) - lengths_row
    pair_start = (s // 2) * (2 * rows)
    row_ids = pair_start - tail + jnp.arange(ext_rows, dtype=jnp.int32)
    position = positions(row_ids, seq_starts)

    offset = core * half
    w_t = in_weight.T.reshape(in_weight.shape[1] // LANE, LANE, channels)
    w_part = lax.dynamic_slice_in_dim(w_t, offset, half, axis=1)
    w_all = lax.all_gather(w_part, "fsdp", axis=0, tiled=True)
    w_all = w_all.reshape(3 * n_lblk * half, channels)
    own = 3 * n_lblk * half // 3

    projected = jnp.dot(
        ext_tokens, w_all.T, preferred_element_type=jnp.float32
    ).astype(jnp.bfloat16)

    taps = short_filter.reshape(width, 3, n_lblk, LANE)
    taps = lax.dynamic_slice_in_dim(taps, offset, half, axis=3).reshape(width, 3 * own)

    start = 8
    feat_rows = ext_rows - start
    pos_f = position[start:]
    featured = jnp.zeros((feat_rows, 3 * own), jnp.float32)
    for tap_index in range(width):
        part = projected[start - tap_index : ext_rows - tap_index].astype(jnp.float32)
        featured = featured + taps[tap_index] * jnp.where(
            (pos_f >= tap_index)[:, None], part, 0.0
        )
    queries = featured[feat_rows - 2 * rows :, :own]
    mixed_in = (featured[:, own : 2 * own] * featured[:, 2 * own :]).astype(jnp.bfloat16)

    sub = LANE // per_group
    lf = long_filter.reshape(filter_len, n_lblk, sub)
    lf = lax.dynamic_slice_in_dim(lf, offset // per_group, half // per_group, axis=2)
    lf = lf.reshape(filter_len, own // per_group)
    n_groups = own // per_group

    out_rows = jnp.arange(filter_len, dtype=jnp.int32)[:, None]
    src_rows = jnp.arange(filter_len, dtype=jnp.int32)[None, :]
    cur_tap = out_rows - src_rows
    prev_tap = out_rows + filter_len - src_rows
    cur_table = tap_table(cur_tap, lf)
    prev_table = tap_table(prev_tap, lf)

    n_blocks = 2 * rows // filter_len
    mi_blocks = mixed_in.reshape(n_blocks + 1, filter_len, n_groups, per_group)
    pos_out = position[tail:].reshape(n_blocks, filter_len)
    cur_kernel = jnp.where(
        (cur_tap[None] <= pos_out[:, :, None])[:, None], cur_table[None], 0.0
    ).astype(jnp.bfloat16)
    prev_kernel = jnp.where(
        (prev_tap[None] <= pos_out[:, :, None])[:, None], prev_table[None], 0.0
    ).astype(jnp.bfloat16)
    filtered = jnp.einsum(
        "bgij,bjgc->bigc", cur_kernel, mi_blocks[1:], preferred_element_type=jnp.float32
    )
    filtered = filtered + jnp.einsum(
        "bgij,bjgc->bigc", prev_kernel, mi_blocks[:-1], preferred_element_type=jnp.float32
    )
    filtered = filtered.reshape(2 * rows, own)
    gated = (queries * filtered).astype(jnp.bfloat16)

    mine = jnp.where(core == 0, gated[:rows], gated[rows:])
    theirs = jnp.where(core == 0, gated[rows:], gated[:rows])
    from_sib = lax.ppermute(theirs, "seq", sib_perm)
    ow = out_weight.reshape(n_lblk, LANE, channels)
    ow_own = lax.dynamic_slice_in_dim(ow, offset, half, axis=1).reshape(own, channels)
    ow_sib = lax.dynamic_slice_in_dim(ow, half - offset, half, axis=1).reshape(own, channels)
    result = tokens.astype(jnp.float32) + jnp.dot(
        jnp.concatenate([mine, from_sib], axis=1),
        jnp.concatenate([ow_own, ow_sib], axis=0),
        preferred_element_type=jnp.float32,
    )
    return result.astype(jnp.bfloat16)


def solution(mesh):
    in_specs = (P(("fsdp", "seq"), None), P("fsdp", None), P(None, "fsdp"), P(), P(), P())
    out_specs = P(("fsdp", "seq"), None)
    return jax.shard_map(local, mesh=mesh, in_specs=in_specs, out_specs=out_specs, check_vma=False)
```

time: 276 us -> 172 us (0.62)
  waiting for transfers between devices: 154 us -> 65.3 us
  matrix products: 54.6 us -> 35 us
  other arithmetic: 11.8 us -> 19 us
  local copies, waits for them, and re-layouts: 34.5 us -> 27.9 us
  starting transfers between devices: 6.97 us -> 10.9 us
    all_gather x1, waiting for transfers between devices: 153 us -> 65.3 us  [local(): w_all = lax.all_gather(w_part, 'fsdp', axis=0, tiled=True)]
    select_n x4 -> x0, local copies, waits for them, and re-layouts: 27.7 us -> none  [the longest x2 14.4 us: local(): jnp.where((prev_tap <= block_pos[:, None])[:, :, None], prev_table, 0.0)]
    dot_general x8 -> x6, matrix products: 54.6 us -> 35 us  [the longest x1 11.5 us: local(): jnp.dot(ext_tokens, w_all.T, preferred_element_type=jnp.float32)]
    convert_element_type x0 -> x2, local copies, waits for them, and re-layouts: none -> 5.36 us  [tap_table(): return jnp.einsum('ijt,tg->gij', one_hot, long_filter, preferred_element_...]
    dynamic_slice x0 -> x3, local copies, waits for them, and re-layouts: none -> 5.34 us  [the longest x1 4.39 us: local(): lax.dynamic_slice_in_dim(ow, offset, half, axis=1).reshape(own, channels)]
    ppermute x2 -> x4, starting transfers between devices: 6.97 us -> 10.9 us  [the longest x1 5.75 us: local(): tail_a = lax.ppermute(tail_src, 'seq', to_even)]
    unnamed x10 -> x24, local copies, waits for them, and re-layouts: 2.65 us -> 6.3 us
    select_n x0 -> x3, other arithmetic: none -> 3.38 us  [the longest x1 1.94 us: local(): tail_tok = jnp.where(core == 0, tail_a, tail_b)]
  transfers between devices with their start and end apart: 3 -> 5, of which waited for: 1 -> 1; matrix products, arithmetic and copies ran while one was open for 22% -> 16% of each run, Pallas kernels for 0% -> 0%
where the time goes in v1:
time: 172 us
  waiting for transfers between devices  65.3 us (38%)
  matrix products  35 us (20%)
  local copies, waits for them, and re-layouts  27.9 us (16%)
  other arithmetic  19 us (11%)
  between operations  13.7 us (8%)
  starting transfers between devices  10.9 us (6%)
    all_gather x1, waiting for transfers between devices, local(): w_all = lax.all_gather(w_part, 'fsdp', axis=0, tiled=True)  65.3 us
    add x1, other arithmetic, local(): featured + taps[tap_index] * jnp.where((pos_f >= tap_index)[:, None], par...  12.8 us
    dot_general x1, matrix products, local(): jnp.dot(ext_tokens, w_all.T, preferred_element_type=jnp.float32)  11.5 us
    dot_general x2, matrix products, tap_table(): jnp.einsum('ijt,tg->gij', one_hot, long_filter, preferred_element_type=jn...  9.53 us
    unnamed x24, local copies, waits for them, and re-layouts  6.3 us
    dot_general x1, matrix products, local(): jnp.einsum('bgij,bjgc->bigc', prev_kernel, mi_blocks[:-1], preferred_elem...  6.19 us
    ppermute x1, starting transfers between devices, local(): tail_a = lax.ppermute(tail_src, 'seq', to_even)  5.75 us
    convert_element_type x2, local copies, waits for them, and re-layouts, tap_table(): return jnp.einsum('ijt,tg->gij', one_hot, long_filter, preferred_element_...  5.36 us
  transfers between devices with their start and end apart: 5, of which 1 were waited for; matrix products, arithmetic and copies ran while one was open for 16% of the time, Pallas kernels for 0%

profile of v1, /device:TPU:1, one launch (start us, length us, event | category | flops | bytes accessed | tf_op | source)
XLA Modules:
  0.0 171.9 jit_solution(13038339132425501216)
XLA Ops:
  6.6 1.8 %copy.28 = bf16[2048,384]{0,1:T(8,128)(2,1)S(1)} copy(bf16[2048,384]{1,0:T(8,128)(2,1)} %param.8) | data formatting | bytes 3145728 | tf_op args[2]
  8.4 0.9 constant_dynamic-slice_fusion.9
  9.4 0.9 slice.89
  10.2 5.7 %collective-permute-start = (bf16[136,2048]{1,0:T(8,128)(2,1)}, bf16[136,2048]{1,0:T(8,128)(2,1)}, u32[]{:S(2)}, u32[]{:S(2)}) collective-permute-start(bf16[136,2048]{1,0:T(8,128)(2,1)} %slice.89), channel_id=1, source_target_pairs={{1,2},{3,4},{5,6},{7,8},{9,10},{11,12},{13,14},{17,18},{19,20},{21... | collective-permute-start | bytes 1671176 | tf_op jit(solution)/shard_map/ppermute | solution.py:46
  16.0 4.3 %collective-permute-start.1 = (bf16[136,2048]{1,0:T(8,128)(2,1)}, bf16[136,2048]{1,0:T(8,128)(2,1)}, u32[]{:S(2)}, u32[]{:S(2)}) collective-permute-start(bf16[136,2048]{1,0:T(8,128)(2,1)} %slice.89), channel_id=1, source_target_pairs={{1,3},{3,5},{5,7},{7,9},{9,11},{11,13},{13,15},{17,19},{19,21},{21... | collective-permute-start | bytes 1671176 | tf_op jit(solution)/shard_map/ppermute | solution.py:47
  21.0 4.1 %fusion.31 = bf16[64,128,128]{2,0,1:T(8,128)(2,1)S(1)} fusion(bf16[128,64,1]{0,1,2:T(8,128)(2,1)S(1)} %bitcast.57, s32[128,128]{1,0:T(8,128)S(1)} %get-tuple-element.29), kind=kOutput, calls=%fused_computation.35 | convolution fusion | flops 271581184 | bytes 2179072 | tf_op jit(solution)/shard_map/ijt,tg->gij/dot_general | solution.py:21
  25.2 5.4 %fusion.32 = bf16[64,128,128]{2,0,1:T(8,128)(2,1)} fusion(bf16[128,64,1]{0,1,2:T(8,128)(2,1)S(1)} %bitcast.58, s32[128,128]{1,0:T(8,128)S(1)} %get-tuple-element.30), kind=kOutput, calls=%fused_computation.36 | convolution fusion | flops 271581184 | bytes 2179072 | tf_op jit(solution)/shard_map/ijt,tg->gij/dot_general | solution.py:21
  30.6 0.7 constant_dynamic-slice_fusion.5
  31.3 0.8 mul.102
  32.1 0.8 mul.83
  32.9 0.8 mul.87
  33.7 0.7 mul.90
  34.6 2.7 %copy.34 = bf16[64,128,128]{2,1,0:T(8,128)(2,1)} copy(bf16[64,128,128]{2,0,1:T(8,128)(2,1)S(1)} %fusion.31) | data formatting | bytes 4194304 | tf_op jit(solution)/shard_map/convert_element_type | solution.py:23
  37.3 2.6 %copy.31 = bf16[64,128,128]{2,1,0:T(8,128)(2,1)} copy(bf16[64,128,128]{2,0,1:T(8,128)(2,1)S(1)} %copy-done.4) | data formatting | bytes 4194304 | tf_op jit(solution)/shard_map/convert_element_type | solution.py:23
  40.2 1.9 %broadcast_select_fusion.2 = bf16[136,2048]{1,0:T(8,128)(2,1)} fusion(bf16[136,2048]{1,0:T(8,128)(2,1)} %collective-permute-done, bf16[136,2048]{1,0:T(8,128)(2,1)} %collective-permute-done.1, pred[]{:T(512)S(6)} %eq.16), kind=kLoop, calls=%fused_computation.44 | loop fusion | flops 278528 | bytes 1671169 | tf_op jit(solution)/shard_map/jit(_where)/select_n | solution.py:48
  42.1 1.4 broadcast_select_fusion.1
  43.5 65.3 %all-gather.2.cloned.1.call-done = bf16[48,64,2048]{2,1,0:T(8,128)(2,1)} async-done(((bf16[3,64,2048]{2,1,0:T(8,128)(2,1)}), bf16[48,64,2048]{2,1,0:T(8,128)(2,1)}) %all-gather.2.cloned.1.call-update) | async-done | bytes 12582928 | tf_op jit(solution)/shard_map/all_gather | solution.py:60
  108.8 11.5 %convolution_convert_fusion = bf16[648,3072]{1,0:T(8,128)(2,1)S(1)} fusion(bf16[3072,2048]{1,0:T(8,128)(2,1)} %bitcast.59, bf16[256,2048]{1,0:T(8,128)(2,1)S(1)} %get-tuple-element.8, bf16[256,2048]{1,0:T(8,128)(2,1)S(1)} %get-tuple-element.7, bf16[136,2048]{1,0:T(8,128)(2,1)} %broadcast_select_fusion.2), kind=kOutput, calls=%fused_computation.15 | convolution fusion | flops 8163680256 | bytes 19218432 | tf_op jit(solution)/shard_map/dot_general | solution.py:64
  120.3 12.8 %multiply_add_fusion = f32[640,3072]{1,0:T(8,128)S(1)} fusion(bf16[648,3072]{1,0:T(8,128)(2,1)S(1)} %convolution_convert_fusion, f32[3072]{0:T(1024)S(1)} %mul.102, f32[3072]{0:T(1024)S(1)} %mul.99, f32[3072]{0:T(1024)S(1)} %mul.96, f32[3072]{0:T(1024)S(1)} %mul.93, f32[3072]{0:T(1024)S(1)} %copy-done.7, f32[3072]{0:T(1024)S(1)} %mul.87, f32[3072]{0:T(1024)S(1)} %mul.83, ...), kind=kLoop, calls=%fused_computation.14 | loop fusion | flops 53084160 | bytes 35479936 | tf_op jit(solution)/shard_map/add | solution.py:77
  133.8 2.4 %copy-done = f32[640,3072]{1,0:T(8,128)} copy-done((f32[640,3072]{1,0:T(8,128)}, f32[640,3072]{1,0:T(8,128)S(1)}, u32[]{:S(2)}) %copy-start) | copy-done | bytes 7864344
  136.2 0.5 copy.33
  136.7 1.1 slice.110
  137.8 0.5 copy.29
  139.1 6.2 %fusion.4 = f32[4,64,16,128]{3,2,1,0:T(8,128)S(1)} fusion(pred[4,128,128]{2,1,0:T(8,128)(4,1)S(1)} %get-tuple-element.28, bf16[64,128,128]{2,1,0:T(8,128)(2,1)} %copy.34, bf16[4,128,64,16]{1,0,3,2:T(4,128)(2,1)S(1)} %copy-done.5), kind=kOutput, calls=%fused_computation.4 | convolution fusion | flops 138412032 | bytes 5308416 | tf_op jit(solution)/shard_map/bgij,bjgc->bigc/dot_general | solution.py:108
  145.2 4.5 %add_bitcast_fusion = f32[4,128,64,16]{1,3,2,0:T(8,128)S(1)} fusion(f32[4,64,16,128]{3,2,1,0:T(8,128)S(1)} %fusion.4, pred[4,128,128]{2,1,0:T(8,128)(4,1)S(1)} %get-tuple-element.27, bf16[64,128,128]{2,1,0:T(8,128)(2,1)S(1)} %copy-done.3, bf16[4,128,64,16]{1,0,3,2:T(4,128)(2,1)S(1)} %slice.107), kind=kOutput, calls=%fused_computation.34 | convolution fusion | flops 138936320 | bytes 7405568 | tf_op jit(solution)/shard_map/bgij,bjgc->bigc/dot_general | solution.py:105
  149.7 1.4 copy.36
  151.1 1.6 copy.45
  152.7 1.9 %copy.37 = f32[512,1024]{1,0:T(8,128)S(1)} copy(f32[512,1024]{0,1:T(8,128)} %bitcast.50) | data formatting | bytes 4194304 | tf_op jit(solution)/shard_map/reshape | solution.py:111
  154.6 1.9 %fusion.30 = bf16[512,1024]{1,0:T(8,128)(2,1)S(1)} fusion(f32[512,1024]{1,0:T(8,128)S(1)} %copy.37, f32[640,3072]{1,0:T(8,128)} %copy-done), kind=kLoop, calls=%fused_computation.33 | loop fusion | flops 1048576 | bytes 5242880 | tf_op jit(solution)/shard_map/convert_element_type | solution.py:112
  156.6 0.8 collective-permute-start.3
  157.4 4.4 %constant_dynamic-slice_fusion.7 = (bf16[16,64,2048]{2,1,0:T(8,128)(2,1)S(1)}, bf16[16,64,2048]{2,1,0:T(8,128)(2,1)S(1)}) fusion(bf16[16,128,2048]{2,1,0:T(8,128)(2,1)} %bitcast.48, s32[]{:T(128)S(6)} %select_n.92, s32[]{:T(128)S(6)} %select_n.113), kind=kLoop, calls=%fused_computation.60 | loop fusion | bytes 16777224 | tf_op jit(solution)/shard_map/dynamic_slice | solution.py:118
  161.8 3.3 %fusion.27 = bf16[256,2048]{1,0:T(8,128)(2,1)} fusion(bf16[1024,2048]{1,0:T(8,128)(2,1)S(1)} %bitcast.52, bf16[1024,2048]{1,0:T(8,128)(2,1)S(1)} %bitcast.51, bf16[256,2048]{1,0:T(8,128)(2,1)S(1)} %copy-done.2, bf16[256,1024]{1,0:T(8,128)(2,1)S(1)} %collective-permute-done.3, bf16[256,1024]{1,0:T(8,128)(2,1)S(1)} %get-tuple-element.11), kind=kOutput, calls=%fused_computation.30 | convolution fusion | flops 2167930880 | bytes 11534336 | tf_op jit(solution)/shard_map/dot_general | solution.py:120
  (46 shorter events, 2.5 us)
Async XLA Ops:
  6.5 2.8 %copy-start.1 = (bf16[256,2048]{1,0:T(8,128)(2,1)S(1)}, bf16[256,2048]{1,0:T(8,128)(2,1)}, u32[]{:S(2)}) copy-start(bf16[256,2048]{1,0:T(8,128)(2,1)} %param.6) | copy-start | bytes 3145732
  6.5 13.8 %copy-start.6 = (f32[7,6144]{1,0:T(8,128)S(1)}, f32[7,6144]{1,0:T(8,128)}, u32[]{:S(2)}) copy-start(f32[7,6144]{1,0:T(8,128)} %param.9) | copy-start | bytes 516100
  6.5 13.9 %copy-start.9 = (s32[1,4]{1,0:T(1,128)S(1)}, s32[1,4]{1,0:T(1,128)}, u32[]{:S(2)}) copy-start(s32[1,4]{1,0:T(1,128)} %param.7) | copy-start | bytes 52
  6.5 14.0 %copy-start.8 = (bf16[128,128]{1,0:T(8,128)(2,1)S(1)}, bf16[128,128]{1,0:T(8,128)(2,1)}, u32[]{:S(2)}) copy-start(bf16[128,128]{1,0:T(8,128)(2,1)} %param.10) | copy-start | bytes 98308
  6.5 102.3 %all-gather.2.cloned.1.call-start = ((), (), s32[]{:S(2)}) async-start(), calls=%async_computation | async-start | bytes 13369344 | tf_op jit(solution)/shard_map/all_gather | solution.py:60
  10.2 29.9 %collective-permute-start = (bf16[136,2048]{1,0:T(8,128)(2,1)}, bf16[136,2048]{1,0:T(8,128)(2,1)}, u32[]{:S(2)}, u32[]{:S(2)}) collective-permute-start(bf16[136,2048]{1,0:T(8,128)(2,1)} %slice.89), channel_id=1, source_target_pairs={{1,2},{3,4},{5,6},{7,8},{9,10},{11,12},{13,14},{17,18},{19,20},{21... | collective-permute-start | bytes 1671176 | tf_op jit(solution)/shard_map/ppermute | solution.py:46
  16.0 24.2 %collective-permute-start.1 = (bf16[136,2048]{1,0:T(8,128)(2,1)}, bf16[136,2048]{1,0:T(8,128)(2,1)}, u32[]{:S(2)}, u32[]{:S(2)}) collective-permute-start(bf16[136,2048]{1,0:T(8,128)(2,1)} %slice.89), channel_id=1, source_target_pairs={{1,3},{3,5},{5,7},{7,9},{9,11},{11,13},{13,15},{17,19},{19,21},{21... | collective-permute-start | bytes 1671176 | tf_op jit(solution)/shard_map/ppermute | solution.py:47
  20.3 21.8 %collective-permute-start.2 = (bf16[256,2048]{1,0:T(8,128)(2,1)S(1)}, bf16[256,2048]{1,0:T(8,128)(2,1)}, u32[]{:S(2)}, u32[]{:S(2)}) collective-permute-start(bf16[256,2048]{1,0:T(8,128)(2,1)S(1)} %copy-done.1), channel_id=1, source_target_pairs={{0,1},{1,0},{2,3},{3,2},{4,5},{5,4},{6,7},{7,6},{8,9},{9,8},{10,11... | collective-permute-start | bytes 3145736 | tf_op jit(solution)/shard_map/ppermute | solution.py:40
  34.6 2.7 %copy-start.4 = (bf16[64,128,128]{2,0,1:T(8,128)(2,1)S(1)}, bf16[64,128,128]{2,0,1:T(8,128)(2,1)}, u32[]{:S(2)}) copy-start(bf16[64,128,128]{2,0,1:T(8,128)(2,1)} %fusion.32) | copy-start | bytes 6291460
  108.8 11.5 %copy-start.7 = (f32[3072]{0:T(1024)S(1)}, f32[3072]{0:T(1024)}, u32[]{:S(2)}) copy-start(f32[3072]{0:T(1024)} %mul.90) | copy-start | bytes 36868
  133.1 3.1 %copy-start = (f32[640,3072]{1,0:T(8,128)}, f32[640,3072]{1,0:T(8,128)S(1)}, u32[]{:S(2)}) copy-start(f32[640,3072]{1,0:T(8,128)S(1)} %multiply_add_fusion) | copy-start | bytes 23592964
  137.8 1.2 copy-start.5
  139.1 6.2 %copy-start.3 = (bf16[64,128,128]{2,1,0:T(8,128)(2,1)S(1)}, bf16[64,128,128]{2,1,0:T(8,128)(2,1)}, u32[]{:S(2)}) copy-start(bf16[64,128,128]{2,1,0:T(8,128)(2,1)} %copy.31) | copy-start | bytes 6291460
  156.6 5.2 %collective-permute-start.3 = (bf16[256,1024]{1,0:T(8,128)(2,1)S(1)}, bf16[256,1024]{1,0:T(8,128)(2,1)S(1)}, u32[]{:S(2)}, u32[]{:S(2)}) collective-permute-start(bf16[256,1024]{1,0:T(8,128)(2,1)S(1)} %get-tuple-element.12), channel_id=1, source_target_pairs={{0,1},{1,0},{2,3},{3,2},{4,5},{5,4},{6,7},{7,6},{8,9},{9,8},{10,11... | collective-permute-start | bytes 1572872 | tf_op jit(solution)/shard_map/ppermute | solution.py:116
  157.4 4.4 %copy-start.2 = (bf16[256,2048]{1,0:T(8,128)(2,1)S(1)}, bf16[256,2048]{1,0:T(8,128)(2,1)}, u32[]{:S(2)}) copy-start(bf16[256,2048]{1,0:T(8,128)(2,1)} %param.6) | copy-start | bytes 3145732
Sparse Core Ops, SparseCore 0:
  9.8 98.9 all-gather.1

commit v2 on v1

v2 whole, which is shorter than its diff:
```python
import jax
import jax.numpy as jnp
from jax import lax
from jax.sharding import PartitionSpec as P

LANE = 128
N_CHUNK = 2


def positions(row_ids, seq_starts):
    seq_begin = jnp.max(
        jnp.where(seq_starts[None, :] <= row_ids[:, None], seq_starts[None, :], 0), axis=1
    )
    return row_ids - seq_begin


def tap_table(tap_ids, long_filter):
    filter_len = long_filter.shape[0]
    one_hot = (
        tap_ids[:, :, None] == jnp.arange(filter_len, dtype=jnp.int32)[None, None, :]
    ).astype(jnp.bfloat16)
    return jnp.einsum(
        "ijt,tg->gij", one_hot, long_filter, preferred_element_type=jnp.float32
    ).astype(jnp.bfloat16)


def local(tokens, seq_lengths, in_weight, short_filter, long_filter, out_weight):
    rows, channels = tokens.shape
    width = short_filter.shape[0]
    filter_len, group_count = long_filter.shape
    per_group = channels // group_count
    n_seq = lax.axis_size("seq")
    s = lax.axis_index("seq")
    core = s % 2
    half = LANE // 2
    n_lblk = channels // LANE
    tail = filter_len + 8
    ext_rows = tail + 2 * rows

    sib_perm = [(i, i ^ 1) for i in range(n_seq)]
    sib_tokens = lax.ppermute(tokens, "seq", sib_perm)
    first = jnp.where(core == 0, tokens, sib_tokens)
    second = jnp.where(core == 0, sib_tokens, tokens)
    tail_src = tokens[rows - tail :]
    to_even = [(i - 1, i) for i in range(2, n_seq, 2)]
    to_odd = [(i - 2, i) for i in range(3, n_seq, 2)]
    tail_a = lax.ppermute(tail_src, "seq", to_even)
    tail_b = lax.ppermute(tail_src, "seq", to_odd)
    tail_tok = jnp.where(core == 0, tail_a, tail_b)
    ext_tokens = jnp.concatenate([tail_tok, first, second], axis=0)

    lengths_row = seq_lengths[0]
    seq_starts = jnp.cumsum(lengths_row) - lengths_row
    pair_start = (s // 2) * (2 * rows)
    row_ids = pair_start - tail + jnp.arange(ext_rows, dtype=jnp.int32)
    position = positions(row_ids, seq_starts)

    n_chunk = N_CHUNK
    w = half // n_chunk
    own = 3 * n_lblk * w // 3
    n_groups = own // per_group
    sub = LANE // per_group
    w_t = in_weight.T.reshape(in_weight.shape[1] // LANE, LANE, channels)
    taps_all = short_filter.reshape(width, 3, n_lblk, LANE)
    lf_all = long_filter.reshape(filter_len, n_lblk, sub)
    ow = out_weight.reshape(n_lblk, LANE, channels)

    start = 8
    feat_rows = ext_rows - start
    pos_f = position[start:]
    out_rows = jnp.arange(filter_len, dtype=jnp.int32)[:, None]
    src_rows = jnp.arange(filter_len, dtype=jnp.int32)[None, :]
    cur_tap = out_rows - src_rows
    prev_tap = out_rows + filter_len - src_rows
    n_blocks = 2 * rows // filter_len
    pos_out = position[tail:].reshape(n_blocks, filter_len)
    cur_mask = (cur_tap[None] <= pos_out[:, :, None])[:, None]
    prev_mask = (prev_tap[None] <= pos_out[:, :, None])[:, None]

    pieces = []
    for chunk in range(n_chunk):
        offset = core * half + chunk * w
        w_part = lax.dynamic_slice_in_dim(w_t, offset, w, axis=1)
        w_all = lax.all_gather(w_part, "fsdp", axis=0, tiled=True)
        w_all = w_all.reshape(3 * own, channels)
        projected = jnp.dot(
            ext_tokens, w_all.T, preferred_element_type=jnp.float32
        ).astype(jnp.bfloat16)
        taps = lax.dynamic_slice_in_dim(taps_all, offset, w, axis=3).reshape(width, 3 * own)
        featured = jnp.zeros((feat_rows, 3 * own), jnp.float32)
        for tap_index in range(width):
            part = projected[start - tap_index : ext_rows - tap_index].astype(jnp.float32)
            featured = featured + taps[tap_index] * jnp.where(
                (pos_f >= tap_index)[:, None], part, 0.0
            )
        queries = featured[feat_rows - 2 * rows :, :own]
        mixed_in = (featured[:, own : 2 * own] * featured[:, 2 * own :]).astype(jnp.bfloat16)

        lf = lax.dynamic_slice_in_dim(lf_all, offset // per_group, w // per_group, axis=2)
        lf = lf.reshape(filter_len, n_groups)
        cur_table = tap_table(cur_tap, lf)
        prev_table = tap_table(prev_tap, lf)
        mi_blocks = mixed_in.reshape(n_blocks + 1, filter_len, n_groups, per_group)
        cur_kernel = jnp.where(cur_mask, cur_table[None], 0.0).astype(jnp.bfloat16)
        prev_kernel = jnp.where(prev_mask, prev_table[None], 0.0).astype(jnp.bfloat16)
        filtered = jnp.einsum(
            "bgij,bjgc->bigc", cur_kernel, mi_blocks[1:], preferred_element_type=jnp.float32
        )
        filtered = filtered + jnp.einsum(
            "bgij,bjgc->bigc", prev_kernel, mi_blocks[:-1], preferred_element_type=jnp.float32
        )
        filtered = filtered.reshape(2 * rows, own)
        gated = (queries * filtered).astype(jnp.bfloat16)

        mine = jnp.where(core == 0, gated[:rows], gated[rows:])
        theirs = jnp.where(core == 0, gated[rows:], gated[:rows])
        from_sib = lax.ppermute(theirs, "seq", sib_perm)
        sib_offset = (1 - core) * half + chunk * w
        ow_own = lax.dynamic_slice_in_dim(ow, offset, w, axis=1).reshape(own, channels)
        ow_sib = lax.dynamic_slice_in_dim(ow, sib_offset, w, axis=1).reshape(own, channels)
        pieces.append(jnp.dot(
            jnp.concatenate([mine, from_sib], axis=1),
            jnp.concatenate([ow_own, ow_sib], axis=0),
            preferred_element_type=jnp.float32,
        ))
    mixed = pieces[0]
    for piece in pieces[1:]:
        mixed = mixed + piece
    result = tokens.astype(jnp.float32) + mixed
    return result.astype(jnp.bfloat16)


def solution(mesh):
    in_specs = (P(("fsdp", "seq"), None), P("fsdp", None), P(None, "fsdp"), P(), P(), P())
    out_specs = P(("fsdp", "seq"), None)
    return jax.shard_map(local, mesh=mesh, in_specs=in_specs, out_specs=out_specs, check_vma=False)
```

time: 172 us -> 193 us (1.12)
  matrix products: 35 us -> 51.3 us
  local copies, waits for them, and re-layouts: 27.9 us -> 38.1 us
  waiting for transfers between devices: 65.3 us -> 56.3 us
    dot_general x2 -> x4, matrix products: 9.53 us -> 19.3 us  [tap_table(): jnp.einsum('ijt,tg->gij', one_hot, long_filter, preferred_element_type=jn...]
    all_gather x1 -> x2, waiting for transfers between devices: 65.3 us -> 55.6 us  [local(): w_all = lax.all_gather(w_part, 'fsdp', axis=0, tiled=True)]
    mul x7 -> x14, local copies, waits for them, and re-layouts: 3.31 us -> 9.18 us  [local(): taps[tap_index] * jnp.where((pos_f >= tap_index)[:, None], part, 0.0)]
    convert_element_type x2 -> x4, local copies, waits for them, and re-layouts: 5.36 us -> 9.47 us  [tap_table(): return jnp.einsum('ijt,tg->gij', one_hot, long_filter, preferred_element_...]
    dot_general x1 -> x2, matrix products: 11.5 us -> 15.5 us  [local(): jnp.dot(ext_tokens, w_all.T, preferred_element_type=jnp.float32)]
    dot_general x1 -> x2, matrix products: 3.31 us -> 4.55 us  [local(): jnp.dot(jnp.concatenate([mine, from_sib], axis=1), jnp.concatenate([ow_ow...]
    dot_general x1 -> x2, matrix products: 6.19 us -> 7.34 us  [local(): jnp.einsum('bgij,bjgc->bigc', prev_kernel, mi_blocks[:-1], preferred_elem...]
    add x1 -> x2, other arithmetic: 12.8 us -> 12.2 us  [local(): featured + taps[tap_index] * jnp.where((pos_f >= tap_index)[:, None], par...]
  transfers between devices with their start and end apart: 5 -> 7, of which waited for: 1 -> 2; matrix products, arithmetic and copies ran while one was open for 16% -> 52% of each run, Pallas kernels for 0% -> 0%
where the time goes in v2:
time: 193 us; the launch traced here: 192 us
  waiting for transfers between devices  56.3 us (29%)
  matrix products  51.3 us (27%)
  local copies, waits for them, and re-layouts  38.1 us (20%)
  other arithmetic  20.4 us (11%)
  between operations  14.1 us (7%)
  starting transfers between devices  11.6 us (6%)
    all_gather x2, waiting for transfers between devices, local(): w_all = lax.all_gather(w_part, 'fsdp', axis=0, tiled=True)  55.6 us
    dot_general x4, matrix products, tap_table(): jnp.einsum('ijt,tg->gij', one_hot, long_filter, preferred_element_type=jn...  19.3 us
    dot_general x2, matrix products, local(): jnp.dot(ext_tokens, w_all.T, preferred_element_type=jnp.float32)  15.5 us
    add x2, other arithmetic, local(): featured + taps[tap_index] * jnp.where((pos_f >= tap_index)[:, None], par...  12.2 us
    convert_element_type x4, local copies, waits for them, and re-layouts, tap_table(): return jnp.einsum('ijt,tg->gij', one_hot, long_filter, preferred_element_...  9.47 us
    mul x14, local copies, waits for them, and re-layouts, local(): taps[tap_index] * jnp.where((pos_f >= tap_index)[:, None], part, 0.0)  9.18 us
    dot_general x2, matrix products, local(): jnp.einsum('bgij,bjgc->bigc', prev_kernel, mi_blocks[:-1], preferred_elem...  7.34 us
    unnamed x75, local copies, waits for them, and re-layouts  6.65 us
  transfers between devices with their start and end apart: 7, of which 2 were waited for; matrix products, arithmetic and copies ran while one was open for 52% of the time, Pallas kernels for 0%

profile of v2, /device:TPU:1, one launch (start us, length us, event | category | flops | bytes accessed | tf_op | source)
XLA Modules:
  0.0 191.8 jit_solution(6374610960236351517)
XLA Ops:
  6.6 1.8 copy.45
  8.4 0.9 constant_dynamic-slice_fusion.20
  11.0 5.7 %collective-permute-start = (bf16[136,2048]{1,0:T(8,128)(2,1)}, bf16[136,2048]{1,0:T(8,128)(2,1)}, u32[]{:S(2)}, u32[]{:S(2)}) collective-permute-start(bf16[136,2048]{1,0:T(8,128)(2,1)} %slice.167), channel_id=1, source_target_pairs={{1,2},{3,4},{5,6},{7,8},{9,10},{11,12},{13,14},{17,18},{19,20},{21... | collective-permute-start | bytes 1671176 | tf_op jit(solution)/shard_map/ppermute | solution.py:47
  16.7 4.3 %collective-permute-start.1 = (bf16[136,2048]{1,0:T(8,128)(2,1)}, bf16[136,2048]{1,0:T(8,128)(2,1)}, u32[]{:S(2)}, u32[]{:S(2)}) collective-permute-start(bf16[136,2048]{1,0:T(8,128)(2,1)} %slice.167), channel_id=1, source_target_pairs={{1,3},{3,5},{5,7},{7,9},{9,11},{11,13},{13,15},{17,19},{19,21},{21... | collective-permute-start | bytes 1671176 | tf_op jit(solution)/shard_map/ppermute | solution.py:48
  23.0 5.1 %fusion.47 = bf16[32,128,128]{2,0,1:T(8,128)(2,1)} fusion(bf16[128,32,1]{0,1,2:T(8,128)(2,1)S(1)} %bitcast.99, s32[128,128]{1,0:T(8,128)S(1)} %get-tuple-element.46), kind=kOutput, calls=%fused_computation.48 | convolution fusion | flops 136839168 | bytes 1122304 | tf_op jit(solution)/shard_map/ijt,tg->gij/dot_general | solution.py:22
  28.1 5.1 %fusion.45 = bf16[32,128,128]{2,0,1:T(8,128)(2,1)} fusion(bf16[128,32,1]{0,1,2:T(8,128)(2,1)S(1)} %bitcast.100, s32[128,128]{1,0:T(8,128)S(1)} %get-tuple-element.47), kind=kOutput, calls=%fused_computation.46 | convolution fusion | flops 136839168 | bytes 1122304 | tf_op jit(solution)/shard_map/ijt,tg->gij/dot_general | solution.py:22
  33.2 5.1 %fusion.48 = bf16[32,128,128]{2,0,1:T(8,128)(2,1)} fusion(bf16[128,32,1]{0,1,2:T(8,128)(2,1)S(1)} %bitcast.97, s32[128,128]{1,0:T(8,128)S(1)} %get-tuple-element.46), kind=kOutput, calls=%fused_computation.49 | convolution fusion | flops 136839168 | bytes 1122304 | tf_op jit(solution)/shard_map/ijt,tg->gij/dot_general | solution.py:22
  38.3 4.0 %fusion.46 = bf16[32,128,128]{2,0,1:T(8,128)(2,1)S(1)} fusion(bf16[128,32,1]{0,1,2:T(8,128)(2,1)S(1)} %bitcast.98, s32[128,128]{1,0:T(8,128)S(1)} %get-tuple-element.47), kind=kOutput, calls=%fused_computation.47 | convolution fusion | flops 136839168 | bytes 1122304 | tf_op jit(solution)/shard_map/ijt,tg->gij/dot_general | solution.py:22
  48.8 2.6 %copy.51 = bf16[32,128,128]{2,1,0:T(8,128)(2,1)} copy(bf16[32,128,128]{2,0,1:T(8,128)(2,1)} %fusion.47) | data formatting | bytes 2097152 | tf_op jit(solution)/shard_map/convert_element_type | solution.py:24
  51.5 2.8 %copy.48 = bf16[32,128,128]{2,1,0:T(8,128)(2,1)} copy(bf16[32,128,128]{2,0,1:T(8,128)(2,1)} %fusion.45) | data formatting | bytes 2097152 | tf_op jit(solution)/shard_map/convert_element_type | solution.py:24
  57.8 2.6 %copy.59 = bf16[32,128,128]{2,1,0:T(8,128)(2,1)} copy(bf16[32,128,128]{2,0,1:T(8,128)(2,1)} %fusion.48) | data formatting | bytes 2097152 | tf_op jit(solution)/shard_map/convert_element_type | solution.py:24
  60.4 1.4 copy.56
  62.7 1.9 %broadcast_select_fusion.2 = bf16[136,2048]{1,0:T(8,128)(2,1)} fusion(bf16[136,2048]{1,0:T(8,128)(2,1)} %collective-permute-done, bf16[136,2048]{1,0:T(8,128)(2,1)} %collective-permute-done.1, pred[]{:T(512)S(6)} %eq.28), kind=kLoop, calls=%fused_computation.66 | loop fusion | flops 278528 | bytes 1671169 | tf_op jit(solution)/shard_map/jit(_where)/select_n | solution.py:49
  64.6 1.1 broadcast_select_fusion.1
  65.8 14.4 %all-gather.3.cloned.1.call-done = bf16[48,32,2048]{2,1,0:T(8,128)(2,1)} async-done(((bf16[3,32,2048]{2,1,0:T(8,128)(2,1)}), bf16[48,32,2048]{2,1,0:T(8,128)(2,1)}) %all-gather.3.cloned.1.call-update) | async-done | bytes 6291472 | tf_op jit(solution)/shard_map/all_gather | solution.py:84
  80.2 7.6 %convolution_convert_fusion.1 = bf16[648,1536]{1,0:T(8,128)(2,1)S(1)} fusion(bf16[1536,2048]{1,0:T(8,128)(2,1)} %bitcast.102, bf16[256,2048]{1,0:T(8,128)(2,1)} %get-tuple-element.10, bf16[256,2048]{1,0:T(8,128)(2,1)S(1)} %get-tuple-element.9, bf16[136,2048]{1,0:T(8,128)(2,1)} %broadcast_select_fusion.2), kind=kOutput, calls=%fused_computation.33 | convolution fusion | flops 4085821440 | bytes 10936320 | tf_op jit(solution)/shard_map/dot_general | solution.py:86
  87.9 6.1 %multiply_add_fusion.1 = f32[640,1536]{1,0:T(8,128)S(1)} fusion(bf16[648,1536]{1,0:T(8,128)(2,1)S(1)} %convolution_convert_fusion.1, f32[1536]{0:T(1024)S(1)} %mul.183, f32[1536]{0:T(1024)S(1)} %mul.180, f32[1536]{0:T(1024)S(1)} %mul.177, f32[1536]{0:T(1024)S(1)} %mul.174, f32[1536]{0:T(1024)S(1)} %mul.171, f32[1536]{0:T(1024)S(1)} %mul.168, ...), kind=kLoop, calls=%fused_computation.31 | loop fusion | flops 26542080 | bytes 17742208 | tf_op jit(solution)/shard_map/add | solution.py:93
  94.0 2.0 %copy-done.1 = f32[640,1536]{1,0:T(8,128)} copy-done((f32[640,1536]{1,0:T(8,128)}, f32[640,1536]{1,0:T(8,128)S(1)}, u32[]{:S(2)}) %copy-start.1) | copy-done | bytes 3932184
  96.5 0.9 slice.188
  97.8 3.7 %fusion.16 = f32[4,32,16,128]{3,2,1,0:T(8,128)S(1)} fusion(pred[4,128,128]{2,1,0:T(8,128)(4,1)S(1)} %copy-done.10, bf16[32,128,128]{2,1,0:T(8,128)(2,1)} %copy.51, bf16[4,128,32,16]{1,0,3,2:T(4,128)(2,1)} %slice.188), kind=kOutput, calls=%fused_computation.18 | convolution fusion | flops 69206016 | bytes 2686976 | tf_op jit(solution)/shard_map/bgij,bjgc->bigc/dot_general | solution.py:109
  101.4 2.3 %fusion.52 = f32[4,128,32,16]{1,3,2,0:T(8,128)S(1)} fusion(f32[4,32,16,128]{3,2,1,0:T(8,128)S(1)} %fusion.16, pred[4,128,128]{2,1,0:T(8,128)(4,1)S(1)} %get-tuple-element.44, bf16[32,128,128]{2,1,0:T(8,128)(2,1)S(1)} %copy-done.5, bf16[4,128,32,16]{1,0,3,2:T(4,128)(2,1)S(1)} %slice.185), kind=kOutput, calls=%fused_computation.51 | convolution fusion | flops 69468160 | bytes 3735552 | tf_op jit(solution)/shard_map/bgij,bjgc->bigc/dot_general | solution.py:106
  104.9 1.4 fusion.64
  107.7 41.1 %all-gather.5.cloned.1.call-done = bf16[48,32,2048]{2,1,0:T(8,128)(2,1)} async-done(((bf16[3,32,2048]{2,1,0:T(8,128)(2,1)}), bf16[48,32,2048]{2,1,0:T(8,128)(2,1)}) %all-gather.5.cloned.1.call-update) | async-done | bytes 6291472 | tf_op jit(solution)/shard_map/all_gather | solution.py:84
  148.9 7.9 %convolution_convert_fusion = bf16[648,1536]{1,0:T(8,128)(2,1)S(1)} fusion(bf16[1536,2048]{1,0:T(8,128)(2,1)} %bitcast.101, bf16[256,2048]{1,0:T(8,128)(2,1)} %get-tuple-element.10, bf16[256,2048]{1,0:T(8,128)(2,1)} %copy-done.3, bf16[136,2048]{1,0:T(8,128)(2,1)} %broadcast_select_fusion.2), kind=kOutput, calls=%fused_computation.32 | convolution fusion | flops 4085821440 | bytes 10936320 | tf_op jit(solution)/shard_map/dot_general | solution.py:86
  157.0 6.1 %multiply_add_fusion = f32[640,1536]{1,0:T(8,128)S(1)} fusion(bf16[648,1536]{1,0:T(8,128)(2,1)S(1)} %convolution_convert_fusion, f32[1536]{0:T(1024)S(1)} %copy-done.15, f32[1536]{0:T(1024)S(1)} %copy-done.14, f32[1536]{0:T(1024)S(1)} %mul.201, f32[1536]{0:T(1024)S(1)} %copy-done.13, f32[1536]{0:T(1024)S(1)} %copy-done.12, f32[1536]{0:T(1024)S(1)} %copy-done.11, ...), kind=kLoop, calls=%fused_computation.30 | loop fusion | flops 26542080 | bytes 17742208 | tf_op jit(solution)/shard_map/add | solution.py:93
  163.1 1.9 copy-done
  166.7 3.7 %fusion.12 = f32[4,32,16,128]{3,2,1,0:T(8,128)S(1)} fusion(pred[4,128,128]{2,1,0:T(8,128)(4,1)} %get-tuple-element.45, bf16[32,128,128]{2,1,0:T(8,128)(2,1)} %copy.59, bf16[4,128,32,16]{1,0,3,2:T(4,128)(2,1)} %slice.211), kind=kOutput, calls=%fused_computation.14 | convolution fusion | flops 69206016 | bytes 2686976 | tf_op jit(solution)/shard_map/bgij,bjgc->bigc/dot_general | solution.py:109
  170.4 2.3 %fusion.58 = f32[4,128,32,16]{1,3,2,0:T(8,128)S(1)} fusion(f32[4,32,16,128]{3,2,1,0:T(8,128)S(1)} %fusion.12, pred[4,128,128]{2,1,0:T(8,128)(4,1)S(1)} %get-tuple-element.44, bf16[32,128,128]{2,1,0:T(8,128)(2,1)S(1)} %copy-done.4, bf16[4,128,32,16]{1,0,3,2:T(4,128)(2,1)S(1)} %slice.209), kind=kOutput, calls=%fused_computation.53 | convolution fusion | flops 69468160 | bytes 3735552 | tf_op jit(solution)/shard_map/bgij,bjgc->bigc/dot_general | solution.py:106
  173.9 1.4 fusion.63
  176.0 4.3 %constant_dynamic-slice_fusion.18 = (bf16[16,32,2048]{2,1,0:T(8,128)(2,1)S(1)}, bf16[16,32,2048]{2,1,0:T(8,128)(2,1)S(1)}, bf16[16,32,2048]{2,1,0:T(8,128)(2,1)S(1)}, bf16[16,32,2048]{2,1,0:T(8,128)(2,1)S(1)}) fusion(bf16[16,128,2048]{2,1,0:T(8,128)(2,1)} %bitcast.84, s32[]{:T(128)S(6)} %select_n.141, s32[]{:T(128)S(6)} %select_n.177, s32[]{:T(128)S(6)} %select_n.163, ...), kind=kLoop, calls=%fused_computation.104 | loop fusion | bytes 16777232 | tf_op jit(solution)/shard_map/dynamic_slice | solution.py:119
  180.4 1.2 fusion.8
  181.6 3.3 %fusion.34 = bf16[256,2048]{1,0:T(8,128)(2,1)} fusion(f32[256,2048]{1,0:T(8,128)S(1)} %fusion.8, bf16[512,2048]{1,0:T(8,128)(2,1)S(1)} %bitcast.91, bf16[512,2048]{1,0:T(8,128)(2,1)S(1)} %bitcast.90, bf16[256,2048]{1,0:T(8,128)(2,1)S(1)} %copy-done.2, bf16[256,512]{1,0:T(8,128)(2,1)} %collective-permute-done.3, bf16[256,512]{1,0:T(8,128)(2,1)S(1)} %get-tuple-element.17), kind=kOutput, calls=%fused_computation.37 | convolution fusion | flops 1085276160 | bytes 8912896 | tf_op jit(solution)/shard_map/dot_general | solution.py:121
  (128 shorter events, 21.4 us)
Async XLA Ops:
  6.5 14.6 %copy-start.6 = (f32[7,6144]{1,0:T(8,128)S(1)}, f32[7,6144]{1,0:T(8,128)}, u32[]{:S(2)}) copy-start(f32[7,6144]{1,0:T(8,128)} %param.9) | copy-start | bytes 516100
  6.5 14.6 %copy-start.34 = (s32[1,4]{1,0:T(1,128)S(1)}, s32[1,4]{1,0:T(1,128)}, u32[]{:S(2)}) copy-start(s32[1,4]{1,0:T(1,128)} %param.7) | copy-start | bytes 52
  6.5 14.8 %copy-start.16 = (bf16[128,128]{1,0:T(8,128)(2,1)S(1)}, bf16[128,128]{1,0:T(8,128)(2,1)}, u32[]{:S(2)}) copy-start(bf16[128,128]{1,0:T(8,128)(2,1)} %param.10) | copy-start | bytes 98308
  6.5 73.7 %all-gather.3.cloned.1.call-start = ((), (), s32[]{:S(2)}) async-start(), calls=%async_computation | async-start | bytes 6684672 | tf_op jit(solution)/shard_map/all_gather | solution.py:84
  9.4 139.4 %all-gather.5.cloned.1.call-start = ((), (), s32[]{:S(2)}) async-start(), calls=%async_computation.1 | async-start | bytes 6684672 | tf_op jit(solution)/shard_map/all_gather | solution.py:84
  11.0 51.7 %collective-permute-start = (bf16[136,2048]{1,0:T(8,128)(2,1)}, bf16[136,2048]{1,0:T(8,128)(2,1)}, u32[]{:S(2)}, u32[]{:S(2)}) collective-permute-start(bf16[136,2048]{1,0:T(8,128)(2,1)} %slice.167), channel_id=1, source_target_pairs={{1,2},{3,4},{5,6},{7,8},{9,10},{11,12},{13,14},{17,18},{19,20},{21... | collective-permute-start | bytes 1671176 | tf_op jit(solution)/shard_map/ppermute | solution.py:47
  16.7 46.0 %collective-permute-start.1 = (bf16[136,2048]{1,0:T(8,128)(2,1)}, bf16[136,2048]{1,0:T(8,128)(2,1)}, u32[]{:S(2)}, u32[]{:S(2)}) collective-permute-start(bf16[136,2048]{1,0:T(8,128)(2,1)} %slice.167), channel_id=1, source_target_pairs={{1,3},{3,5},{5,7},{7,9},{9,11},{11,13},{13,15},{17,19},{19,21},{21... | collective-permute-start | bytes 1671176 | tf_op jit(solution)/shard_map/ppermute | solution.py:48
  21.1 43.6 %collective-permute-start.2 = (bf16[256,2048]{1,0:T(8,128)(2,1)S(1)}, bf16[256,2048]{1,0:T(8,128)(2,1)S(1)}, u32[]{:S(2)}, u32[]{:S(2)}) collective-permute-start(bf16[256,2048]{1,0:T(8,128)(2,1)S(1)} %copy-done.2), channel_id=1, source_target_pairs={{0,1},{1,0},{2,3},{3,2},{4,5},{5,4},{6,7},{7,6},{8,9},{9,8},{10,11... | collective-permute-start | bytes 3145736 | tf_op jit(solution)/shard_map/ppermute | solution.py:41
  43.1 11.2 %copy-start.9 = (f32[1,3,16,32]{3,2,1,0:T(8,128)S(1)}, f32[1,3,16,32]{3,2,1,0:T(8,128)}, u32[]{:S(2)}) copy-start(f32[1,3,16,32]{3,2,1,0:T(8,128)} %get-tuple-element.27) | copy-start | bytes 18436
  43.1 11.2 %copy-start.8 = (f32[1,3,16,32]{3,2,1,0:T(8,128)S(1)}, f32[1,3,16,32]{3,2,1,0:T(8,128)}, u32[]{:S(2)}) copy-start(f32[1,3,16,32]{3,2,1,0:T(8,128)} %get-tuple-element.26) | copy-start | bytes 18436
  43.1 11.9 %copy-start.7 = (f32[1,3,16,32]{3,2,1,0:T(8,128)S(1)}, f32[1,3,16,32]{3,2,1,0:T(8,128)}, u32[]{:S(2)}) copy-start(f32[1,3,16,32]{3,2,1,0:T(8,128)} %get-tuple-element.25) | copy-start | bytes 18436
  48.8 13.0 %copy-start.18 = (s32[648]{0:T(1024)S(1)}, s32[648]{0:T(1024)}, u32[]{:S(2)}) copy-start(s32[648]{0:T(1024)} %copy-done.17) | copy-start | bytes 7780
  48.8 13.1 %copy-start.33 = (s32[4,128]{1,0:T(4,128)S(1)}, s32[4,128]{1,0:T(4,128)}, u32[]{:S(2)}) copy-start(s32[4,128]{1,0:T(4,128)} %slice_bitcast_fusion) | copy-start | bytes 6148
  61.9 25.9 %copy-start.19 = (pred[640]{0:T(1024)(128)(4,1)}, pred[640]{0:T(1024)(128)(4,1)S(1)}, u32[]{:S(2)}) copy-start(pred[640]{0:T(1024)(128)(4,1)S(1)} %get-tuple-element.37) | copy-start | bytes 1924
  61.9 25.9 %copy-start.21 = (pred[640]{0:T(1024)(128)(4,1)}, pred[640]{0:T(1024)(128)(4,1)S(1)}, u32[]{:S(2)}) copy-start(pred[640]{0:T(1024)(128)(4,1)S(1)} %get-tuple-element.38) | copy-start | bytes 1924
  61.9 25.9 %copy-start.23 = (pred[640]{0:T(1024)(128)(4,1)}, pred[640]{0:T(1024)(128)(4,1)S(1)}, u32[]{:S(2)}) copy-start(pred[640]{0:T(1024)(128)(4,1)S(1)} %get-tuple-element.39) | copy-start | bytes 1924
  61.9 25.9 %copy-start.25 = (pred[640]{0:T(1024)(128)(4,1)}, pred[640]{0:T(1024)(128)(4,1)S(1)}, u32[]{:S(2)}) copy-start(pred[640]{0:T(1024)(128)(4,1)S(1)} %get-tuple-element.40) | copy-start | bytes 1924
  61.9 25.9 %copy-start.27 = (pred[640]{0:T(1024)(128)(4,1)}, pred[640]{0:T(1024)(128)(4,1)S(1)}, u32[]{:S(2)}) copy-start(pred[640]{0:T(1024)(128)(4,1)S(1)} %get-tuple-element.41) | copy-start | bytes 1924
  61.9 25.9 %copy-start.29 = (pred[640]{0:T(1024)(128)(4,1)}, pred[640]{0:T(1024)(128)(4,1)S(1)}, u32[]{:S(2)}) copy-start(pred[640]{0:T(1024)(128)(4,1)S(1)} %get-tuple-element.42) | copy-start | bytes 1924
  61.9 25.9 %copy-start.31 = (pred[640]{0:T(1024)(128)(4,1)}, pred[640]{0:T(1024)(128)(4,1)S(1)}, u32[]{:S(2)}) copy-start(pred[640]{0:T(1024)(128)(4,1)S(1)} %get-tuple-element.43) | copy-start | bytes 1924
  65.8 22.1 %copy-start.3 = (bf16[256,2048]{1,0:T(8,128)(2,1)}, bf16[256,2048]{1,0:T(8,128)(2,1)S(1)}, u32[]{:S(2)}) copy-start(bf16[256,2048]{1,0:T(8,128)(2,1)S(1)} %get-tuple-element.9) | copy-start | bytes 3145732
  107.0 74.6 %collective-permute-start.3 = (bf16[256,512]{1,0:T(8,128)(2,1)}, bf16[256,512]{1,0:T(8,128)(2,1)}, u32[]{:S(2)}, u32[]{:S(2)}) collective-permute-start(bf16[256,512]{1,0:T(8,128)(2,1)} %get-tuple-element.18), channel_id=1, source_target_pairs={{0,1},{1,0},{2,3},{3,2},{4,5},{5,4},{6,7},{7,6},{8,9},{9,8},{10,11... | collective-permute-start | bytes 786440 | tf_op jit(solution)/shard_map/ppermute | solution.py:117
  148.8 8.0 %copy-start.14 = (f32[1536]{0:T(1024)S(1)}, f32[1536]{0:T(1024)}, u32[]{:S(2)}) copy-start(f32[1536]{0:T(1024)} %mul.204) | copy-start | bytes 18436
  148.8 8.1 %copy-start.15 = (f32[1536]{0:T(1024)S(1)}, f32[1536]{0:T(1024)}, u32[]{:S(2)}) copy-start(f32[1536]{0:T(1024)} %mul.207) | copy-start | bytes 18436
  148.8 8.1 %copy-start.20 = (pred[640]{0:T(1024)(128)(4,1)S(1)}, pred[640]{0:T(1024)(128)(4,1)}, u32[]{:S(2)}) copy-start(pred[640]{0:T(1024)(128)(4,1)} %copy-done.19) | copy-start | bytes 1924
  148.8 8.1 %copy-start.22 = (pred[640]{0:T(1024)(128)(4,1)S(1)}, pred[640]{0:T(1024)(128)(4,1)}, u32[]{:S(2)}) copy-start(pred[640]{0:T(1024)(128)(4,1)} %copy-done.21) | copy-start | bytes 1924
  148.8 8.1 %copy-start.24 = (pred[640]{0:T(1024)(128)(4,1)S(1)}, pred[640]{0:T(1024)(128)(4,1)}, u32[]{:S(2)}) copy-start(pred[640]{0:T(1024)(128)(4,1)} %copy-done.23) | copy-start | bytes 1924
  148.9 8.1 %copy-start.26 = (pred[640]{0:T(1024)(128)(4,1)S(1)}, pred[640]{0:T(1024)(128)(4,1)}, u32[]{:S(2)}) copy-start(pred[640]{0:T(1024)(128)(4,1)} %copy-done.25) | copy-start | bytes 1924
  148.9 8.1 %copy-start.28 = (pred[640]{0:T(1024)(128)(4,1)S(1)}, pred[640]{0:T(1024)(128)(4,1)}, u32[]{:S(2)}) copy-start(pred[640]{0:T(1024)(128)(4,1)} %copy-done.27) | copy-start | bytes 1924
  148.9 8.1 %copy-start.30 = (pred[640]{0:T(1024)(128)(4,1)S(1)}, pred[640]{0:T(1024)(128)(4,1)}, u32[]{:S(2)}) copy-start(pred[640]{0:T(1024)(128)(4,1)} %copy-done.29) | copy-start | bytes 1924
  148.9 8.1 %copy-start.32 = (pred[640]{0:T(1024)(128)(4,1)S(1)}, pred[640]{0:T(1024)(128)(4,1)}, u32[]{:S(2)}) copy-start(pred[640]{0:T(1024)(128)(4,1)} %copy-done.31) | copy-start | bytes 1924
  175.3 5.1 %collective-permute-start.4 = (bf16[256,512]{1,0:T(8,128)(2,1)S(1)}, bf16[256,512]{1,0:T(8,128)(2,1)S(1)}, u32[]{:S(2)}, u32[]{:S(2)}) collective-permute-start(bf16[256,512]{1,0:T(8,128)(2,1)S(1)} %get-tuple-element.20), channel_id=1, source_target_pairs={{0,1},{1,0},{2,3},{3,2},{4,5},{5,4},{6,7},{7,6},{8,9},{9,8},{10,11... | collective-permute-start | bytes 786440 | tf_op jit(solution)/shard_map/ppermute | solution.py:117
  (10 other events, 41.8 us)
Sparse Core Ops, SparseCore 0:
  9.8 70.3 all-gather.2
  82.7 66.0 all-gather.4

commit v3 on v1

v3 whole, which is shorter than its diff:
```python
import jax
import jax.numpy as jnp
from jax import lax
from jax.sharding import PartitionSpec as P

LANE = 128
GROUP_DEVS = 4


def positions(row_ids, seq_starts):
    seq_begin = jnp.max(
        jnp.where(seq_starts[None, :] <= row_ids[:, None], seq_starts[None, :], 0), axis=1
    )
    return row_ids - seq_begin


def tap_table(tap_ids, long_filter):
    filter_len = long_filter.shape[0]
    one_hot = (
        tap_ids[:, :, None] == jnp.arange(filter_len, dtype=jnp.int32)[None, None, :]
    ).astype(jnp.bfloat16)
    return jnp.einsum(
        "ijt,tg->gij", one_hot, long_filter, preferred_element_type=jnp.float32
    ).astype(jnp.bfloat16)


def local(tokens, seq_lengths, in_weight, short_filter, long_filter, out_weight):
    rows, channels = tokens.shape
    width = short_filter.shape[0]
    filter_len, group_count = long_filter.shape
    per_group = channels // group_count
    n_seq = lax.axis_size("seq")
    s = lax.axis_index("seq")
    member = s % GROUP_DEVS
    part = LANE // GROUP_DEVS
    n_lblk = channels // LANE
    tail = filter_len + 8
    span = GROUP_DEVS * rows
    ext_rows = tail + span

    swaps = [[(i, i ^ d) for i in range(n_seq)] for d in range(1, GROUP_DEVS)]
    from_member = [tokens] + [lax.ppermute(tokens, "seq", perm) for perm in swaps]
    blocks = []
    for m in range(GROUP_DEVS):
        pick = from_member[0]
        for d in range(1, GROUP_DEVS):
            pick = jnp.where((member ^ d) == m, from_member[d], pick)
        blocks.append(pick)
    tail_src = tokens[rows - tail :]
    tail_tok = jnp.zeros_like(tail_src)
    for m in range(GROUP_DEVS):
        dist = m + 1
        perm = [(i - dist, i) for i in range(GROUP_DEVS, n_seq) if i % GROUP_DEVS == m]
        got = lax.ppermute(tail_src, "seq", perm)
        tail_tok = jnp.where(member == m, got, tail_tok)
    ext_tokens = jnp.concatenate([tail_tok] + blocks, axis=0)

    lengths_row = seq_lengths[0]
    seq_starts = jnp.cumsum(lengths_row) - lengths_row
    pair_start = (s // GROUP_DEVS) * span
    row_ids = pair_start - tail + jnp.arange(ext_rows, dtype=jnp.int32)
    position = positions(row_ids, seq_starts)

    offset = member * part
    w_t = in_weight.T.reshape(in_weight.shape[1] // LANE, LANE, channels)
    w_part = lax.dynamic_slice_in_dim(w_t, offset, part, axis=1)
    w_all = lax.all_gather(w_part, "fsdp", axis=0, tiled=True)
    own = n_lblk * part
    w_all = w_all.reshape(3 * own, channels)

    projected = jnp.dot(
        ext_tokens, w_all.T, preferred_element_type=jnp.float32
    ).astype(jnp.bfloat16)

    taps = short_filter.reshape(width, 3, n_lblk, LANE)
    taps = lax.dynamic_slice_in_dim(taps, offset, part, axis=3).reshape(width, 3 * own)

    start = 8
    feat_rows = ext_rows - start
    pos_f = position[start:]
    featured = jnp.zeros((feat_rows, 3 * own), jnp.float32)
    for tap_index in range(width):
        shifted = projected[start - tap_index : ext_rows - tap_index].astype(jnp.float32)
        featured = featured + taps[tap_index] * jnp.where(
            (pos_f >= tap_index)[:, None], shifted, 0.0
        )
    queries = featured[feat_rows - span :, :own]
    mixed_in = (featured[:, own : 2 * own] * featured[:, 2 * own :]).astype(jnp.bfloat16)

    sub = LANE // per_group
    lf = long_filter.reshape(filter_len, n_lblk, sub)
    lf = lax.dynamic_slice_in_dim(lf, offset // per_group, part // per_group, axis=2)
    lf = lf.reshape(filter_len, own // per_group)
    n_groups = own // per_group

    out_rows = jnp.arange(filter_len, dtype=jnp.int32)[:, None]
    src_rows = jnp.arange(filter_len, dtype=jnp.int32)[None, :]
    cur_tap = out_rows - src_rows
    prev_tap = out_rows + filter_len - src_rows
    cur_table = tap_table(cur_tap, lf)
    prev_table = tap_table(prev_tap, lf)

    n_blocks = span // filter_len
    mi_blocks = mixed_in.reshape(n_blocks + 1, filter_len, n_groups, per_group)
    pos_out = position[tail:].reshape(n_blocks, filter_len)
    cur_kernel = jnp.where(
        (cur_tap[None] <= pos_out[:, :, None])[:, None], cur_table[None], 0.0
    ).astype(jnp.bfloat16)
    prev_kernel = jnp.where(
        (prev_tap[None] <= pos_out[:, :, None])[:, None], prev_table[None], 0.0
    ).astype(jnp.bfloat16)
    filtered = jnp.einsum(
        "bgij,bjgc->bigc", cur_kernel, mi_blocks[1:], preferred_element_type=jnp.float32
    )
    filtered = filtered + jnp.einsum(
        "bgij,bjgc->bigc", prev_kernel, mi_blocks[:-1], preferred_element_type=jnp.float32
    )
    filtered = filtered.reshape(span, own)
    gated = (queries * filtered).astype(jnp.bfloat16)

    gated = gated.reshape(GROUP_DEVS, rows, own)
    ow = out_weight.reshape(n_lblk, LANE, channels)
    pieces = []
    weights = []
    for d in range(GROUP_DEVS):
        send = lax.dynamic_index_in_dim(gated, member ^ d, axis=0, keepdims=False)
        got = send if d == 0 else lax.ppermute(send, "seq", swaps[d - 1])
        pieces.append(got)
        src_offset = (member ^ d) * part
        weights.append(lax.dynamic_slice_in_dim(ow, src_offset, part, axis=1).reshape(own, channels))
    result = tokens.astype(jnp.float32) + jnp.dot(
        jnp.concatenate(pieces, axis=1),
        jnp.concatenate(weights, axis=0),
        preferred_element_type=jnp.float32,
    )
    return result.astype(jnp.bfloat16)


def solution(mesh):
    in_specs = (P(("fsdp", "seq"), None), P("fsdp", None), P(None, "fsdp"), P(), P(), P())
    out_specs = P(("fsdp", "seq"), None)
    return jax.shard_map(local, mesh=mesh, in_specs=in_specs, out_specs=out_specs, check_vma=False)
```

time: 172 us -> 158 us (0.919)
  the two profiles are of different devices: /device:TPU:1 before, /device:TPU:191 now
where the time goes in v3:
time: 158 us; the launch traced here: 157 us
  matrix products  35.3 us (22%)
  waiting for transfers between devices  34.9 us (22%)
  local copies, waits for them, and re-layouts  32.7 us (21%)
  other arithmetic  25.9 us (16%)
  starting transfers between devices  14.6 us (9%)
  between operations  13.7 us (9%)
    ppermute x3, waiting for transfers between devices, local(): lax.ppermute(tokens, 'seq', perm)  27.3 us
    dot_general x1, matrix products, local(): jnp.dot(ext_tokens, w_all.T, preferred_element_type=jnp.float32)  11.2 us
    add x1, other arithmetic, local(): featured + taps[tap_index] * jnp.where((pos_f >= tap_index)[:, None], shi...  10.7 us
    dot_general x2, matrix products, tap_table(): jnp.einsum('ijt,tg->gij', one_hot, long_filter, preferred_element_type=jn...  10.2 us
    ppermute x4, starting transfers between devices, local(): got = lax.ppermute(tail_src, 'seq', perm)  10.1 us
    unnamed x4, other arithmetic  8.56 us
    ppermute x3, waiting for transfers between devices, local(): got = send if d == 0 else lax.ppermute(send, 'seq', swaps[d - 1])  7.61 us
    unnamed x20, local copies, waits for them, and re-layouts  7.33 us
  transfers between devices with their start and end apart: 11, of which 4 were waited for; matrix products, arithmetic and copies ran while one was open for 24% of the time, Pallas kernels for 0%

profile of v3, /device:TPU:191, one launch (start us, length us, event | category | flops | bytes accessed | tf_op | source)
XLA Modules:
  0.0 157.2 jit_solution(12705590557110594950)
XLA Ops:
  6.6 2.7 %copy.28 = bf16[2048,384]{0,1:T(8,128)(2,1)} copy(bf16[2048,384]{1,0:T(8,128)(2,1)} %param.8) | data formatting | bytes 3145728 | tf_op args[2]
  9.3 1.8 %constant_dynamic-slice_fusion.11 = bf16[3,32,2048]{2,1,0:T(8,128)(2,1)} fusion(bf16[3,128,2048]{2,1,0:T(8,128)(2,1)} %bitcast.72, s32[]{:T(128)S(6)} %select_n.178), kind=kLoop, calls=%fused_computation.78 | loop fusion | bytes 786436 | tf_op jit(solution)/shard_map/dynamic_slice | solution.py:66
  11.1 1.9 %slice.81 = bf16[136,2048]{1,0:T(8,128)(2,1)} slice(bf16[256,2048]{1,0:T(8,128)(2,1)} %param.6), slice={[120:256], [0:2048]} | slice | bytes 1114112 | tf_op jit(solution)/shard_map/slice | solution.py:49
  13.0 3.1 %collective-permute-start = (bf16[136,2048]{1,0:T(8,128)(2,1)}, bf16[136,2048]{1,0:T(8,128)(2,1)}, u32[]{:S(2)}, u32[]{:S(2)}) collective-permute-start(bf16[136,2048]{1,0:T(8,128)(2,1)} %slice.81), channel_id=1, source_target_pairs={{3,7},{7,11},{11,15},{19,23},{23,27},{27,31},{35,39},{39,43},{43,4... | collective-permute-start | bytes 1671176 | tf_op jit(solution)/shard_map/ppermute | solution.py:54
  16.1 2.8 %collective-permute-start.1 = (bf16[136,2048]{1,0:T(8,128)(2,1)}, bf16[136,2048]{1,0:T(8,128)(2,1)}, u32[]{:S(2)}, u32[]{:S(2)}) collective-permute-start(bf16[136,2048]{1,0:T(8,128)(2,1)} %slice.81), channel_id=1, source_target_pairs={{3,6},{7,10},{11,14},{19,22},{23,26},{27,30},{35,38},{39,42},{43,4... | collective-permute-start | bytes 1671176 | tf_op jit(solution)/shard_map/ppermute | solution.py:54
  18.9 2.1 %collective-permute-start.2 = (bf16[136,2048]{1,0:T(8,128)(2,1)}, bf16[136,2048]{1,0:T(8,128)(2,1)}, u32[]{:S(2)}, u32[]{:S(2)}) collective-permute-start(bf16[136,2048]{1,0:T(8,128)(2,1)} %slice.81), channel_id=1, source_target_pairs={{3,5},{7,9},{11,13},{19,21},{23,25},{27,29},{35,37},{39,41},{43,45... | collective-permute-start | bytes 1671176 | tf_op jit(solution)/shard_map/ppermute | solution.py:54
  21.0 2.1 %collective-permute-start.3 = (bf16[136,2048]{1,0:T(8,128)(2,1)}, bf16[136,2048]{1,0:T(8,128)(2,1)}, u32[]{:S(2)}, u32[]{:S(2)}) collective-permute-start(bf16[136,2048]{1,0:T(8,128)(2,1)} %slice.81), channel_id=1, source_target_pairs={{3,4},{7,8},{11,12},{19,20},{23,24},{27,28},{35,36},{39,40},{43,44... | collective-permute-start | bytes 1671176 | tf_op jit(solution)/shard_map/ppermute | solution.py:54
  24.4 5.1 %fusion.32 = bf16[32,128,128]{2,0,1:T(8,128)(2,1)} fusion(bf16[128,32,1]{0,1,2:T(8,128)(2,1)S(1)} %bitcast.82, s32[128,128]{1,0:T(8,128)S(1)} %get-tuple-element.31), kind=kOutput, calls=%fused_computation.34 | convolution fusion | flops 136839168 | bytes 1122304 | tf_op jit(solution)/shard_map/ijt,tg->gij/dot_general | solution.py:22
  29.6 5.1 %fusion.33 = bf16[32,128,128]{2,0,1:T(8,128)(2,1)} fusion(bf16[128,32,1]{0,1,2:T(8,128)(2,1)S(1)} %bitcast.83, s32[128,128]{1,0:T(8,128)S(1)} %get-tuple-element.32), kind=kOutput, calls=%fused_computation.35 | convolution fusion | flops 136839168 | bytes 1122304 | tf_op jit(solution)/shard_map/ijt,tg->gij/dot_general | solution.py:22
  34.7 2.1 %collective-permute-start.6 = (bf16[256,2048]{1,0:T(8,128)(2,1)S(1)}, bf16[256,2048]{1,0:T(8,128)(2,1)}, u32[]{:S(2)}, u32[]{:S(2)}) collective-permute-start(bf16[256,2048]{1,0:T(8,128)(2,1)S(1)} %copy-done.1), channel_id=1, source_target_pairs={{0,1},{1,0},{2,3},{3,2},{4,5},{5,4},{6,7},{7,6},{8,9},{9,8},{10,11... | collective-permute-start | bytes 3145736 | tf_op jit(solution)/shard_map/ppermute | solution.py:42
  40.3 2.6 %copy.34 = bf16[32,128,128]{2,1,0:T(8,128)(2,1)} copy(bf16[32,128,128]{2,0,1:T(8,128)(2,1)} %fusion.32) | data formatting | bytes 2097152 | tf_op jit(solution)/shard_map/convert_element_type | solution.py:24
  42.8 2.6 %copy.31 = bf16[32,128,128]{2,1,0:T(8,128)(2,1)} copy(bf16[32,128,128]{2,0,1:T(8,128)(2,1)} %fusion.33) | data formatting | bytes 2097152 | tf_op jit(solution)/shard_map/convert_element_type | solution.py:24
  47.1 2.3 %select_dynamic-update-slice_fusion.4 = bf16[1160,2048]{1,0:T(8,128)(2,1)} fusion(bf16[136,2048]{1,0:T(8,128)(2,1)} %collective-permute-done, bf16[136,2048]{1,0:T(8,128)(2,1)} %collective-permute-done.1, bf16[136,2048]{1,0:T(8,128)(2,1)} %collective-permute-done.2, bf16[136,2048]{1,0:T(8,128)(2,1)} %collective-permute-done.3, pred[]{:T(512)S(6)} %eq.79, ...), kind=kLoop, calls=%fused_computation.49 | loop fusion | flops 1114111 | bytes 2785284
  49.4 5.1 %collective-permute-done.4 = bf16[256,2048]{1,0:T(8,128)(2,1)S(1)} collective-permute-done((bf16[256,2048]{1,0:T(8,128)(2,1)S(1)}, bf16[256,2048]{1,0:T(8,128)(2,1)S(1)}, u32[]{:S(2)}, u32[]{:S(2)}) %collective-permute-start.4) | collective-permute-done | bytes 1048608 | tf_op jit(solution)/shard_map/ppermute | solution.py:42
  54.5 22.2 %collective-permute-done.5 = bf16[256,2048]{1,0:T(8,128)(2,1)S(1)} collective-permute-done((bf16[256,2048]{1,0:T(8,128)(2,1)S(1)}, bf16[256,2048]{1,0:T(8,128)(2,1)S(1)}, u32[]{:S(2)}, u32[]{:S(2)}) %collective-permute-start.5) | collective-permute-done | bytes 1048608 | tf_op jit(solution)/shard_map/ppermute | solution.py:42
  76.7 1.7 %select_dynamic-update-slice_fusion.3 = bf16[1160,2048]{1,0:T(8,128)(2,1)} fusion(bf16[1160,2048]{1,0:T(8,128)(2,1)} %select_dynamic-update-slice_fusion.4, bf16[256,2048]{1,0:T(8,128)(2,1)S(1)} %collective-permute-done.4, bf16[256,2048]{1,0:T(8,128)(2,1)S(1)} %collective-permute-done.5, bf16[256,2048]{1,0:T(8,128)(2,1)} %collective-permute-done.6, ...), kind=kLoop, calls=%fused_computation.48 | loop fusion | flops 1572864 | bytes 5242883
  78.3 1.7 %select_dynamic-update-slice_fusion.2 = bf16[1160,2048]{1,0:T(8,128)(2,1)} fusion(bf16[1160,2048]{1,0:T(8,128)(2,1)} %select_dynamic-update-slice_fusion.3, bf16[256,2048]{1,0:T(8,128)(2,1)S(1)} %collective-permute-done.4, bf16[256,2048]{1,0:T(8,128)(2,1)S(1)} %collective-permute-done.5, bf16[256,2048]{1,0:T(8,128)(2,1)} %collective-permute-done.6, ...), kind=kLoop, calls=%fused_computation.47 | loop fusion | flops 1572864 | bytes 5242883
  80.1 2.9 %select_dynamic-update-slice_fusion.1 = bf16[1160,2048]{1,0:T(8,128)(2,1)} fusion(bf16[1160,2048]{1,0:T(8,128)(2,1)} %select_dynamic-update-slice_fusion.2, bf16[256,2048]{1,0:T(8,128)(2,1)S(1)} %collective-permute-done.4, bf16[256,2048]{1,0:T(8,128)(2,1)S(1)} %collective-permute-done.5, bf16[256,2048]{1,0:T(8,128)(2,1)} %collective-permute-done.6, ...), kind=kLoop, calls=%fused_computation.46 | loop fusion | flops 1572864 | bytes 5242883
  83.0 1.7 %select_dynamic-update-slice_fusion = bf16[1160,2048]{1,0:T(8,128)(2,1)} fusion(bf16[1160,2048]{1,0:T(8,128)(2,1)} %select_dynamic-update-slice_fusion.1, bf16[256,2048]{1,0:T(8,128)(2,1)S(1)} %collective-permute-done.4, bf16[256,2048]{1,0:T(8,128)(2,1)S(1)} %collective-permute-done.5, bf16[256,2048]{1,0:T(8,128)(2,1)} %collective-permute-done.6, ...), kind=kLoop, calls=%fused_computation.45 | loop fusion | flops 1572864 | bytes 5242883 | tf_op jit(solution)/shard_map/concatenate | solution.py:56
  84.6 11.2 %convolution_convert_fusion = bf16[1160,1536]{1,0:T(8,128)(2,1)S(1)} fusion(bf16[1160,2048]{1,0:T(8,128)(2,1)} %select_dynamic-update-slice_fusion, bf16[1536,2048]{1,0:T(8,128)(2,1)} %bitcast.84), kind=kOutput, calls=%fused_computation.18 | convolution fusion | flops 7299870720 | bytes 14606336 | tf_op jit(solution)/shard_map/dot_general | solution.py:71
  95.8 10.7 %multiply_add_fusion = f32[1152,1536]{1,0:T(8,128)S(1)} fusion(bf16[1160,1536]{1,0:T(8,128)(2,1)S(1)} %convolution_convert_fusion, f32[1536]{0:T(1024)S(1)} %mul.112, f32[1536]{0:T(1024)S(1)} %mul.109, f32[1536]{0:T(1024)S(1)} %mul.106, f32[1536]{0:T(1024)S(1)} %mul.103, f32[1536]{0:T(1024)S(1)} %mul.100, f32[1536]{0:T(1024)S(1)} %mul.97, f32[1536]{0:T(1024)S(1)} %mul.93, ...), kind=kLoop, calls=%fused_computation.19 | loop fusion | flops 47775744 | bytes 31901568 | tf_op jit(solution)/shard_map/add | solution.py:84
  106.9 1.5 fusion.47
  113.5 6.1 %fusion.8 = f32[8,32,16,128]{3,2,1,0:T(8,128)S(1)} fusion(pred[8,128,128]{2,1,0:T(8,128)(4,1)S(1)} %copy-done.4, bf16[32,128,128]{2,1,0:T(8,128)(2,1)} %copy.34, bf16[8,128,32,16]{1,0,3,2:T(8,128)(2,1)} %bitcast.77), kind=kOutput, calls=%fused_computation.8 | convolution fusion | flops 138412032 | bytes 4325376 | tf_op jit(solution)/shard_map/bgij,bjgc->bigc/dot_general | solution.py:115
  119.6 4.5 %add_bitcast_fusion = f32[8,128,32,16]{1,3,2,0:T(8,128)S(1)} fusion(f32[8,32,16,128]{3,2,1,0:T(8,128)S(1)} %fusion.8, pred[8,128,128]{2,1,0:T(8,128)(4,1)S(1)} %get-tuple-element.29, bf16[32,128,128]{2,1,0:T(8,128)(2,1)S(1)} %copy-done.2, bf16[8,128,32,16]{1,0,3,2:T(8,128)(2,1)S(1)} %bitcast.78), kind=kOutput, calls=%fused_computation.33 | convolution fusion | flops 138936320 | bytes 6422528 | tf_op jit(solution)/shard_map/bgij,bjgc->bigc/dot_general | solution.py:112
  125.3 1.8 %copy.47 = f32[64,8,8,128]{3,1,2,0:T(8,128)} copy(f32[64,8,8,128]{3,2,1,0:T(8,128)S(1)} %bitcast.67) | data formatting | bytes 4194304
  127.1 2.9 %copy.37 = f32[1024,512]{1,0:T(8,128)} copy(f32[1024,512]{0,1:T(8,128)} %bitcast.68) | data formatting | bytes 4194304 | tf_op jit(solution)/shard_map/reshape | solution.py:118
  130.0 2.6 %fusion.29 = bf16[1024,512]{1,0:T(8,128)(2,1)S(1)} fusion(f32[1024,512]{1,0:T(8,128)} %copy.37, f32[1152,1536]{1,0:T(8,128)} %copy-done), kind=kLoop, calls=%fused_computation.32 | loop fusion | flops 1048576 | bytes 5242880 | tf_op jit(solution)/shard_map/convert_element_type | solution.py:119
  133.3 1.7 %collective-permute-start.9 = (bf16[256,512]{1,0:T(8,128)(2,1)S(1)}, bf16[256,512]{1,0:T(8,128)(2,1)S(1)}, u32[]{:S(2)}, u32[]{:S(2)}) collective-permute-start(bf16[256,512]{1,0:T(8,128)(2,1)S(1)} %get-tuple-element.12), channel_id=1, source_target_pairs={{0,3},{1,2},{2,1},{3,0},{4,7},{5,6},{6,5},{7,4},{8,11},{9,10},{10,... | collective-permute-start | bytes 786440 | tf_op jit(solution)/shard_map/ppermute | solution.py:127
  135.0 4.3 %constant_dynamic-slice_fusion.9 = (bf16[16,32,2048]{2,1,0:T(8,128)(2,1)S(1)}, bf16[16,32,2048]{2,1,0:T(8,128)(2,1)S(1)}, bf16[16,32,2048]{2,1,0:T(8,128)(2,1)S(1)}, bf16[16,32,2048]{2,1,0:T(8,128)(2,1)S(1)}) fusion(bf16[16,128,2048]{2,1,0:T(8,128)(2,1)} %bitcast.66, s32[]{:T(128)S(6)} %select_n.178, s32[]{:T(128)S(6)} %select_n.230, s32[]{:T(128)S(6)} %select_n.229, ...), kind=kLoop, calls=%fused_computation.76 | loop fusion | bytes 16777232 | tf_op jit(solution)/shard_map/dynamic_slice | solution.py:130
  139.4 1.8 %collective-permute-done.8 = bf16[256,512]{1,0:T(8,128)(2,1)S(1)} collective-permute-done((bf16[256,512]{1,0:T(8,128)(2,1)S(1)}, bf16[256,512]{1,0:T(8,128)(2,1)S(1)}, u32[]{:S(2)}, u32[]{:S(2)}) %collective-permute-start.8) | collective-permute-done | bytes 262176 | tf_op jit(solution)/shard_map/ppermute | solution.py:127
  141.2 5.8 %collective-permute-done.9 = bf16[256,512]{1,0:T(8,128)(2,1)S(1)} collective-permute-done((bf16[256,512]{1,0:T(8,128)(2,1)S(1)}, bf16[256,512]{1,0:T(8,128)(2,1)S(1)}, u32[]{:S(2)}, u32[]{:S(2)}) %collective-permute-start.9) | collective-permute-done | bytes 262176 | tf_op jit(solution)/shard_map/ppermute | solution.py:127
  147.0 3.3 %fusion.25 = bf16[256,2048]{1,0:T(8,128)(2,1)} fusion(bf16[512,2048]{1,0:T(8,128)(2,1)S(1)} %bitcast.74, bf16[512,2048]{1,0:T(8,128)(2,1)S(1)} %bitcast.75, bf16[512,2048]{1,0:T(8,128)(2,1)S(1)} %bitcast.76, bf16[512,2048]{1,0:T(8,128)(2,1)S(1)} %bitcast.73, bf16[256,2048]{1,0:T(8,128)(2,1)S(1)} %copy-done.1, ...), kind=kOutput, calls=%fused_computation.27 | convolution fusion | flops 2186805248 | bytes 11534336 | tf_op jit(solution)/shard_map/dot_general | solution.py:131
  (55 shorter events, 13.6 us)
Async XLA Ops:
  6.5 16.6 %copy-start.1 = (bf16[256,2048]{1,0:T(8,128)(2,1)S(1)}, bf16[256,2048]{1,0:T(8,128)(2,1)}, u32[]{:S(2)}) copy-start(bf16[256,2048]{1,0:T(8,128)(2,1)} %param.6) | copy-start | bytes 3145732
  6.5 16.6 %copy-start.6 = (s32[1,4]{1,0:T(1,128)S(1)}, s32[1,4]{1,0:T(1,128)}, u32[]{:S(2)}) copy-start(s32[1,4]{1,0:T(1,128)} %param.7) | copy-start | bytes 52
  6.5 16.8 %copy-start.5 = (bf16[128,128]{1,0:T(8,128)(2,1)S(1)}, bf16[128,128]{1,0:T(8,128)(2,1)}, u32[]{:S(2)}) copy-start(bf16[128,128]{1,0:T(8,128)(2,1)} %param.10) | copy-start | bytes 98308
  6.5 17.9 %copy-start.3 = (f32[7,6144]{1,0:T(8,128)S(1)}, f32[7,6144]{1,0:T(8,128)}, u32[]{:S(2)}) copy-start(f32[7,6144]{1,0:T(8,128)} %param.9) | copy-start | bytes 516100
  6.5 78.1 %all-gather.2.cloned.1.call-start = ((), (), s32[]{:S(2)}) async-start(), calls=%async_computation | async-start | bytes 6684672 | tf_op jit(solution)/shard_map/all_gather | solution.py:67
  13.0 21.7 %collective-permute-start = (bf16[136,2048]{1,0:T(8,128)(2,1)}, bf16[136,2048]{1,0:T(8,128)(2,1)}, u32[]{:S(2)}, u32[]{:S(2)}) collective-permute-start(bf16[136,2048]{1,0:T(8,128)(2,1)} %slice.81), channel_id=1, source_target_pairs={{3,7},{7,11},{11,15},{19,23},{23,27},{27,31},{35,39},{39,43},{43,4... | collective-permute-start | bytes 1671176 | tf_op jit(solution)/shard_map/ppermute | solution.py:54
  16.1 18.6 %collective-permute-start.1 = (bf16[136,2048]{1,0:T(8,128)(2,1)}, bf16[136,2048]{1,0:T(8,128)(2,1)}, u32[]{:S(2)}, u32[]{:S(2)}) collective-permute-start(bf16[136,2048]{1,0:T(8,128)(2,1)} %slice.81), channel_id=1, source_target_pairs={{3,6},{7,10},{11,14},{19,22},{23,26},{27,30},{35,38},{39,42},{43,4... | collective-permute-start | bytes 1671176 | tf_op jit(solution)/shard_map/ppermute | solution.py:54
  18.9 28.2 %collective-permute-start.2 = (bf16[136,2048]{1,0:T(8,128)(2,1)}, bf16[136,2048]{1,0:T(8,128)(2,1)}, u32[]{:S(2)}, u32[]{:S(2)}) collective-permute-start(bf16[136,2048]{1,0:T(8,128)(2,1)} %slice.81), channel_id=1, source_target_pairs={{3,5},{7,9},{11,13},{19,21},{23,25},{27,29},{35,37},{39,41},{43,45... | collective-permute-start | bytes 1671176 | tf_op jit(solution)/shard_map/ppermute | solution.py:54
  21.0 26.1 %collective-permute-start.3 = (bf16[136,2048]{1,0:T(8,128)(2,1)}, bf16[136,2048]{1,0:T(8,128)(2,1)}, u32[]{:S(2)}, u32[]{:S(2)}) collective-permute-start(bf16[136,2048]{1,0:T(8,128)(2,1)} %slice.81), channel_id=1, source_target_pairs={{3,4},{7,8},{11,12},{19,20},{23,24},{27,28},{35,36},{39,40},{43,44... | collective-permute-start | bytes 1671176 | tf_op jit(solution)/shard_map/ppermute | solution.py:54
  23.1 31.4 %collective-permute-start.4 = (bf16[256,2048]{1,0:T(8,128)(2,1)S(1)}, bf16[256,2048]{1,0:T(8,128)(2,1)S(1)}, u32[]{:S(2)}, u32[]{:S(2)}) collective-permute-start(bf16[256,2048]{1,0:T(8,128)(2,1)S(1)} %copy-done.1), channel_id=1, source_target_pairs={{0,3},{1,2},{2,1},{3,0},{4,7},{5,6},{6,5},{7,4},{8,11},{9,10},{10,... | collective-permute-start | bytes 3145736 | tf_op jit(solution)/shard_map/ppermute | solution.py:42
  34.7 42.0 %collective-permute-start.5 = (bf16[256,2048]{1,0:T(8,128)(2,1)S(1)}, bf16[256,2048]{1,0:T(8,128)(2,1)S(1)}, u32[]{:S(2)}, u32[]{:S(2)}) collective-permute-start(bf16[256,2048]{1,0:T(8,128)(2,1)S(1)} %copy-done.1), channel_id=1, source_target_pairs={{0,2},{1,3},{2,0},{3,1},{4,6},{5,7},{6,4},{7,5},{8,10},{9,11},{10,... | collective-permute-start | bytes 3145736 | tf_op jit(solution)/shard_map/ppermute | solution.py:42
  34.7 42.0 %collective-permute-start.6 = (bf16[256,2048]{1,0:T(8,128)(2,1)S(1)}, bf16[256,2048]{1,0:T(8,128)(2,1)}, u32[]{:S(2)}, u32[]{:S(2)}) collective-permute-start(bf16[256,2048]{1,0:T(8,128)(2,1)S(1)} %copy-done.1), channel_id=1, source_target_pairs={{0,1},{1,0},{2,3},{3,2},{4,5},{5,4},{6,7},{7,6},{8,9},{9,8},{10,11... | collective-permute-start | bytes 3145736 | tf_op jit(solution)/shard_map/ppermute | solution.py:42
  106.5 3.2 %copy-start = (f32[1152,1536]{1,0:T(8,128)}, f32[1152,1536]{1,0:T(8,128)S(1)}, u32[]{:S(2)}) copy-start(f32[1152,1536]{1,0:T(8,128)S(1)} %multiply_add_fusion) | copy-start | bytes 21233668
  109.7 3.8 %copy-start.4 = (pred[8,128,128]{2,1,0:T(8,128)(4,1)S(1)}, pred[8,128,128]{2,1,0:T(8,128)(4,1)}, u32[]{:S(2)}) copy-start(pred[8,128,128]{2,1,0:T(8,128)(4,1)} %get-tuple-element.30) | copy-start | bytes 393220
  113.5 6.1 %copy-start.2 = (bf16[32,128,128]{2,1,0:T(8,128)(2,1)S(1)}, bf16[32,128,128]{2,1,0:T(8,128)(2,1)}, u32[]{:S(2)}) copy-start(bf16[32,128,128]{2,1,0:T(8,128)(2,1)} %copy.31) | copy-start | bytes 3145732
  132.7 6.6 %collective-permute-start.7 = (bf16[256,512]{1,0:T(8,128)(2,1)S(1)}, bf16[256,512]{1,0:T(8,128)(2,1)S(1)}, u32[]{:S(2)}, u32[]{:S(2)}) collective-permute-start(bf16[256,512]{1,0:T(8,128)(2,1)S(1)} %get-tuple-element.14), channel_id=1, source_target_pairs={{0,1},{1,0},{2,3},{3,2},{4,5},{5,4},{6,7},{7,6},{8,9},{9,8},{10,11... | collective-permute-start | bytes 786440 | tf_op jit(solution)/shard_map/ppermute | solution.py:127
  133.3 7.9 %collective-permute-start.8 = (bf16[256,512]{1,0:T(8,128)(2,1)S(1)}, bf16[256,512]{1,0:T(8,128)(2,1)S(1)}, u32[]{:S(2)}, u32[]{:S(2)}) collective-permute-start(bf16[256,512]{1,0:T(8,128)(2,1)S(1)} %get-tuple-element.13), channel_id=1, source_target_pairs={{0,2},{1,3},{2,0},{3,1},{4,6},{5,7},{6,4},{7,5},{8,10},{9,11},{10,... | collective-permute-start | bytes 786440 | tf_op jit(solution)/shard_map/ppermute | solution.py:127
  133.3 13.7 %collective-permute-start.9 = (bf16[256,512]{1,0:T(8,128)(2,1)S(1)}, bf16[256,512]{1,0:T(8,128)(2,1)S(1)}, u32[]{:S(2)}, u32[]{:S(2)}) collective-permute-start(bf16[256,512]{1,0:T(8,128)(2,1)S(1)} %get-tuple-element.12), channel_id=1, source_target_pairs={{0,3},{1,2},{2,1},{3,0},{4,7},{5,6},{6,5},{7,4},{8,11},{9,10},{10,... | collective-permute-start | bytes 786440 | tf_op jit(solution)/shard_map/ppermute | solution.py:127
Sparse Core Ops, SparseCore 0:
  11.2 65.3 all-gather.1

commit v4 on v3

--- a/solution.py
+++ b/solution.py
@@ -68,6 +68,13 @@
     own = n_lblk * part
     w_all = w_all.reshape(3 * own, channels)
 
+    ow = out_weight.reshape(n_lblk, LANE, channels)
+    weights = []
+    for d in range(GROUP_DEVS):
+        src_offset = (member ^ d) * part
+        weights.append(lax.dynamic_slice_in_dim(ow, src_offset, part, axis=1).reshape(own, channels))
+    ow_cat = jnp.concatenate(weights, axis=0)
+    ext_tokens, ow_cat = lax.optimization_barrier((ext_tokens, ow_cat))
     projected = jnp.dot(
         ext_tokens, w_all.T, preferred_element_type=jnp.float32
     ).astype(jnp.bfloat16)
@@ -101,7 +108,6 @@
     prev_table = tap_table(prev_tap, lf)
 
     n_blocks = span // filter_len
-    mi_blocks = mixed_in.reshape(n_blocks + 1, filter_len, n_groups, per_group)
     pos_out = position[tail:].reshape(n_blocks, filter_len)
     cur_kernel = jnp.where(
         (cur_tap[None] <= pos_out[:, :, None])[:, None], cur_table[None], 0.0
@@ -109,28 +115,28 @@
     prev_kernel = jnp.where(
         (prev_tap[None] <= pos_out[:, :, None])[:, None], prev_table[None], 0.0
     ).astype(jnp.bfloat16)
+
+    mi_t = mixed_in.T.reshape(n_groups, per_group, n_blocks + 1, filter_len)
     filtered = jnp.einsum(
-        "bgij,bjgc->bigc", cur_kernel, mi_blocks[1:], preferred_element_type=jnp.float32
+        "gcbj,bgij->gcbi", mi_t[:, :, 1:], cur_kernel, preferred_element_type=jnp.float32
     )
     filtered = filtered + jnp.einsum(
-        "bgij,bjgc->bigc", prev_kernel, mi_blocks[:-1], preferred_element_type=jnp.float32
+        "gcbj,bgij->gcbi", mi_t[:, :, :-1], prev_kernel, preferred_element_type=jnp.float32
     )
-    filtered = filtered.reshape(span, own)
-    gated = (queries * filtered).astype(jnp.bfloat16)
+    filtered = filtered.reshape(own, span)
+    gated = (queries.T * filtered).astype(jnp.bfloat16)
 
-    gated = gated.reshape(GROUP_DEVS, rows, own)
-    ow = out_weight.reshape(n_lblk, LANE, channels)
+
+    gated = gated.reshape(own, GROUP_DEVS, rows)
     pieces = []
-    weights = []
     for d in range(GROUP_DEVS):
-        send = lax.dynamic_index_in_dim(gated, member ^ d, axis=0, keepdims=False)
+        send = lax.dynamic_index_in_dim(gated, member ^ d, axis=1, keepdims=False)
         got = send if d == 0 else lax.ppermute(send, "seq", swaps[d - 1])
         pieces.append(got)
-        src_offset = (member ^ d) * part
-        weights.append(lax.dynamic_slice_in_dim(ow, src_offset, part, axis=1).reshape(own, channels))
-    result = tokens.astype(jnp.float32) + jnp.dot(
-        jnp.concatenate(pieces, axis=1),
-        jnp.concatenate(weights, axis=0),
+    result = tokens.astype(jnp.float32) + lax.dot_general(
+        jnp.concatenate(pieces, axis=0),
+        ow_cat,
+        (((0,), (0,)), ((), ())),
         preferred_element_type=jnp.float32,
     )
     return result.astype(jnp.bfloat16)

time: 158 us -> 155 us (0.981)
  the two profiles are of different devices: /device:TPU:191 before, /device:TPU:1 now
where the time goes in v4:
time: 155 us
  matrix products  36 us (23%)
  waiting for transfers between devices  34.4 us (22%)
  other arithmetic  28.2 us (18%)
  local copies, waits for them, and re-layouts  25.5 us (16%)
  starting transfers between devices  16.9 us (11%)
  between operations  13.6 us (9%)
    ppermute x3, waiting for transfers between devices, local(): lax.ppermute(tokens, 'seq', perm)  15.4 us
    ppermute x3, waiting for transfers between devices, local(): got = send if d == 0 else lax.ppermute(send, 'seq', swaps[d - 1])  11.9 us
    dot_general x1, matrix products, local(): jnp.dot(ext_tokens, w_all.T, preferred_element_type=jnp.float32)  11.2 us
    add x1, other arithmetic, local(): featured + taps[tap_index] * jnp.where((pos_f >= tap_index)[:, None], shi...  10.7 us
    ppermute x3, starting transfers between devices, local(): lax.ppermute(tokens, 'seq', perm)  9.3 us
    unnamed x14, local copies, waits for them, and re-layouts  8.3 us
    dot_general x2, matrix products, tap_table(): jnp.einsum('ijt,tg->gij', one_hot, long_filter, preferred_element_type=jn...  7.92 us
    unnamed x4, other arithmetic  7.38 us
  transfers between devices with their start and end apart: 11, of which 4 were waited for; matrix products, arithmetic and copies ran while one was open for 22% of the time, Pallas kernels for 0%

profile of v4, /device:TPU:1, one launch (start us, length us, event | category | flops | bytes accessed | tf_op | source)
XLA Modules:
  0.0 154.6 jit_solution(15902551098110903809)
XLA Ops:
  6.5 1.8 %copy.26 = bf16[2048,384]{0,1:T(8,128)(2,1)S(1)} copy(bf16[2048,384]{1,0:T(8,128)(2,1)} %param.8) | data formatting | bytes 3145728 | tf_op args[2]
  11.0 1.5 collective-permute-start.1
  12.4 1.5 collective-permute-start.2
  13.9 1.5 collective-permute-start.3
  15.4 3.0 %collective-permute-start.4 = (bf16[256,2048]{1,0:T(8,128)(2,1)S(1)}, bf16[256,2048]{1,0:T(8,128)(2,1)S(1)}, u32[]{:S(2)}, u32[]{:S(2)}) collective-permute-start(bf16[256,2048]{1,0:T(8,128)(2,1)S(1)} %copy-done.1), channel_id=1, source_target_pairs={{0,3},{1,2},{2,1},{3,0},{4,7},{5,6},{6,5},{7,4},{8,11},{9,10},{10,... | collective-permute-start | bytes 3145736 | tf_op jit(solution)/shard_map/ppermute | solution.py:42
  21.8 4.0 %fusion.20 = bf16[32,128,128]{2,0,1:T(8,128)(2,1)S(1)} fusion(bf16[128,32,1]{0,1,2:T(8,128)(2,1)S(1)} %bitcast.75, s32[128,128]{1,0:T(8,128)S(1)} %get-tuple-element.35), kind=kOutput, calls=%fused_computation.28 | convolution fusion | flops 136839168 | bytes 1122304 | tf_op jit(solution)/shard_map/ijt,tg->gij/dot_general | solution.py:22
  25.8 1.4 copy.31
  27.2 3.9 %fusion.21 = bf16[32,128,128]{2,0,1:T(8,128)(2,1)S(1)} fusion(bf16[128,32,1]{0,1,2:T(8,128)(2,1)S(1)} %bitcast.76, s32[128,128]{1,0:T(8,128)S(1)} %get-tuple-element.36), kind=kOutput, calls=%fused_computation.29 | convolution fusion | flops 136839168 | bytes 1122304 | tf_op jit(solution)/shard_map/ijt,tg->gij/dot_general | solution.py:22
  31.1 1.4 copy.28
  33.7 4.4 %constant_dynamic-slice_fusion.11 = (bf16[16,32,2048]{2,1,0:T(8,128)(2,1)S(1)}, bf16[16,32,2048]{2,1,0:T(8,128)(2,1)S(1)}, bf16[16,32,2048]{2,1,0:T(8,128)(2,1)S(1)}, bf16[16,32,2048]{2,1,0:T(8,128)(2,1)S(1)}) fusion(bf16[16,128,2048]{2,1,0:T(8,128)(2,1)} %bitcast.63, s32[]{:T(128)S(6)} %select_n.178, s32[]{:T(128)S(6)} %select_n.215, s32[]{:T(128)S(6)} %select_n.214, ...), kind=kLoop, calls=%fused_computation.73 | loop fusion | bytes 16777232 | tf_op jit(solution)/shard_map/dynamic_slice | solution.py:75
  38.1 5.6 %collective-permute-start.5 = (bf16[256,2048]{1,0:T(8,128)(2,1)S(1)}, bf16[256,2048]{1,0:T(8,128)(2,1)S(1)}, u32[]{:S(2)}, u32[]{:S(2)}) collective-permute-start(bf16[256,2048]{1,0:T(8,128)(2,1)S(1)} %copy-done.1), channel_id=1, source_target_pairs={{0,2},{1,3},{2,0},{3,1},{4,6},{5,7},{6,4},{7,5},{8,10},{9,11},{10,... | collective-permute-start | bytes 3145736 | tf_op jit(solution)/shard_map/ppermute | solution.py:42
  44.4 4.1 %pad_maximum_fusion = bf16[2048,2048]{1,0:T(8,128)(2,1)} fusion(bf16[512,2048]{1,0:T(8,128)(2,1)S(1)} %bitcast.67, bf16[512,2048]{1,0:T(8,128)(2,1)S(1)} %bitcast.68, bf16[512,2048]{1,0:T(8,128)(2,1)S(1)} %bitcast.69, bf16[512,2048]{1,0:T(8,128)(2,1)S(1)} %bitcast.66), kind=kLoop, calls=%fused_computation | loop fusion | flops 33554432 | bytes 16777216 | tf_op jit(solution)/shard_map/concatenate | solution.py:76
  48.5 2.3 %select_dynamic-update-slice_fusion.4 = bf16[1160,2048]{1,0:T(8,128)(2,1)} fusion(bf16[136,2048]{1,0:T(8,128)(2,1)S(1)} %collective-permute-done, bf16[136,2048]{1,0:T(8,128)(2,1)} %collective-permute-done.1, bf16[136,2048]{1,0:T(8,128)(2,1)} %collective-permute-done.2, bf16[136,2048]{1,0:T(8,128)(2,1)} %collective-permute-done.3, pred[]{:T(512)S(6)} %eq.79, ...), kind=kLoop, calls=%fused_computation.44 | loop fusion | flops 1114111 | bytes 2785284
  50.7 15.4 %collective-permute-done.5 = bf16[256,2048]{1,0:T(8,128)(2,1)S(1)} collective-permute-done((bf16[256,2048]{1,0:T(8,128)(2,1)S(1)}, bf16[256,2048]{1,0:T(8,128)(2,1)S(1)}, u32[]{:S(2)}, u32[]{:S(2)}) %collective-permute-start.5) | collective-permute-done | bytes 1048608 | tf_op jit(solution)/shard_map/ppermute | solution.py:42
  66.1 1.7 %select_dynamic-update-slice_fusion.3 = bf16[1160,2048]{1,0:T(8,128)(2,1)} fusion(bf16[1160,2048]{1,0:T(8,128)(2,1)} %select_dynamic-update-slice_fusion.4, bf16[256,2048]{1,0:T(8,128)(2,1)S(1)} %collective-permute-done.4, bf16[256,2048]{1,0:T(8,128)(2,1)S(1)} %collective-permute-done.5, bf16[256,2048]{1,0:T(8,128)(2,1)S(1)} %collective-permute-done.6, ...), kind=kLoop, calls=%fused_computation.43 | loop fusion | flops 1572864 | bytes 5242883
  67.8 1.7 %select_dynamic-update-slice_fusion.2 = bf16[1160,2048]{1,0:T(8,128)(2,1)} fusion(bf16[1160,2048]{1,0:T(8,128)(2,1)} %select_dynamic-update-slice_fusion.3, bf16[256,2048]{1,0:T(8,128)(2,1)S(1)} %collective-permute-done.4, bf16[256,2048]{1,0:T(8,128)(2,1)S(1)} %collective-permute-done.5, bf16[256,2048]{1,0:T(8,128)(2,1)S(1)} %collective-permute-done.6, ...), kind=kLoop, calls=%fused_computation.42 | loop fusion | flops 1572864 | bytes 5242883
  69.5 1.7 %select_dynamic-update-slice_fusion.1 = bf16[1160,2048]{1,0:T(8,128)(2,1)} fusion(bf16[1160,2048]{1,0:T(8,128)(2,1)} %select_dynamic-update-slice_fusion.2, bf16[256,2048]{1,0:T(8,128)(2,1)S(1)} %collective-permute-done.4, bf16[256,2048]{1,0:T(8,128)(2,1)S(1)} %collective-permute-done.5, bf16[256,2048]{1,0:T(8,128)(2,1)S(1)} %collective-permute-done.6, ...), kind=kLoop, calls=%fused_computation.41 | loop fusion | flops 1572864 | bytes 5242883
  71.2 1.7 %select_dynamic-update-slice_fusion = bf16[1160,2048]{1,0:T(8,128)(2,1)} fusion(bf16[1160,2048]{1,0:T(8,128)(2,1)} %select_dynamic-update-slice_fusion.1, bf16[256,2048]{1,0:T(8,128)(2,1)S(1)} %collective-permute-done.4, bf16[256,2048]{1,0:T(8,128)(2,1)S(1)} %collective-permute-done.5, bf16[256,2048]{1,0:T(8,128)(2,1)S(1)} %collective-permute-done.6, ...), kind=kLoop, calls=%fused_computation.40 | loop fusion | flops 1572864 | bytes 5242883 | tf_op jit(solution)/shard_map/concatenate | solution.py:56
  72.9 7.1 %all-gather.2.cloned.1.call-done = bf16[48,32,2048]{2,1,0:T(8,128)(2,1)} async-done(((bf16[3,32,2048]{2,1,0:T(8,128)(2,1)}), bf16[48,32,2048]{2,1,0:T(8,128)(2,1)}) %all-gather.2.cloned.1.call-update) | async-done | bytes 6291472 | tf_op jit(solution)/shard_map/all_gather | solution.py:67
  80.0 11.2 %convolution_convert_fusion = bf16[1160,1536]{1,0:T(8,128)(2,1)S(1)} fusion(bf16[1160,2048]{1,0:T(8,128)(2,1)} %select_dynamic-update-slice_fusion, bf16[1536,2048]{1,0:T(8,128)(2,1)} %bitcast.77), kind=kOutput, calls=%fused_computation.11 | convolution fusion | flops 7299870720 | bytes 14606336 | tf_op jit(solution)/shard_map/dot_general | solution.py:78
  91.2 10.7 %multiply_add_fusion = f32[1152,1536]{1,0:T(8,128)S(1)} fusion(bf16[1160,1536]{1,0:T(8,128)(2,1)S(1)} %convolution_convert_fusion, f32[1536]{0:T(1024)S(1)} %mul.115, f32[1536]{0:T(1024)S(1)} %mul.112, f32[1536]{0:T(1024)S(1)} %mul.109, f32[1536]{0:T(1024)S(1)} %mul.106, f32[1536]{0:T(1024)S(1)} %mul.103, f32[1536]{0:T(1024)S(1)} %mul.100, ...), kind=kLoop, calls=%fused_computation.12 | loop fusion | flops 47775744 | bytes 31901568 | tf_op jit(solution)/shard_map/add | solution.py:91
  101.9 2.9 %copy-done = f32[1152,1536]{1,0:T(8,128)} copy-done((f32[1152,1536]{1,0:T(8,128)}, f32[1152,1536]{1,0:T(8,128)S(1)}, u32[]{:S(2)}) %copy-start) | copy-done | bytes 7077912
  105.2 1.4 copy.29
  106.6 2.7 %reshape.154 = bf16[32,16,9,128]{3,2,1,0:T(8,128)(2,1)S(1)} reshape(bf16[512,1152]{1,0:T(8,128)(2,1)} %copy.29) | data formatting | bytes 2359296 | tf_op jit(solution)/shard_map/reshape | solution.py:119
  109.8 5.8 %fusion = f32[32,8,128,16]{2,3,1,0:T(8,128)S(1)} fusion(pred[8,128,128]{2,1,0:T(8,128)(4,1)S(1)} %copy-done.3, bf16[32,128,128]{2,1,0:T(8,128)(2,1)} %copy.31, bf16[32,16,8,128]{3,2,1,0:T(8,128)(2,1)S(1)} %get-tuple-element.14), kind=kOutput, calls=%fused_computation.1 | convolution fusion | flops 138412032 | bytes 4325376 | tf_op jit(solution)/shard_map/gcbj,bgij->gcbi/dot_general | solution.py:123
  115.6 4.5 %add_bitcast_fusion = f32[32,16,8,128]{3,1,2,0:T(8,128)S(1)} fusion(f32[32,8,128,16]{2,3,1,0:T(8,128)S(1)} %fusion, pred[8,128,128]{2,1,0:T(8,128)(4,1)S(1)} %get-tuple-element.33, bf16[32,128,128]{2,1,0:T(8,128)(2,1)S(1)} %copy-done.2, bf16[32,16,8,128]{3,2,1,0:T(8,128)(2,1)S(1)} %get-tuple-element.13), kind=kOutput, calls=%fused_computation.27 | convolution fusion | flops 138936320 | bytes 6422528 | tf_op jit(solution)/shard_map/gcbj,bgij->gcbi/dot_general | solution.py:120
  121.0 1.8 %copy.44 = f32[64,8,8,128]{3,1,2,0:T(8,128)} copy(f32[64,8,8,128]{3,2,1,0:T(8,128)S(1)} %bitcast.64) | data formatting | bytes 4194304
  122.7 1.9 %copy.34 = f32[512,1024]{0,1:T(8,128)S(1)} copy(f32[512,1024]{1,0:T(8,128)} %bitcast.65) | data formatting | bytes 4194304 | tf_op jit(solution)/shard_map/reshape | solution.py:126
  124.6 1.9 %fusion.17 = bf16[512,1024]{0,1:T(8,128)(2,1)S(1)} fusion(f32[512,1024]{0,1:T(8,128)S(1)} %copy.34, f32[1152,1536]{1,0:T(8,128)} %copy-done), kind=kLoop, calls=%fused_computation.26 | loop fusion | flops 1048576 | bytes 5242880 | tf_op jit(solution)/shard_map/convert_element_type | solution.py:127
  129.2 6.1 %collective-permute-done.8 = bf16[512,256]{0,1:T(8,128)(2,1)S(1)} collective-permute-done((bf16[512,256]{0,1:T(8,128)(2,1)S(1)}, bf16[512,256]{0,1:T(8,128)(2,1)S(1)}, u32[]{:S(2)}, u32[]{:S(2)}) %collective-permute-start.8) | collective-permute-done | bytes 262176 | tf_op jit(solution)/shard_map/ppermute | solution.py:134
  135.3 5.8 %collective-permute-done.9 = bf16[512,256]{0,1:T(8,128)(2,1)S(1)} collective-permute-done((bf16[512,256]{0,1:T(8,128)(2,1)S(1)}, bf16[512,256]{0,1:T(8,128)(2,1)S(1)}, u32[]{:S(2)}, u32[]{:S(2)}) %collective-permute-start.9) | collective-permute-done | bytes 262176 | tf_op jit(solution)/shard_map/ppermute | solution.py:134
  141.1 6.7 %fusion.14 = bf16[256,2048]{1,0:T(8,128)(2,1)} fusion(bf16[2048,2048]{1,0:T(8,128)(2,1)} %pad_maximum_fusion, bf16[256,2048]{1,0:T(8,128)(2,1)S(1)} %copy-done.1, bf16[512,256]{0,1:T(8,128)(2,1)S(1)} %collective-permute-done.9, bf16[512,256]{0,1:T(8,128)(2,1)S(1)} %collective-permute-done.8, bf16[512,256]{0,1:T(8,128)(2,1)S(1)} %collective-permute-done.7, ...), kind=kOutput, calls=%fused_computation.20 | convolution fusion | flops 2153250816 | bytes 11534336 | tf_op jit(solution)/shard_map/dot_general | solution.py:136
  (50 shorter events, 12.1 us)
Async XLA Ops:
  6.5 8.8 %copy-start.1 = (bf16[256,2048]{1,0:T(8,128)(2,1)S(1)}, bf16[256,2048]{1,0:T(8,128)(2,1)}, u32[]{:S(2)}) copy-start(bf16[256,2048]{1,0:T(8,128)(2,1)} %param.6) | copy-start | bytes 3145732
  6.5 73.5 %all-gather.2.cloned.1.call-start = ((), (), s32[]{:S(2)}) async-start(), calls=%async_computation | async-start | bytes 6684672 | tf_op jit(solution)/shard_map/all_gather | solution.py:67
  10.3 27.8 %collective-permute-start = (bf16[136,2048]{1,0:T(8,128)(2,1)S(1)}, bf16[136,2048]{1,0:T(8,128)(2,1)S(1)}, u32[]{:S(2)}, u32[]{:S(2)}) collective-permute-start(bf16[136,2048]{1,0:T(8,128)(2,1)S(1)} %slice.75), channel_id=1, source_target_pairs={{3,7},{7,11},{11,15},{19,23},{23,27},{27,31},{35,39},{39,43},{43,4... | collective-permute-start | bytes 1671176 | tf_op jit(solution)/shard_map/ppermute | solution.py:54
  11.0 32.7 %collective-permute-start.1 = (bf16[136,2048]{1,0:T(8,128)(2,1)S(1)}, bf16[136,2048]{1,0:T(8,128)(2,1)}, u32[]{:S(2)}, u32[]{:S(2)}) collective-permute-start(bf16[136,2048]{1,0:T(8,128)(2,1)S(1)} %slice.75), channel_id=1, source_target_pairs={{3,6},{7,10},{11,14},{19,22},{23,26},{27,30},{35,38},{39,42},{43,4... | collective-permute-start | bytes 1671176 | tf_op jit(solution)/shard_map/ppermute | solution.py:54
  12.4 36.0 %collective-permute-start.2 = (bf16[136,2048]{1,0:T(8,128)(2,1)S(1)}, bf16[136,2048]{1,0:T(8,128)(2,1)}, u32[]{:S(2)}, u32[]{:S(2)}) collective-permute-start(bf16[136,2048]{1,0:T(8,128)(2,1)S(1)} %slice.75), channel_id=1, source_target_pairs={{3,5},{7,9},{11,13},{19,21},{23,25},{27,29},{35,37},{39,41},{43,45... | collective-permute-start | bytes 1671176 | tf_op jit(solution)/shard_map/ppermute | solution.py:54
  13.9 34.5 %collective-permute-start.3 = (bf16[136,2048]{1,0:T(8,128)(2,1)S(1)}, bf16[136,2048]{1,0:T(8,128)(2,1)}, u32[]{:S(2)}, u32[]{:S(2)}) collective-permute-start(bf16[136,2048]{1,0:T(8,128)(2,1)S(1)} %slice.75), channel_id=1, source_target_pairs={{3,4},{7,8},{11,12},{19,20},{23,24},{27,28},{35,36},{39,40},{43,44... | collective-permute-start | bytes 1671176 | tf_op jit(solution)/shard_map/ppermute | solution.py:54
  15.4 35.4 %collective-permute-start.4 = (bf16[256,2048]{1,0:T(8,128)(2,1)S(1)}, bf16[256,2048]{1,0:T(8,128)(2,1)S(1)}, u32[]{:S(2)}, u32[]{:S(2)}) collective-permute-start(bf16[256,2048]{1,0:T(8,128)(2,1)S(1)} %copy-done.1), channel_id=1, source_target_pairs={{0,3},{1,2},{2,1},{3,0},{4,7},{5,6},{6,5},{7,4},{8,11},{9,10},{10,... | collective-permute-start | bytes 3145736 | tf_op jit(solution)/shard_map/ppermute | solution.py:42
  19.9 12.6 %copy-start.4 = (s32[1,4]{1,0:T(1,128)S(1)}, s32[1,4]{1,0:T(1,128)}, u32[]{:S(2)}) copy-start(s32[1,4]{1,0:T(1,128)} %param.7) | copy-start | bytes 52
  38.1 28.0 %collective-permute-start.5 = (bf16[256,2048]{1,0:T(8,128)(2,1)S(1)}, bf16[256,2048]{1,0:T(8,128)(2,1)S(1)}, u32[]{:S(2)}, u32[]{:S(2)}) collective-permute-start(bf16[256,2048]{1,0:T(8,128)(2,1)S(1)} %copy-done.1), channel_id=1, source_target_pairs={{0,2},{1,3},{2,0},{3,1},{4,6},{5,7},{6,4},{7,5},{8,10},{9,11},{10,... | collective-permute-start | bytes 3145736 | tf_op jit(solution)/shard_map/ppermute | solution.py:42
  43.7 22.5 %collective-permute-start.6 = (bf16[256,2048]{1,0:T(8,128)(2,1)S(1)}, bf16[256,2048]{1,0:T(8,128)(2,1)S(1)}, u32[]{:S(2)}, u32[]{:S(2)}) collective-permute-start(bf16[256,2048]{1,0:T(8,128)(2,1)S(1)} %copy-done.1), channel_id=1, source_target_pairs={{0,1},{1,0},{2,3},{3,2},{4,5},{5,4},{6,7},{7,6},{8,9},{9,8},{10,11... | collective-permute-start | bytes 3145736 | tf_op jit(solution)/shard_map/ppermute | solution.py:42
  101.9 2.9 %copy-start = (f32[1152,1536]{1,0:T(8,128)}, f32[1152,1536]{1,0:T(8,128)S(1)}, u32[]{:S(2)}) copy-start(f32[1152,1536]{1,0:T(8,128)S(1)} %multiply_add_fusion) | copy-start | bytes 21233668
  105.2 4.6 %copy-start.3 = (pred[8,128,128]{2,1,0:T(8,128)(4,1)S(1)}, pred[8,128,128]{2,1,0:T(8,128)(4,1)}, u32[]{:S(2)}) copy-start(pred[8,128,128]{2,1,0:T(8,128)(4,1)} %get-tuple-element.34) | copy-start | bytes 393220
  109.8 5.8 %copy-start.2 = (bf16[32,128,128]{2,1,0:T(8,128)(2,1)S(1)}, bf16[32,128,128]{2,1,0:T(8,128)(2,1)}, u32[]{:S(2)}) copy-start(bf16[32,128,128]{2,1,0:T(8,128)(2,1)} %copy.28) | copy-start | bytes 3145732
  126.7 2.5 %collective-permute-start.7 = (bf16[512,256]{0,1:T(8,128)(2,1)S(1)}, bf16[512,256]{0,1:T(8,128)(2,1)S(1)}, u32[]{:S(2)}, u32[]{:S(2)}) collective-permute-start(bf16[512,256]{0,1:T(8,128)(2,1)S(1)} %get-tuple-element.18), channel_id=1, source_target_pairs={{0,1},{1,0},{2,3},{3,2},{4,5},{5,4},{6,7},{7,6},{8,9},{9,8},{10,11... | collective-permute-start | bytes 786440 | tf_op jit(solution)/shard_map/ppermute | solution.py:134
  127.4 7.9 %collective-permute-start.8 = (bf16[512,256]{0,1:T(8,128)(2,1)S(1)}, bf16[512,256]{0,1:T(8,128)(2,1)S(1)}, u32[]{:S(2)}, u32[]{:S(2)}) collective-permute-start(bf16[512,256]{0,1:T(8,128)(2,1)S(1)} %get-tuple-element.17), channel_id=1, source_target_pairs={{0,2},{1,3},{2,0},{3,1},{4,6},{5,7},{6,4},{7,5},{8,10},{9,11},{10,... | collective-permute-start | bytes 786440 | tf_op jit(solution)/shard_map/ppermute | solution.py:134
  128.7 12.4 %collective-permute-start.9 = (bf16[512,256]{0,1:T(8,128)(2,1)S(1)}, bf16[512,256]{0,1:T(8,128)(2,1)S(1)}, u32[]{:S(2)}, u32[]{:S(2)}) collective-permute-start(bf16[512,256]{0,1:T(8,128)(2,1)S(1)} %get-tuple-element.16), channel_id=1, source_target_pairs={{0,3},{1,2},{2,1},{3,0},{4,7},{5,6},{6,5},{7,4},{8,11},{9,10},{10,... | collective-permute-start | bytes 786440 | tf_op jit(solution)/shard_map/ppermute | solution.py:134
Sparse Core Ops, SparseCore 0:
  9.8 70.1 all-gather.1

commit v5 on v4

--- a/solution.py
+++ b/solution.py
@@ -83,16 +83,21 @@
     taps = lax.dynamic_slice_in_dim(taps, offset, part, axis=3).reshape(width, 3 * own)
 
     start = 8
-    feat_rows = ext_rows - start
     pos_f = position[start:]
-    featured = jnp.zeros((feat_rows, 3 * own), jnp.float32)
-    for tap_index in range(width):
-        shifted = projected[start - tap_index : ext_rows - tap_index].astype(jnp.float32)
-        featured = featured + taps[tap_index] * jnp.where(
-            (pos_f >= tap_index)[:, None], shifted, 0.0
-        )
-    queries = featured[feat_rows - span :, :own]
-    mixed_in = (featured[:, own : 2 * own] * featured[:, 2 * own :]).astype(jnp.bfloat16)
+    pos_q = position[tail:]
+
+    def featurize(first, lo, hi, pos):
+        total = None
+        for tap_index in range(width):
+            shifted = projected[first - tap_index : ext_rows - tap_index, lo:hi].astype(jnp.float32)
+            term = taps[tap_index, lo:hi] * jnp.where((pos >= tap_index)[:, None], shifted, 0.0)
+            total = term if total is None else total + term
+        return total
+
+    queries = featurize(tail, 0, own, pos_q)
+    mixed_in = (
+        featurize(start, own, 2 * own, pos_f) * featurize(start, 2 * own, 3 * own, pos_f)
+    ).astype(jnp.bfloat16)
 
     sub = LANE // per_group
     lf = long_filter.reshape(filter_len, n_lblk, sub)
@@ -118,27 +123,25 @@
 
     mi_t = mixed_in.T.reshape(n_groups, per_group, n_blocks + 1, filter_len)
     filtered = jnp.einsum(
-        "gcbj,bgij->gcbi", mi_t[:, :, 1:], cur_kernel, preferred_element_type=jnp.float32
+        "gcbj,bgij->gbci", mi_t[:, :, 1:], cur_kernel, preferred_element_type=jnp.float32
     )
     filtered = filtered + jnp.einsum(
-        "gcbj,bgij->gcbi", mi_t[:, :, :-1], prev_kernel, preferred_element_type=jnp.float32
+        "gcbj,bgij->gbci", mi_t[:, :, :-1], prev_kernel, preferred_element_type=jnp.float32
     )
-    filtered = filtered.reshape(own, span)
-    gated = (queries.T * filtered).astype(jnp.bfloat16)
+    q_t = queries.reshape(n_blocks, filter_len, n_groups, per_group).transpose(2, 0, 3, 1)
+    gated = (q_t * filtered).astype(jnp.bfloat16)
 
-
-    gated = gated.reshape(own, GROUP_DEVS, rows)
-    pieces = []
+    per_member = rows // filter_len
+    gated = gated.reshape(n_groups, GROUP_DEVS, per_member, per_group, filter_len)
+    ow_cat = ow_cat.reshape(GROUP_DEVS, n_groups, per_group, channels)
+    result = tokens.astype(jnp.float32)
     for d in range(GROUP_DEVS):
         send = lax.dynamic_index_in_dim(gated, member ^ d, axis=1, keepdims=False)
         got = send if d == 0 else lax.ppermute(send, "seq", swaps[d - 1])
-        pieces.append(got)
-    result = tokens.astype(jnp.float32) + lax.dot_general(
-        jnp.concatenate(pieces, axis=0),
-        ow_cat,
-        (((0,), (0,)), ((), ())),
-        preferred_element_type=jnp.float32,
-    )
+        part_out = lax.dot_general(
+            got, ow_cat[d], (((0, 2), (0, 1)), ((), ())), preferred_element_type=jnp.float32
+        )
+        result = result + part_out.reshape(rows, channels)
     return result.astype(jnp.bfloat16)
 
 

time: 155 us -> 158 us (1.019)
  the two profiles are of different devices: /device:TPU:1 before, /device:TPU:163 now
where the time goes in v5:
time: 158 us
  matrix products  37.6 us (24%)
  waiting for transfers between devices  36.9 us (23%)
  local copies, waits for them, and re-layouts  32.9 us (21%)
  other arithmetic  22.4 us (14%)
  between operations  14 us (9%)
  starting transfers between devices  13.7 us (9%)
    ppermute x3, waiting for transfers between devices, local(): lax.ppermute(tokens, 'seq', perm)  29.2 us
    dot_general x1, matrix products, local(): jnp.dot(ext_tokens, w_all.T, preferred_element_type=jnp.float32)  11.2 us
    dot_general x4, matrix products, local(): lax.dot_general(got, ow_cat[d], (((0, 2), (0, 1)), ((), ())), preferred_e...  9.54 us
    ppermute x4, starting transfers between devices, local(): got = lax.ppermute(tail_src, 'seq', perm)  9.47 us
    unnamed x70, local copies, waits for them, and re-layouts  8.02 us
    dot_general x2, matrix products, tap_table(): jnp.einsum('ijt,tg->gij', one_hot, long_filter, preferred_element_type=jn...  7.92 us
    ppermute x3, waiting for transfers between devices, local(): got = send if d == 0 else lax.ppermute(send, 'seq', swaps[d - 1])  7.66 us
    transpose x1, other arithmetic, local(): mi_t = mixed_in.T.reshape(n_groups, per_group, n_blocks + 1, filter_len)  6.71 us
  transfers between devices with their start and end apart: 11, of which 4 were waited for; matrix products, arithmetic and copies ran while one was open for 25% of the time, Pallas kernels for 0%

profile of v5, /device:TPU:163, one launch (start us, length us, event | category | flops | bytes accessed | tf_op | source)
XLA Modules:
  0.0 157.6 jit_solution(16402180637793465985)
XLA Ops:
  6.5 1.8 %copy.50 = bf16[2048,384]{0,1:T(8,128)(2,1)S(1)} copy(bf16[2048,384]{1,0:T(8,128)(2,1)} %param.8) | data formatting | bytes 3145728 | tf_op args[2]
  9.2 3.1 %collective-permute-start = (bf16[136,2048]{1,0:T(8,128)(2,1)S(1)}, bf16[136,2048]{1,0:T(8,128)(2,1)S(1)}, u32[]{:S(2)}, u32[]{:S(2)}) collective-permute-start(bf16[136,2048]{1,0:T(8,128)(2,1)S(1)} %slice.160), channel_id=1, source_target_pairs={{3,7},{7,11},{11,15},{19,23},{23,27},{27,31},{35,39},{39,43},{43,4... | collective-permute-start | bytes 1671176 | tf_op jit(solution)/shard_map/ppermute | solution.py:54
  12.3 2.1 %collective-permute-start.1 = (bf16[136,2048]{1,0:T(8,128)(2,1)S(1)}, bf16[136,2048]{1,0:T(8,128)(2,1)}, u32[]{:S(2)}, u32[]{:S(2)}) collective-permute-start(bf16[136,2048]{1,0:T(8,128)(2,1)S(1)} %slice.160), channel_id=1, source_target_pairs={{3,6},{7,10},{11,14},{19,22},{23,26},{27,30},{35,38},{39,42},{43,4... | collective-permute-start | bytes 1671176 | tf_op jit(solution)/shard_map/ppermute | solution.py:54
  14.5 2.1 %collective-permute-start.2 = (bf16[136,2048]{1,0:T(8,128)(2,1)S(1)}, bf16[136,2048]{1,0:T(8,128)(2,1)}, u32[]{:S(2)}, u32[]{:S(2)}) collective-permute-start(bf16[136,2048]{1,0:T(8,128)(2,1)S(1)} %slice.160), channel_id=1, source_target_pairs={{3,5},{7,9},{11,13},{19,21},{23,25},{27,29},{35,37},{39,41},{43,45... | collective-permute-start | bytes 1671176 | tf_op jit(solution)/shard_map/ppermute | solution.py:54
  16.6 2.1 %collective-permute-start.3 = (bf16[136,2048]{1,0:T(8,128)(2,1)S(1)}, bf16[136,2048]{1,0:T(8,128)(2,1)}, u32[]{:S(2)}, u32[]{:S(2)}) collective-permute-start(bf16[136,2048]{1,0:T(8,128)(2,1)S(1)} %slice.160), channel_id=1, source_target_pairs={{3,4},{7,8},{11,12},{19,20},{23,24},{27,28},{35,36},{39,40},{43,44... | collective-permute-start | bytes 1671176 | tf_op jit(solution)/shard_map/ppermute | solution.py:54
  20.4 4.0 %fusion.26 = bf16[32,128,128]{2,0,1:T(8,128)(2,1)S(1)} fusion(bf16[128,32,1]{0,1,2:T(8,128)(2,1)S(1)} %bitcast.153, s32[128,128]{1,0:T(8,128)S(1)} %get-tuple-element.60), kind=kOutput, calls=%fused_computation.35 | convolution fusion | flops 136839168 | bytes 1122304 | tf_op jit(solution)/shard_map/ijt,tg->gij/dot_general | solution.py:22
  25.7 3.9 %fusion.27 = bf16[32,128,128]{2,0,1:T(8,128)(2,1)S(1)} fusion(bf16[128,32,1]{0,1,2:T(8,128)(2,1)S(1)} %bitcast.154, s32[128,128]{1,0:T(8,128)S(1)} %get-tuple-element.61), kind=kOutput, calls=%fused_computation.36 | convolution fusion | flops 136839168 | bytes 1122304 | tf_op jit(solution)/shard_map/ijt,tg->gij/dot_general | solution.py:22
  34.7 4.3 %constant_dynamic-slice_fusion.5 = (bf16[16,32,2048]{2,1,0:T(8,128)(2,1)S(1)}, bf16[16,32,2048]{2,1,0:T(8,128)(2,1)S(1)}, bf16[16,32,2048]{2,1,0:T(8,128)(2,1)S(1)}, bf16[16,32,2048]{2,1,0:T(8,128)(2,1)S(1)}) fusion(bf16[16,128,2048]{2,1,0:T(8,128)(2,1)} %bitcast.114, s32[]{:T(128)S(6)} %select_n.221, s32[]{:T(128)S(6)} %select_n.258, s32[]{:T(128)S(6)} %select_n.257, ...), kind=kLoop, calls=%fused_computation.68 | loop fusion | bytes 16777232 | tf_op jit(solution)/shard_map/dynamic_slice | solution.py:75
  39.2 2.1 %collective-permute-start.6 = (bf16[256,2048]{1,0:T(8,128)(2,1)S(1)}, bf16[256,2048]{1,0:T(8,128)(2,1)S(1)}, u32[]{:S(2)}, u32[]{:S(2)}) collective-permute-start(bf16[256,2048]{1,0:T(8,128)(2,1)S(1)} %copy-done.2), channel_id=1, source_target_pairs={{0,1},{1,0},{2,3},{3,2},{4,5},{5,4},{6,7},{7,6},{8,9},{9,8},{10,11... | collective-permute-start | bytes 3145736 | tf_op jit(solution)/shard_map/ppermute | solution.py:42
  43.6 7.0 %collective-permute-done.4 = bf16[256,2048]{1,0:T(8,128)(2,1)S(1)} collective-permute-done((bf16[256,2048]{1,0:T(8,128)(2,1)S(1)}, bf16[256,2048]{1,0:T(8,128)(2,1)S(1)}, u32[]{:S(2)}, u32[]{:S(2)}) %collective-permute-start.4) | collective-permute-done | bytes 1048608 | tf_op jit(solution)/shard_map/ppermute | solution.py:42
  50.6 22.3 %collective-permute-done.5 = bf16[256,2048]{1,0:T(8,128)(2,1)S(1)} collective-permute-done((bf16[256,2048]{1,0:T(8,128)(2,1)S(1)}, bf16[256,2048]{1,0:T(8,128)(2,1)S(1)}, u32[]{:S(2)}, u32[]{:S(2)}) %collective-permute-start.5) | collective-permute-done | bytes 1048608 | tf_op jit(solution)/shard_map/ppermute | solution.py:42
  72.8 1.8 %select_dynamic-update-slice_fusion.3 = bf16[1160,2048]{1,0:T(8,128)(2,1)} fusion(bf16[1160,2048]{1,0:T(8,128)(2,1)} %select_dynamic-update-slice_fusion.4, bf16[256,2048]{1,0:T(8,128)(2,1)S(1)} %collective-permute-done.4, bf16[256,2048]{1,0:T(8,128)(2,1)S(1)} %collective-permute-done.5, bf16[256,2048]{1,0:T(8,128)(2,1)S(1)} %collective-permute-done.6, ...), kind=kLoop, calls=%fused_computation.43 | loop fusion | flops 1572864 | bytes 5242883
  74.6 1.8 %select_dynamic-update-slice_fusion.2 = bf16[1160,2048]{1,0:T(8,128)(2,1)} fusion(bf16[1160,2048]{1,0:T(8,128)(2,1)} %select_dynamic-update-slice_fusion.3, bf16[256,2048]{1,0:T(8,128)(2,1)S(1)} %collective-permute-done.4, bf16[256,2048]{1,0:T(8,128)(2,1)S(1)} %collective-permute-done.5, bf16[256,2048]{1,0:T(8,128)(2,1)S(1)} %collective-permute-done.6, ...), kind=kLoop, calls=%fused_computation.42 | loop fusion | flops 1572864 | bytes 5242883
  76.4 1.7 %select_dynamic-update-slice_fusion.1 = bf16[1160,2048]{1,0:T(8,128)(2,1)} fusion(bf16[1160,2048]{1,0:T(8,128)(2,1)} %select_dynamic-update-slice_fusion.2, bf16[256,2048]{1,0:T(8,128)(2,1)S(1)} %collective-permute-done.4, bf16[256,2048]{1,0:T(8,128)(2,1)S(1)} %collective-permute-done.5, bf16[256,2048]{1,0:T(8,128)(2,1)S(1)} %collective-permute-done.6, ...), kind=kLoop, calls=%fused_computation.41 | loop fusion | flops 1572864 | bytes 5242883
  78.1 1.7 %select_dynamic-update-slice_fusion = bf16[1160,2048]{1,0:T(8,128)(2,1)} fusion(bf16[1160,2048]{1,0:T(8,128)(2,1)} %select_dynamic-update-slice_fusion.1, bf16[256,2048]{1,0:T(8,128)(2,1)S(1)} %collective-permute-done.4, bf16[256,2048]{1,0:T(8,128)(2,1)S(1)} %collective-permute-done.5, bf16[256,2048]{1,0:T(8,128)(2,1)S(1)} %collective-permute-done.6, ...), kind=kLoop, calls=%fused_computation.40 | loop fusion | flops 1572864 | bytes 5242883 | tf_op jit(solution)/shard_map/concatenate | solution.py:56
  79.8 3.5 %fusion.34 = (bf16[512,2048]{1,0:T(8,128)(2,1)}, bf16[512,2048]{1,0:T(8,128)(2,1)}, bf16[512,2048]{1,0:T(8,128)(2,1)}, bf16[512,2048]{1,0:T(8,128)(2,1)}) fusion(bf16[2048,2048]{1,0:T(8,128)(2,1)S(1)} %pad_maximum_fusion), kind=kLoop, calls=%fused_computation.82 | loop fusion | bytes 16777216 | tf_op jit(solution)/shard_map/slice | solution.py:142
  83.4 11.2 %convolution_convert_fusion = bf16[1160,1536]{1,0:T(8,128)(2,1)S(1)} fusion(bf16[1160,2048]{1,0:T(8,128)(2,1)} %select_dynamic-update-slice_fusion, bf16[1536,2048]{1,0:T(8,128)(2,1)} %bitcast.155), kind=kOutput, calls=%fused_computation.11 | convolution fusion | flops 7299870720 | bytes 14606336 | tf_op jit(solution)/shard_map/dot_general | solution.py:78
  94.6 1.8 %copy-done = bf16[1160,1536]{1,0:T(8,128)(2,1)} copy-done((bf16[1160,1536]{1,0:T(8,128)(2,1)}, bf16[1160,1536]{1,0:T(8,128)(2,1)S(1)}, u32[]{:S(2)}) %copy-start) | copy-done | bytes 3563544
  96.4 6.7 %fusion.28 = bf16[512,1152]{0,1:T(8,128)(2,1)S(1)} fusion(bf16[1160,1536]{1,0:T(8,128)(2,1)S(1)} %convolution_convert_fusion, f32[512]{0:T(512)S(1)} %bitcast.138, f32[512]{0:T(512)S(1)} %bitcast.139, f32[512]{0:T(512)S(1)} %bitcast.140, f32[512]{0:T(512)S(1)} %bitcast.141, f32[512]{0:T(512)S(1)} %bitcast.142, f32[512]{0:T(512)S(1)} %bitcast.143, ...), kind=kLoop, calls=%fused_computation.37 | loop fusion | flops 33030144 | bytes 17731456 | tf_op jit(solution)/shard_map/transpose | solution.py:124
  104.5 2.5 %reshape.166 = bf16[32,16,9,128]{3,2,1,0:T(8,128)(2,1)S(1)} reshape(bf16[512,1152]{1,0:T(8,128)(2,1)} %copy.53) | data formatting | bytes 2359296 | tf_op jit(solution)/shard_map/reshape | solution.py:124
  107.1 1.7 %fusion.35 = (bf16[32,16,8,128]{3,2,1,0:T(8,128)(2,1)}, bf16[32,16,8,128]{3,2,1,0:T(8,128)(2,1)}) fusion(bf16[32,16,9,128]{3,2,1,0:T(8,128)(2,1)S(1)} %reshape.166), kind=kLoop, calls=%fused_computation.83 | loop fusion | bytes 4194304 | tf_op jit(solution)/shard_map/slice | solution.py:126
  109.8 3.9 %multiply_add_fusion = f32[1024,512]{1,0:T(8,128)} fusion(bf16[1160,1536]{1,0:T(8,128)(2,1)S(1)} %copy-done.1, f32[512]{0:T(512)S(1)} %bitcast.132, f32[512]{0:T(512)S(1)} %bitcast.133, f32[512]{0:T(512)S(1)} %bitcast.134, f32[512]{0:T(512)S(1)} %bitcast.135, f32[512]{0:T(512)S(1)} %bitcast.136, f32[512]{0:T(512)S(1)} %bitcast.152, f32[512]{0:T(512)S(1)} %bitcast.151, ...), kind=kLoop, calls=%fused_computation.34 | loop fusion | flops 14155776 | bytes 9458688 | tf_op jit(solution)/shard_map/add | solution.py:94
  113.7 2.1 %copy.51 = f32[1024,512]{0,1:T(8,128)S(1)} copy(f32[1024,512]{1,0:T(8,128)} %multiply_add_fusion) | data formatting | bytes 4194304 | tf_op jit(solution)/shard_map/add | solution.py:94
  117.4 4.5 %fusion = f32[32,8,16,128]{3,2,1,0:T(8,128)S(1)} fusion(pred[8,128,128]{2,1,0:T(8,128)(4,1)S(1)} %copy-done.11, bf16[32,128,128]{2,1,0:T(8,128)(2,1)S(1)} %copy-done.8, bf16[32,16,8,128]{3,2,1,0:T(8,128)(2,1)S(1)} %copy-done.10), kind=kOutput, calls=%fused_computation.1 | convolution fusion | flops 138412032 | bytes 4325376 | tf_op jit(solution)/shard_map/gcbj,bgij->gbci/dot_general | solution.py:128
  121.9 4.5 %fusion.19 = bf16[32,8,16,128]{3,2,1,0:T(8,128)(2,1)S(1)} fusion(f32[8,128,32,16]{1,0,3,2:T(8,128)S(1)} %bitcast.121, f32[32,8,16,128]{3,2,1,0:T(8,128)S(1)} %fusion, pred[8,128,128]{2,1,0:T(8,128)(4,1)S(1)} %get-tuple-element.58, bf16[32,128,128]{2,1,0:T(8,128)(2,1)S(1)} %copy-done.7, bf16[32,16,8,128]{3,2,1,0:T(8,128)(2,1)S(1)} %copy-done.9), kind=kOutput, calls=%fused_computation.29 | convolution fusion | flops 139984896 | bytes 7471104 | tf_op jit(solution)/shard_map/gcbj,bgij->gbci/dot_general | solution.py:125
  128.4 2.0 %collective-permute-start.9 = (bf16[32,2,16,128]{3,2,1,0:T(8,128)(2,1)}, bf16[32,2,16,128]{3,2,1,0:T(8,128)(2,1)}, u32[]{:S(2)}, u32[]{:S(2)}) collective-permute-start(bf16[32,2,16,128]{3,2,1,0:T(8,128)(2,1)} %get-tuple-element.22), channel_id=1, source_target_pairs={{0,3},{1,2},{2,1},{3,0},{4,7},{5,6},{6,5},{7,4},{8,11},{9,10},{10,... | collective-permute-start | bytes 786440 | tf_op jit(solution)/shard_map/ppermute | solution.py:140
  130.5 3.8 %fusion.14 = f32[256,2048]{1,0:T(8,128)} fusion(bf16[256,32,16]{0,1,2:T(8,128)(2,1)} %dot_general.49, bf16[32,16,2048]{2,1,0:T(8,128)(2,1)S(1)} %bitcast.125, bf16[256,2048]{1,0:T(8,128)(2,1)S(1)} %copy-done.2), kind=kOutput, calls=%fused_computation.22 | convolution fusion | flops 537919488 | bytes 5505024 | tf_op jit(solution)/shard_map/dot_general | solution.py:141
  134.3 1.8 %collective-permute-done.8 = bf16[32,2,16,128]{3,2,1,0:T(8,128)(2,1)S(1)} collective-permute-done((bf16[32,2,16,128]{3,2,1,0:T(8,128)(2,1)}, bf16[32,2,16,128]{3,2,1,0:T(8,128)(2,1)S(1)}, u32[]{:S(2)}, u32[]{:S(2)}) %collective-permute-start.8) | collective-permute-done | bytes 262176 | tf_op jit(solution)/shard_map/ppermute | solution.py:140
  136.6 5.8 %collective-permute-done.9 = bf16[32,2,16,128]{3,2,1,0:T(8,128)(2,1)} collective-permute-done((bf16[32,2,16,128]{3,2,1,0:T(8,128)(2,1)}, bf16[32,2,16,128]{3,2,1,0:T(8,128)(2,1)}, u32[]{:S(2)}, u32[]{:S(2)}) %collective-permute-start.9) | collective-permute-done | bytes 262176 | tf_op jit(solution)/shard_map/ppermute | solution.py:140
  144.2 1.5 convolution_bitcast_fusion.1
  145.8 1.5 convolution_bitcast_fusion
  148.1 2.7 %fusion.18 = bf16[256,2048]{1,0:T(8,128)(2,1)} fusion(f32[256,2048]{1,0:T(8,128)S(1)} %convolution_bitcast_fusion, f32[256,2048]{1,0:T(8,128)S(1)} %convolution_bitcast_fusion.1, f32[256,2048]{1,0:T(8,128)S(1)} %copy-done.32, bf16[256,32,16]{0,1,2:T(8,128)(2,1)S(1)} %dot_general.52, bf16[32,16,2048]{2,1,0:T(8,128)(2,1)S(1)} %bitcast.122), kind=kOutput, calls=%fused_computation.26 | convolution fusion | flops 538968064 | bytes 9699328 | tf_op jit(solution)/shard_map/dot_general | solution.py:141
  (113 shorter events, 20.3 us)
Async XLA Ops:
  6.5 76.8 %all-gather.2.cloned.1.call-start = ((), (), s32[]{:S(2)}) async-start(), calls=%async_computation | async-start | bytes 6684672 | tf_op jit(solution)/shard_map/all_gather | solution.py:67
  8.3 11.6 %copy-start.31 = (s32[1,4]{1,0:T(1,128)S(1)}, s32[1,4]{1,0:T(1,128)}, u32[]{:S(2)}) copy-start(s32[1,4]{1,0:T(1,128)} %param.7) | copy-start | bytes 52
  8.4 11.8 %copy-start.12 = (bf16[128,128]{1,0:T(8,128)(2,1)S(1)}, bf16[128,128]{1,0:T(8,128)(2,1)}, u32[]{:S(2)}) copy-start(bf16[128,128]{1,0:T(8,128)(2,1)} %param.10) | copy-start | bytes 98308
  9.2 29.8 %collective-permute-start = (bf16[136,2048]{1,0:T(8,128)(2,1)S(1)}, bf16[136,2048]{1,0:T(8,128)(2,1)S(1)}, u32[]{:S(2)}, u32[]{:S(2)}) collective-permute-start(bf16[136,2048]{1,0:T(8,128)(2,1)S(1)} %slice.160), channel_id=1, source_target_pairs={{3,7},{7,11},{11,15},{19,23},{23,27},{27,31},{35,39},{39,43},{43,4... | collective-permute-start | bytes 1671176 | tf_op jit(solution)/shard_map/ppermute | solution.py:54
  12.3 26.8 %collective-permute-start.1 = (bf16[136,2048]{1,0:T(8,128)(2,1)S(1)}, bf16[136,2048]{1,0:T(8,128)(2,1)}, u32[]{:S(2)}, u32[]{:S(2)}) collective-permute-start(bf16[136,2048]{1,0:T(8,128)(2,1)S(1)} %slice.160), channel_id=1, source_target_pairs={{3,6},{7,10},{11,14},{19,22},{23,26},{27,30},{35,38},{39,42},{43,4... | collective-permute-start | bytes 1671176 | tf_op jit(solution)/shard_map/ppermute | solution.py:54
  14.5 27.9 %collective-permute-start.2 = (bf16[136,2048]{1,0:T(8,128)(2,1)S(1)}, bf16[136,2048]{1,0:T(8,128)(2,1)}, u32[]{:S(2)}, u32[]{:S(2)}) collective-permute-start(bf16[136,2048]{1,0:T(8,128)(2,1)S(1)} %slice.160), channel_id=1, source_target_pairs={{3,5},{7,9},{11,13},{19,21},{23,25},{27,29},{35,37},{39,41},{43,45... | collective-permute-start | bytes 1671176 | tf_op jit(solution)/shard_map/ppermute | solution.py:54
  16.6 25.8 %collective-permute-start.3 = (bf16[136,2048]{1,0:T(8,128)(2,1)S(1)}, bf16[136,2048]{1,0:T(8,128)(2,1)}, u32[]{:S(2)}, u32[]{:S(2)}) collective-permute-start(bf16[136,2048]{1,0:T(8,128)(2,1)S(1)} %slice.160), channel_id=1, source_target_pairs={{3,4},{7,8},{11,12},{19,20},{23,24},{27,28},{35,36},{39,40},{43,44... | collective-permute-start | bytes 1671176 | tf_op jit(solution)/shard_map/ppermute | solution.py:54
  18.7 31.8 %collective-permute-start.4 = (bf16[256,2048]{1,0:T(8,128)(2,1)S(1)}, bf16[256,2048]{1,0:T(8,128)(2,1)S(1)}, u32[]{:S(2)}, u32[]{:S(2)}) collective-permute-start(bf16[256,2048]{1,0:T(8,128)(2,1)S(1)} %copy-done.2), channel_id=1, source_target_pairs={{0,3},{1,2},{2,1},{3,0},{4,7},{5,6},{6,5},{7,4},{8,11},{9,10},{10,... | collective-permute-start | bytes 3145736 | tf_op jit(solution)/shard_map/ppermute | solution.py:42
  39.1 33.7 %collective-permute-start.5 = (bf16[256,2048]{1,0:T(8,128)(2,1)S(1)}, bf16[256,2048]{1,0:T(8,128)(2,1)S(1)}, u32[]{:S(2)}, u32[]{:S(2)}) collective-permute-start(bf16[256,2048]{1,0:T(8,128)(2,1)S(1)} %copy-done.2), channel_id=1, source_target_pairs={{0,2},{1,3},{2,0},{3,1},{4,6},{5,7},{6,4},{7,5},{8,10},{9,11},{10,... | collective-permute-start | bytes 3145736 | tf_op jit(solution)/shard_map/ppermute | solution.py:42
  39.2 33.6 %collective-permute-start.6 = (bf16[256,2048]{1,0:T(8,128)(2,1)S(1)}, bf16[256,2048]{1,0:T(8,128)(2,1)S(1)}, u32[]{:S(2)}, u32[]{:S(2)}) collective-permute-start(bf16[256,2048]{1,0:T(8,128)(2,1)S(1)} %copy-done.2), channel_id=1, source_target_pairs={{0,1},{1,0},{2,3},{3,2},{4,5},{5,4},{6,7},{7,6},{8,9},{9,8},{10,11... | collective-permute-start | bytes 3145736 | tf_op jit(solution)/shard_map/ppermute | solution.py:42
  83.3 13.0 %copy-start.13 = (f32[1,512]{1,0:T(1,128)S(1)}, f32[1,512]{1,0:T(1,128)}, u32[]{:S(2)}) copy-start(f32[1,512]{1,0:T(1,128)} %get-tuple-element.35) | copy-start | bytes 6148
  83.3 13.0 %copy-start.14 = (f32[1,512]{1,0:T(1,128)S(1)}, f32[1,512]{1,0:T(1,128)}, u32[]{:S(2)}) copy-start(f32[1,512]{1,0:T(1,128)} %get-tuple-element.36) | copy-start | bytes 6148
  83.3 13.0 %copy-start.17 = (pred[1152]{0:T(1024)(128)(4,1)S(1)}, pred[1152]{0:T(1024)(128)(4,1)}, u32[]{:S(2)}) copy-start(pred[1152]{0:T(1024)(128)(4,1)} %get-tuple-element.44) | copy-start | bytes 3460
  83.3 13.0 %copy-start.18 = (pred[1152]{0:T(1024)(128)(4,1)S(1)}, pred[1152]{0:T(1024)(128)(4,1)}, u32[]{:S(2)}) copy-start(pred[1152]{0:T(1024)(128)(4,1)} %get-tuple-element.45) | copy-start | bytes 3460
  83.3 13.0 %copy-start.19 = (pred[1152]{0:T(1024)(128)(4,1)S(1)}, pred[1152]{0:T(1024)(128)(4,1)}, u32[]{:S(2)}) copy-start(pred[1152]{0:T(1024)(128)(4,1)} %get-tuple-element.46) | copy-start | bytes 3460
  83.3 13.0 %copy-start.20 = (pred[1152]{0:T(1024)(128)(4,1)S(1)}, pred[1152]{0:T(1024)(128)(4,1)}, u32[]{:S(2)}) copy-start(pred[1152]{0:T(1024)(128)(4,1)} %get-tuple-element.47) | copy-start | bytes 3460
  83.3 13.0 %copy-start.21 = (pred[1152]{0:T(1024)(128)(4,1)S(1)}, pred[1152]{0:T(1024)(128)(4,1)}, u32[]{:S(2)}) copy-start(pred[1152]{0:T(1024)(128)(4,1)} %get-tuple-element.48) | copy-start | bytes 3460
  83.4 13.0 %copy-start.22 = (pred[1152]{0:T(1024)(128)(4,1)S(1)}, pred[1152]{0:T(1024)(128)(4,1)}, u32[]{:S(2)}) copy-start(pred[1152]{0:T(1024)(128)(4,1)} %get-tuple-element.49) | copy-start | bytes 3460
  83.4 13.0 %copy-start.23 = (pred[1152]{0:T(1024)(128)(4,1)S(1)}, pred[1152]{0:T(1024)(128)(4,1)}, u32[]{:S(2)}) copy-start(pred[1152]{0:T(1024)(128)(4,1)} %get-tuple-element.50) | copy-start | bytes 3460
  107.0 2.8 %copy-start.1 = (bf16[1160,1536]{1,0:T(8,128)(2,1)S(1)}, bf16[1160,1536]{1,0:T(8,128)(2,1)}, u32[]{:S(2)}) copy-start(bf16[1160,1536]{1,0:T(8,128)(2,1)} %copy-done) | copy-start | bytes 10690564
  107.0 2.8 %copy-start.15 = (f32[1,512]{1,0:T(1,128)S(1)}, f32[1,512]{1,0:T(1,128)}, u32[]{:S(2)}) copy-start(f32[1,512]{1,0:T(1,128)} %get-tuple-element.42) | copy-start | bytes 6148
  107.0 2.8 %copy-start.16 = (f32[1,512]{1,0:T(1,128)S(1)}, f32[1,512]{1,0:T(1,128)}, u32[]{:S(2)}) copy-start(f32[1,512]{1,0:T(1,128)} %get-tuple-element.43) | copy-start | bytes 6148
  107.0 2.7 %copy-start.24 = (pred[1024]{0:T(1024)(128)(4,1)S(1)}, pred[1024]{0:T(1024)(128)(4,1)}, u32[]{:S(2)}) copy-start(pred[1024]{0:T(1024)(128)(4,1)} %get-tuple-element.51) | copy-start | bytes 3076
  107.1 2.7 %copy-start.25 = (pred[1024]{0:T(1024)(128)(4,1)S(1)}, pred[1024]{0:T(1024)(128)(4,1)}, u32[]{:S(2)}) copy-start(pred[1024]{0:T(1024)(128)(4,1)} %get-tuple-element.52) | copy-start | bytes 3076
  107.1 2.7 %copy-start.26 = (pred[1024]{0:T(1024)(128)(4,1)S(1)}, pred[1024]{0:T(1024)(128)(4,1)}, u32[]{:S(2)}) copy-start(pred[1024]{0:T(1024)(128)(4,1)} %get-tuple-element.53) | copy-start | bytes 3076
  117.4 4.5 %copy-start.7 = (bf16[32,128,128]{2,1,0:T(8,128)(2,1)S(1)}, bf16[32,128,128]{2,1,0:T(8,128)(2,1)}, u32[]{:S(2)}) copy-start(bf16[32,128,128]{2,1,0:T(8,128)(2,1)} %copy.56) | copy-start | bytes 3145732
  117.4 4.5 %copy-start.9 = (bf16[32,16,8,128]{3,2,1,0:T(8,128)(2,1)S(1)}, bf16[32,16,8,128]{3,2,1,0:T(8,128)(2,1)}, u32[]{:S(2)}) copy-start(bf16[32,16,8,128]{3,2,1,0:T(8,128)(2,1)} %get-tuple-element.17) | copy-start | bytes 3145732
  126.4 4.1 %copy-start.6 = (bf16[512,2048]{1,0:T(8,128)(2,1)S(1)}, bf16[512,2048]{1,0:T(8,128)(2,1)}, u32[]{:S(2)}) copy-start(bf16[512,2048]{1,0:T(8,128)(2,1)} %get-tuple-element.12) | copy-start | bytes 6291460
  128.4 7.7 %collective-permute-start.8 = (bf16[32,2,16,128]{3,2,1,0:T(8,128)(2,1)}, bf16[32,2,16,128]{3,2,1,0:T(8,128)(2,1)S(1)}, u32[]{:S(2)}, u32[]{:S(2)}) collective-permute-start(bf16[32,2,16,128]{3,2,1,0:T(8,128)(2,1)} %get-tuple-element.20), channel_id=1, source_target_pairs={{0,2},{1,3},{2,0},{3,1},{4,6},{5,7},{6,4},{7,5},{8,10},{9,11},{10,... | collective-permute-start | bytes 786440 | tf_op jit(solution)/shard_map/ppermute | solution.py:140
  128.4 14.0 %collective-permute-start.9 = (bf16[32,2,16,128]{3,2,1,0:T(8,128)(2,1)}, bf16[32,2,16,128]{3,2,1,0:T(8,128)(2,1)}, u32[]{:S(2)}, u32[]{:S(2)}) collective-permute-start(bf16[32,2,16,128]{3,2,1,0:T(8,128)(2,1)} %get-tuple-element.22), channel_id=1, source_target_pairs={{0,3},{1,2},{2,1},{3,0},{4,7},{5,6},{6,5},{7,4},{8,11},{9,10},{10,... | collective-permute-start | bytes 786440 | tf_op jit(solution)/shard_map/ppermute | solution.py:140
  130.5 13.3 %collective-permute-start.7 = (bf16[32,2,16,128]{3,2,1,0:T(8,128)(2,1)}, bf16[32,2,16,128]{3,2,1,0:T(8,128)(2,1)S(1)}, u32[]{:S(2)}, u32[]{:S(2)}) collective-permute-start(bf16[32,2,16,128]{3,2,1,0:T(8,128)(2,1)} %get-tuple-element.19), channel_id=1, source_target_pairs={{0,1},{1,0},{2,3},{3,2},{4,5},{5,4},{6,7},{7,6},{8,9},{9,8},{10,11... | collective-permute-start | bytes 786440 | tf_op jit(solution)/shard_map/ppermute | solution.py:140
  134.3 9.9 %copy-start.5 = (bf16[512,2048]{1,0:T(8,128)(2,1)S(1)}, bf16[512,2048]{1,0:T(8,128)(2,1)}, u32[]{:S(2)}) copy-start(bf16[512,2048]{1,0:T(8,128)(2,1)} %get-tuple-element.11) | copy-start | bytes 6291460
  (12 other events, 25.0 us)
Sparse Core Ops, SparseCore 0:
  9.8 67.3 all-gather.1

commit v6 on v4

--- a/solution.py
+++ b/solution.py
@@ -128,17 +128,16 @@
 
 
     gated = gated.reshape(own, GROUP_DEVS, rows)
-    pieces = []
+    result = tokens.astype(jnp.float32)
     for d in range(GROUP_DEVS):
         send = lax.dynamic_index_in_dim(gated, member ^ d, axis=1, keepdims=False)
         got = send if d == 0 else lax.ppermute(send, "seq", swaps[d - 1])
-        pieces.append(got)
-    result = tokens.astype(jnp.float32) + lax.dot_general(
-        jnp.concatenate(pieces, axis=0),
-        ow_cat,
-        (((0,), (0,)), ((), ())),
-        preferred_element_type=jnp.float32,
-    )
+        result = result + lax.dot_general(
+            got,
+            ow_cat[d * own : (d + 1) * own],
+            (((0,), (0,)), ((), ())),
+            preferred_element_type=jnp.float32,
+        )
     return result.astype(jnp.bfloat16)
 
 

time: 155 us -> 157 us (1.013)
  waiting for transfers between devices: 34.4 us -> 28.3 us
  local copies, waits for them, and re-layouts: 25.5 us -> 29.5 us
  other arithmetic: 28.2 us -> 30.2 us
    ppermute x3, waiting for transfers between devices: 11.9 us -> 6.54 us  [local(): got = send if d == 0 else lax.ppermute(send, 'seq', swaps[d - 1])]
    slice x1, local copies, waits for them, and re-layouts: 0.44 us -> 2.3 us  [local(): mi_t[:, :, 1:]]
    unnamed x14 -> x16, local copies, waits for them, and re-layouts: 8.3 us -> 9.24 us
    dot_general x1 -> x4, matrix products: 6.68 us -> 7.4 us  [local(): lax.dot_general(got, ow_cat[d * own:(d + 1) * own], (((0,), (0,)), ((), (...]
    unnamed x4 -> x5, other arithmetic: 7.38 us -> 7.53 us
  transfers between devices with their start and end apart: 11 -> 11, of which waited for: 4 -> 4; matrix products, arithmetic and copies ran while one was open for 22% -> 25% of each run, Pallas kernels for 0% -> 0%
where the time goes in v6:
time: 157 us; the launch traced here: 155 us
  matrix products  36.8 us (23%)
  other arithmetic  30.2 us (19%)
  local copies, waits for them, and re-layouts  29.5 us (19%)
  waiting for transfers between devices  28.3 us (18%)
  starting transfers between devices  16.8 us (11%)
  between operations  13.6 us (9%)
    ppermute x3, waiting for transfers between devices, local(): lax.ppermute(tokens, 'seq', perm)  15.4 us
    dot_general x1, matrix products, local(): jnp.dot(ext_tokens, w_all.T, preferred_element_type=jnp.float32)  11.2 us
    add x1, other arithmetic, local(): featured + taps[tap_index] * jnp.where((pos_f >= tap_index)[:, None], shi...  10.7 us
    ppermute x3, starting transfers between devices, local(): lax.ppermute(tokens, 'seq', perm)  9.3 us
    unnamed x16, local copies, waits for them, and re-layouts  9.24 us
    dot_general x2, matrix products, tap_table(): jnp.einsum('ijt,tg->gij', one_hot, long_filter, preferred_element_type=jn...  7.92 us
    unnamed x5, other arithmetic  7.53 us
    dot_general x4, matrix products, local(): lax.dot_general(got, ow_cat[d * own:(d + 1) * own], (((0,), (0,)), ((), (...  7.4 us
  transfers between devices with their start and end apart: 11, of which 4 were waited for; matrix products, arithmetic and copies ran while one was open for 25% of the time, Pallas kernels for 0%

profile of v6, /device:TPU:1, one launch (start us, length us, event | category | flops | bytes accessed | tf_op | source)
XLA Modules:
  0.0 155.2 jit_solution(13304042874522965981)
XLA Ops:
  6.5 2.7 %copy.26 = bf16[2048,384]{0,1:T(8,128)(2,1)} copy(bf16[2048,384]{1,0:T(8,128)(2,1)} %param.8) | data formatting | bytes 3145728 | tf_op args[2]
  9.2 1.8 %constant_dynamic-slice_fusion.7 = bf16[3,32,2048]{2,1,0:T(8,128)(2,1)} fusion(bf16[3,128,2048]{2,1,0:T(8,128)(2,1)} %bitcast.77, s32[]{:T(128)S(6)} %select_n.178), kind=kLoop, calls=%fused_computation.73 | loop fusion | bytes 786436 | tf_op jit(solution)/shard_map/dynamic_slice | solution.py:66
  15.8 1.5 collective-permute-start.3
  17.3 3.0 %collective-permute-start.4 = (bf16[256,2048]{1,0:T(8,128)(2,1)S(1)}, bf16[256,2048]{1,0:T(8,128)(2,1)S(1)}, u32[]{:S(2)}, u32[]{:S(2)}) collective-permute-start(bf16[256,2048]{1,0:T(8,128)(2,1)S(1)} %copy-done), channel_id=1, source_target_pairs={{0,3},{1,2},{2,1},{3,0},{4,7},{5,6},{6,5},{7,4},{8,11},{9,10},{10,... | collective-permute-start | bytes 3145736 | tf_op jit(solution)/shard_map/ppermute | solution.py:42
  23.7 4.0 %fusion.28 = bf16[32,128,128]{2,0,1:T(8,128)(2,1)S(1)} fusion(bf16[128,32,1]{0,1,2:T(8,128)(2,1)S(1)} %bitcast.81, s32[128,128]{1,0:T(8,128)S(1)} %get-tuple-element.34), kind=kOutput, calls=%fused_computation.37 | convolution fusion | flops 136839168 | bytes 1122304 | tf_op jit(solution)/shard_map/ijt,tg->gij/dot_general | solution.py:22
  29.1 3.9 %fusion.29 = bf16[32,128,128]{2,0,1:T(8,128)(2,1)S(1)} fusion(bf16[128,32,1]{0,1,2:T(8,128)(2,1)S(1)} %bitcast.82, s32[128,128]{1,0:T(8,128)S(1)} %get-tuple-element.35), kind=kOutput, calls=%fused_computation.38 | convolution fusion | flops 136839168 | bytes 1122304 | tf_op jit(solution)/shard_map/ijt,tg->gij/dot_general | solution.py:22
  35.6 4.4 %constant_dynamic-slice_fusion.11 = (bf16[16,32,2048]{2,1,0:T(8,128)(2,1)S(1)}, bf16[16,32,2048]{2,1,0:T(8,128)(2,1)S(1)}, bf16[16,32,2048]{2,1,0:T(8,128)(2,1)S(1)}, bf16[16,32,2048]{2,1,0:T(8,128)(2,1)S(1)}) fusion(bf16[16,128,2048]{2,1,0:T(8,128)(2,1)} %bitcast.68, s32[]{:T(128)S(6)} %select_n.178, s32[]{:T(128)S(6)} %select_n.215, s32[]{:T(128)S(6)} %select_n.214, ...), kind=kLoop, calls=%fused_computation.77 | loop fusion | bytes 16777232 | tf_op jit(solution)/shard_map/dynamic_slice | solution.py:75
  40.0 5.6 %collective-permute-start.5 = (bf16[256,2048]{1,0:T(8,128)(2,1)S(1)}, bf16[256,2048]{1,0:T(8,128)(2,1)S(1)}, u32[]{:S(2)}, u32[]{:S(2)}) collective-permute-start(bf16[256,2048]{1,0:T(8,128)(2,1)S(1)} %copy-done), channel_id=1, source_target_pairs={{0,2},{1,3},{2,0},{3,1},{4,6},{5,7},{6,4},{7,5},{8,10},{9,11},{10,... | collective-permute-start | bytes 3145736 | tf_op jit(solution)/shard_map/ppermute | solution.py:42
  46.3 4.1 %pad_maximum_fusion = bf16[2048,2048]{1,0:T(8,128)(2,1)} fusion(bf16[512,2048]{1,0:T(8,128)(2,1)S(1)} %bitcast.72, bf16[512,2048]{1,0:T(8,128)(2,1)S(1)} %bitcast.73, bf16[512,2048]{1,0:T(8,128)(2,1)S(1)} %bitcast.74, bf16[512,2048]{1,0:T(8,128)(2,1)S(1)} %bitcast.71), kind=kLoop, calls=%fused_computation | loop fusion | flops 33554432 | bytes 16777216 | tf_op jit(solution)/shard_map/concatenate | solution.py:76
  50.4 2.3 %select_dynamic-update-slice_fusion.4 = bf16[1160,2048]{1,0:T(8,128)(2,1)} fusion(bf16[136,2048]{1,0:T(8,128)(2,1)S(1)} %collective-permute-done, bf16[136,2048]{1,0:T(8,128)(2,1)} %collective-permute-done.1, bf16[136,2048]{1,0:T(8,128)(2,1)} %collective-permute-done.2, bf16[136,2048]{1,0:T(8,128)(2,1)} %collective-permute-done.3, pred[]{:T(512)S(6)} %eq.79, ...), kind=kLoop, calls=%fused_computation.46 | loop fusion | flops 1114111 | bytes 2785284
  52.6 15.4 %collective-permute-done.5 = bf16[256,2048]{1,0:T(8,128)(2,1)S(1)} collective-permute-done((bf16[256,2048]{1,0:T(8,128)(2,1)S(1)}, bf16[256,2048]{1,0:T(8,128)(2,1)S(1)}, u32[]{:S(2)}, u32[]{:S(2)}) %collective-permute-start.5) | collective-permute-done | bytes 1048608 | tf_op jit(solution)/shard_map/ppermute | solution.py:42
  68.1 1.8 %select_dynamic-update-slice_fusion.3 = bf16[1160,2048]{1,0:T(8,128)(2,1)} fusion(bf16[1160,2048]{1,0:T(8,128)(2,1)} %select_dynamic-update-slice_fusion.4, bf16[256,2048]{1,0:T(8,128)(2,1)S(1)} %collective-permute-done.4, bf16[256,2048]{1,0:T(8,128)(2,1)S(1)} %collective-permute-done.5, bf16[256,2048]{1,0:T(8,128)(2,1)S(1)} %collective-permute-done.6, ...), kind=kLoop, calls=%fused_computation.45 | loop fusion | flops 1572864 | bytes 5242883
  69.8 1.7 %select_dynamic-update-slice_fusion.2 = bf16[1160,2048]{1,0:T(8,128)(2,1)} fusion(bf16[1160,2048]{1,0:T(8,128)(2,1)} %select_dynamic-update-slice_fusion.3, bf16[256,2048]{1,0:T(8,128)(2,1)S(1)} %collective-permute-done.4, bf16[256,2048]{1,0:T(8,128)(2,1)S(1)} %collective-permute-done.5, bf16[256,2048]{1,0:T(8,128)(2,1)S(1)} %collective-permute-done.6, ...), kind=kLoop, calls=%fused_computation.44 | loop fusion | flops 1572864 | bytes 5242883
  71.6 1.8 %select_dynamic-update-slice_fusion.1 = bf16[1160,2048]{1,0:T(8,128)(2,1)} fusion(bf16[1160,2048]{1,0:T(8,128)(2,1)} %select_dynamic-update-slice_fusion.2, bf16[256,2048]{1,0:T(8,128)(2,1)S(1)} %collective-permute-done.4, bf16[256,2048]{1,0:T(8,128)(2,1)S(1)} %collective-permute-done.5, bf16[256,2048]{1,0:T(8,128)(2,1)S(1)} %collective-permute-done.6, ...), kind=kLoop, calls=%fused_computation.43 | loop fusion | flops 1572864 | bytes 5242883
  73.3 1.7 %select_dynamic-update-slice_fusion = bf16[1160,2048]{1,0:T(8,128)(2,1)} fusion(bf16[1160,2048]{1,0:T(8,128)(2,1)} %select_dynamic-update-slice_fusion.1, bf16[256,2048]{1,0:T(8,128)(2,1)S(1)} %collective-permute-done.4, bf16[256,2048]{1,0:T(8,128)(2,1)S(1)} %collective-permute-done.5, bf16[256,2048]{1,0:T(8,128)(2,1)S(1)} %collective-permute-done.6, ...), kind=kLoop, calls=%fused_computation.42 | loop fusion | flops 1572864 | bytes 5242883 | tf_op jit(solution)/shard_map/concatenate | solution.py:56
  75.1 6.3 %all-gather.2.cloned.1.call-done = bf16[48,32,2048]{2,1,0:T(8,128)(2,1)} async-done(((bf16[3,32,2048]{2,1,0:T(8,128)(2,1)}), bf16[48,32,2048]{2,1,0:T(8,128)(2,1)}) %all-gather.2.cloned.1.call-update) | async-done | bytes 6291472 | tf_op jit(solution)/shard_map/all_gather | solution.py:67
  81.4 11.2 %convolution_convert_fusion = bf16[1160,1536]{1,0:T(8,128)(2,1)S(1)} fusion(bf16[1160,2048]{1,0:T(8,128)(2,1)} %select_dynamic-update-slice_fusion, bf16[1536,2048]{1,0:T(8,128)(2,1)} %bitcast.83), kind=kOutput, calls=%fused_computation.11 | convolution fusion | flops 7299870720 | bytes 14606336 | tf_op jit(solution)/shard_map/dot_general | solution.py:78
  92.5 10.7 %multiply_add_fusion = f32[1152,1536]{1,0:T(8,128)S(1)} fusion(bf16[1160,1536]{1,0:T(8,128)(2,1)S(1)} %convolution_convert_fusion, f32[1536]{0:T(1024)S(1)} %mul.115, f32[1536]{0:T(1024)S(1)} %mul.112, f32[1536]{0:T(1024)S(1)} %mul.109, f32[1536]{0:T(1024)S(1)} %mul.106, f32[1536]{0:T(1024)S(1)} %mul.103, f32[1536]{0:T(1024)S(1)} %mul.100, ...), kind=kLoop, calls=%fused_computation.12 | loop fusion | flops 47775744 | bytes 31901568 | tf_op jit(solution)/shard_map/add | solution.py:91
  103.2 2.9 %copy-done.1 = f32[1152,1536]{1,0:T(8,128)} copy-done((f32[1152,1536]{1,0:T(8,128)}, f32[1152,1536]{1,0:T(8,128)S(1)}, u32[]{:S(2)}) %copy-start.1) | copy-done | bytes 7077912
  107.6 1.7 %copy.29 = bf16[512,1152]{1,0:T(8,128)(2,1)S(1)} copy(bf16[512,1152]{0,1:T(8,128)(2,1)} %fusion.30) | data formatting | bytes 2359296 | tf_op jit(solution)/shard_map/transpose | solution.py:119
  109.2 1.7 %reshape.154 = bf16[32,16,9,128]{3,2,1,0:T(8,128)(2,1)} reshape(bf16[512,1152]{1,0:T(8,128)(2,1)S(1)} %copy.29) | data formatting | bytes 2359296 | tf_op jit(solution)/shard_map/reshape | solution.py:119
  110.9 2.3 %fusion.39 = (bf16[32,16,8,128]{3,2,1,0:T(8,128)(2,1)S(1)}, bf16[32,16,8,128]{3,2,1,0:T(8,128)(2,1)S(1)}) fusion(bf16[32,16,9,128]{3,2,1,0:T(8,128)(2,1)} %reshape.154), kind=kLoop, calls=%fused_computation.85 | loop fusion | bytes 4194304 | tf_op jit(solution)/shard_map/slice | solution.py:121
  113.2 5.8 %fusion = f32[32,8,128,16]{2,3,1,0:T(8,128)S(1)} fusion(pred[8,128,128]{2,1,0:T(8,128)(4,1)} %get-tuple-element.33, bf16[32,128,128]{2,1,0:T(8,128)(2,1)} %copy.31, bf16[32,16,8,128]{3,2,1,0:T(8,128)(2,1)S(1)} %get-tuple-element.14), kind=kOutput, calls=%fused_computation.1 | convolution fusion | flops 138412032 | bytes 4325376 | tf_op jit(solution)/shard_map/gcbj,bgij->gcbi/dot_general | solution.py:123
  119.1 4.5 %add_bitcast_fusion = f32[32,16,8,128]{3,1,2,0:T(8,128)S(1)} fusion(f32[32,8,128,16]{2,3,1,0:T(8,128)S(1)} %fusion, pred[8,128,128]{2,1,0:T(8,128)(4,1)S(1)} %get-tuple-element.32, bf16[32,128,128]{2,1,0:T(8,128)(2,1)S(1)} %copy-done.2, bf16[32,16,8,128]{3,2,1,0:T(8,128)(2,1)S(1)} %get-tuple-element.13), kind=kOutput, calls=%fused_computation.36 | convolution fusion | flops 138936320 | bytes 6422528 | tf_op jit(solution)/shard_map/gcbj,bgij->gcbi/dot_general | solution.py:120
  124.4 1.8 %copy.44 = f32[64,8,8,128]{3,1,2,0:T(8,128)} copy(f32[64,8,8,128]{3,2,1,0:T(8,128)S(1)} %bitcast.69) | data formatting | bytes 4194304
  126.2 2.9 %copy.34 = f32[512,1024]{0,1:T(8,128)} copy(f32[512,1024]{1,0:T(8,128)} %bitcast.70) | data formatting | bytes 4194304 | tf_op jit(solution)/shard_map/reshape | solution.py:126
  129.1 2.7 %fusion.19 = bf16[512,1024]{0,1:T(8,128)(2,1)S(1)} fusion(f32[512,1024]{0,1:T(8,128)} %copy.34, f32[1152,1536]{1,0:T(8,128)} %copy-done.1), kind=kLoop, calls=%fused_computation.29 | loop fusion | flops 1048576 | bytes 5242880 | tf_op jit(solution)/shard_map/convert_element_type | solution.py:127
  134.3 2.5 %convolution_add_fusion.1 = f32[256,2048]{1,0:T(8,128)S(1)} fusion(bf16[2048,2048]{1,0:T(8,128)(2,1)} %pad_maximum_fusion, bf16[256,2048]{1,0:T(8,128)(2,1)S(1)} %copy-done, bf16[512,4,256]{0,2,1:T(8,128)(2,1)S(1)} %bitcast.76, s32[]{:T(128)S(6)} %select_n.227), kind=kOutput, calls=%fused_computation.21 | convolution fusion | flops 537919488 | bytes 5505028 | tf_op jit(solution)/shard_map/dot_general | solution.py:135
  136.8 2.4 %collective-permute-done.8 = bf16[512,256]{0,1:T(8,128)(2,1)S(1)} collective-permute-done((bf16[512,256]{0,1:T(8,128)(2,1)S(1)}, bf16[512,256]{0,1:T(8,128)(2,1)S(1)}, u32[]{:S(2)}, u32[]{:S(2)}) %collective-permute-start.8) | collective-permute-done | bytes 262176 | tf_op jit(solution)/shard_map/ppermute | solution.py:134
  139.2 2.3 %fusion.22 = f32[256,2048]{1,0:T(8,128)S(1)} fusion(bf16[512,256]{0,1:T(8,128)(2,1)S(1)} %collective-permute-done.8, bf16[2048,2048]{1,0:T(8,128)(2,1)} %pad_maximum_fusion), kind=kOutput, calls=%fused_computation.32 | convolution fusion | flops 536870912 | bytes 4456448 | tf_op jit(solution)/shard_map/dot_general | solution.py:135
  141.5 4.1 %collective-permute-done.9 = bf16[512,256]{0,1:T(8,128)(2,1)S(1)} collective-permute-done((bf16[512,256]{0,1:T(8,128)(2,1)S(1)}, bf16[512,256]{0,1:T(8,128)(2,1)S(1)}, u32[]{:S(2)}, u32[]{:S(2)}) %collective-permute-start.9) | collective-permute-done | bytes 262176 | tf_op jit(solution)/shard_map/ppermute | solution.py:134
  146.4 1.9 %fusion.16 = bf16[256,2048]{1,0:T(8,128)(2,1)} fusion(f32[256,2048]{1,0:T(8,128)S(1)} %fusion.20, f32[256,2048]{1,0:T(8,128)S(1)} %fusion.22, f32[256,2048]{1,0:T(8,128)S(1)} %convolution_add_fusion.1, bf16[512,256]{0,1:T(8,128)(2,1)S(1)} %collective-permute-done.7, bf16[2048,2048]{1,0:T(8,128)(2,1)S(1)} %bitcast.67), kind=kOutput, calls=%fused_computation.23 | convolution fusion | flops 538968064 | bytes 9699328 | tf_op jit(solution)/shard_map/dot_general | solution.py:135
  (56 shorter events, 18.2 us)
Async XLA Ops:
  6.5 10.7 %copy-start = (bf16[256,2048]{1,0:T(8,128)(2,1)S(1)}, bf16[256,2048]{1,0:T(8,128)(2,1)}, u32[]{:S(2)}) copy-start(bf16[256,2048]{1,0:T(8,128)(2,1)} %param.6) | copy-start | bytes 3145732
  6.5 74.8 %all-gather.2.cloned.1.call-start = ((), (), s32[]{:S(2)}) async-start(), calls=%async_computation | async-start | bytes 6684672 | tf_op jit(solution)/shard_map/all_gather | solution.py:67
  12.1 27.9 %collective-permute-start = (bf16[136,2048]{1,0:T(8,128)(2,1)S(1)}, bf16[136,2048]{1,0:T(8,128)(2,1)S(1)}, u32[]{:S(2)}, u32[]{:S(2)}) collective-permute-start(bf16[136,2048]{1,0:T(8,128)(2,1)S(1)} %slice.87), channel_id=1, source_target_pairs={{3,7},{7,11},{11,15},{19,23},{23,27},{27,31},{35,39},{39,43},{43,4... | collective-permute-start | bytes 1671176 | tf_op jit(solution)/shard_map/ppermute | solution.py:54
  12.8 32.8 %collective-permute-start.1 = (bf16[136,2048]{1,0:T(8,128)(2,1)S(1)}, bf16[136,2048]{1,0:T(8,128)(2,1)}, u32[]{:S(2)}, u32[]{:S(2)}) collective-permute-start(bf16[136,2048]{1,0:T(8,128)(2,1)S(1)} %slice.87), channel_id=1, source_target_pairs={{3,6},{7,10},{11,14},{19,22},{23,26},{27,30},{35,38},{39,42},{43,4... | collective-permute-start | bytes 1671176 | tf_op jit(solution)/shard_map/ppermute | solution.py:54
  14.3 36.1 %collective-permute-start.2 = (bf16[136,2048]{1,0:T(8,128)(2,1)S(1)}, bf16[136,2048]{1,0:T(8,128)(2,1)}, u32[]{:S(2)}, u32[]{:S(2)}) collective-permute-start(bf16[136,2048]{1,0:T(8,128)(2,1)S(1)} %slice.87), channel_id=1, source_target_pairs={{3,5},{7,9},{11,13},{19,21},{23,25},{27,29},{35,37},{39,41},{43,45... | collective-permute-start | bytes 1671176 | tf_op jit(solution)/shard_map/ppermute | solution.py:54
  15.8 34.6 %collective-permute-start.3 = (bf16[136,2048]{1,0:T(8,128)(2,1)S(1)}, bf16[136,2048]{1,0:T(8,128)(2,1)}, u32[]{:S(2)}, u32[]{:S(2)}) collective-permute-start(bf16[136,2048]{1,0:T(8,128)(2,1)S(1)} %slice.87), channel_id=1, source_target_pairs={{3,4},{7,8},{11,12},{19,20},{23,24},{27,28},{35,36},{39,40},{43,44... | collective-permute-start | bytes 1671176 | tf_op jit(solution)/shard_map/ppermute | solution.py:54
  17.3 35.4 %collective-permute-start.4 = (bf16[256,2048]{1,0:T(8,128)(2,1)S(1)}, bf16[256,2048]{1,0:T(8,128)(2,1)S(1)}, u32[]{:S(2)}, u32[]{:S(2)}) collective-permute-start(bf16[256,2048]{1,0:T(8,128)(2,1)S(1)} %copy-done), channel_id=1, source_target_pairs={{0,3},{1,2},{2,1},{3,0},{4,7},{5,6},{6,5},{7,4},{8,11},{9,10},{10,... | collective-permute-start | bytes 3145736 | tf_op jit(solution)/shard_map/ppermute | solution.py:42
  21.8 12.6 %copy-start.3 = (s32[1,4]{1,0:T(1,128)S(1)}, s32[1,4]{1,0:T(1,128)}, u32[]{:S(2)}) copy-start(s32[1,4]{1,0:T(1,128)} %param.7) | copy-start | bytes 52
  40.0 28.1 %collective-permute-start.5 = (bf16[256,2048]{1,0:T(8,128)(2,1)S(1)}, bf16[256,2048]{1,0:T(8,128)(2,1)S(1)}, u32[]{:S(2)}, u32[]{:S(2)}) collective-permute-start(bf16[256,2048]{1,0:T(8,128)(2,1)S(1)} %copy-done), channel_id=1, source_target_pairs={{0,2},{1,3},{2,0},{3,1},{4,6},{5,7},{6,4},{7,5},{8,10},{9,11},{10,... | collective-permute-start | bytes 3145736 | tf_op jit(solution)/shard_map/ppermute | solution.py:42
  45.6 22.5 %collective-permute-start.6 = (bf16[256,2048]{1,0:T(8,128)(2,1)S(1)}, bf16[256,2048]{1,0:T(8,128)(2,1)S(1)}, u32[]{:S(2)}, u32[]{:S(2)}) collective-permute-start(bf16[256,2048]{1,0:T(8,128)(2,1)S(1)} %copy-done), channel_id=1, source_target_pairs={{0,1},{1,0},{2,3},{3,2},{4,5},{5,4},{6,7},{7,6},{8,9},{9,8},{10,11... | collective-permute-start | bytes 3145736 | tf_op jit(solution)/shard_map/ppermute | solution.py:42
  103.2 2.9 %copy-start.1 = (f32[1152,1536]{1,0:T(8,128)}, f32[1152,1536]{1,0:T(8,128)S(1)}, u32[]{:S(2)}) copy-start(f32[1152,1536]{1,0:T(8,128)S(1)} %multiply_add_fusion) | copy-start | bytes 21233668
  113.2 5.8 %copy-start.2 = (bf16[32,128,128]{2,1,0:T(8,128)(2,1)S(1)}, bf16[32,128,128]{2,1,0:T(8,128)(2,1)}, u32[]{:S(2)}) copy-start(bf16[32,128,128]{2,1,0:T(8,128)(2,1)} %copy.28) | copy-start | bytes 3145732
  129.1 16.6 %slice-start = ((s8[8388608]{0:T(1024)(128)(4,1)}), s8[4194304]{0:T(1024)(128)(4,1)S(1)}, s32[]{:S(2)}) async-start(s8[8388608]{0:T(1024)(128)(4,1)} %bitcast.66), calls=%async_computation.1 | async-start | bytes 8388608
  131.9 7.3 %collective-permute-start.8 = (bf16[512,256]{0,1:T(8,128)(2,1)S(1)}, bf16[512,256]{0,1:T(8,128)(2,1)S(1)}, u32[]{:S(2)}, u32[]{:S(2)}) collective-permute-start(bf16[512,256]{0,1:T(8,128)(2,1)S(1)} %get-tuple-element.17), channel_id=1, source_target_pairs={{0,2},{1,3},{2,0},{3,1},{4,6},{5,7},{6,4},{7,5},{8,10},{9,11},{10,... | collective-permute-start | bytes 786440 | tf_op jit(solution)/shard_map/ppermute | solution.py:134
  133.3 12.4 %collective-permute-start.9 = (bf16[512,256]{0,1:T(8,128)(2,1)S(1)}, bf16[512,256]{0,1:T(8,128)(2,1)S(1)}, u32[]{:S(2)}, u32[]{:S(2)}) collective-permute-start(bf16[512,256]{0,1:T(8,128)(2,1)S(1)} %get-tuple-element.16), channel_id=1, source_target_pairs={{0,3},{1,2},{2,1},{3,0},{4,7},{5,6},{6,5},{7,4},{8,11},{9,10},{10,... | collective-permute-start | bytes 786440 | tf_op jit(solution)/shard_map/ppermute | solution.py:134
  134.3 11.3 %slice-start.1 = ((s8[8388608]{0:T(1024)(128)(4,1)}), s8[4194304]{0:T(1024)(128)(4,1)S(1)}, s32[]{:S(2)}) async-start(s8[8388608]{0:T(1024)(128)(4,1)} %bitcast.66), calls=%async_computation.2 | async-start | bytes 8388608
  134.3 12.1 %collective-permute-start.7 = (bf16[512,256]{0,1:T(8,128)(2,1)S(1)}, bf16[512,256]{0,1:T(8,128)(2,1)S(1)}, u32[]{:S(2)}, u32[]{:S(2)}) collective-permute-start(bf16[512,256]{0,1:T(8,128)(2,1)S(1)} %get-tuple-element.15), channel_id=1, source_target_pairs={{0,1},{1,0},{2,3},{3,2},{4,5},{5,4},{6,7},{7,6},{8,9},{9,8},{10,11... | collective-permute-start | bytes 786440 | tf_op jit(solution)/shard_map/ppermute | solution.py:134
Sparse Core Ops, SparseCore 0:
  11.2 70.1 all-gather.1

commit v7 on v6

--- a/solution.py
+++ b/solution.py
@@ -118,26 +118,25 @@
 
     mi_t = mixed_in.T.reshape(n_groups, per_group, n_blocks + 1, filter_len)
     filtered = jnp.einsum(
-        "gcbj,bgij->gcbi", mi_t[:, :, 1:], cur_kernel, preferred_element_type=jnp.float32
+        "gcbj,bgij->gbci", mi_t[:, :, 1:], cur_kernel, preferred_element_type=jnp.float32
     )
     filtered = filtered + jnp.einsum(
-        "gcbj,bgij->gcbi", mi_t[:, :, :-1], prev_kernel, preferred_element_type=jnp.float32
+        "gcbj,bgij->gbci", mi_t[:, :, :-1], prev_kernel, preferred_element_type=jnp.float32
     )
-    filtered = filtered.reshape(own, span)
-    gated = (queries.T * filtered).astype(jnp.bfloat16)
+    q_t = queries.reshape(n_blocks, filter_len, n_groups, per_group).transpose(2, 0, 3, 1)
+    gated = (q_t * filtered).astype(jnp.bfloat16)
 
-
-    gated = gated.reshape(own, GROUP_DEVS, rows)
+    per_member = rows // filter_len
+    gated = gated.reshape(n_groups, GROUP_DEVS, per_member, per_group, filter_len)
+    ow_cat = ow_cat.reshape(GROUP_DEVS, n_groups, per_group, channels)
     result = tokens.astype(jnp.float32)
     for d in range(GROUP_DEVS):
         send = lax.dynamic_index_in_dim(gated, member ^ d, axis=1, keepdims=False)
         got = send if d == 0 else lax.ppermute(send, "seq", swaps[d - 1])
-        result = result + lax.dot_general(
-            got,
-            ow_cat[d * own : (d + 1) * own],
-            (((0,), (0,)), ((), ())),
-            preferred_element_type=jnp.float32,
+        part_out = lax.dot_general(
+            got, ow_cat[d], (((0, 2), (0, 1)), ((), ())), preferred_element_type=jnp.float32
         )
+        result = result + part_out.reshape(rows, channels)
     return result.astype(jnp.bfloat16)
 
 

time: 157 us -> 162 us (1.032)
  the two profiles are of different devices: /device:TPU:1 before, /device:TPU:183 now
where the time goes in v7:
time: 162 us; the launch traced here: 161 us
  matrix products  40 us (25%)
  waiting for transfers between devices  36.7 us (23%)
  local copies, waits for them, and re-layouts  33.6 us (21%)
  other arithmetic  23.4 us (14%)
  starting transfers between devices  13.8 us (9%)
  between operations  13.8 us (9%)
    ppermute x3, waiting for transfers between devices, local(): lax.ppermute(tokens, 'seq', perm)  30 us
    dot_general x4, matrix products, local(): lax.dot_general(got, ow_cat[d], (((0, 2), (0, 1)), ((), ())), preferred_e...  11.9 us
    dot_general x1, matrix products, local(): jnp.dot(ext_tokens, w_all.T, preferred_element_type=jnp.float32)  11.2 us
    add x1, other arithmetic, local(): featured + taps[tap_index] * jnp.where((pos_f >= tap_index)[:, None], shi...  10.7 us
    ppermute x4, starting transfers between devices, local(): got = lax.ppermute(tail_src, 'seq', perm)  9.44 us
    dot_general x2, matrix products, tap_table(): jnp.einsum('ijt,tg->gij', one_hot, long_filter, preferred_element_type=jn...  7.92 us
    unnamed x22, local copies, waits for them, and re-layouts  7.37 us
    ppermute x3, waiting for transfers between devices, local(): got = send if d == 0 else lax.ppermute(send, 'seq', swaps[d - 1])  6.71 us
  transfers between devices with their start and end apart: 11, of which 4 were waited for; matrix products, arithmetic and copies ran while one was open for 23% of the time, Pallas kernels for 0%

profile of v7, /device:TPU:183, one launch (start us, length us, event | category | flops | bytes accessed | tf_op | source)
XLA Modules:
  0.0 161.2 jit_solution(14988435403437711492)
XLA Ops:
  6.5 2.7 %copy.50 = bf16[2048,384]{0,1:T(8,128)(2,1)} copy(bf16[2048,384]{1,0:T(8,128)(2,1)} %param.8) | data formatting | bytes 3145728 | tf_op args[2]
  9.2 1.8 %constant_dynamic-slice_fusion.7 = bf16[3,32,2048]{2,1,0:T(8,128)(2,1)} fusion(bf16[3,128,2048]{2,1,0:T(8,128)(2,1)} %bitcast.111, s32[]{:T(128)S(6)} %select_n.178), kind=kLoop, calls=%fused_computation.70 | loop fusion | bytes 786436 | tf_op jit(solution)/shard_map/dynamic_slice | solution.py:66
  11.1 3.1 %collective-permute-start = (bf16[136,2048]{1,0:T(8,128)(2,1)S(1)}, bf16[136,2048]{1,0:T(8,128)(2,1)S(1)}, u32[]{:S(2)}, u32[]{:S(2)}) collective-permute-start(bf16[136,2048]{1,0:T(8,128)(2,1)S(1)} %slice.91), channel_id=1, source_target_pairs={{3,7},{7,11},{11,15},{19,23},{23,27},{27,31},{35,39},{39,43},{43,4... | collective-permute-start | bytes 1671176 | tf_op jit(solution)/shard_map/ppermute | solution.py:54
  14.2 2.1 %collective-permute-start.1 = (bf16[136,2048]{1,0:T(8,128)(2,1)S(1)}, bf16[136,2048]{1,0:T(8,128)(2,1)}, u32[]{:S(2)}, u32[]{:S(2)}) collective-permute-start(bf16[136,2048]{1,0:T(8,128)(2,1)S(1)} %slice.91), channel_id=1, source_target_pairs={{3,6},{7,10},{11,14},{19,22},{23,26},{27,30},{35,38},{39,42},{43,4... | collective-permute-start | bytes 1671176 | tf_op jit(solution)/shard_map/ppermute | solution.py:54
  16.3 2.1 %collective-permute-start.2 = (bf16[136,2048]{1,0:T(8,128)(2,1)S(1)}, bf16[136,2048]{1,0:T(8,128)(2,1)}, u32[]{:S(2)}, u32[]{:S(2)}) collective-permute-start(bf16[136,2048]{1,0:T(8,128)(2,1)S(1)} %slice.91), channel_id=1, source_target_pairs={{3,5},{7,9},{11,13},{19,21},{23,25},{27,29},{35,37},{39,41},{43,45... | collective-permute-start | bytes 1671176 | tf_op jit(solution)/shard_map/ppermute | solution.py:54
  18.4 2.1 %collective-permute-start.3 = (bf16[136,2048]{1,0:T(8,128)(2,1)S(1)}, bf16[136,2048]{1,0:T(8,128)(2,1)}, u32[]{:S(2)}, u32[]{:S(2)}) collective-permute-start(bf16[136,2048]{1,0:T(8,128)(2,1)S(1)} %slice.91), channel_id=1, source_target_pairs={{3,4},{7,8},{11,12},{19,20},{23,24},{27,28},{35,36},{39,40},{43,44... | collective-permute-start | bytes 1671176 | tf_op jit(solution)/shard_map/ppermute | solution.py:54
  24.0 4.0 %fusion.27 = bf16[32,128,128]{2,0,1:T(8,128)(2,1)S(1)} fusion(bf16[128,32,1]{0,1,2:T(8,128)(2,1)S(1)} %bitcast.124, s32[128,128]{1,0:T(8,128)S(1)} %get-tuple-element.39), kind=kOutput, calls=%fused_computation.36 | convolution fusion | flops 136839168 | bytes 1122304 | tf_op jit(solution)/shard_map/ijt,tg->gij/dot_general | solution.py:22
  29.3 3.9 %fusion.28 = bf16[32,128,128]{2,0,1:T(8,128)(2,1)S(1)} fusion(bf16[128,32,1]{0,1,2:T(8,128)(2,1)S(1)} %bitcast.125, s32[128,128]{1,0:T(8,128)S(1)} %get-tuple-element.40), kind=kOutput, calls=%fused_computation.37 | convolution fusion | flops 136839168 | bytes 1122304 | tf_op jit(solution)/shard_map/ijt,tg->gij/dot_general | solution.py:22
  35.8 4.3 %constant_dynamic-slice_fusion.11 = (bf16[16,32,2048]{2,1,0:T(8,128)(2,1)S(1)}, bf16[16,32,2048]{2,1,0:T(8,128)(2,1)S(1)}, bf16[16,32,2048]{2,1,0:T(8,128)(2,1)S(1)}, bf16[16,32,2048]{2,1,0:T(8,128)(2,1)S(1)}) fusion(bf16[16,128,2048]{2,1,0:T(8,128)(2,1)} %bitcast.105, s32[]{:T(128)S(6)} %select_n.178, s32[]{:T(128)S(6)} %select_n.215, s32[]{:T(128)S(6)} %select_n.214, ...), kind=kLoop, calls=%fused_computation.74 | loop fusion | bytes 16777232 | tf_op jit(solution)/shard_map/dynamic_slice | solution.py:75
  40.3 2.1 %collective-permute-start.6 = (bf16[256,2048]{1,0:T(8,128)(2,1)S(1)}, bf16[256,2048]{1,0:T(8,128)(2,1)S(1)}, u32[]{:S(2)}, u32[]{:S(2)}) collective-permute-start(bf16[256,2048]{1,0:T(8,128)(2,1)S(1)} %copy-done), channel_id=1, source_target_pairs={{0,1},{1,0},{2,3},{3,2},{4,5},{5,4},{6,7},{7,6},{8,9},{9,8},{10,11... | collective-permute-start | bytes 3145736 | tf_op jit(solution)/shard_map/ppermute | solution.py:42
  44.7 7.7 %collective-permute-done.4 = bf16[256,2048]{1,0:T(8,128)(2,1)S(1)} collective-permute-done((bf16[256,2048]{1,0:T(8,128)(2,1)S(1)}, bf16[256,2048]{1,0:T(8,128)(2,1)S(1)}, u32[]{:S(2)}, u32[]{:S(2)}) %collective-permute-start.4) | collective-permute-done | bytes 1048608 | tf_op jit(solution)/shard_map/ppermute | solution.py:42
  52.4 22.3 %collective-permute-done.5 = bf16[256,2048]{1,0:T(8,128)(2,1)S(1)} collective-permute-done((bf16[256,2048]{1,0:T(8,128)(2,1)S(1)}, bf16[256,2048]{1,0:T(8,128)(2,1)S(1)}, u32[]{:S(2)}, u32[]{:S(2)}) %collective-permute-start.5) | collective-permute-done | bytes 1048608 | tf_op jit(solution)/shard_map/ppermute | solution.py:42
  74.7 1.8 %select_dynamic-update-slice_fusion.3 = bf16[1160,2048]{1,0:T(8,128)(2,1)} fusion(bf16[1160,2048]{1,0:T(8,128)(2,1)} %select_dynamic-update-slice_fusion.4, bf16[256,2048]{1,0:T(8,128)(2,1)S(1)} %collective-permute-done.4, bf16[256,2048]{1,0:T(8,128)(2,1)S(1)} %collective-permute-done.5, bf16[256,2048]{1,0:T(8,128)(2,1)S(1)} %collective-permute-done.6, ...), kind=kLoop, calls=%fused_computation.44 | loop fusion | flops 1572864 | bytes 5242883
  76.4 1.8 %select_dynamic-update-slice_fusion.2 = bf16[1160,2048]{1,0:T(8,128)(2,1)} fusion(bf16[1160,2048]{1,0:T(8,128)(2,1)} %select_dynamic-update-slice_fusion.3, bf16[256,2048]{1,0:T(8,128)(2,1)S(1)} %collective-permute-done.4, bf16[256,2048]{1,0:T(8,128)(2,1)S(1)} %collective-permute-done.5, bf16[256,2048]{1,0:T(8,128)(2,1)S(1)} %collective-permute-done.6, ...), kind=kLoop, calls=%fused_computation.43 | loop fusion | flops 1572864 | bytes 5242883
  78.3 1.7 %select_dynamic-update-slice_fusion.1 = bf16[1160,2048]{1,0:T(8,128)(2,1)} fusion(bf16[1160,2048]{1,0:T(8,128)(2,1)} %select_dynamic-update-slice_fusion.2, bf16[256,2048]{1,0:T(8,128)(2,1)S(1)} %collective-permute-done.4, bf16[256,2048]{1,0:T(8,128)(2,1)S(1)} %collective-permute-done.5, bf16[256,2048]{1,0:T(8,128)(2,1)S(1)} %collective-permute-done.6, ...), kind=kLoop, calls=%fused_computation.42 | loop fusion | flops 1572864 | bytes 5242883
  80.0 1.7 %select_dynamic-update-slice_fusion = bf16[1160,2048]{1,0:T(8,128)(2,1)} fusion(bf16[1160,2048]{1,0:T(8,128)(2,1)} %select_dynamic-update-slice_fusion.1, bf16[256,2048]{1,0:T(8,128)(2,1)S(1)} %collective-permute-done.4, bf16[256,2048]{1,0:T(8,128)(2,1)S(1)} %collective-permute-done.5, bf16[256,2048]{1,0:T(8,128)(2,1)S(1)} %collective-permute-done.6, ...), kind=kLoop, calls=%fused_computation.41 | loop fusion | flops 1572864 | bytes 5242883 | tf_op jit(solution)/shard_map/concatenate | solution.py:56
  81.7 3.6 %fusion.35 = (bf16[512,2048]{1,0:T(8,128)(2,1)}, bf16[512,2048]{1,0:T(8,128)(2,1)}, bf16[512,2048]{1,0:T(8,128)(2,1)}, bf16[512,2048]{1,0:T(8,128)(2,1)}) fusion(bf16[2048,2048]{1,0:T(8,128)(2,1)S(1)} %pad_maximum_fusion), kind=kLoop, calls=%fused_computation.82 | loop fusion | bytes 16777216 | tf_op jit(solution)/shard_map/slice | solution.py:137
  85.3 11.2 %convolution_convert_fusion = bf16[1160,1536]{1,0:T(8,128)(2,1)S(1)} fusion(bf16[1160,2048]{1,0:T(8,128)(2,1)} %select_dynamic-update-slice_fusion, bf16[1536,2048]{1,0:T(8,128)(2,1)} %bitcast.126), kind=kOutput, calls=%fused_computation.11 | convolution fusion | flops 7299870720 | bytes 14606336 | tf_op jit(solution)/shard_map/dot_general | solution.py:78
  96.5 10.7 %multiply_add_fusion = f32[1152,1536]{1,0:T(8,128)S(1)} fusion(bf16[1160,1536]{1,0:T(8,128)(2,1)S(1)} %convolution_convert_fusion, f32[1536]{0:T(1024)S(1)} %mul.115, f32[1536]{0:T(1024)S(1)} %mul.112, f32[1536]{0:T(1024)S(1)} %mul.109, f32[1536]{0:T(1024)S(1)} %mul.106, f32[1536]{0:T(1024)S(1)} %mul.103, f32[1536]{0:T(1024)S(1)} %mul.100, ...), kind=kLoop, calls=%fused_computation.12 | loop fusion | flops 47775744 | bytes 31901568 | tf_op jit(solution)/shard_map/add | solution.py:91
  110.1 1.7 %copy.53 = bf16[512,1152]{1,0:T(8,128)(2,1)S(1)} copy(bf16[512,1152]{0,1:T(8,128)(2,1)} %fusion.29) | data formatting | bytes 2359296 | tf_op jit(solution)/shard_map/transpose | solution.py:119
  111.8 1.7 %reshape.170 = bf16[32,16,9,128]{3,2,1,0:T(8,128)(2,1)} reshape(bf16[512,1152]{1,0:T(8,128)(2,1)S(1)} %copy.53) | data formatting | bytes 2359296 | tf_op jit(solution)/shard_map/reshape | solution.py:119
  113.5 3.4 %fusion.36 = (bf16[32,16,8,128]{3,2,1,0:T(8,128)(2,1)S(1)}, bf16[32,16,8,128]{3,2,1,0:T(8,128)(2,1)}) fusion(bf16[32,16,9,128]{3,2,1,0:T(8,128)(2,1)} %reshape.170), kind=kLoop, calls=%fused_computation.83 | loop fusion | bytes 4194304 | tf_op jit(solution)/shard_map/slice | solution.py:121
  116.9 3.0 %copy.51 = f32[1024,512]{0,1:T(8,128)} copy(f32[1024,512]{1,0:T(8,128)} %slice.123) | data formatting | bytes 4194304 | tf_op jit(solution)/shard_map/slice | solution.py:94
  119.8 2.1 %copy.78 = f32[64,8,8,128]{3,2,1,0:T(8,128)S(1)} copy(f32[64,8,8,128]{3,1,2,0:T(8,128)} %bitcast.106) | data formatting | bytes 4194304
  122.0 4.5 %fusion = f32[32,8,16,128]{3,2,1,0:T(8,128)S(1)} fusion(pred[8,128,128]{2,1,0:T(8,128)(4,1)S(1)} %copy-done.6, bf16[32,128,128]{2,1,0:T(8,128)(2,1)S(1)} %copy-done.4, bf16[32,16,8,128]{3,2,1,0:T(8,128)(2,1)S(1)} %copy-done.5), kind=kOutput, calls=%fused_computation.1 | convolution fusion | flops 138412032 | bytes 4325376 | tf_op jit(solution)/shard_map/gcbj,bgij->gbci/dot_general | solution.py:123
  126.5 4.5 %fusion.20 = bf16[32,8,16,128]{3,2,1,0:T(8,128)(2,1)S(1)} fusion(f32[8,128,32,16]{1,0,3,2:T(8,128)S(1)} %bitcast.112, f32[32,8,16,128]{3,2,1,0:T(8,128)S(1)} %fusion, pred[8,128,128]{2,1,0:T(8,128)(4,1)S(1)} %get-tuple-element.37, bf16[32,128,128]{2,1,0:T(8,128)(2,1)S(1)} %copy-done.3, bf16[32,16,8,128]{3,2,1,0:T(8,128)(2,1)S(1)} %get-tuple-element.17), kind=kOutput, calls=%fused_computation.31 | convolution fusion | flops 139984896 | bytes 7471104 | tf_op jit(solution)/shard_map/gcbj,bgij->gbci/dot_general | solution.py:120
  131.7 2.0 %collective-permute-start.9 = (bf16[32,2,16,128]{3,2,1,0:T(8,128)(2,1)S(1)}, bf16[32,2,16,128]{3,2,1,0:T(8,128)(2,1)S(1)}, u32[]{:S(2)}, u32[]{:S(2)}) collective-permute-start(bf16[32,2,16,128]{3,2,1,0:T(8,128)(2,1)S(1)} %get-tuple-element.22), channel_id=1, source_target_pairs={{0,3},{1,2},{2,1},{3,0},{4,7},{5,6},{6,5},{7,4},{8,11},{9,10},{10,... | collective-permute-start | bytes 786440 | tf_op jit(solution)/shard_map/ppermute | solution.py:135
  133.7 4.5 %fusion.14 = f32[256,2048]{1,0:T(8,128)} fusion(bf16[256,32,16]{0,1,2:T(8,128)(2,1)S(1)} %dot_general.49, bf16[32,16,2048]{2,1,0:T(8,128)(2,1)} %bitcast.116, bf16[256,2048]{1,0:T(8,128)(2,1)S(1)} %copy-done), kind=kOutput, calls=%fused_computation.23 | convolution fusion | flops 537919488 | bytes 5505024 | tf_op jit(solution)/shard_map/dot_general | solution.py:136
  139.6 5.7 %collective-permute-done.9 = bf16[32,2,16,128]{3,2,1,0:T(8,128)(2,1)S(1)} collective-permute-done((bf16[32,2,16,128]{3,2,1,0:T(8,128)(2,1)S(1)}, bf16[32,2,16,128]{3,2,1,0:T(8,128)(2,1)S(1)}, u32[]{:S(2)}, u32[]{:S(2)}) %collective-permute-start.9) | collective-permute-done | bytes 262176 | tf_op jit(solution)/shard_map/ppermute | solution.py:135
  146.2 3.3 %convolution_bitcast_fusion.1 = f32[256,2048]{1,0:T(8,128)S(1)} fusion(bf16[256,32,16]{0,1,2:T(8,128)(2,1)S(1)} %dot_general.55, bf16[32,16,2048]{2,1,0:T(8,128)(2,1)} %bitcast.115), kind=kOutput, calls=%fused_computation.20 | convolution fusion | flops 536870912 | bytes 4456448 | tf_op jit(solution)/shard_map/dot_general | solution.py:136
  149.5 1.5 convolution_bitcast_fusion
  151.7 2.7 %fusion.18 = bf16[256,2048]{1,0:T(8,128)(2,1)} fusion(f32[256,2048]{1,0:T(8,128)S(1)} %convolution_bitcast_fusion, f32[256,2048]{1,0:T(8,128)S(1)} %convolution_bitcast_fusion.1, f32[256,2048]{1,0:T(8,128)S(1)} %copy-done.8, bf16[256,32,16]{0,1,2:T(8,128)(2,1)S(1)} %dot_general.52, bf16[32,16,2048]{2,1,0:T(8,128)(2,1)S(1)} %bitcast.113), kind=kOutput, calls=%fused_computation.27 | convolution fusion | flops 538968064 | bytes 9699328 | tf_op jit(solution)/shard_map/dot_general | solution.py:136
  (69 shorter events, 16.3 us)
Async XLA Ops:
  6.5 4.5 %copy-start = (bf16[256,2048]{1,0:T(8,128)(2,1)S(1)}, bf16[256,2048]{1,0:T(8,128)(2,1)}, u32[]{:S(2)}) copy-start(bf16[256,2048]{1,0:T(8,128)(2,1)} %param.6) | copy-start | bytes 3145732
  6.5 78.8 %all-gather.2.cloned.1.call-start = ((), (), s32[]{:S(2)}) async-start(), calls=%async_computation | async-start | bytes 6684672 | tf_op jit(solution)/shard_map/all_gather | solution.py:67
  11.1 29.1 %collective-permute-start = (bf16[136,2048]{1,0:T(8,128)(2,1)S(1)}, bf16[136,2048]{1,0:T(8,128)(2,1)S(1)}, u32[]{:S(2)}, u32[]{:S(2)}) collective-permute-start(bf16[136,2048]{1,0:T(8,128)(2,1)S(1)} %slice.91), channel_id=1, source_target_pairs={{3,7},{7,11},{11,15},{19,23},{23,27},{27,31},{35,39},{39,43},{43,4... | collective-permute-start | bytes 1671176 | tf_op jit(solution)/shard_map/ppermute | solution.py:54
  14.2 26.1 %collective-permute-start.1 = (bf16[136,2048]{1,0:T(8,128)(2,1)S(1)}, bf16[136,2048]{1,0:T(8,128)(2,1)}, u32[]{:S(2)}, u32[]{:S(2)}) collective-permute-start(bf16[136,2048]{1,0:T(8,128)(2,1)S(1)} %slice.91), channel_id=1, source_target_pairs={{3,6},{7,10},{11,14},{19,22},{23,26},{27,30},{35,38},{39,42},{43,4... | collective-permute-start | bytes 1671176 | tf_op jit(solution)/shard_map/ppermute | solution.py:54
  16.3 27.2 %collective-permute-start.2 = (bf16[136,2048]{1,0:T(8,128)(2,1)S(1)}, bf16[136,2048]{1,0:T(8,128)(2,1)}, u32[]{:S(2)}, u32[]{:S(2)}) collective-permute-start(bf16[136,2048]{1,0:T(8,128)(2,1)S(1)} %slice.91), channel_id=1, source_target_pairs={{3,5},{7,9},{11,13},{19,21},{23,25},{27,29},{35,37},{39,41},{43,45... | collective-permute-start | bytes 1671176 | tf_op jit(solution)/shard_map/ppermute | solution.py:54
  18.4 25.1 %collective-permute-start.3 = (bf16[136,2048]{1,0:T(8,128)(2,1)S(1)}, bf16[136,2048]{1,0:T(8,128)(2,1)}, u32[]{:S(2)}, u32[]{:S(2)}) collective-permute-start(bf16[136,2048]{1,0:T(8,128)(2,1)S(1)} %slice.91), channel_id=1, source_target_pairs={{3,4},{7,8},{11,12},{19,20},{23,24},{27,28},{35,36},{39,40},{43,44... | collective-permute-start | bytes 1671176 | tf_op jit(solution)/shard_map/ppermute | solution.py:54
  20.5 31.9 %collective-permute-start.4 = (bf16[256,2048]{1,0:T(8,128)(2,1)S(1)}, bf16[256,2048]{1,0:T(8,128)(2,1)S(1)}, u32[]{:S(2)}, u32[]{:S(2)}) collective-permute-start(bf16[256,2048]{1,0:T(8,128)(2,1)S(1)} %copy-done), channel_id=1, source_target_pairs={{0,3},{1,2},{2,1},{3,0},{4,7},{5,6},{6,5},{7,4},{8,11},{9,10},{10,... | collective-permute-start | bytes 3145736 | tf_op jit(solution)/shard_map/ppermute | solution.py:42
  28.0 6.7 %copy-start.7 = (s32[1,4]{1,0:T(1,128)S(1)}, s32[1,4]{1,0:T(1,128)}, u32[]{:S(2)}) copy-start(s32[1,4]{1,0:T(1,128)} %param.7) | copy-start | bytes 52
  40.2 34.5 %collective-permute-start.5 = (bf16[256,2048]{1,0:T(8,128)(2,1)S(1)}, bf16[256,2048]{1,0:T(8,128)(2,1)S(1)}, u32[]{:S(2)}, u32[]{:S(2)}) collective-permute-start(bf16[256,2048]{1,0:T(8,128)(2,1)S(1)} %copy-done), channel_id=1, source_target_pairs={{0,2},{1,3},{2,0},{3,1},{4,6},{5,7},{6,4},{7,5},{8,10},{9,11},{10,... | collective-permute-start | bytes 3145736 | tf_op jit(solution)/shard_map/ppermute | solution.py:42
  40.3 34.4 %collective-permute-start.6 = (bf16[256,2048]{1,0:T(8,128)(2,1)S(1)}, bf16[256,2048]{1,0:T(8,128)(2,1)S(1)}, u32[]{:S(2)}, u32[]{:S(2)}) collective-permute-start(bf16[256,2048]{1,0:T(8,128)(2,1)S(1)} %copy-done), channel_id=1, source_target_pairs={{0,1},{1,0},{2,3},{3,2},{4,5},{5,4},{6,7},{7,6},{8,9},{9,8},{10,11... | collective-permute-start | bytes 3145736 | tf_op jit(solution)/shard_map/ppermute | solution.py:42
  116.9 5.1 %copy-start.4 = (bf16[32,128,128]{2,1,0:T(8,128)(2,1)S(1)}, bf16[32,128,128]{2,1,0:T(8,128)(2,1)}, u32[]{:S(2)}) copy-start(bf16[32,128,128]{2,1,0:T(8,128)(2,1)} %copy.58) | copy-start | bytes 3145732
  116.9 5.1 %copy-start.6 = (pred[8,128,128]{2,1,0:T(8,128)(4,1)S(1)}, pred[8,128,128]{2,1,0:T(8,128)(4,1)}, u32[]{:S(2)}) copy-start(pred[8,128,128]{2,1,0:T(8,128)(4,1)} %get-tuple-element.38) | copy-start | bytes 393220
  119.8 2.2 %copy-start.5 = (bf16[32,16,8,128]{3,2,1,0:T(8,128)(2,1)S(1)}, bf16[32,16,8,128]{3,2,1,0:T(8,128)(2,1)}, u32[]{:S(2)}) copy-start(bf16[32,16,8,128]{3,2,1,0:T(8,128)(2,1)} %get-tuple-element.18) | copy-start | bytes 3145732
  122.0 4.5 %copy-start.3 = (bf16[32,128,128]{2,1,0:T(8,128)(2,1)S(1)}, bf16[32,128,128]{2,1,0:T(8,128)(2,1)}, u32[]{:S(2)}) copy-start(bf16[32,128,128]{2,1,0:T(8,128)(2,1)} %copy.56) | copy-start | bytes 3145732
  131.6 7.6 %collective-permute-start.8 = (bf16[32,2,16,128]{3,2,1,0:T(8,128)(2,1)S(1)}, bf16[32,2,16,128]{3,2,1,0:T(8,128)(2,1)S(1)}, u32[]{:S(2)}, u32[]{:S(2)}) collective-permute-start(bf16[32,2,16,128]{3,2,1,0:T(8,128)(2,1)S(1)} %get-tuple-element.20), channel_id=1, source_target_pairs={{0,2},{1,3},{2,0},{3,1},{4,6},{5,7},{6,4},{7,5},{8,10},{9,11},{10,... | collective-permute-start | bytes 786440 | tf_op jit(solution)/shard_map/ppermute | solution.py:135
  131.7 13.6 %collective-permute-start.9 = (bf16[32,2,16,128]{3,2,1,0:T(8,128)(2,1)S(1)}, bf16[32,2,16,128]{3,2,1,0:T(8,128)(2,1)S(1)}, u32[]{:S(2)}, u32[]{:S(2)}) collective-permute-start(bf16[32,2,16,128]{3,2,1,0:T(8,128)(2,1)S(1)} %get-tuple-element.22), channel_id=1, source_target_pairs={{0,3},{1,2},{2,1},{3,0},{4,7},{5,6},{6,5},{7,4},{8,11},{9,10},{10,... | collective-permute-start | bytes 786440 | tf_op jit(solution)/shard_map/ppermute | solution.py:135
  133.7 12.1 %collective-permute-start.7 = (bf16[32,2,16,128]{3,2,1,0:T(8,128)(2,1)S(1)}, bf16[32,2,16,128]{3,2,1,0:T(8,128)(2,1)S(1)}, u32[]{:S(2)}, u32[]{:S(2)}) collective-permute-start(bf16[32,2,16,128]{3,2,1,0:T(8,128)(2,1)S(1)} %get-tuple-element.19), channel_id=1, source_target_pairs={{0,1},{1,0},{2,3},{3,2},{4,5},{5,4},{6,7},{7,6},{8,9},{9,8},{10,11... | collective-permute-start | bytes 786440 | tf_op jit(solution)/shard_map/ppermute | solution.py:135
  146.2 3.3 %copy-start.2 = (bf16[512,2048]{1,0:T(8,128)(2,1)S(1)}, bf16[512,2048]{1,0:T(8,128)(2,1)}, u32[]{:S(2)}) copy-start(bf16[512,2048]{1,0:T(8,128)(2,1)} %get-tuple-element.10) | copy-start | bytes 6291460
  149.5 1.6 copy-start.1
  149.5 2.2 %copy-start.8 = (f32[256,2048]{1,0:T(8,128)S(1)}, f32[256,2048]{1,0:T(8,128)}, u32[]{:S(2)}) copy-start(f32[256,2048]{1,0:T(8,128)} %fusion.14) | copy-start | bytes 6291460
Sparse Core Ops, SparseCore 0:
  11.1 65.7 all-gather.1

commit v8 on v4

--- a/solution.py
+++ b/solution.py
@@ -1,7 +1,10 @@
 import jax
 import jax.numpy as jnp
 from jax import lax
+from jax.experimental import pallas as pl
+from jax.experimental.pallas import tpu as pltpu
 from jax.sharding import PartitionSpec as P
+import functools
 
 LANE = 128
 GROUP_DEVS = 4
@@ -22,6 +25,59 @@
     return jnp.einsum(
         "ijt,tg->gij", one_hot, long_filter, preferred_element_type=jnp.float32
     ).astype(jnp.bfloat16)
+
+
+def proj_feat_kernel(tok_ref, w_ref, taps_ref, pos_ref, q_ref, mi_ref, proj_ref, *, width, start, n_out, chunk):
+    for qkv in range(3):
+        p = lax.dot_general(tok_ref[...], w_ref[qkv, 0], (((1,), (1,)), ((), ())),
+                            preferred_element_type=jnp.float32)
+        proj_ref[qkv] = p.astype(jnp.bfloat16).astype(jnp.float32)
+    feat_rows = pos_ref.shape[0]
+    q_first = feat_rows - n_out
+    for c in range(feat_rows // chunk):
+        lo = c * chunk
+        pos = pos_ref[lo:lo + chunk, :]
+        accs = []
+        for qkv in range(3):
+            if qkv == 0 and lo < q_first:
+                accs.append(None)
+                continue
+            acc = None
+            for t in range(width):
+                sh = proj_ref[qkv, pl.ds(start + lo - t, chunk), :]
+                term = taps_ref[t, qkv:qkv + 1, :] * jnp.where(pos >= t, sh, 0.0)
+                acc = term if acc is None else acc + term
+            accs.append(acc)
+        if accs[0] is not None:
+            q_ref[lo - q_first:lo - q_first + chunk, :] = accs[0]
+        mi_ref[lo:lo + chunk, :] = (accs[1] * accs[2]).astype(mi_ref.dtype)
+
+
+def proj_feat(ext_tokens, w4, taps3, pos_b, *, start, n_out, tile=128, chunk=128):
+    ext_rows, d = ext_tokens.shape
+    n_tiles = w4.shape[1]
+    width = taps3.shape[0]
+    feat_rows = pos_b.shape[0]
+    kern = functools.partial(proj_feat_kernel, width=width, start=start, n_out=n_out, chunk=chunk)
+    return pl.pallas_call(
+        kern,
+        grid=(n_tiles,),
+        in_specs=[
+            pl.BlockSpec((ext_rows, d), lambda j: (0, 0)),
+            pl.BlockSpec((3, 1, tile, d), lambda j: (0, j, 0, 0)),
+            pl.BlockSpec((width, 3, tile), lambda j: (0, 0, j)),
+            pl.BlockSpec((feat_rows, tile), lambda j: (0, 0)),
+        ],
+        out_specs=[
+            pl.BlockSpec((n_out, tile), lambda j: (0, j)),
+            pl.BlockSpec((feat_rows, tile), lambda j: (0, j)),
+        ],
+        out_shape=[
+            jax.ShapeDtypeStruct((n_out, n_tiles * tile), jnp.float32),
+            jax.ShapeDtypeStruct((feat_rows, n_tiles * tile), jnp.bfloat16),
+        ],
+        scratch_shapes=[pltpu.VMEM((3, ext_rows, tile), jnp.float32)],
+    )(ext_tokens, w4, taps3, pos_b)
 
 
 def local(tokens, seq_lengths, in_weight, short_filter, long_filter, out_weight):
@@ -75,24 +131,15 @@
         weights.append(lax.dynamic_slice_in_dim(ow, src_offset, part, axis=1).reshape(own, channels))
     ow_cat = jnp.concatenate(weights, axis=0)
     ext_tokens, ow_cat = lax.optimization_barrier((ext_tokens, ow_cat))
-    projected = jnp.dot(
-        ext_tokens, w_all.T, preferred_element_type=jnp.float32
-    ).astype(jnp.bfloat16)
-
     taps = short_filter.reshape(width, 3, n_lblk, LANE)
-    taps = lax.dynamic_slice_in_dim(taps, offset, part, axis=3).reshape(width, 3 * own)
-
+    taps = lax.dynamic_slice_in_dim(taps, offset, part, axis=3).reshape(width, 3, own)
     start = 8
     feat_rows = ext_rows - start
-    pos_f = position[start:]
-    featured = jnp.zeros((feat_rows, 3 * own), jnp.float32)
-    for tap_index in range(width):
-        shifted = projected[start - tap_index : ext_rows - tap_index].astype(jnp.float32)
-        featured = featured + taps[tap_index] * jnp.where(
-            (pos_f >= tap_index)[:, None], shifted, 0.0
-        )
-    queries = featured[feat_rows - span :, :own]
-    mixed_in = (featured[:, own : 2 * own] * featured[:, 2 * own :]).astype(jnp.bfloat16)
+    pos_b = jnp.broadcast_to(position[start:, None], (feat_rows, LANE))
+    queries, mixed_in = proj_feat(
+        ext_tokens, w_all.reshape(3, own // LANE, LANE, channels), taps, pos_b,
+        start=start, n_out=span,
+    )
 
     sub = LANE // per_group
     lf = long_filter.reshape(filter_len, n_lblk, sub)

time: 155 us -> 157 us (1.013)
  Pallas kernels: 0 us -> 23.2 us
  matrix products: 36 us -> 23.5 us
  other arithmetic: 28.2 us -> 17.2 us
    pallas_call x0 -> x1, Pallas kernels: none -> 23.2 us  [proj_feat(): pl.pallas_call(kern, grid=(n_tiles,), in_specs=[pl.BlockSpec((ext_rows, d...]
    dot_general x1 -> x0, matrix products: 11.2 us -> none  [local(): jnp.dot(ext_tokens, w_all.T, preferred_element_type=jnp.float32)]
    add x1 -> x0, other arithmetic: 10.7 us -> none  [local(): featured + taps[tap_index] * jnp.where((pos_f >= tap_index)[:, None], shi...]
    unnamed x14 -> x16, local copies, waits for them, and re-layouts: 8.3 us -> 5.58 us
    slice x1, local copies, waits for them, and re-layouts: 0.44 us -> 2.41 us  [local(): mi_t[:, :, 1:]]
  transfers between devices with their start and end apart: 11 -> 11, of which waited for: 4 -> 4; matrix products, arithmetic and copies ran while one was open for 22% -> 20% of each run, Pallas kernels for 0% -> 0%
where the time goes in v8:
time: 157 us
  waiting for transfers between devices  35.9 us (23%)
  local copies, waits for them, and re-layouts  26.4 us (17%)
  matrix products  23.5 us (15%)
  Pallas kernels  23.2 us (15%)
  other arithmetic  17.2 us (11%)
  starting transfers between devices  16.9 us (11%)
  between operations  13.6 us (9%)
    pallas_call x1, Pallas kernels, proj_feat(): pl.pallas_call(kern, grid=(n_tiles,), in_specs=[pl.BlockSpec((ext_rows, d...  23.2 us
    ppermute x3, waiting for transfers between devices, local(): lax.ppermute(tokens, 'seq', perm)  15.4 us
    ppermute x3, waiting for transfers between devices, local(): got = send if d == 0 else lax.ppermute(send, 'seq', swaps[d - 1])  11.9 us
    ppermute x3, starting transfers between devices, local(): lax.ppermute(tokens, 'seq', perm)  9.33 us
    all_gather x1, waiting for transfers between devices, local(): w_all = lax.all_gather(w_part, 'fsdp', axis=0, tiled=True)  8.55 us
    dot_general x2, matrix products, tap_table(): jnp.einsum('ijt,tg->gij', one_hot, long_filter, preferred_element_type=jn...  7.92 us
    unnamed x4, other arithmetic  7.54 us
    dot_general x1, matrix products, local(): lax.dot_general(jnp.concatenate(pieces, axis=0), ow_cat, (((0,), (0,)), (...  6.68 us
  transfers between devices with their start and end apart: 11, of which 4 were waited for; matrix products, arithmetic and copies ran while one was open for 20% of the time, Pallas kernels for 0%

profile of v8, /device:TPU:1, one launch (start us, length us, event | category | flops | bytes accessed | tf_op | source)
XLA Modules:
  0.0 156.6 jit_solution(10647708373021080804)
XLA Ops:
  6.5 2.7 %copy.31 = bf16[2048,384]{0,1:T(8,128)(2,1)} copy(bf16[2048,384]{1,0:T(8,128)(2,1)} %param.8) | data formatting | bytes 3145728 | tf_op args[2]
  9.2 1.8 %constant_dynamic-slice_fusion.2 = bf16[3,32,2048]{2,1,0:T(8,128)(2,1)} fusion(bf16[3,128,2048]{2,1,0:T(8,128)(2,1)} %bitcast.55, s32[]{:T(128)S(6)} %select_n.188), kind=kLoop, calls=%fused_computation.53 | loop fusion | bytes 786436 | tf_op jit(solution)/shard_map/dynamic_slice | solution.py:122
  11.8 1.5 collective-permute-start.1
  13.3 1.5 collective-permute-start.2
  14.7 1.5 collective-permute-start.3
  16.2 3.0 %collective-permute-start.4 = (bf16[256,2048]{1,0:T(8,128)(2,1)S(1)}, bf16[256,2048]{1,0:T(8,128)(2,1)S(1)}, u32[]{:S(2)}, u32[]{:S(2)}) collective-permute-start(bf16[256,2048]{1,0:T(8,128)(2,1)S(1)} %copy-done), channel_id=1, source_target_pairs={{0,3},{1,2},{2,1},{3,0},{4,7},{5,6},{6,5},{7,4},{8,11},{9,10},{10,... | collective-permute-start | bytes 3145736 | tf_op jit(solution)/shard_map/ppermute | solution.py:98
  21.7 4.0 %fusion.18 = bf16[32,128,128]{2,0,1:T(8,128)(2,1)S(1)} fusion(bf16[128,32,1]{0,1,2:T(8,128)(2,1)S(1)} %bitcast.60, s32[128,128]{1,0:T(8,128)S(1)} %get-tuple-element.25), kind=kOutput, calls=%fused_computation.23 | convolution fusion | flops 136839168 | bytes 1122304 | tf_op jit(solution)/shard_map/ijt,tg->gij/dot_general | solution.py:25
  25.6 1.4 copy.38
  27.0 4.0 %fusion.19 = bf16[32,128,128]{2,0,1:T(8,128)(2,1)S(1)} fusion(bf16[128,32,1]{0,1,2:T(8,128)(2,1)S(1)} %bitcast.61, s32[128,128]{1,0:T(8,128)S(1)} %get-tuple-element.26), kind=kOutput, calls=%fused_computation.24 | convolution fusion | flops 136839168 | bytes 1122304 | tf_op jit(solution)/shard_map/ijt,tg->gij/dot_general | solution.py:25
  31.0 1.4 copy.35
  33.3 4.4 %constant_dynamic-slice_fusion.6 = (bf16[16,32,2048]{2,1,0:T(8,128)(2,1)S(1)}, bf16[16,32,2048]{2,1,0:T(8,128)(2,1)S(1)}, bf16[16,32,2048]{2,1,0:T(8,128)(2,1)S(1)}, bf16[16,32,2048]{2,1,0:T(8,128)(2,1)S(1)}) fusion(bf16[16,128,2048]{2,1,0:T(8,128)(2,1)} %bitcast.46, s32[]{:T(128)S(6)} %select_n.188, s32[]{:T(128)S(6)} %select_n.191, s32[]{:T(128)S(6)} %select_n.190, ...), kind=kLoop, calls=%fused_computation.57 | loop fusion | bytes 16777232 | tf_op jit(solution)/shard_map/dynamic_slice | solution.py:131
  37.7 5.6 %collective-permute-start.5 = (bf16[256,2048]{1,0:T(8,128)(2,1)S(1)}, bf16[256,2048]{1,0:T(8,128)(2,1)S(1)}, u32[]{:S(2)}, u32[]{:S(2)}) collective-permute-start(bf16[256,2048]{1,0:T(8,128)(2,1)S(1)} %copy-done), channel_id=1, source_target_pairs={{0,2},{1,3},{2,0},{3,1},{4,6},{5,7},{6,4},{7,5},{8,10},{9,11},{10,... | collective-permute-start | bytes 3145736 | tf_op jit(solution)/shard_map/ppermute | solution.py:98
  44.0 4.1 %pad_maximum_fusion = bf16[2048,2048]{1,0:T(8,128)(2,1)} fusion(bf16[512,2048]{1,0:T(8,128)(2,1)S(1)} %bitcast.50, bf16[512,2048]{1,0:T(8,128)(2,1)S(1)} %bitcast.51, bf16[512,2048]{1,0:T(8,128)(2,1)S(1)} %bitcast.52, bf16[512,2048]{1,0:T(8,128)(2,1)S(1)} %bitcast.49), kind=kLoop, calls=%fused_computation | loop fusion | flops 33554432 | bytes 16777216 | tf_op jit(solution)/shard_map/concatenate | solution.py:132
  48.1 2.3 %select_dynamic-update-slice_fusion.4 = bf16[1160,2048]{1,0:T(8,128)(2,1)} fusion(bf16[136,2048]{1,0:T(8,128)(2,1)S(1)} %collective-permute-done, bf16[136,2048]{1,0:T(8,128)(2,1)} %collective-permute-done.1, bf16[136,2048]{1,0:T(8,128)(2,1)} %collective-permute-done.2, bf16[136,2048]{1,0:T(8,128)(2,1)} %collective-permute-done.3, pred[]{:T(512)S(6)} %eq.79, ...), kind=kLoop, calls=%fused_computation.38 | loop fusion | flops 1114111 | bytes 2785284
  50.4 15.4 %collective-permute-done.5 = bf16[256,2048]{1,0:T(8,128)(2,1)S(1)} collective-permute-done((bf16[256,2048]{1,0:T(8,128)(2,1)S(1)}, bf16[256,2048]{1,0:T(8,128)(2,1)S(1)}, u32[]{:S(2)}, u32[]{:S(2)}) %collective-permute-start.5) | collective-permute-done | bytes 1048608 | tf_op jit(solution)/shard_map/ppermute | solution.py:98
  65.8 1.8 %select_dynamic-update-slice_fusion.3 = bf16[1160,2048]{1,0:T(8,128)(2,1)} fusion(bf16[1160,2048]{1,0:T(8,128)(2,1)} %select_dynamic-update-slice_fusion.4, bf16[256,2048]{1,0:T(8,128)(2,1)S(1)} %collective-permute-done.4, bf16[256,2048]{1,0:T(8,128)(2,1)S(1)} %collective-permute-done.5, bf16[256,2048]{1,0:T(8,128)(2,1)S(1)} %collective-permute-done.6, ...), kind=kLoop, calls=%fused_computation.37 | loop fusion | flops 1572864 | bytes 5242883
  67.5 1.8 %select_dynamic-update-slice_fusion.2 = bf16[1160,2048]{1,0:T(8,128)(2,1)} fusion(bf16[1160,2048]{1,0:T(8,128)(2,1)} %select_dynamic-update-slice_fusion.3, bf16[256,2048]{1,0:T(8,128)(2,1)S(1)} %collective-permute-done.4, bf16[256,2048]{1,0:T(8,128)(2,1)S(1)} %collective-permute-done.5, bf16[256,2048]{1,0:T(8,128)(2,1)S(1)} %collective-permute-done.6, ...), kind=kLoop, calls=%fused_computation.36 | loop fusion | flops 1572864 | bytes 5242883
  69.3 1.8 %select_dynamic-update-slice_fusion.1 = bf16[1160,2048]{1,0:T(8,128)(2,1)} fusion(bf16[1160,2048]{1,0:T(8,128)(2,1)} %select_dynamic-update-slice_fusion.2, bf16[256,2048]{1,0:T(8,128)(2,1)S(1)} %collective-permute-done.4, bf16[256,2048]{1,0:T(8,128)(2,1)S(1)} %collective-permute-done.5, bf16[256,2048]{1,0:T(8,128)(2,1)S(1)} %collective-permute-done.6, ...), kind=kLoop, calls=%fused_computation.35 | loop fusion | flops 1572864 | bytes 5242883
  71.1 1.7 %select_dynamic-update-slice_fusion.tok_ref = bf16[1160,2048]{1,0:T(8,128)(2,1)} fusion(bf16[1160,2048]{1,0:T(8,128)(2,1)} %select_dynamic-update-slice_fusion.1, bf16[256,2048]{1,0:T(8,128)(2,1)S(1)} %collective-permute-done.4, bf16[256,2048]{1,0:T(8,128)(2,1)S(1)} %collective-permute-done.5, bf16[256,2048]{1,0:T(8,128)(2,1)S(1)} %collective-permute-done.6, ...), kind=kLoop, calls=%fused_computation.34 | loop fusion | flops 1572864 | bytes 5242883 | tf_op jit(solution)/shard_map/concatenate | solution.py:112
  72.8 8.5 %all-gather.2.cloned.1.call-done = bf16[48,32,2048]{2,1,0:T(8,128)(2,1)} async-done(((bf16[3,32,2048]{2,1,0:T(8,128)(2,1)}), bf16[48,32,2048]{2,1,0:T(8,128)(2,1)}) %all-gather.2.cloned.1.call-update) | async-done | bytes 6291472 | tf_op jit(solution)/shard_map/all_gather | solution.py:123
  82.4 23.2 %shard_map.64 = (f32[1024,512]{1,0:T(8,128)}, bf16[1152,512]{1,0:T(8,128)(2,1)}) custom-call(bf16[1160,2048]{1,0:T(8,128)(2,1)} %select_dynamic-update-slice_fusion.tok_ref, bf16[3,4,128,2048]{3,2,1,0:T(8,128)(2,1)} %bitcast.53, f32[7,3,512]{2,1,0:T(4,128)} %reshape.137.taps_ref, s32[1152,128]{1,0:T(8,128)} %broadcast_in_dim.67.pos_ref), custom_call_target="tpu_custom_call" | custom-call | tf_op jit(solution)/shard_map/pallas_call | solution.py:62
  105.6 1.7 %copy.36 = bf16[512,1152]{1,0:T(8,128)(2,1)S(1)} copy(bf16[512,1152]{0,1:T(8,128)(2,1)} %bitcast.56) | data formatting | bytes 2359296 | tf_op jit(solution)/shard_map/transpose | solution.py:166
  107.2 1.7 %reshape.133 = bf16[32,16,9,128]{3,2,1,0:T(8,128)(2,1)} reshape(bf16[512,1152]{1,0:T(8,128)(2,1)S(1)} %copy.36) | data formatting | bytes 2359296 | tf_op jit(solution)/shard_map/reshape | solution.py:166
  109.0 2.4 %fusion.33 = (bf16[32,16,8,128]{3,2,1,0:T(8,128)(2,1)S(1)}, bf16[32,16,8,128]{3,2,1,0:T(8,128)(2,1)S(1)}) fusion(bf16[32,16,9,128]{3,2,1,0:T(8,128)(2,1)} %reshape.133), kind=kLoop, calls=%fused_computation.63 | loop fusion | bytes 4194304 | tf_op jit(solution)/shard_map/slice | solution.py:168
  111.4 4.5 %fusion = f32[32,8,128,16]{2,3,1,0:T(8,128)S(1)} fusion(pred[8,128,128]{2,1,0:T(8,128)(4,1)S(1)} %copy-done.3, bf16[32,128,128]{2,1,0:T(8,128)(2,1)S(1)} %copy-done.2, bf16[32,16,8,128]{3,2,1,0:T(8,128)(2,1)S(1)} %get-tuple-element.18), kind=kOutput, calls=%fused_computation.1 | convolution fusion | flops 138412032 | bytes 4325376 | tf_op jit(solution)/shard_map/gcbj,bgij->gcbi/dot_general | solution.py:170
  115.9 4.5 %add_bitcast_fusion = f32[32,16,8,128]{3,1,2,0:T(8,128)S(1)} fusion(f32[32,8,128,16]{2,3,1,0:T(8,128)S(1)} %fusion, pred[8,128,128]{2,1,0:T(8,128)(4,1)S(1)} %get-tuple-element.23, bf16[32,128,128]{2,1,0:T(8,128)(2,1)S(1)} %copy-done.1, bf16[32,16,8,128]{3,2,1,0:T(8,128)(2,1)S(1)} %get-tuple-element.17), kind=kOutput, calls=%fused_computation.22 | convolution fusion | flops 138936320 | bytes 6422528 | tf_op jit(solution)/shard_map/gcbj,bgij->gcbi/dot_general | solution.py:167
  121.3 1.8 %copy.53 = f32[64,8,8,128]{3,1,2,0:T(8,128)} copy(f32[64,8,8,128]{3,2,1,0:T(8,128)S(1)} %bitcast.47) | data formatting | bytes 4194304
  123.1 3.0 %copy.41 = f32[512,1024]{0,1:T(8,128)} copy(f32[512,1024]{1,0:T(8,128)} %bitcast.48) | data formatting | bytes 4194304 | tf_op jit(solution)/shard_map/reshape | solution.py:173
  126.0 2.6 %fusion.15 = bf16[512,1024]{0,1:T(8,128)(2,1)S(1)} fusion(f32[512,1024]{0,1:T(8,128)} %copy.41, f32[1024,512]{1,0:T(8,128)} %get-tuple-element.10), kind=kLoop, calls=%fused_computation.21 | loop fusion | flops 1048576 | bytes 5242880 | tf_op jit(solution)/shard_map/convert_element_type | solution.py:174
  131.2 6.1 %collective-permute-done.8 = bf16[512,256]{0,1:T(8,128)(2,1)S(1)} collective-permute-done((bf16[512,256]{0,1:T(8,128)(2,1)S(1)}, bf16[512,256]{0,1:T(8,128)(2,1)S(1)}, u32[]{:S(2)}, u32[]{:S(2)}) %collective-permute-start.8) | collective-permute-done | bytes 262176 | tf_op jit(solution)/shard_map/ppermute | solution.py:181
  137.3 5.8 %collective-permute-done.9 = bf16[512,256]{0,1:T(8,128)(2,1)S(1)} collective-permute-done((bf16[512,256]{0,1:T(8,128)(2,1)S(1)}, bf16[512,256]{0,1:T(8,128)(2,1)S(1)}, u32[]{:S(2)}, u32[]{:S(2)}) %collective-permute-start.9) | collective-permute-done | bytes 262176 | tf_op jit(solution)/shard_map/ppermute | solution.py:181
  143.1 6.7 %fusion.14 = bf16[256,2048]{1,0:T(8,128)(2,1)} fusion(bf16[2048,2048]{1,0:T(8,128)(2,1)} %pad_maximum_fusion, bf16[256,2048]{1,0:T(8,128)(2,1)S(1)} %copy-done, bf16[512,256]{0,1:T(8,128)(2,1)S(1)} %collective-permute-done.9, bf16[512,256]{0,1:T(8,128)(2,1)S(1)} %collective-permute-done.8, bf16[512,256]{0,1:T(8,128)(2,1)S(1)} %collective-permute-done.7, ...), kind=kOutput, calls=%fused_computation.18 | convolution fusion | flops 2153250816 | bytes 11534336 | tf_op jit(solution)/shard_map/dot_general | solution.py:183
  (45 shorter events, 9.3 us)
Async XLA Ops:
  6.5 4.5 %copy-start = (bf16[256,2048]{1,0:T(8,128)(2,1)S(1)}, bf16[256,2048]{1,0:T(8,128)(2,1)}, u32[]{:S(2)}) copy-start(bf16[256,2048]{1,0:T(8,128)(2,1)} %param.6) | copy-start | bytes 3145732
  6.5 12.7 %copy-start.5 = (s32[1,4]{1,0:T(1,128)S(1)}, s32[1,4]{1,0:T(1,128)}, u32[]{:S(2)}) copy-start(s32[1,4]{1,0:T(1,128)} %param.7) | copy-start | bytes 52
  6.5 14.9 %copy-start.4 = (bf16[128,128]{1,0:T(8,128)(2,1)S(1)}, bf16[128,128]{1,0:T(8,128)(2,1)}, u32[]{:S(2)}) copy-start(bf16[128,128]{1,0:T(8,128)(2,1)} %param.10) | copy-start | bytes 98308
  6.5 74.8 %all-gather.2.cloned.1.call-start = ((), (), s32[]{:S(2)}) async-start(), calls=%async_computation | async-start | bytes 6684672 | tf_op jit(solution)/shard_map/all_gather | solution.py:123
  11.1 26.6 %collective-permute-start = (bf16[136,2048]{1,0:T(8,128)(2,1)S(1)}, bf16[136,2048]{1,0:T(8,128)(2,1)S(1)}, u32[]{:S(2)}, u32[]{:S(2)}) collective-permute-start(bf16[136,2048]{1,0:T(8,128)(2,1)S(1)} %slice.15), channel_id=1, source_target_pairs={{3,7},{7,11},{11,15},{19,23},{23,27},{27,31},{35,39},{39,43},{43,4... | collective-permute-start | bytes 1671176 | tf_op jit(solution)/shard_map/ppermute | solution.py:110
  11.8 31.6 %collective-permute-start.1 = (bf16[136,2048]{1,0:T(8,128)(2,1)S(1)}, bf16[136,2048]{1,0:T(8,128)(2,1)}, u32[]{:S(2)}, u32[]{:S(2)}) collective-permute-start(bf16[136,2048]{1,0:T(8,128)(2,1)S(1)} %slice.15), channel_id=1, source_target_pairs={{3,6},{7,10},{11,14},{19,22},{23,26},{27,30},{35,38},{39,42},{43,4... | collective-permute-start | bytes 1671176 | tf_op jit(solution)/shard_map/ppermute | solution.py:110
  13.3 34.9 %collective-permute-start.2 = (bf16[136,2048]{1,0:T(8,128)(2,1)S(1)}, bf16[136,2048]{1,0:T(8,128)(2,1)}, u32[]{:S(2)}, u32[]{:S(2)}) collective-permute-start(bf16[136,2048]{1,0:T(8,128)(2,1)S(1)} %slice.15), channel_id=1, source_target_pairs={{3,5},{7,9},{11,13},{19,21},{23,25},{27,29},{35,37},{39,41},{43,45... | collective-permute-start | bytes 1671176 | tf_op jit(solution)/shard_map/ppermute | solution.py:110
  14.7 33.4 %collective-permute-start.3 = (bf16[136,2048]{1,0:T(8,128)(2,1)S(1)}, bf16[136,2048]{1,0:T(8,128)(2,1)}, u32[]{:S(2)}, u32[]{:S(2)}) collective-permute-start(bf16[136,2048]{1,0:T(8,128)(2,1)S(1)} %slice.15), channel_id=1, source_target_pairs={{3,4},{7,8},{11,12},{19,20},{23,24},{27,28},{35,36},{39,40},{43,44... | collective-permute-start | bytes 1671176 | tf_op jit(solution)/shard_map/ppermute | solution.py:110
  16.2 34.2 %collective-permute-start.4 = (bf16[256,2048]{1,0:T(8,128)(2,1)S(1)}, bf16[256,2048]{1,0:T(8,128)(2,1)S(1)}, u32[]{:S(2)}, u32[]{:S(2)}) collective-permute-start(bf16[256,2048]{1,0:T(8,128)(2,1)S(1)} %copy-done), channel_id=1, source_target_pairs={{0,3},{1,2},{2,1},{3,0},{4,7},{5,6},{6,5},{7,4},{8,11},{9,10},{10,... | collective-permute-start | bytes 3145736 | tf_op jit(solution)/shard_map/ppermute | solution.py:98
  37.7 28.1 %collective-permute-start.5 = (bf16[256,2048]{1,0:T(8,128)(2,1)S(1)}, bf16[256,2048]{1,0:T(8,128)(2,1)S(1)}, u32[]{:S(2)}, u32[]{:S(2)}) collective-permute-start(bf16[256,2048]{1,0:T(8,128)(2,1)S(1)} %copy-done), channel_id=1, source_target_pairs={{0,2},{1,3},{2,0},{3,1},{4,6},{5,7},{6,4},{7,5},{8,10},{9,11},{10,... | collective-permute-start | bytes 3145736 | tf_op jit(solution)/shard_map/ppermute | solution.py:98
  43.3 22.4 %collective-permute-start.6 = (bf16[256,2048]{1,0:T(8,128)(2,1)S(1)}, bf16[256,2048]{1,0:T(8,128)(2,1)S(1)}, u32[]{:S(2)}, u32[]{:S(2)}) collective-permute-start(bf16[256,2048]{1,0:T(8,128)(2,1)S(1)} %copy-done), channel_id=1, source_target_pairs={{0,1},{1,0},{2,3},{3,2},{4,5},{5,4},{6,7},{7,6},{8,9},{9,8},{10,11... | collective-permute-start | bytes 3145736 | tf_op jit(solution)/shard_map/ppermute | solution.py:98
  109.0 2.4 %copy-start.2 = (bf16[32,128,128]{2,1,0:T(8,128)(2,1)S(1)}, bf16[32,128,128]{2,1,0:T(8,128)(2,1)}, u32[]{:S(2)}) copy-start(bf16[32,128,128]{2,1,0:T(8,128)(2,1)} %copy.38) | copy-start | bytes 3145732
  109.0 2.4 %copy-start.3 = (pred[8,128,128]{2,1,0:T(8,128)(4,1)S(1)}, pred[8,128,128]{2,1,0:T(8,128)(4,1)}, u32[]{:S(2)}) copy-start(pred[8,128,128]{2,1,0:T(8,128)(4,1)} %get-tuple-element.24) | copy-start | bytes 393220
  111.4 4.5 %copy-start.1 = (bf16[32,128,128]{2,1,0:T(8,128)(2,1)S(1)}, bf16[32,128,128]{2,1,0:T(8,128)(2,1)}, u32[]{:S(2)}) copy-start(bf16[32,128,128]{2,1,0:T(8,128)(2,1)} %copy.35) | copy-start | bytes 3145732
  128.7 2.5 %collective-permute-start.7 = (bf16[512,256]{0,1:T(8,128)(2,1)S(1)}, bf16[512,256]{0,1:T(8,128)(2,1)S(1)}, u32[]{:S(2)}, u32[]{:S(2)}) collective-permute-start(bf16[512,256]{0,1:T(8,128)(2,1)S(1)} %get-tuple-element.22), channel_id=1, source_target_pairs={{0,1},{1,0},{2,3},{3,2},{4,5},{5,4},{6,7},{7,6},{8,9},{9,8},{10,11... | collective-permute-start | bytes 786440 | tf_op jit(solution)/shard_map/ppermute | solution.py:181
  129.4 7.9 %collective-permute-start.8 = (bf16[512,256]{0,1:T(8,128)(2,1)S(1)}, bf16[512,256]{0,1:T(8,128)(2,1)S(1)}, u32[]{:S(2)}, u32[]{:S(2)}) collective-permute-start(bf16[512,256]{0,1:T(8,128)(2,1)S(1)} %get-tuple-element.21), channel_id=1, source_target_pairs={{0,2},{1,3},{2,0},{3,1},{4,6},{5,7},{6,4},{7,5},{8,10},{9,11},{10,... | collective-permute-start | bytes 786440 | tf_op jit(solution)/shard_map/ppermute | solution.py:181
  130.7 12.4 %collective-permute-start.9 = (bf16[512,256]{0,1:T(8,128)(2,1)S(1)}, bf16[512,256]{0,1:T(8,128)(2,1)S(1)}, u32[]{:S(2)}, u32[]{:S(2)}) collective-permute-start(bf16[512,256]{0,1:T(8,128)(2,1)S(1)} %get-tuple-element.20), channel_id=1, source_target_pairs={{0,3},{1,2},{2,1},{3,0},{4,7},{5,6},{6,5},{7,4},{8,11},{9,10},{10,... | collective-permute-start | bytes 786440 | tf_op jit(solution)/shard_map/ppermute | solution.py:181
Sparse Core Ops, SparseCore 0:
  11.1 70.1 all-gather.1

commit v9 on v4

--- a/solution.py
+++ b/solution.py
@@ -109,19 +109,22 @@
 
     n_blocks = span // filter_len
     pos_out = position[tail:].reshape(n_blocks, filter_len)
-    cur_kernel = jnp.where(
-        (cur_tap[None] <= pos_out[:, :, None])[:, None], cur_table[None], 0.0
-    ).astype(jnp.bfloat16)
-    prev_kernel = jnp.where(
-        (prev_tap[None] <= pos_out[:, :, None])[:, None], prev_table[None], 0.0
+    window_kernel = jnp.where(
+        jnp.concatenate(
+            [
+                jnp.broadcast_to(prev_tap[None] <= pos_out[:, :, None], (n_blocks,) + prev_tap.shape),
+                jnp.broadcast_to(cur_tap[None] <= pos_out[:, :, None], (n_blocks,) + cur_tap.shape),
+            ],
+            axis=2,
+        )[:, None],
+        jnp.concatenate([prev_table, cur_table], axis=2)[None],
+        0.0,
     ).astype(jnp.bfloat16)
 
     mi_t = mixed_in.T.reshape(n_groups, per_group, n_blocks + 1, filter_len)
+    window = jnp.concatenate([mi_t[:, :, :-1], mi_t[:, :, 1:]], axis=3)
     filtered = jnp.einsum(
-        "gcbj,bgij->gcbi", mi_t[:, :, 1:], cur_kernel, preferred_element_type=jnp.float32
-    )
-    filtered = filtered + jnp.einsum(
-        "gcbj,bgij->gcbi", mi_t[:, :, :-1], prev_kernel, preferred_element_type=jnp.float32
+        "gcbj,bgij->gcbi", window, window_kernel, preferred_element_type=jnp.float32
     )
     filtered = filtered.reshape(own, span)
     gated = (queries.T * filtered).astype(jnp.bfloat16)

time: 155 us -> 165 us (1.065)
  local copies, waits for them, and re-layouts: 25.5 us -> 40 us
  waiting for transfers between devices: 34.4 us -> 27.1 us
  other arithmetic: 28.2 us -> 31.9 us
  matrix products: 36 us -> 33.1 us
    all_gather x1, waiting for transfers between devices: 7.07 us -> 0.01 us  [local(): w_all = lax.all_gather(w_part, 'fsdp', axis=0, tiled=True)]
    mul x7, local copies, waits for them, and re-layouts: 0.51 us -> 5.39 us  [local(): taps[tap_index] * jnp.where((pos_f >= tap_index)[:, None], shifted, 0.0)]
    concatenate x0 -> x1, local copies, waits for them, and re-layouts: none -> 4.14 us  [local(): jnp.concatenate([prev_table, cur_table], axis=2)[None]]
    dot_general x2 -> x1, matrix products: 10.3 us -> 7.35 us  [local(): jnp.einsum('gcbj,bgij->gcbi', window, window_kernel, preferred_element_ty...]
    convert_element_type x2 -> x0, local copies, waits for them, and re-layouts: 2.75 us -> none  [tap_table(): return jnp.einsum('ijt,tg->gij', one_hot, long_filter, preferred_element_...]
    unnamed x14 -> x38, local copies, waits for them, and re-layouts: 8.3 us -> 11 us
    transpose x0 -> x1, local copies, waits for them, and re-layouts: none -> 2.47 us  [local(): jnp.einsum('gcbj,bgij->gcbi', window, window_kernel, preferred_element_ty...]
    concatenate x0 -> x2, other arithmetic: none -> 2.44 us  [the longest x1 1.65 us: local(): jnp.concatenate([prev_table, cur_table], axis=2)[None]]
  transfers between devices with their start and end apart: 11 -> 11, of which waited for: 4 -> 3; matrix products, arithmetic and copies ran while one was open for 22% -> 26% of each run, Pallas kernels for 0% -> 0%
where the time goes in v9:
time: 165 us; the launch traced here: 164 us
  local copies, waits for them, and re-layouts  40 us (24%)
  matrix products  33.1 us (20%)
  other arithmetic  31.9 us (19%)
  waiting for transfers between devices  27.1 us (16%)
  starting transfers between devices  18.1 us (11%)
  between operations  13.8 us (8%)
    ppermute x3, waiting for transfers between devices, local(): lax.ppermute(tokens, 'seq', perm)  15.3 us
    ppermute x3, waiting for transfers between devices, local(): got = send if d == 0 else lax.ppermute(send, 'seq', swaps[d - 1])  11.7 us
    dot_general x1, matrix products, local(): jnp.dot(ext_tokens, w_all.T, preferred_element_type=jnp.float32)  11.2 us
    unnamed x38, local copies, waits for them, and re-layouts  11 us
    add x1, other arithmetic, local(): featured + taps[tap_index] * jnp.where((pos_f >= tap_index)[:, None], shi...  10.7 us
    ppermute x3, starting transfers between devices, local(): lax.ppermute(tokens, 'seq', perm)  9.35 us
    dot_general x2, matrix products, tap_table(): jnp.einsum('ijt,tg->gij', one_hot, long_filter, preferred_element_type=jn...  7.93 us
    unnamed x4, other arithmetic  7.64 us
  transfers between devices with their start and end apart: 11, of which 3 were waited for; matrix products, arithmetic and copies ran while one was open for 26% of the time, Pallas kernels for 0%

profile of v9, /device:TPU:1, one launch (start us, length us, event | category | flops | bytes accessed | tf_op | source)
XLA Modules:
  0.0 163.9 jit_solution(6075424306232034962)
XLA Ops:
  6.5 2.7 %copy.25 = bf16[2048,384]{0,1:T(8,128)(2,1)} copy(bf16[2048,384]{1,0:T(8,128)(2,1)} %param.8) | data formatting | bytes 3145728 | tf_op args[2]
  9.2 1.8 %constant_dynamic-slice_fusion.7 = bf16[3,32,2048]{2,1,0:T(8,128)(2,1)} fusion(bf16[3,128,2048]{2,1,0:T(8,128)(2,1)} %bitcast.71, s32[]{:T(128)S(6)} %select_n.175), kind=kLoop, calls=%fused_computation.67 | loop fusion | bytes 786436 | tf_op jit(solution)/shard_map/dynamic_slice | solution.py:66
  12.8 1.5 collective-permute-start.1
  17.3 3.0 %collective-permute-start.4 = (bf16[256,2048]{1,0:T(8,128)(2,1)S(1)}, bf16[256,2048]{1,0:T(8,128)(2,1)S(1)}, u32[]{:S(2)}, u32[]{:S(2)}) collective-permute-start(bf16[256,2048]{1,0:T(8,128)(2,1)S(1)} %copy-done.1), channel_id=1, source_target_pairs={{0,3},{1,2},{2,1},{3,0},{4,7},{5,6},{6,5},{7,4},{8,11},{9,10},{10,... | collective-permute-start | bytes 3145736 | tf_op jit(solution)/shard_map/ppermute | solution.py:42
  22.7 4.0 %fusion.21 = bf16[32,128,128]{2,0,1:T(8,128)(2,1)S(1)} fusion(bf16[128,32,1]{0,1,2:T(8,128)(2,1)S(1)} %bitcast.75, s32[128,128]{1,0:T(8,128)S(1)} %get-tuple-element.35), kind=kOutput, calls=%fused_computation.27 | convolution fusion | flops 136839168 | bytes 1122304 | tf_op jit(solution)/shard_map/ijt,tg->gij/dot_general | solution.py:22
  26.7 4.0 %fusion.22 = bf16[32,128,128]{2,0,1:T(8,128)(2,1)S(1)} fusion(bf16[128,32,1]{0,1,2:T(8,128)(2,1)S(1)} %bitcast.76, s32[128,128]{1,0:T(8,128)S(1)} %get-tuple-element.36), kind=kOutput, calls=%fused_computation.28 | convolution fusion | flops 136839168 | bytes 1122304 | tf_op jit(solution)/shard_map/ijt,tg->gij/dot_general | solution.py:22
  30.6 1.7 %pad_maximum_fusion.1 = bf16[32,128,256]{2,0,1:T(8,128)(2,1)} fusion(bf16[32,128,128]{2,0,1:T(8,128)(2,1)S(1)} %fusion.21, bf16[32,128,128]{2,0,1:T(8,128)(2,1)S(1)} %fusion.22), kind=kLoop, calls=%fused_computation.22 | loop fusion | flops 4194304 | bytes 4194304 | tf_op jit(solution)/shard_map/concatenate | solution.py:120
  38.7 4.1 %copy.27 = bf16[32,128,256]{2,1,0:T(8,128)(2,1)} copy(bf16[32,128,256]{2,0,1:T(8,128)(2,1)} %pad_maximum_fusion.1) | data formatting | bytes 4194304 | tf_op jit(solution)/shard_map/concatenate | solution.py:120
  43.6 4.3 %constant_dynamic-slice_fusion.11 = (bf16[16,32,2048]{2,1,0:T(8,128)(2,1)S(1)}, bf16[16,32,2048]{2,1,0:T(8,128)(2,1)S(1)}, bf16[16,32,2048]{2,1,0:T(8,128)(2,1)S(1)}, bf16[16,32,2048]{2,1,0:T(8,128)(2,1)S(1)}) fusion(bf16[16,128,2048]{2,1,0:T(8,128)(2,1)} %bitcast.63, s32[]{:T(128)S(6)} %select_n.175, s32[]{:T(128)S(6)} %select_n.212, s32[]{:T(128)S(6)} %select_n.211, ...), kind=kLoop, calls=%fused_computation.71 | loop fusion | bytes 16777232 | tf_op jit(solution)/shard_map/dynamic_slice | solution.py:75
  48.0 5.6 %collective-permute-start.5 = (bf16[256,2048]{1,0:T(8,128)(2,1)S(1)}, bf16[256,2048]{1,0:T(8,128)(2,1)S(1)}, u32[]{:S(2)}, u32[]{:S(2)}) collective-permute-start(bf16[256,2048]{1,0:T(8,128)(2,1)S(1)} %copy-done.1), channel_id=1, source_target_pairs={{0,2},{1,3},{2,0},{3,1},{4,6},{5,7},{6,4},{7,5},{8,10},{9,11},{10,... | collective-permute-start | bytes 3145736 | tf_op jit(solution)/shard_map/ppermute | solution.py:42
  54.3 4.1 %pad_maximum_fusion = bf16[2048,2048]{1,0:T(8,128)(2,1)} fusion(bf16[512,2048]{1,0:T(8,128)(2,1)S(1)} %bitcast.67, bf16[512,2048]{1,0:T(8,128)(2,1)S(1)} %bitcast.68, bf16[512,2048]{1,0:T(8,128)(2,1)S(1)} %bitcast.69, bf16[512,2048]{1,0:T(8,128)(2,1)S(1)} %bitcast.66), kind=kLoop, calls=%fused_computation.3 | loop fusion | flops 33554432 | bytes 16777216 | tf_op jit(solution)/shard_map/concatenate | solution.py:76
  58.4 2.3 %select_dynamic-update-slice_fusion.4 = bf16[1160,2048]{1,0:T(8,128)(2,1)} fusion(bf16[136,2048]{1,0:T(8,128)(2,1)S(1)} %collective-permute-done, bf16[136,2048]{1,0:T(8,128)(2,1)} %collective-permute-done.1, bf16[136,2048]{1,0:T(8,128)(2,1)} %collective-permute-done.2, bf16[136,2048]{1,0:T(8,128)(2,1)} %collective-permute-done.3, pred[]{:T(512)S(6)} %eq.79, ...), kind=kLoop, calls=%fused_computation.42 | loop fusion | flops 1114111 | bytes 2785284
  60.7 15.3 %collective-permute-done.5 = bf16[256,2048]{1,0:T(8,128)(2,1)S(1)} collective-permute-done((bf16[256,2048]{1,0:T(8,128)(2,1)S(1)}, bf16[256,2048]{1,0:T(8,128)(2,1)S(1)}, u32[]{:S(2)}, u32[]{:S(2)}) %collective-permute-start.5) | collective-permute-done | bytes 1048608 | tf_op jit(solution)/shard_map/ppermute | solution.py:42
  76.1 1.8 %select_dynamic-update-slice_fusion.3 = bf16[1160,2048]{1,0:T(8,128)(2,1)} fusion(bf16[1160,2048]{1,0:T(8,128)(2,1)} %select_dynamic-update-slice_fusion.4, bf16[256,2048]{1,0:T(8,128)(2,1)S(1)} %collective-permute-done.4, bf16[256,2048]{1,0:T(8,128)(2,1)S(1)} %collective-permute-done.5, bf16[256,2048]{1,0:T(8,128)(2,1)S(1)} %collective-permute-done.6, ...), kind=kLoop, calls=%fused_computation.40 | loop fusion | flops 1572864 | bytes 5242883
  77.8 1.8 %select_dynamic-update-slice_fusion.2 = bf16[1160,2048]{1,0:T(8,128)(2,1)} fusion(bf16[1160,2048]{1,0:T(8,128)(2,1)} %select_dynamic-update-slice_fusion.3, bf16[256,2048]{1,0:T(8,128)(2,1)S(1)} %collective-permute-done.4, bf16[256,2048]{1,0:T(8,128)(2,1)S(1)} %collective-permute-done.5, bf16[256,2048]{1,0:T(8,128)(2,1)S(1)} %collective-permute-done.6, ...), kind=kLoop, calls=%fused_computation.39 | loop fusion | flops 1572864 | bytes 5242883
  79.6 1.8 %select_dynamic-update-slice_fusion.1 = bf16[1160,2048]{1,0:T(8,128)(2,1)} fusion(bf16[1160,2048]{1,0:T(8,128)(2,1)} %select_dynamic-update-slice_fusion.2, bf16[256,2048]{1,0:T(8,128)(2,1)S(1)} %collective-permute-done.4, bf16[256,2048]{1,0:T(8,128)(2,1)S(1)} %collective-permute-done.5, bf16[256,2048]{1,0:T(8,128)(2,1)S(1)} %collective-permute-done.6, ...), kind=kLoop, calls=%fused_computation.38 | loop fusion | flops 1572864 | bytes 5242883
  81.4 1.8 %select_dynamic-update-slice_fusion = bf16[1160,2048]{1,0:T(8,128)(2,1)} fusion(bf16[1160,2048]{1,0:T(8,128)(2,1)} %select_dynamic-update-slice_fusion.1, bf16[256,2048]{1,0:T(8,128)(2,1)S(1)} %collective-permute-done.4, bf16[256,2048]{1,0:T(8,128)(2,1)S(1)} %collective-permute-done.5, bf16[256,2048]{1,0:T(8,128)(2,1)S(1)} %collective-permute-done.6, ...), kind=kLoop, calls=%fused_computation.37 | loop fusion | flops 1572864 | bytes 5242883 | tf_op jit(solution)/shard_map/concatenate | solution.py:56
  83.2 11.2 %convolution_convert_fusion = bf16[1160,1536]{1,0:T(8,128)(2,1)S(1)} fusion(bf16[1160,2048]{1,0:T(8,128)(2,1)} %select_dynamic-update-slice_fusion, bf16[1536,2048]{1,0:T(8,128)(2,1)} %bitcast.77), kind=kOutput, calls=%fused_computation.10 | convolution fusion | flops 7299870720 | bytes 14606336 | tf_op jit(solution)/shard_map/dot_general | solution.py:78
  94.5 10.7 %multiply_add_fusion = f32[1152,1536]{1,0:T(8,128)S(1)} fusion(bf16[1160,1536]{1,0:T(8,128)(2,1)S(1)} %convolution_convert_fusion, f32[1536]{0:T(1024)S(1)} %mul.115, f32[1536]{0:T(1024)S(1)} %mul.112, f32[1536]{0:T(1024)S(1)} %mul.109, f32[1536]{0:T(1024)S(1)} %mul.106, f32[1536]{0:T(1024)S(1)} %copy-done.5, f32[1536]{0:T(1024)S(1)} %copy-done.6, ...), kind=kLoop, calls=%fused_computation.11 | loop fusion | flops 47775744 | bytes 31901568 | tf_op jit(solution)/shard_map/add | solution.py:91
  105.2 2.9 %copy-done = f32[1152,1536]{1,0:T(8,128)} copy-done((f32[1152,1536]{1,0:T(8,128)}, f32[1152,1536]{1,0:T(8,128)S(1)}, u32[]{:S(2)}) %copy-start) | copy-done | bytes 7077912
  109.5 1.7 %copy.28 = bf16[512,1152]{1,0:T(8,128)(2,1)S(1)} copy(bf16[512,1152]{0,1:T(8,128)(2,1)} %fusion.23) | data formatting | bytes 2359296 | tf_op jit(solution)/shard_map/transpose | solution.py:124
  111.2 1.7 %reshape.152 = bf16[32,16,9,128]{3,2,1,0:T(8,128)(2,1)} reshape(bf16[512,1152]{1,0:T(8,128)(2,1)S(1)} %copy.28) | data formatting | bytes 2359296 | tf_op jit(solution)/shard_map/reshape | solution.py:124
  112.9 2.6 %fusion.35 = (bf16[32,16,8,128]{3,2,1,0:T(8,128)(2,1)S(1)}, bf16[32,16,8,128]{3,2,1,0:T(8,128)(2,1)S(1)}) fusion(bf16[32,16,9,128]{3,2,1,0:T(8,128)(2,1)} %reshape.152), kind=kLoop, calls=%fused_computation.80 | loop fusion | bytes 4194304 | tf_op jit(solution)/shard_map/slice | solution.py:125
  117.9 7.3 %fusion.16 = f32[32,16,8,128]{3,1,2,0:T(8,128)} fusion(bf16[32,16,8,128]{3,1,2,0:T(8,128)(2,1)} %copy.34, bf16[32,16,8,128]{3,1,2,0:T(8,128)(2,1)} %copy.33, pred[8,128,256]{2,1,0:T(8,128)(4,1)S(1)} %copy-done.3, bf16[32,128,256]{2,1,0:T(8,128)(2,1)S(1)} %copy-done.2), kind=kOutput, calls=%fused_computation.26 | convolution fusion | flops 281018368 | bytes 6553600 | tf_op jit(solution)/shard_map/gcbj,bgij->gcbi/dot_general | solution.py:126
  125.3 2.5 %copy.31 = f32[32,16,8,128]{3,2,1,0:T(8,128)S(1)} copy(f32[32,16,8,128]{3,1,2,0:T(8,128)} %fusion.16) | data formatting | bytes 4194304 | tf_op jit(solution)/shard_map/gcbj,bgij->gcbi/transpose | solution.py:126
  127.8 1.8 %copy.38 = f32[64,8,8,128]{3,1,2,0:T(8,128)} copy(f32[64,8,8,128]{3,2,1,0:T(8,128)S(1)} %bitcast.64) | data formatting | bytes 4194304
  129.5 2.9 %copy.32 = f32[512,1024]{0,1:T(8,128)} copy(f32[512,1024]{1,0:T(8,128)} %bitcast.65) | data formatting | bytes 4194304 | tf_op jit(solution)/shard_map/reshape | solution.py:129
  132.4 2.6 %fusion.12 = bf16[512,1024]{0,1:T(8,128)(2,1)S(1)} fusion(f32[512,1024]{0,1:T(8,128)} %copy.32, f32[1152,1536]{1,0:T(8,128)} %copy-done), kind=kLoop, calls=%fused_computation.21 | loop fusion | flops 1048576 | bytes 5242880 | tf_op jit(solution)/shard_map/convert_element_type | solution.py:130
  135.1 3.1 %collective-permute-start.9 = (bf16[512,256]{0,1:T(8,128)(2,1)S(1)}, bf16[512,256]{0,1:T(8,128)(2,1)S(1)}, u32[]{:S(2)}, u32[]{:S(2)}) collective-permute-start(bf16[512,256]{0,1:T(8,128)(2,1)S(1)} %get-tuple-element.16), channel_id=1, source_target_pairs={{0,3},{1,2},{2,1},{3,0},{4,7},{5,6},{6,5},{7,4},{8,11},{9,10},{10,... | collective-permute-start | bytes 786440 | tf_op jit(solution)/shard_map/ppermute | solution.py:137
  138.7 6.4 %collective-permute-done.9 = bf16[512,256]{0,1:T(8,128)(2,1)S(1)} collective-permute-done((bf16[512,256]{0,1:T(8,128)(2,1)S(1)}, bf16[512,256]{0,1:T(8,128)(2,1)S(1)}, u32[]{:S(2)}, u32[]{:S(2)}) %collective-permute-start.9) | collective-permute-done | bytes 262176 | tf_op jit(solution)/shard_map/ppermute | solution.py:137
  145.0 5.3 %collective-permute-done.8 = bf16[512,256]{0,1:T(8,128)(2,1)S(1)} collective-permute-done((bf16[512,256]{0,1:T(8,128)(2,1)S(1)}, bf16[512,256]{0,1:T(8,128)(2,1)S(1)}, u32[]{:S(2)}, u32[]{:S(2)}) %collective-permute-start.8) | collective-permute-done | bytes 262176 | tf_op jit(solution)/shard_map/ppermute | solution.py:137
  150.4 6.7 %fusion.9 = bf16[256,2048]{1,0:T(8,128)(2,1)} fusion(bf16[2048,2048]{1,0:T(8,128)(2,1)} %pad_maximum_fusion, bf16[256,2048]{1,0:T(8,128)(2,1)S(1)} %copy-done.1, bf16[512,256]{0,1:T(8,128)(2,1)S(1)} %collective-permute-done.9, bf16[512,256]{0,1:T(8,128)(2,1)S(1)} %collective-permute-done.8, bf16[512,256]{0,1:T(8,128)(2,1)S(1)} %collective-permute-done.7, ...), kind=kOutput, calls=%fused_computation.15 | convolution fusion | flops 2153250816 | bytes 11534336 | tf_op jit(solution)/shard_map/dot_general | solution.py:139
  (74 shorter events, 19.4 us)
Async XLA Ops:
  6.5 10.8 %copy-start.1 = (bf16[256,2048]{1,0:T(8,128)(2,1)S(1)}, bf16[256,2048]{1,0:T(8,128)(2,1)}, u32[]{:S(2)}) copy-start(bf16[256,2048]{1,0:T(8,128)(2,1)} %param.6) | copy-start | bytes 3145732
  6.5 14.8 %copy-start.15 = (s32[1,4]{1,0:T(1,128)S(1)}, s32[1,4]{1,0:T(1,128)}, u32[]{:S(2)}) copy-start(s32[1,4]{1,0:T(1,128)} %param.7) | copy-start | bytes 52
  6.5 14.9 %copy-start.7 = (bf16[128,128]{1,0:T(8,128)(2,1)S(1)}, bf16[128,128]{1,0:T(8,128)(2,1)}, u32[]{:S(2)}) copy-start(bf16[128,128]{1,0:T(8,128)(2,1)} %param.10) | copy-start | bytes 98308
  6.5 76.6 %all-gather.2.cloned.1.call-start = ((), (), s32[]{:S(2)}) async-start(), calls=%async_computation | async-start | bytes 6684672 | tf_op jit(solution)/shard_map/all_gather | solution.py:67
  12.1 35.8 %collective-permute-start = (bf16[136,2048]{1,0:T(8,128)(2,1)S(1)}, bf16[136,2048]{1,0:T(8,128)(2,1)S(1)}, u32[]{:S(2)}, u32[]{:S(2)}) collective-permute-start(bf16[136,2048]{1,0:T(8,128)(2,1)S(1)} %slice.75), channel_id=1, source_target_pairs={{3,7},{7,11},{11,15},{19,23},{23,27},{27,31},{35,39},{39,43},{43,4... | collective-permute-start | bytes 1671176 | tf_op jit(solution)/shard_map/ppermute | solution.py:54
  12.8 40.8 %collective-permute-start.1 = (bf16[136,2048]{1,0:T(8,128)(2,1)S(1)}, bf16[136,2048]{1,0:T(8,128)(2,1)}, u32[]{:S(2)}, u32[]{:S(2)}) collective-permute-start(bf16[136,2048]{1,0:T(8,128)(2,1)S(1)} %slice.75), channel_id=1, source_target_pairs={{3,6},{7,10},{11,14},{19,22},{23,26},{27,30},{35,38},{39,42},{43,4... | collective-permute-start | bytes 1671176 | tf_op jit(solution)/shard_map/ppermute | solution.py:54
  14.3 44.1 %collective-permute-start.2 = (bf16[136,2048]{1,0:T(8,128)(2,1)S(1)}, bf16[136,2048]{1,0:T(8,128)(2,1)}, u32[]{:S(2)}, u32[]{:S(2)}) collective-permute-start(bf16[136,2048]{1,0:T(8,128)(2,1)S(1)} %slice.75), channel_id=1, source_target_pairs={{3,5},{7,9},{11,13},{19,21},{23,25},{27,29},{35,37},{39,41},{43,45... | collective-permute-start | bytes 1671176 | tf_op jit(solution)/shard_map/ppermute | solution.py:54
  15.8 42.6 %collective-permute-start.3 = (bf16[136,2048]{1,0:T(8,128)(2,1)S(1)}, bf16[136,2048]{1,0:T(8,128)(2,1)}, u32[]{:S(2)}, u32[]{:S(2)}) collective-permute-start(bf16[136,2048]{1,0:T(8,128)(2,1)S(1)} %slice.75), channel_id=1, source_target_pairs={{3,4},{7,8},{11,12},{19,20},{23,24},{27,28},{35,36},{39,40},{43,44... | collective-permute-start | bytes 1671176 | tf_op jit(solution)/shard_map/ppermute | solution.py:54
  17.3 43.4 %collective-permute-start.4 = (bf16[256,2048]{1,0:T(8,128)(2,1)S(1)}, bf16[256,2048]{1,0:T(8,128)(2,1)S(1)}, u32[]{:S(2)}, u32[]{:S(2)}) collective-permute-start(bf16[256,2048]{1,0:T(8,128)(2,1)S(1)} %copy-done.1), channel_id=1, source_target_pairs={{0,3},{1,2},{2,1},{3,0},{4,7},{5,6},{6,5},{7,4},{8,11},{9,10},{10,... | collective-permute-start | bytes 3145736 | tf_op jit(solution)/shard_map/ppermute | solution.py:42
  22.7 15.3 %copy-start.4 = (f32[1,3,16,32]{3,2,1,0:T(8,128)S(1)}, f32[1,3,16,32]{3,2,1,0:T(8,128)}, u32[]{:S(2)}) copy-start(f32[1,3,16,32]{3,2,1,0:T(8,128)} %get-tuple-element.24) | copy-start | bytes 18436
  48.0 28.1 %collective-permute-start.5 = (bf16[256,2048]{1,0:T(8,128)(2,1)S(1)}, bf16[256,2048]{1,0:T(8,128)(2,1)S(1)}, u32[]{:S(2)}, u32[]{:S(2)}) collective-permute-start(bf16[256,2048]{1,0:T(8,128)(2,1)S(1)} %copy-done.1), channel_id=1, source_target_pairs={{0,2},{1,3},{2,0},{3,1},{4,6},{5,7},{6,4},{7,5},{8,10},{9,11},{10,... | collective-permute-start | bytes 3145736 | tf_op jit(solution)/shard_map/ppermute | solution.py:42
  53.6 22.5 %collective-permute-start.6 = (bf16[256,2048]{1,0:T(8,128)(2,1)S(1)}, bf16[256,2048]{1,0:T(8,128)(2,1)S(1)}, u32[]{:S(2)}, u32[]{:S(2)}) collective-permute-start(bf16[256,2048]{1,0:T(8,128)(2,1)S(1)} %copy-done.1), channel_id=1, source_target_pairs={{0,1},{1,0},{2,3},{3,2},{4,5},{5,4},{6,7},{7,6},{8,9},{9,8},{10,11... | collective-permute-start | bytes 3145736 | tf_op jit(solution)/shard_map/ppermute | solution.py:42
  83.2 11.3 %copy-start.5 = (f32[1536]{0:T(1024)S(1)}, f32[1536]{0:T(1024)}, u32[]{:S(2)}) copy-start(f32[1536]{0:T(1024)} %mul.103) | copy-start | bytes 18436
  83.2 11.3 %copy-start.6 = (f32[1536]{0:T(1024)S(1)}, f32[1536]{0:T(1024)}, u32[]{:S(2)}) copy-start(f32[1536]{0:T(1024)} %mul.100) | copy-start | bytes 18436
  83.2 11.3 %copy-start.8 = (pred[1152]{0:T(1024)(128)(4,1)S(1)}, pred[1152]{0:T(1024)(128)(4,1)}, u32[]{:S(2)}) copy-start(pred[1152]{0:T(1024)(128)(4,1)} %get-tuple-element.26) | copy-start | bytes 3460
  83.2 11.3 %copy-start.9 = (pred[1152]{0:T(1024)(128)(4,1)S(1)}, pred[1152]{0:T(1024)(128)(4,1)}, u32[]{:S(2)}) copy-start(pred[1152]{0:T(1024)(128)(4,1)} %get-tuple-element.27) | copy-start | bytes 3460
  83.2 11.3 %copy-start.10 = (pred[1152]{0:T(1024)(128)(4,1)S(1)}, pred[1152]{0:T(1024)(128)(4,1)}, u32[]{:S(2)}) copy-start(pred[1152]{0:T(1024)(128)(4,1)} %get-tuple-element.28) | copy-start | bytes 3460
  83.2 11.3 %copy-start.11 = (pred[1152]{0:T(1024)(128)(4,1)S(1)}, pred[1152]{0:T(1024)(128)(4,1)}, u32[]{:S(2)}) copy-start(pred[1152]{0:T(1024)(128)(4,1)} %get-tuple-element.29) | copy-start | bytes 3460
  83.2 11.3 %copy-start.12 = (pred[1152]{0:T(1024)(128)(4,1)S(1)}, pred[1152]{0:T(1024)(128)(4,1)}, u32[]{:S(2)}) copy-start(pred[1152]{0:T(1024)(128)(4,1)} %get-tuple-element.30) | copy-start | bytes 3460
  83.2 11.3 %copy-start.13 = (pred[1152]{0:T(1024)(128)(4,1)S(1)}, pred[1152]{0:T(1024)(128)(4,1)}, u32[]{:S(2)}) copy-start(pred[1152]{0:T(1024)(128)(4,1)} %get-tuple-element.31) | copy-start | bytes 3460
  83.2 11.3 %copy-start.14 = (pred[1152]{0:T(1024)(128)(4,1)S(1)}, pred[1152]{0:T(1024)(128)(4,1)}, u32[]{:S(2)}) copy-start(pred[1152]{0:T(1024)(128)(4,1)} %get-tuple-element.32) | copy-start | bytes 3460
  105.2 2.9 %copy-start = (f32[1152,1536]{1,0:T(8,128)}, f32[1152,1536]{1,0:T(8,128)S(1)}, u32[]{:S(2)}) copy-start(f32[1152,1536]{1,0:T(8,128)S(1)} %multiply_add_fusion) | copy-start | bytes 21233668
  112.8 5.1 %copy-start.2 = (bf16[32,128,256]{2,1,0:T(8,128)(2,1)S(1)}, bf16[32,128,256]{2,1,0:T(8,128)(2,1)}, u32[]{:S(2)}) copy-start(bf16[32,128,256]{2,1,0:T(8,128)(2,1)} %copy.27) | copy-start | bytes 6291460
  112.8 5.1 %copy-start.3 = (pred[8,128,256]{2,1,0:T(8,128)(4,1)S(1)}, pred[8,128,256]{2,1,0:T(8,128)(4,1)}, u32[]{:S(2)}) copy-start(pred[8,128,256]{2,1,0:T(8,128)(4,1)} %pad_add_fusion) | copy-start | bytes 786436
  135.1 10.0 %collective-permute-start.9 = (bf16[512,256]{0,1:T(8,128)(2,1)S(1)}, bf16[512,256]{0,1:T(8,128)(2,1)S(1)}, u32[]{:S(2)}, u32[]{:S(2)}) collective-permute-start(bf16[512,256]{0,1:T(8,128)(2,1)S(1)} %get-tuple-element.16), channel_id=1, source_target_pairs={{0,3},{1,2},{2,1},{3,0},{4,7},{5,6},{6,5},{7,4},{8,11},{9,10},{10,... | collective-permute-start | bytes 786440 | tf_op jit(solution)/shard_map/ppermute | solution.py:137
  138.2 12.2 %collective-permute-start.8 = (bf16[512,256]{0,1:T(8,128)(2,1)S(1)}, bf16[512,256]{0,1:T(8,128)(2,1)S(1)}, u32[]{:S(2)}, u32[]{:S(2)}) collective-permute-start(bf16[512,256]{0,1:T(8,128)(2,1)S(1)} %get-tuple-element.17), channel_id=1, source_target_pairs={{0,2},{1,3},{2,0},{3,1},{4,6},{5,7},{6,4},{7,5},{8,10},{9,11},{10,... | collective-permute-start | bytes 786440 | tf_op jit(solution)/shard_map/ppermute | solution.py:137
  138.2 12.2 %collective-permute-start.7 = (bf16[512,256]{0,1:T(8,128)(2,1)S(1)}, bf16[512,256]{0,1:T(8,128)(2,1)S(1)}, u32[]{:S(2)}, u32[]{:S(2)}) collective-permute-start(bf16[512,256]{0,1:T(8,128)(2,1)S(1)} %get-tuple-element.18), channel_id=1, source_target_pairs={{0,1},{1,0},{2,3},{3,2},{4,5},{5,4},{6,7},{7,6},{8,9},{9,8},{10,11... | collective-permute-start | bytes 786440 | tf_op jit(solution)/shard_map/ppermute | solution.py:137
Sparse Core Ops, SparseCore 0:
  11.1 70.1 all-gather.1

commit v10 on v6

--- a/solution.py
+++ b/solution.py
@@ -117,23 +117,41 @@
     ).astype(jnp.bfloat16)
 
     mi_t = mixed_in.T.reshape(n_groups, per_group, n_blocks + 1, filter_len)
-    filtered = jnp.einsum(
-        "gcbj,bgij->gcbi", mi_t[:, :, 1:], cur_kernel, preferred_element_type=jnp.float32
+    q_t = queries.T
+    half_blocks = n_blocks // 2
+    half_rows = span // 2
+
+    def conv_half(h, mi_t, cur_kernel, prev_kernel, q_t):
+        src = lax.dynamic_slice_in_dim(mi_t, h * half_blocks, half_blocks + 1, axis=2)
+        ck = lax.dynamic_slice_in_dim(cur_kernel, h * half_blocks, half_blocks, axis=0)
+        pk = lax.dynamic_slice_in_dim(prev_kernel, h * half_blocks, half_blocks, axis=0)
+        filtered = jnp.einsum(
+            "gcbj,bgij->gcbi", src[:, :, 1:], ck, preferred_element_type=jnp.float32
+        )
+        filtered = filtered + jnp.einsum(
+            "gcbj,bgij->gcbi", src[:, :, :-1], pk, preferred_element_type=jnp.float32
+        )
+        q = lax.dynamic_slice_in_dim(q_t, h * half_rows, half_rows, axis=1)
+        gated = (q * filtered.reshape(own, half_rows)).astype(jnp.bfloat16)
+        return gated.reshape(own, 2, rows)
+
+    chip = member // 2
+    far = conv_half(1 - chip, mi_t, cur_kernel, prev_kernel, q_t)
+    got = {}
+    for d in (2, 3):
+        send = lax.dynamic_index_in_dim(far, (member ^ d) % 2, axis=1, keepdims=False)
+        got[d] = lax.ppermute(send, "seq", swaps[d - 1])
+    far, mi_t, cur_kernel, prev_kernel, q_t = lax.optimization_barrier(
+        (far, mi_t, cur_kernel, prev_kernel, q_t)
     )
-    filtered = filtered + jnp.einsum(
-        "gcbj,bgij->gcbi", mi_t[:, :, :-1], prev_kernel, preferred_element_type=jnp.float32
-    )
-    filtered = filtered.reshape(own, span)
-    gated = (queries.T * filtered).astype(jnp.bfloat16)
-
-
-    gated = gated.reshape(own, GROUP_DEVS, rows)
+    near = conv_half(chip, mi_t, cur_kernel, prev_kernel, q_t)
+    got[0] = lax.dynamic_index_in_dim(near, member % 2, axis=1, keepdims=False)
+    send = lax.dynamic_index_in_dim(near, (member ^ 1) % 2, axis=1, keepdims=False)
+    got[1] = lax.ppermute(send, "seq", swaps[0])
     result = tokens.astype(jnp.float32)
     for d in range(GROUP_DEVS):
-        send = lax.dynamic_index_in_dim(gated, member ^ d, axis=1, keepdims=False)
-        got = send if d == 0 else lax.ppermute(send, "seq", swaps[d - 1])
         result = result + lax.dot_general(
-            got,
+            got[d],
             ow_cat[d * own : (d + 1) * own],
             (((0,), (0,)), ((), ())),
             preferred_element_type=jnp.float32,

time: 157 us -> 192 us (1.22)
  matrix products: 36.8 us -> 47.7 us
  waiting for transfers between devices: 28.3 us -> 38.8 us
  other arithmetic: 30.2 us -> 37.5 us
  starting transfers between devices: 16.8 us -> 21.5 us
  local copies, waits for them, and re-layouts: 29.5 us -> 31.9 us
    ppermute x3, waiting for transfers between devices: 15.4 us -> 38.8 us  [local(): lax.ppermute(tokens, 'seq', perm)]
    dot_general x6 -> x8, matrix products: 17.7 us -> 28.5 us  [the longest x4 10.6 us: local(): lax.dot_general(got[d], ow_cat[d * own:(d + 1) * own], (((0,), (0,)), (()...]
    select_n x0 -> x1, other arithmetic: none -> 9.51 us  [local(): jnp.where((prev_tap[None] <= pos_out[:, :, None])[:, None], prev_table[No...]
    ppermute x3, waiting for transfers between devices: 6.54 us -> 0.01 us  [the longest x2 0.01 us: local(): got[d] = lax.ppermute(send, 'seq', swaps[d - 1])]
    all_gather x1, waiting for transfers between devices: 6.28 us -> 0.01 us  [local(): w_all = lax.all_gather(w_part, 'fsdp', axis=0, tiled=True)]
    unnamed x16 -> x27, local copies, waits for them, and re-layouts: 9.24 us -> 4.07 us
    ppermute x3, starting transfers between devices: 9.3 us -> 13.6 us  [local(): lax.ppermute(tokens, 'seq', perm)]
    mul x7, local copies, waits for them, and re-layouts: 0.51 us -> 4.08 us  [local(): taps[tap_index] * jnp.where((pos_f >= tap_index)[:, None], shifted, 0.0)]
  transfers between devices with their start and end apart: 11 -> 11, of which waited for: 4 -> 2; matrix products, arithmetic and copies ran while one was open for 25% -> 34% of each run, Pallas kernels for 0% -> 0%
where the time goes in v10:
time: 192 us; the launch traced here: 191 us
  matrix products  47.7 us (25%)
  waiting for transfers between devices  38.8 us (20%)
  other arithmetic  37.5 us (20%)
  local copies, waits for them, and re-layouts  31.9 us (17%)
  starting transfers between devices  21.5 us (11%)
  between operations  13.8 us (7%)
    ppermute x3, waiting for transfers between devices, local(): lax.ppermute(tokens, 'seq', perm)  38.8 us
    ppermute x3, starting transfers between devices, local(): lax.ppermute(tokens, 'seq', perm)  13.6 us
    dot_general x1, matrix products, local(): jnp.dot(ext_tokens, w_all.T, preferred_element_type=jnp.float32)  11.2 us
    add x1, other arithmetic, local(): featured + taps[tap_index] * jnp.where((pos_f >= tap_index)[:, None], shi...  10.7 us
    dot_general x4, matrix products, local(): lax.dot_general(got[d], ow_cat[d * own:(d + 1) * own], (((0,), (0,)), (()...  10.6 us
    select_n x1, other arithmetic, local(): jnp.where((prev_tap[None] <= pos_out[:, :, None])[:, None], prev_table[No...  9.51 us
    dot_general x2, matrix products, conv_half(): jnp.einsum('gcbj,bgij->gcbi', src[:, :, 1:], ck, preferred_element_type=j...  9 us
    dot_general x2, matrix products, conv_half(): jnp.einsum('gcbj,bgij->gcbi', src[:, :, :-1], pk, preferred_element_type=...  8.92 us
  transfers between devices with their start and end apart: 11, of which 2 were waited for; matrix products, arithmetic and copies ran while one was open for 34% of the time, Pallas kernels for 0%

profile of v10, /device:TPU:1, one launch (start us, length us, event | category | flops | bytes accessed | tf_op | source)
XLA Modules:
  0.0 191.1 jit_solution(14948462244359012777)
XLA Ops:
  6.6 1.8 copy.36
  9.2 1.9 %slice.93 = bf16[136,2048]{1,0:T(8,128)(2,1)} slice(bf16[256,2048]{1,0:T(8,128)(2,1)} %param.6), slice={[120:256], [0:2048]} | slice | bytes 1114112 | tf_op jit(solution)/shard_map/slice | solution.py:49
  12.6 1.5 collective-permute-start.2
  17.0 3.2 %collective-permute-start.6 = (bf16[256,2048]{1,0:T(8,128)(2,1)S(1)}, bf16[256,2048]{1,0:T(8,128)(2,1)S(1)}, u32[]{:S(2)}, u32[]{:S(2)}) collective-permute-start(bf16[256,2048]{1,0:T(8,128)(2,1)S(1)} %copy-done), channel_id=1, source_target_pairs={{0,1},{1,0},{2,3},{3,2},{4,5},{5,4},{6,7},{7,6},{8,9},{9,8},{10,11... | collective-permute-start | bytes 3145736 | tf_op jit(solution)/shard_map/ppermute | solution.py:42
  24.9 4.0 %fusion.22 = bf16[32,128,128]{2,0,1:T(8,128)(2,1)S(1)} fusion(bf16[128,32,1]{0,1,2:T(8,128)(2,1)S(1)} %bitcast.90, s32[128,128]{1,0:T(8,128)S(1)} %iota_subtract_fusion), kind=kOutput, calls=%fused_computation.32 | convolution fusion | flops 136839168 | bytes 1122304 | tf_op jit(solution)/shard_map/ijt,tg->gij/dot_general | solution.py:22
  29.4 4.0 %fusion.23 = bf16[32,128,128]{2,0,1:T(8,128)(2,1)S(1)} fusion(bf16[128,32,1]{0,1,2:T(8,128)(2,1)S(1)} %bitcast.91, s32[128,128]{1,0:T(8,128)S(1)} %iota_subtract_fusion.1), kind=kOutput, calls=%fused_computation.33 | convolution fusion | flops 136839168 | bytes 1122304 | tf_op jit(solution)/shard_map/ijt,tg->gij/dot_general | solution.py:22
  35.1 9.5 %broadcast_select_fusion = (bf16[8,32,128,128]{3,2,0,1:T(8,128)(2,1)}, bf16[8,32,128,128]{3,2,0,1:T(8,128)(2,1)}) fusion(pred[8,128,128]{2,1,0:T(8,128)(4,1)S(1)} %get-tuple-element.42, bf16[32,128,128]{2,1,0:T(8,128)(2,1)S(1)} %copy.41, bf16[32,128,128]{2,1,0:T(8,128)(2,1)} %copy.38, pred[8,128,128]{2,1,0:T(8,128)(4,1)S(1)} %get-tuple-element.41), kind=kLoop, calls=%fused_computation.5 | loop fusion | flops 8388608 | bytes 19136512 | tf_op jit(solution)/shard_map/jit(_where)/select_n | solution.py:115
  44.7 4.3 %constant_dynamic-slice_fusion.13 = (bf16[16,32,2048]{2,1,0:T(8,128)(2,1)S(1)}, bf16[16,32,2048]{2,1,0:T(8,128)(2,1)S(1)}, bf16[16,32,2048]{2,1,0:T(8,128)(2,1)S(1)}, bf16[16,32,2048]{2,1,0:T(8,128)(2,1)S(1)}) fusion(bf16[16,128,2048]{2,1,0:T(8,128)(2,1)} %bitcast.74, s32[]{:T(128)S(6)} %select_n.217, s32[]{:T(128)S(6)} %select_n.254, s32[]{:T(128)S(6)} %select_n.253, ...), kind=kLoop, calls=%fused_computation.82 | loop fusion | bytes 16777232 | tf_op jit(solution)/shard_map/dynamic_slice | solution.py:75
  49.1 9.7 %collective-permute-start.5 = (bf16[256,2048]{1,0:T(8,128)(2,1)S(1)}, bf16[256,2048]{1,0:T(8,128)(2,1)S(1)}, u32[]{:S(2)}, u32[]{:S(2)}) collective-permute-start(bf16[256,2048]{1,0:T(8,128)(2,1)S(1)} %copy-done), channel_id=1, source_target_pairs={{0,2},{1,3},{2,0},{3,1},{4,6},{5,7},{6,4},{7,5},{8,10},{9,11},{10,... | collective-permute-start | bytes 3145736 | tf_op jit(solution)/shard_map/ppermute | solution.py:42
  59.5 4.1 %pad_maximum_fusion = bf16[2048,2048]{1,0:T(8,128)(2,1)} fusion(bf16[512,2048]{1,0:T(8,128)(2,1)S(1)} %bitcast.76, bf16[512,2048]{1,0:T(8,128)(2,1)S(1)} %bitcast.77, bf16[512,2048]{1,0:T(8,128)(2,1)S(1)} %bitcast.78, bf16[512,2048]{1,0:T(8,128)(2,1)S(1)} %bitcast.75), kind=kLoop, calls=%fused_computation | loop fusion | flops 33554432 | bytes 16777216 | tf_op jit(solution)/shard_map/concatenate | solution.py:76
  63.5 2.3 %select_dynamic-update-slice_fusion.4 = bf16[1160,2048]{1,0:T(8,128)(2,1)} fusion(bf16[136,2048]{1,0:T(8,128)(2,1)} %collective-permute-done, bf16[136,2048]{1,0:T(8,128)(2,1)} %collective-permute-done.1, bf16[136,2048]{1,0:T(8,128)(2,1)} %collective-permute-done.2, bf16[136,2048]{1,0:T(8,128)(2,1)} %collective-permute-done.3, pred[]{:T(512)S(6)} %eq.83, ...), kind=kLoop, calls=%fused_computation.48 | loop fusion | flops 1114111 | bytes 2785284
  65.9 16.0 %collective-permute-done.5 = bf16[256,2048]{1,0:T(8,128)(2,1)S(1)} collective-permute-done((bf16[256,2048]{1,0:T(8,128)(2,1)S(1)}, bf16[256,2048]{1,0:T(8,128)(2,1)S(1)}, u32[]{:S(2)}, u32[]{:S(2)}) %collective-permute-start.5) | collective-permute-done | bytes 1048608 | tf_op jit(solution)/shard_map/ppermute | solution.py:42
  81.8 22.8 %collective-permute-done.4 = bf16[256,2048]{1,0:T(8,128)(2,1)S(1)} collective-permute-done((bf16[256,2048]{1,0:T(8,128)(2,1)S(1)}, bf16[256,2048]{1,0:T(8,128)(2,1)S(1)}, u32[]{:S(2)}, u32[]{:S(2)}) %collective-permute-start.4) | collective-permute-done | bytes 1048608 | tf_op jit(solution)/shard_map/ppermute | solution.py:42
  104.7 1.7 select_dynamic-update-slice_fusion.3
  106.4 1.7 select_dynamic-update-slice_fusion.2
  108.0 1.7 select_dynamic-update-slice_fusion.1
  109.7 1.7 select_dynamic-update-slice_fusion
  111.4 11.2 %convolution_convert_fusion = bf16[1160,1536]{1,0:T(8,128)(2,1)S(1)} fusion(bf16[1160,2048]{1,0:T(8,128)(2,1)} %select_dynamic-update-slice_fusion, bf16[1536,2048]{1,0:T(8,128)(2,1)} %bitcast.92), kind=kOutput, calls=%fused_computation.7 | convolution fusion | flops 7299870720 | bytes 14606336 | tf_op jit(solution)/shard_map/dot_general | solution.py:78
  122.7 10.7 %multiply_add_fusion = f32[1152,1536]{1,0:T(8,128)S(1)} fusion(bf16[1160,1536]{1,0:T(8,128)(2,1)S(1)} %convolution_convert_fusion, f32[1536]{0:T(1024)S(1)} %copy-done.8, f32[1536]{0:T(1024)S(1)} %copy-done.3, f32[1536]{0:T(1024)S(1)} %copy-done.4, f32[1536]{0:T(1024)S(1)} %copy-done.5, f32[1536]{0:T(1024)S(1)} %copy-done.6, f32[1536]{0:T(1024)S(1)} %copy-done.7, ...), kind=kLoop, calls=%fused_computation.8 | loop fusion | flops 47775744 | bytes 31901568 | tf_op jit(solution)/shard_map/add | solution.py:91
  133.8 2.6 %slice_bitcast_fusion.1 = (f32[512,1024]{0,1:T(8,128)}, f32[1024,512]{1,0:T(8,128)}) fusion(f32[1152,1536]{1,0:T(8,128)S(1)} %multiply_add_fusion), kind=kLoop, calls=%fused_computation.95 | loop fusion | bytes 6291456 | tf_op jit(solution)/shard_map/transpose | solution.py:120
  137.8 2.7 %reshape.160 = bf16[32,16,9,128]{3,2,1,0:T(8,128)(2,1)S(1)} reshape(bf16[512,1152]{1,0:T(8,128)(2,1)} %copy.39) | data formatting | bytes 2359296 | tf_op jit(solution)/shard_map/reshape | solution.py:119
  141.3 4.5 %fusion.6 = f32[32,4,128,16]{2,3,1,0:T(8,128)S(1)} fusion(bf16[8,32,128,128]{3,2,0,1:T(8,128)(2,1)} %get-tuple-element.15, s32[]{:T(128)S(6)} %select_n.267, bf16[32,16,4,128]{3,2,1,0:T(4,128)(2,1)S(1)} %get-tuple-element.24), kind=kOutput, calls=%fused_computation.13 | convolution fusion | flops 67108864 | bytes 5767172 | tf_op jit(solution)/shard_map/gcbj,bgij->gcbi/dot_general | solution.py:131
  145.8 4.5 %fusion.27 = f32[32,16,4,128]{3,1,2,0:T(8,128)S(1)} fusion(f32[32,4,128,16]{2,3,1,0:T(8,128)S(1)} %fusion.6, bf16[8,32,128,128]{3,2,0,1:T(8,128)(2,1)} %get-tuple-element.13, s32[]{:T(128)S(6)} %select_n.267, bf16[32,16,4,128]{3,2,1,0:T(4,128)(2,1)S(1)} %get-tuple-element.23), kind=kOutput, calls=%fused_computation.35 | convolution fusion | flops 67371008 | bytes 6815748 | tf_op jit(solution)/shard_map/gcbj,bgij->gcbi/dot_general | solution.py:128
  151.8 2.6 %copy.43 = f32[512,512]{0,1:T(8,128)} copy(f32[512,512]{1,0:T(8,128)} %bitcast.80) | data formatting | bytes 2097152 | tf_op jit(solution)/shard_map/reshape | solution.py:135
  154.3 1.7 fusion.37
  158.8 4.5 %fusion.2 = f32[32,4,128,16]{2,3,1,0:T(8,128)S(1)} fusion(bf16[8,32,128,128]{3,2,0,1:T(8,128)(2,1)} %get-tuple-element.15, s32[]{:T(128)S(6)} %select_n.271, bf16[32,16,9,128]{3,1,2,0:T(8,128)(2,1)S(1)} %copy.44, s32[]{:T(128)S(6)} %select_n.272), kind=kOutput, calls=%fused_computation.9 | convolution fusion | flops 67108864 | bytes 5767176 | tf_op jit(solution)/shard_map/gcbj,bgij->gcbi/dot_general | solution.py:131
  163.3 4.5 %fusion.33 = f32[32,16,4,128]{3,1,2,0:T(8,128)S(1)} fusion(f32[32,4,128,16]{2,3,1,0:T(8,128)S(1)} %fusion.2, bf16[8,32,128,128]{3,2,0,1:T(8,128)(2,1)} %get-tuple-element.13, s32[]{:T(128)S(6)} %select_n.271, bf16[32,16,9,128]{3,1,2,0:T(8,128)(2,1)S(1)} %copy.44, s32[]{:T(128)S(6)} %add.180), kind=kOutput, calls=%fused_computation.37 | convolution fusion | flops 67371008 | bytes 6815752 | tf_op jit(solution)/shard_map/gcbj,bgij->gcbi/dot_general | solution.py:128
  169.3 2.6 %copy.46 = f32[512,512]{0,1:T(8,128)} copy(f32[512,512]{1,0:T(8,128)} %bitcast.82) | data formatting | bytes 2097152 | tf_op jit(solution)/shard_map/reshape | solution.py:135
  173.6 2.3 %convolution_add_fusion.1 = f32[256,2048]{1,0:T(8,128)S(1)} fusion(bf16[2048,2048]{1,0:T(8,128)(2,1)} %pad_maximum_fusion, bf16[256,2048]{1,0:T(8,128)(2,1)S(1)} %copy-done, bf16[512,2,256]{0,2,1:T(8,128)(2,1)S(1)} %bitcast.85, s32[]{:T(128)S(6)} %select_n.274), kind=kOutput, calls=%fused_computation.21 | convolution fusion | flops 537919488 | bytes 5505028 | tf_op jit(solution)/shard_map/dot_general | solution.py:153
  176.0 2.4 %fusion.16 = f32[256,2048]{1,0:T(8,128)S(1)} fusion(bf16[512,256]{0,1:T(8,128)(2,1)} %collective-permute-done.9, bf16[2048,2048]{1,0:T(8,128)(2,1)} %pad_maximum_fusion), kind=kOutput, calls=%fused_computation.26 | convolution fusion | flops 536870912 | bytes 4456448 | tf_op jit(solution)/shard_map/dot_general | solution.py:153
  178.4 2.4 %fusion.18 = f32[256,2048]{1,0:T(8,128)S(1)} fusion(bf16[512,256]{0,1:T(8,128)(2,1)} %collective-permute-done.8, bf16[2048,2048]{1,0:T(8,128)(2,1)} %pad_maximum_fusion), kind=kOutput, calls=%fused_computation.28 | convolution fusion | flops 536870912 | bytes 4456448 | tf_op jit(solution)/shard_map/dot_general | solution.py:153
  180.8 3.5 %fusion.14 = bf16[256,2048]{1,0:T(8,128)(2,1)} fusion(f32[256,2048]{1,0:T(8,128)S(1)} %fusion.16, f32[256,2048]{1,0:T(8,128)S(1)} %fusion.18, f32[256,2048]{1,0:T(8,128)S(1)} %convolution_add_fusion.1, bf16[512,256]{0,1:T(8,128)(2,1)S(1)} %collective-permute-done.7, bf16[2048,2048]{1,0:T(8,128)(2,1)} %pad_maximum_fusion), kind=kOutput, calls=%fused_computation.23 | convolution fusion | flops 538968064 | bytes 9699328 | tf_op jit(solution)/shard_map/dot_general | solution.py:153
  (76 shorter events, 22.9 us)
Async XLA Ops:
  6.5 10.5 %copy-start = (bf16[256,2048]{1,0:T(8,128)(2,1)S(1)}, bf16[256,2048]{1,0:T(8,128)(2,1)}, u32[]{:S(2)}) copy-start(bf16[256,2048]{1,0:T(8,128)(2,1)} %param.6) | copy-start | bytes 3145732
  6.5 13.7 %copy-start.10 = (s32[1,4]{1,0:T(1,128)S(1)}, s32[1,4]{1,0:T(1,128)}, u32[]{:S(2)}) copy-start(s32[1,4]{1,0:T(1,128)} %param.7) | copy-start | bytes 52
  6.5 13.9 %copy-start.9 = (bf16[128,128]{1,0:T(8,128)(2,1)S(1)}, bf16[128,128]{1,0:T(8,128)(2,1)}, u32[]{:S(2)}) copy-start(bf16[128,128]{1,0:T(8,128)(2,1)} %param.10) | copy-start | bytes 98308
  6.5 14.0 %copy-start.2 = (f32[7,6144]{1,0:T(8,128)S(1)}, f32[7,6144]{1,0:T(8,128)}, u32[]{:S(2)}) copy-start(f32[7,6144]{1,0:T(8,128)} %param.9) | copy-start | bytes 516100
  6.5 104.9 %all-gather.2.cloned.1.call-start = ((), (), s32[]{:S(2)}) async-start(), calls=%async_computation | async-start | bytes 6684672 | tf_op jit(solution)/shard_map/all_gather | solution.py:67
  11.1 37.9 %collective-permute-start.3 = (bf16[136,2048]{1,0:T(8,128)(2,1)}, bf16[136,2048]{1,0:T(8,128)(2,1)}, u32[]{:S(2)}, u32[]{:S(2)}) collective-permute-start(bf16[136,2048]{1,0:T(8,128)(2,1)} %slice.93), channel_id=1, source_target_pairs={{3,4},{7,8},{11,12},{19,20},{23,24},{27,28},{35,36},{39,40},{43,44... | collective-permute-start | bytes 1671176 | tf_op jit(solution)/shard_map/ppermute | solution.py:54
  12.6 46.2 %collective-permute-start.2 = (bf16[136,2048]{1,0:T(8,128)(2,1)}, bf16[136,2048]{1,0:T(8,128)(2,1)}, u32[]{:S(2)}, u32[]{:S(2)}) collective-permute-start(bf16[136,2048]{1,0:T(8,128)(2,1)} %slice.93), channel_id=1, source_target_pairs={{3,5},{7,9},{11,13},{19,21},{23,25},{27,29},{35,37},{39,41},{43,45... | collective-permute-start | bytes 1671176 | tf_op jit(solution)/shard_map/ppermute | solution.py:54
  14.1 49.5 %collective-permute-start.1 = (bf16[136,2048]{1,0:T(8,128)(2,1)}, bf16[136,2048]{1,0:T(8,128)(2,1)}, u32[]{:S(2)}, u32[]{:S(2)}) collective-permute-start(bf16[136,2048]{1,0:T(8,128)(2,1)} %slice.93), channel_id=1, source_target_pairs={{3,6},{7,10},{11,14},{19,22},{23,26},{27,30},{35,38},{39,42},{43,4... | collective-permute-start | bytes 1671176 | tf_op jit(solution)/shard_map/ppermute | solution.py:54
  15.6 48.0 %collective-permute-start = (bf16[136,2048]{1,0:T(8,128)(2,1)}, bf16[136,2048]{1,0:T(8,128)(2,1)}, u32[]{:S(2)}, u32[]{:S(2)}) collective-permute-start(bf16[136,2048]{1,0:T(8,128)(2,1)} %slice.93), channel_id=1, source_target_pairs={{3,7},{7,11},{11,15},{19,23},{23,27},{27,31},{35,39},{39,43},{43,4... | collective-permute-start | bytes 1671176 | tf_op jit(solution)/shard_map/ppermute | solution.py:54
  17.0 48.8 %collective-permute-start.6 = (bf16[256,2048]{1,0:T(8,128)(2,1)S(1)}, bf16[256,2048]{1,0:T(8,128)(2,1)S(1)}, u32[]{:S(2)}, u32[]{:S(2)}) collective-permute-start(bf16[256,2048]{1,0:T(8,128)(2,1)S(1)} %copy-done), channel_id=1, source_target_pairs={{0,1},{1,0},{2,3},{3,2},{4,5},{5,4},{6,7},{7,6},{8,9},{9,8},{10,11... | collective-permute-start | bytes 3145736 | tf_op jit(solution)/shard_map/ppermute | solution.py:42
  49.1 32.8 %collective-permute-start.5 = (bf16[256,2048]{1,0:T(8,128)(2,1)S(1)}, bf16[256,2048]{1,0:T(8,128)(2,1)S(1)}, u32[]{:S(2)}, u32[]{:S(2)}) collective-permute-start(bf16[256,2048]{1,0:T(8,128)(2,1)S(1)} %copy-done), channel_id=1, source_target_pairs={{0,2},{1,3},{2,0},{3,1},{4,6},{5,7},{6,4},{7,5},{8,10},{9,11},{10,... | collective-permute-start | bytes 3145736 | tf_op jit(solution)/shard_map/ppermute | solution.py:42
  58.8 45.9 %collective-permute-start.4 = (bf16[256,2048]{1,0:T(8,128)(2,1)S(1)}, bf16[256,2048]{1,0:T(8,128)(2,1)S(1)}, u32[]{:S(2)}, u32[]{:S(2)}) collective-permute-start(bf16[256,2048]{1,0:T(8,128)(2,1)S(1)} %copy-done), channel_id=1, source_target_pairs={{0,3},{1,2},{2,1},{3,0},{4,7},{5,6},{6,5},{7,4},{8,11},{9,10},{10,... | collective-permute-start | bytes 3145736 | tf_op jit(solution)/shard_map/ppermute | solution.py:42
  111.4 11.3 %copy-start.3 = (f32[1536]{0:T(1024)S(1)}, f32[1536]{0:T(1024)}, u32[]{:S(2)}) copy-start(f32[1536]{0:T(1024)} %mul.131) | copy-start | bytes 18436
  111.4 11.3 %copy-start.4 = (f32[1536]{0:T(1024)S(1)}, f32[1536]{0:T(1024)}, u32[]{:S(2)}) copy-start(f32[1536]{0:T(1024)} %mul.128) | copy-start | bytes 18436
  111.4 11.3 %copy-start.5 = (f32[1536]{0:T(1024)S(1)}, f32[1536]{0:T(1024)}, u32[]{:S(2)}) copy-start(f32[1536]{0:T(1024)} %mul.125) | copy-start | bytes 18436
  111.4 11.3 %copy-start.6 = (f32[1536]{0:T(1024)S(1)}, f32[1536]{0:T(1024)}, u32[]{:S(2)}) copy-start(f32[1536]{0:T(1024)} %mul.122) | copy-start | bytes 18436
  111.4 11.3 %copy-start.7 = (f32[1536]{0:T(1024)S(1)}, f32[1536]{0:T(1024)}, u32[]{:S(2)}) copy-start(f32[1536]{0:T(1024)} %mul.119) | copy-start | bytes 18436
  111.4 11.3 %copy-start.8 = (f32[1536]{0:T(1024)S(1)}, f32[1536]{0:T(1024)}, u32[]{:S(2)}) copy-start(f32[1536]{0:T(1024)} %mul.134) | copy-start | bytes 18436
  156.8 21.6 %collective-permute-start.8 = (bf16[512,256]{0,1:T(8,128)(2,1)S(1)}, bf16[512,256]{0,1:T(8,128)(2,1)}, u32[]{:S(2)}, u32[]{:S(2)}) collective-permute-start(bf16[512,256]{0,1:T(8,128)(2,1)S(1)} %get-tuple-element.25), channel_id=1, source_target_pairs={{0,2},{1,3},{2,0},{3,1},{4,6},{5,7},{6,4},{7,5},{8,10},{9,11},{10,... | collective-permute-start | bytes 786440 | tf_op jit(solution)/shard_map/ppermute | solution.py:143
  158.3 17.7 %collective-permute-start.9 = (bf16[512,256]{0,1:T(8,128)(2,1)}, bf16[512,256]{0,1:T(8,128)(2,1)}, u32[]{:S(2)}, u32[]{:S(2)}) collective-permute-start(bf16[512,256]{0,1:T(8,128)(2,1)} %get-tuple-element.26), channel_id=1, source_target_pairs={{0,3},{1,2},{2,1},{3,0},{4,7},{5,6},{6,5},{7,4},{8,11},{9,10},{10,... | collective-permute-start | bytes 786440 | tf_op jit(solution)/shard_map/ppermute | solution.py:143
  167.8 4.1 %copy-start.1 = (f32[512,1024]{0,1:T(8,128)S(1)}, f32[512,1024]{0,1:T(8,128)}, u32[]{:S(2)}) copy-start(f32[512,1024]{0,1:T(8,128)} %get-tuple-element.12) | copy-start | bytes 6291460
  173.3 7.5 %collective-permute-start.7 = (bf16[512,256]{0,1:T(8,128)(2,1)S(1)}, bf16[512,256]{0,1:T(8,128)(2,1)S(1)}, u32[]{:S(2)}, u32[]{:S(2)}) collective-permute-start(bf16[512,256]{0,1:T(8,128)(2,1)S(1)} %dynamic-slice_bitcast_fusion.2), channel_id=1, source_target_pairs={{0,1},{1,0},{2,3},{3,2},{4,5},{5,4},{6,7},{7,6},{8,9},{9,8},{10,11... | collective-permute-start | bytes 786440 | tf_op jit(solution)/shard_map/ppermute | solution.py:150
Sparse Core Ops, SparseCore 0:
  9.8 70.0 all-gather.1

commit v11 on v3

--- a/solution.py
+++ b/solution.py
@@ -68,6 +68,13 @@
     own = n_lblk * part
     w_all = w_all.reshape(3 * own, channels)
 
+    ow = out_weight.reshape(n_lblk, LANE, channels)
+    weights = []
+    for d in range(GROUP_DEVS):
+        src_offset = (member ^ d) * part
+        weights.append(lax.dynamic_slice_in_dim(ow, src_offset, part, axis=1).reshape(own, channels))
+    ow_cat = jnp.concatenate(weights, axis=0)
+    ext_tokens, ow_cat = lax.optimization_barrier((ext_tokens, ow_cat))
     projected = jnp.dot(
         ext_tokens, w_all.T, preferred_element_type=jnp.float32
     ).astype(jnp.bfloat16)
@@ -119,19 +126,13 @@
     gated = (queries * filtered).astype(jnp.bfloat16)
 
     gated = gated.reshape(GROUP_DEVS, rows, own)
-    ow = out_weight.reshape(n_lblk, LANE, channels)
     pieces = []
-    weights = []
     for d in range(GROUP_DEVS):
         send = lax.dynamic_index_in_dim(gated, member ^ d, axis=0, keepdims=False)
         got = send if d == 0 else lax.ppermute(send, "seq", swaps[d - 1])
         pieces.append(got)
-        src_offset = (member ^ d) * part
-        weights.append(lax.dynamic_slice_in_dim(ow, src_offset, part, axis=1).reshape(own, channels))
     result = tokens.astype(jnp.float32) + jnp.dot(
-        jnp.concatenate(pieces, axis=1),
-        jnp.concatenate(weights, axis=0),
-        preferred_element_type=jnp.float32,
+        jnp.concatenate(pieces, axis=1), ow_cat, preferred_element_type=jnp.float32
     )
     return result.astype(jnp.bfloat16)
 

time: 158 us -> 159 us (level)
  the two profiles are of different devices: /device:TPU:191 before, /device:TPU:1 now
where the time goes in v11:
time: 159 us; the launch traced here: 157 us
  matrix products  36.4 us (23%)
  waiting for transfers between devices  33.7 us (21%)
  other arithmetic  29 us (18%)
  local copies, waits for them, and re-layouts  27.9 us (18%)
  starting transfers between devices  16.9 us (11%)
  between operations  13.6 us (9%)
    ppermute x3, waiting for transfers between devices, local(): lax.ppermute(tokens, 'seq', perm)  15.4 us
    ppermute x3, waiting for transfers between devices, local(): got = send if d == 0 else lax.ppermute(send, 'seq', swaps[d - 1])  11.9 us
    dot_general x1, matrix products, local(): jnp.dot(ext_tokens, w_all.T, preferred_element_type=jnp.float32)  11.2 us
    add x1, other arithmetic, local(): featured + taps[tap_index] * jnp.where((pos_f >= tap_index)[:, None], shi...  10.7 us
    ppermute x3, starting transfers between devices, local(): lax.ppermute(tokens, 'seq', perm)  9.3 us
    unnamed x16, local copies, waits for them, and re-layouts  9.03 us
    dot_general x2, matrix products, tap_table(): jnp.einsum('ijt,tg->gij', one_hot, long_filter, preferred_element_type=jn...  7.92 us
    unnamed x4, other arithmetic  7.54 us
  transfers between devices with their start and end apart: 11, of which 4 were waited for; matrix products, arithmetic and copies ran while one was open for 22% of the time, Pallas kernels for 0%

profile of v11, /device:TPU:1, one launch (start us, length us, event | category | flops | bytes accessed | tf_op | source)
XLA Modules:
  0.0 157.4 jit_solution(15012132261296262613)
XLA Ops:
  6.5 2.7 %copy.28 = bf16[2048,384]{0,1:T(8,128)(2,1)} copy(bf16[2048,384]{1,0:T(8,128)(2,1)} %param.8) | data formatting | bytes 3145728 | tf_op args[2]
  9.2 1.8 %constant_dynamic-slice_fusion.7 = bf16[3,32,2048]{2,1,0:T(8,128)(2,1)} fusion(bf16[3,128,2048]{2,1,0:T(8,128)(2,1)} %bitcast.77, s32[]{:T(128)S(6)} %select_n.178), kind=kLoop, calls=%fused_computation.67 | loop fusion | bytes 786436 | tf_op jit(solution)/shard_map/dynamic_slice | solution.py:66
  12.8 1.5 collective-permute-start.1
  14.3 1.5 collective-permute-start.2
  15.8 1.5 collective-permute-start.3
  17.2 3.0 %collective-permute-start.4 = (bf16[256,2048]{1,0:T(8,128)(2,1)S(1)}, bf16[256,2048]{1,0:T(8,128)(2,1)S(1)}, u32[]{:S(2)}, u32[]{:S(2)}) collective-permute-start(bf16[256,2048]{1,0:T(8,128)(2,1)S(1)} %copy-done.1), channel_id=1, source_target_pairs={{0,3},{1,2},{2,1},{3,0},{4,7},{5,6},{6,5},{7,4},{8,11},{9,10},{10,... | collective-permute-start | bytes 3145736 | tf_op jit(solution)/shard_map/ppermute | solution.py:42
  23.7 4.0 %fusion.19 = bf16[32,128,128]{2,0,1:T(8,128)(2,1)S(1)} fusion(bf16[128,32,1]{0,1,2:T(8,128)(2,1)S(1)} %bitcast.83, s32[128,128]{1,0:T(8,128)S(1)} %get-tuple-element.35), kind=kOutput, calls=%fused_computation.27 | convolution fusion | flops 136839168 | bytes 1122304 | tf_op jit(solution)/shard_map/ijt,tg->gij/dot_general | solution.py:22
  27.7 1.4 copy.34
  29.1 3.9 %fusion.20 = bf16[32,128,128]{2,0,1:T(8,128)(2,1)S(1)} fusion(bf16[128,32,1]{0,1,2:T(8,128)(2,1)S(1)} %bitcast.84, s32[128,128]{1,0:T(8,128)S(1)} %get-tuple-element.36), kind=kOutput, calls=%fused_computation.28 | convolution fusion | flops 136839168 | bytes 1122304 | tf_op jit(solution)/shard_map/ijt,tg->gij/dot_general | solution.py:22
  33.0 1.4 copy.31
  35.5 4.4 %constant_dynamic-slice_fusion.11 = (bf16[16,32,2048]{2,1,0:T(8,128)(2,1)S(1)}, bf16[16,32,2048]{2,1,0:T(8,128)(2,1)S(1)}, bf16[16,32,2048]{2,1,0:T(8,128)(2,1)S(1)}, bf16[16,32,2048]{2,1,0:T(8,128)(2,1)S(1)}) fusion(bf16[16,128,2048]{2,1,0:T(8,128)(2,1)} %bitcast.67, s32[]{:T(128)S(6)} %select_n.178, s32[]{:T(128)S(6)} %select_n.215, s32[]{:T(128)S(6)} %select_n.214, ...), kind=kLoop, calls=%fused_computation.71 | loop fusion | bytes 16777232 | tf_op jit(solution)/shard_map/dynamic_slice | solution.py:75
  39.9 5.6 %collective-permute-start.5 = (bf16[256,2048]{1,0:T(8,128)(2,1)S(1)}, bf16[256,2048]{1,0:T(8,128)(2,1)S(1)}, u32[]{:S(2)}, u32[]{:S(2)}) collective-permute-start(bf16[256,2048]{1,0:T(8,128)(2,1)S(1)} %copy-done.1), channel_id=1, source_target_pairs={{0,2},{1,3},{2,0},{3,1},{4,6},{5,7},{6,4},{7,5},{8,10},{9,11},{10,... | collective-permute-start | bytes 3145736 | tf_op jit(solution)/shard_map/ppermute | solution.py:42
  46.2 4.1 %pad_maximum_fusion = bf16[2048,2048]{1,0:T(8,128)(2,1)} fusion(bf16[512,2048]{1,0:T(8,128)(2,1)S(1)} %bitcast.71, bf16[512,2048]{1,0:T(8,128)(2,1)S(1)} %bitcast.72, bf16[512,2048]{1,0:T(8,128)(2,1)S(1)} %bitcast.73, bf16[512,2048]{1,0:T(8,128)(2,1)S(1)} %bitcast.70), kind=kLoop, calls=%fused_computation | loop fusion | flops 33554432 | bytes 16777216 | tf_op jit(solution)/shard_map/concatenate | solution.py:76
  50.3 2.3 %select_dynamic-update-slice_fusion.4 = bf16[1160,2048]{1,0:T(8,128)(2,1)} fusion(bf16[136,2048]{1,0:T(8,128)(2,1)S(1)} %collective-permute-done, bf16[136,2048]{1,0:T(8,128)(2,1)} %collective-permute-done.1, bf16[136,2048]{1,0:T(8,128)(2,1)} %collective-permute-done.2, bf16[136,2048]{1,0:T(8,128)(2,1)} %collective-permute-done.3, pred[]{:T(512)S(6)} %eq.79, ...), kind=kLoop, calls=%fused_computation.42 | loop fusion | flops 1114111 | bytes 2785284
  52.6 15.4 %collective-permute-done.5 = bf16[256,2048]{1,0:T(8,128)(2,1)S(1)} collective-permute-done((bf16[256,2048]{1,0:T(8,128)(2,1)S(1)}, bf16[256,2048]{1,0:T(8,128)(2,1)S(1)}, u32[]{:S(2)}, u32[]{:S(2)}) %collective-permute-start.5) | collective-permute-done | bytes 1048608 | tf_op jit(solution)/shard_map/ppermute | solution.py:42
  68.0 1.8 %select_dynamic-update-slice_fusion.3 = bf16[1160,2048]{1,0:T(8,128)(2,1)} fusion(bf16[1160,2048]{1,0:T(8,128)(2,1)} %select_dynamic-update-slice_fusion.4, bf16[256,2048]{1,0:T(8,128)(2,1)S(1)} %collective-permute-done.4, bf16[256,2048]{1,0:T(8,128)(2,1)S(1)} %collective-permute-done.5, bf16[256,2048]{1,0:T(8,128)(2,1)S(1)} %collective-permute-done.6, ...), kind=kLoop, calls=%fused_computation.41 | loop fusion | flops 1572864 | bytes 5242883
  69.8 1.8 %select_dynamic-update-slice_fusion.2 = bf16[1160,2048]{1,0:T(8,128)(2,1)} fusion(bf16[1160,2048]{1,0:T(8,128)(2,1)} %select_dynamic-update-slice_fusion.3, bf16[256,2048]{1,0:T(8,128)(2,1)S(1)} %collective-permute-done.4, bf16[256,2048]{1,0:T(8,128)(2,1)S(1)} %collective-permute-done.5, bf16[256,2048]{1,0:T(8,128)(2,1)S(1)} %collective-permute-done.6, ...), kind=kLoop, calls=%fused_computation.40 | loop fusion | flops 1572864 | bytes 5242883
  71.5 1.8 %select_dynamic-update-slice_fusion.1 = bf16[1160,2048]{1,0:T(8,128)(2,1)} fusion(bf16[1160,2048]{1,0:T(8,128)(2,1)} %select_dynamic-update-slice_fusion.2, bf16[256,2048]{1,0:T(8,128)(2,1)S(1)} %collective-permute-done.4, bf16[256,2048]{1,0:T(8,128)(2,1)S(1)} %collective-permute-done.5, bf16[256,2048]{1,0:T(8,128)(2,1)S(1)} %collective-permute-done.6, ...), kind=kLoop, calls=%fused_computation.39 | loop fusion | flops 1572864 | bytes 5242883
  73.3 1.7 %select_dynamic-update-slice_fusion = bf16[1160,2048]{1,0:T(8,128)(2,1)} fusion(bf16[1160,2048]{1,0:T(8,128)(2,1)} %select_dynamic-update-slice_fusion.1, bf16[256,2048]{1,0:T(8,128)(2,1)S(1)} %collective-permute-done.4, bf16[256,2048]{1,0:T(8,128)(2,1)S(1)} %collective-permute-done.5, bf16[256,2048]{1,0:T(8,128)(2,1)S(1)} %collective-permute-done.6, ...), kind=kLoop, calls=%fused_computation.38 | loop fusion | flops 1572864 | bytes 5242883 | tf_op jit(solution)/shard_map/concatenate | solution.py:56
  75.0 6.3 %all-gather.2.cloned.1.call-done = bf16[48,32,2048]{2,1,0:T(8,128)(2,1)} async-done(((bf16[3,32,2048]{2,1,0:T(8,128)(2,1)}), bf16[48,32,2048]{2,1,0:T(8,128)(2,1)}) %all-gather.2.cloned.1.call-update) | async-done | bytes 6291472 | tf_op jit(solution)/shard_map/all_gather | solution.py:67
  81.3 11.2 %convolution_convert_fusion = bf16[1160,1536]{1,0:T(8,128)(2,1)S(1)} fusion(bf16[1160,2048]{1,0:T(8,128)(2,1)} %select_dynamic-update-slice_fusion, bf16[1536,2048]{1,0:T(8,128)(2,1)} %bitcast.85), kind=kOutput, calls=%fused_computation.11 | convolution fusion | flops 7299870720 | bytes 14606336 | tf_op jit(solution)/shard_map/dot_general | solution.py:78
  92.5 10.7 %multiply_add_fusion = f32[1152,1536]{1,0:T(8,128)S(1)} fusion(bf16[1160,1536]{1,0:T(8,128)(2,1)S(1)} %convolution_convert_fusion, f32[1536]{0:T(1024)S(1)} %mul.115, f32[1536]{0:T(1024)S(1)} %mul.112, f32[1536]{0:T(1024)S(1)} %mul.109, f32[1536]{0:T(1024)S(1)} %mul.106, f32[1536]{0:T(1024)S(1)} %mul.103, f32[1536]{0:T(1024)S(1)} %mul.100, ...), kind=kLoop, calls=%fused_computation.12 | loop fusion | flops 47775744 | bytes 31901568 | tf_op jit(solution)/shard_map/add | solution.py:91
  103.6 1.6 %fusion.34 = (bf16[1024,512]{1,0:T(8,128)(2,1)S(1)}, bf16[1024,512]{1,0:T(8,128)(2,1)}) fusion(bf16[1152,512]{1,0:T(8,128)(2,1)S(1)} %fusion.15), kind=kLoop, calls=%fused_computation.80 | loop fusion | bytes 4194304 | tf_op jit(solution)/shard_map/slice | solution.py:120
  106.4 1.5 copy.33
  110.3 6.1 %fusion = f32[8,32,16,128]{3,2,1,0:T(8,128)S(1)} fusion(pred[8,128,128]{2,1,0:T(8,128)(4,1)S(1)} %copy-done.3, bf16[32,128,128]{2,1,0:T(8,128)(2,1)} %copy.34, bf16[8,128,32,16]{1,0,3,2:T(8,128)(2,1)} %bitcast.78), kind=kOutput, calls=%fused_computation.1 | convolution fusion | flops 138412032 | bytes 4325376 | tf_op jit(solution)/shard_map/bgij,bjgc->bigc/dot_general | solution.py:122
  116.3 4.5 %add_bitcast_fusion = f32[8,128,32,16]{1,3,2,0:T(8,128)S(1)} fusion(f32[8,32,16,128]{3,2,1,0:T(8,128)S(1)} %fusion, pred[8,128,128]{2,1,0:T(8,128)(4,1)S(1)} %get-tuple-element.33, bf16[32,128,128]{2,1,0:T(8,128)(2,1)S(1)} %copy-done.2, bf16[8,128,32,16]{1,0,3,2:T(8,128)(2,1)S(1)} %bitcast.79), kind=kOutput, calls=%fused_computation.26 | convolution fusion | flops 138936320 | bytes 6422528 | tf_op jit(solution)/shard_map/bgij,bjgc->bigc/dot_general | solution.py:119
  122.1 1.8 %copy.47 = f32[64,8,8,128]{3,1,2,0:T(8,128)} copy(f32[64,8,8,128]{3,2,1,0:T(8,128)S(1)} %bitcast.68) | data formatting | bytes 4194304
  123.9 2.9 %copy.37 = f32[1024,512]{1,0:T(8,128)} copy(f32[1024,512]{0,1:T(8,128)} %bitcast.69) | data formatting | bytes 4194304 | tf_op jit(solution)/shard_map/reshape | solution.py:125
  126.8 2.6 %fusion.16 = bf16[1024,512]{1,0:T(8,128)(2,1)S(1)} fusion(f32[1024,512]{1,0:T(8,128)} %copy.37, f32[1152,1536]{1,0:T(8,128)} %copy-done), kind=kLoop, calls=%fused_computation.25 | loop fusion | flops 1048576 | bytes 5242880 | tf_op jit(solution)/shard_map/convert_element_type | solution.py:126
  131.9 6.1 %collective-permute-done.8 = bf16[256,512]{1,0:T(8,128)(2,1)S(1)} collective-permute-done((bf16[256,512]{1,0:T(8,128)(2,1)S(1)}, bf16[256,512]{1,0:T(8,128)(2,1)S(1)}, u32[]{:S(2)}, u32[]{:S(2)}) %collective-permute-start.8) | collective-permute-done | bytes 262176 | tf_op jit(solution)/shard_map/ppermute | solution.py:132
  138.1 5.8 %collective-permute-done.9 = bf16[256,512]{1,0:T(8,128)(2,1)S(1)} collective-permute-done((bf16[256,512]{1,0:T(8,128)(2,1)S(1)}, bf16[256,512]{1,0:T(8,128)(2,1)S(1)}, u32[]{:S(2)}, u32[]{:S(2)}) %collective-permute-start.9) | collective-permute-done | bytes 262176 | tf_op jit(solution)/shard_map/ppermute | solution.py:132
  143.9 6.7 %fusion.14 = bf16[256,2048]{1,0:T(8,128)(2,1)} fusion(bf16[2048,2048]{1,0:T(8,128)(2,1)} %pad_maximum_fusion, bf16[256,2048]{1,0:T(8,128)(2,1)S(1)} %copy-done.1, bf16[256,512]{1,0:T(8,128)(2,1)S(1)} %collective-permute-done.9, bf16[256,512]{1,0:T(8,128)(2,1)S(1)} %collective-permute-done.8, bf16[256,512]{1,0:T(8,128)(2,1)S(1)} %collective-permute-done.7, ...), kind=kOutput, calls=%fused_computation.20 | convolution fusion | flops 2153250816 | bytes 11534336 | tf_op jit(solution)/shard_map/dot_general | solution.py:134
  (52 shorter events, 14.7 us)
Async XLA Ops:
  6.5 10.7 %copy-start.1 = (bf16[256,2048]{1,0:T(8,128)(2,1)S(1)}, bf16[256,2048]{1,0:T(8,128)(2,1)}, u32[]{:S(2)}) copy-start(bf16[256,2048]{1,0:T(8,128)(2,1)} %param.6) | copy-start | bytes 3145732
  6.5 74.8 %all-gather.2.cloned.1.call-start = ((), (), s32[]{:S(2)}) async-start(), calls=%async_computation | async-start | bytes 6684672 | tf_op jit(solution)/shard_map/all_gather | solution.py:67
  12.1 27.8 %collective-permute-start = (bf16[136,2048]{1,0:T(8,128)(2,1)S(1)}, bf16[136,2048]{1,0:T(8,128)(2,1)S(1)}, u32[]{:S(2)}, u32[]{:S(2)}) collective-permute-start(bf16[136,2048]{1,0:T(8,128)(2,1)S(1)} %slice.81), channel_id=1, source_target_pairs={{3,7},{7,11},{11,15},{19,23},{23,27},{27,31},{35,39},{39,43},{43,4... | collective-permute-start | bytes 1671176 | tf_op jit(solution)/shard_map/ppermute | solution.py:54
  12.8 32.7 %collective-permute-start.1 = (bf16[136,2048]{1,0:T(8,128)(2,1)S(1)}, bf16[136,2048]{1,0:T(8,128)(2,1)}, u32[]{:S(2)}, u32[]{:S(2)}) collective-permute-start(bf16[136,2048]{1,0:T(8,128)(2,1)S(1)} %slice.81), channel_id=1, source_target_pairs={{3,6},{7,10},{11,14},{19,22},{23,26},{27,30},{35,38},{39,42},{43,4... | collective-permute-start | bytes 1671176 | tf_op jit(solution)/shard_map/ppermute | solution.py:54
  14.3 36.0 %collective-permute-start.2 = (bf16[136,2048]{1,0:T(8,128)(2,1)S(1)}, bf16[136,2048]{1,0:T(8,128)(2,1)}, u32[]{:S(2)}, u32[]{:S(2)}) collective-permute-start(bf16[136,2048]{1,0:T(8,128)(2,1)S(1)} %slice.81), channel_id=1, source_target_pairs={{3,5},{7,9},{11,13},{19,21},{23,25},{27,29},{35,37},{39,41},{43,45... | collective-permute-start | bytes 1671176 | tf_op jit(solution)/shard_map/ppermute | solution.py:54
  15.8 34.5 %collective-permute-start.3 = (bf16[136,2048]{1,0:T(8,128)(2,1)S(1)}, bf16[136,2048]{1,0:T(8,128)(2,1)}, u32[]{:S(2)}, u32[]{:S(2)}) collective-permute-start(bf16[136,2048]{1,0:T(8,128)(2,1)S(1)} %slice.81), channel_id=1, source_target_pairs={{3,4},{7,8},{11,12},{19,20},{23,24},{27,28},{35,36},{39,40},{43,44... | collective-permute-start | bytes 1671176 | tf_op jit(solution)/shard_map/ppermute | solution.py:54
  17.2 35.4 %collective-permute-start.4 = (bf16[256,2048]{1,0:T(8,128)(2,1)S(1)}, bf16[256,2048]{1,0:T(8,128)(2,1)S(1)}, u32[]{:S(2)}, u32[]{:S(2)}) collective-permute-start(bf16[256,2048]{1,0:T(8,128)(2,1)S(1)} %copy-done.1), channel_id=1, source_target_pairs={{0,3},{1,2},{2,1},{3,0},{4,7},{5,6},{6,5},{7,4},{8,11},{9,10},{10,... | collective-permute-start | bytes 3145736 | tf_op jit(solution)/shard_map/ppermute | solution.py:42
  21.8 12.6 %copy-start.4 = (s32[1,4]{1,0:T(1,128)S(1)}, s32[1,4]{1,0:T(1,128)}, u32[]{:S(2)}) copy-start(s32[1,4]{1,0:T(1,128)} %param.7) | copy-start | bytes 52
  39.9 28.0 %collective-permute-start.5 = (bf16[256,2048]{1,0:T(8,128)(2,1)S(1)}, bf16[256,2048]{1,0:T(8,128)(2,1)S(1)}, u32[]{:S(2)}, u32[]{:S(2)}) collective-permute-start(bf16[256,2048]{1,0:T(8,128)(2,1)S(1)} %copy-done.1), channel_id=1, source_target_pairs={{0,2},{1,3},{2,0},{3,1},{4,6},{5,7},{6,4},{7,5},{8,10},{9,11},{10,... | collective-permute-start | bytes 3145736 | tf_op jit(solution)/shard_map/ppermute | solution.py:42
  45.5 22.5 %collective-permute-start.6 = (bf16[256,2048]{1,0:T(8,128)(2,1)S(1)}, bf16[256,2048]{1,0:T(8,128)(2,1)S(1)}, u32[]{:S(2)}, u32[]{:S(2)}) collective-permute-start(bf16[256,2048]{1,0:T(8,128)(2,1)S(1)} %copy-done.1), channel_id=1, source_target_pairs={{0,1},{1,0},{2,3},{3,2},{4,5},{5,4},{6,7},{7,6},{8,9},{9,8},{10,11... | collective-permute-start | bytes 3145736 | tf_op jit(solution)/shard_map/ppermute | solution.py:42
  103.2 3.2 %copy-start = (f32[1152,1536]{1,0:T(8,128)}, f32[1152,1536]{1,0:T(8,128)S(1)}, u32[]{:S(2)}) copy-start(f32[1152,1536]{1,0:T(8,128)S(1)} %multiply_add_fusion) | copy-start | bytes 21233668
  106.4 3.8 %copy-start.3 = (pred[8,128,128]{2,1,0:T(8,128)(4,1)S(1)}, pred[8,128,128]{2,1,0:T(8,128)(4,1)}, u32[]{:S(2)}) copy-start(pred[8,128,128]{2,1,0:T(8,128)(4,1)} %get-tuple-element.34) | copy-start | bytes 393220
  110.3 6.1 %copy-start.2 = (bf16[32,128,128]{2,1,0:T(8,128)(2,1)S(1)}, bf16[32,128,128]{2,1,0:T(8,128)(2,1)}, u32[]{:S(2)}) copy-start(bf16[32,128,128]{2,1,0:T(8,128)(2,1)} %copy.31) | copy-start | bytes 3145732
  129.4 2.5 %collective-permute-start.7 = (bf16[256,512]{1,0:T(8,128)(2,1)S(1)}, bf16[256,512]{1,0:T(8,128)(2,1)S(1)}, u32[]{:S(2)}, u32[]{:S(2)}) collective-permute-start(bf16[256,512]{1,0:T(8,128)(2,1)S(1)} %get-tuple-element.18), channel_id=1, source_target_pairs={{0,1},{1,0},{2,3},{3,2},{4,5},{5,4},{6,7},{7,6},{8,9},{9,8},{10,11... | collective-permute-start | bytes 786440 | tf_op jit(solution)/shard_map/ppermute | solution.py:132
  130.2 7.9 %collective-permute-start.8 = (bf16[256,512]{1,0:T(8,128)(2,1)S(1)}, bf16[256,512]{1,0:T(8,128)(2,1)S(1)}, u32[]{:S(2)}, u32[]{:S(2)}) collective-permute-start(bf16[256,512]{1,0:T(8,128)(2,1)S(1)} %get-tuple-element.17), channel_id=1, source_target_pairs={{0,2},{1,3},{2,0},{3,1},{4,6},{5,7},{6,4},{7,5},{8,10},{9,11},{10,... | collective-permute-start | bytes 786440 | tf_op jit(solution)/shard_map/ppermute | solution.py:132
  131.5 12.4 %collective-permute-start.9 = (bf16[256,512]{1,0:T(8,128)(2,1)S(1)}, bf16[256,512]{1,0:T(8,128)(2,1)S(1)}, u32[]{:S(2)}, u32[]{:S(2)}) collective-permute-start(bf16[256,512]{1,0:T(8,128)(2,1)S(1)} %get-tuple-element.16), channel_id=1, source_target_pairs={{0,3},{1,2},{2,1},{3,0},{4,7},{5,6},{6,5},{7,4},{8,11},{9,10},{10,... | collective-permute-start | bytes 786440 | tf_op jit(solution)/shard_map/ppermute | solution.py:132
Sparse Core Ops, SparseCore 0:
  11.1 70.1 all-gather.1

commit v12 on v4

--- a/solution.py
+++ b/solution.py
@@ -127,17 +127,14 @@
     gated = (queries.T * filtered).astype(jnp.bfloat16)
 
 
-    gated = gated.reshape(own, GROUP_DEVS, rows)
+    gated = gated.T.reshape(GROUP_DEVS, rows, own)
     pieces = []
     for d in range(GROUP_DEVS):
-        send = lax.dynamic_index_in_dim(gated, member ^ d, axis=1, keepdims=False)
+        send = lax.dynamic_index_in_dim(gated, member ^ d, axis=0, keepdims=False)
         got = send if d == 0 else lax.ppermute(send, "seq", swaps[d - 1])
         pieces.append(got)
-    result = tokens.astype(jnp.float32) + lax.dot_general(
-        jnp.concatenate(pieces, axis=0),
-        ow_cat,
-        (((0,), (0,)), ((), ())),
-        preferred_element_type=jnp.float32,
+    result = tokens.astype(jnp.float32) + jnp.dot(
+        jnp.concatenate(pieces, axis=1), ow_cat, preferred_element_type=jnp.float32
     )
     return result.astype(jnp.bfloat16)
 

time: 155 us -> 155 us (level)
  no operation moved by 1% of the time
where the time goes in v12:
time: 155 us
  matrix products  36 us (23%)
  waiting for transfers between devices  34.4 us (22%)
  other arithmetic  28.2 us (18%)
  local copies, waits for them, and re-layouts  25.5 us (16%)
  starting transfers between devices  16.9 us (11%)
  between operations  13.6 us (9%)
    ppermute x3, waiting for transfers between devices, local(): lax.ppermute(tokens, 'seq', perm)  15.4 us
    ppermute x3, waiting for transfers between devices, local(): got = send if d == 0 else lax.ppermute(send, 'seq', swaps[d - 1])  11.9 us
    dot_general x1, matrix products, local(): jnp.dot(ext_tokens, w_all.T, preferred_element_type=jnp.float32)  11.2 us
    add x1, other arithmetic, local(): featured + taps[tap_index] * jnp.where((pos_f >= tap_index)[:, None], shi...  10.7 us
    ppermute x3, starting transfers between devices, local(): lax.ppermute(tokens, 'seq', perm)  9.3 us
    unnamed x14, local copies, waits for them, and re-layouts  8.3 us
    dot_general x2, matrix products, tap_table(): jnp.einsum('ijt,tg->gij', one_hot, long_filter, preferred_element_type=jn...  7.92 us
    unnamed x4, other arithmetic  7.38 us
  transfers between devices with their start and end apart: 11, of which 4 were waited for; matrix products, arithmetic and copies ran while one was open for 22% of the time, Pallas kernels for 0%

profile of v12, /device:TPU:1, one launch (start us, length us, event | category | flops | bytes accessed | tf_op | source)
XLA Modules:
  0.0 154.6 jit_solution(15902551098110903809)
XLA Ops:
  6.5 1.8 %copy.26 = bf16[2048,384]{0,1:T(8,128)(2,1)S(1)} copy(bf16[2048,384]{1,0:T(8,128)(2,1)} %param.8) | data formatting | bytes 3145728 | tf_op args[2]
  11.0 1.5 collective-permute-start.1
  12.4 1.5 collective-permute-start.2
  13.9 1.5 collective-permute-start.3
  15.4 3.0 %collective-permute-start.4 = (bf16[256,2048]{1,0:T(8,128)(2,1)S(1)}, bf16[256,2048]{1,0:T(8,128)(2,1)S(1)}, u32[]{:S(2)}, u32[]{:S(2)}) collective-permute-start(bf16[256,2048]{1,0:T(8,128)(2,1)S(1)} %copy-done.1), channel_id=1, source_target_pairs={{0,3},{1,2},{2,1},{3,0},{4,7},{5,6},{6,5},{7,4},{8,11},{9,10},{10,... | collective-permute-start | bytes 3145736 | tf_op jit(solution)/shard_map/ppermute | solution.py:42
  21.8 4.0 %fusion.20 = bf16[32,128,128]{2,0,1:T(8,128)(2,1)S(1)} fusion(bf16[128,32,1]{0,1,2:T(8,128)(2,1)S(1)} %bitcast.77, s32[128,128]{1,0:T(8,128)S(1)} %get-tuple-element.35), kind=kOutput, calls=%fused_computation.28 | convolution fusion | flops 136839168 | bytes 1122304 | tf_op jit(solution)/shard_map/ijt,tg->gij/dot_general | solution.py:22
  25.8 1.4 copy.31
  27.2 3.9 %fusion.21 = bf16[32,128,128]{2,0,1:T(8,128)(2,1)S(1)} fusion(bf16[128,32,1]{0,1,2:T(8,128)(2,1)S(1)} %bitcast.78, s32[128,128]{1,0:T(8,128)S(1)} %get-tuple-element.36), kind=kOutput, calls=%fused_computation.29 | convolution fusion | flops 136839168 | bytes 1122304 | tf_op jit(solution)/shard_map/ijt,tg->gij/dot_general | solution.py:22
  31.1 1.4 copy.28
  33.7 4.4 %constant_dynamic-slice_fusion.11 = (bf16[16,32,2048]{2,1,0:T(8,128)(2,1)S(1)}, bf16[16,32,2048]{2,1,0:T(8,128)(2,1)S(1)}, bf16[16,32,2048]{2,1,0:T(8,128)(2,1)S(1)}, bf16[16,32,2048]{2,1,0:T(8,128)(2,1)S(1)}) fusion(bf16[16,128,2048]{2,1,0:T(8,128)(2,1)} %bitcast.65, s32[]{:T(128)S(6)} %select_n.178, s32[]{:T(128)S(6)} %select_n.215, s32[]{:T(128)S(6)} %select_n.214, ...), kind=kLoop, calls=%fused_computation.73 | loop fusion | bytes 16777232 | tf_op jit(solution)/shard_map/dynamic_slice | solution.py:75
  38.1 5.6 %collective-permute-start.5 = (bf16[256,2048]{1,0:T(8,128)(2,1)S(1)}, bf16[256,2048]{1,0:T(8,128)(2,1)S(1)}, u32[]{:S(2)}, u32[]{:S(2)}) collective-permute-start(bf16[256,2048]{1,0:T(8,128)(2,1)S(1)} %copy-done.1), channel_id=1, source_target_pairs={{0,2},{1,3},{2,0},{3,1},{4,6},{5,7},{6,4},{7,5},{8,10},{9,11},{10,... | collective-permute-start | bytes 3145736 | tf_op jit(solution)/shard_map/ppermute | solution.py:42
  44.4 4.1 %pad_maximum_fusion = bf16[2048,2048]{1,0:T(8,128)(2,1)} fusion(bf16[512,2048]{1,0:T(8,128)(2,1)S(1)} %bitcast.69, bf16[512,2048]{1,0:T(8,128)(2,1)S(1)} %bitcast.70, bf16[512,2048]{1,0:T(8,128)(2,1)S(1)} %bitcast.71, bf16[512,2048]{1,0:T(8,128)(2,1)S(1)} %bitcast.68), kind=kLoop, calls=%fused_computation | loop fusion | flops 33554432 | bytes 16777216 | tf_op jit(solution)/shard_map/concatenate | solution.py:76
  48.5 2.3 %select_dynamic-update-slice_fusion.4 = bf16[1160,2048]{1,0:T(8,128)(2,1)} fusion(bf16[136,2048]{1,0:T(8,128)(2,1)S(1)} %collective-permute-done, bf16[136,2048]{1,0:T(8,128)(2,1)} %collective-permute-done.1, bf16[136,2048]{1,0:T(8,128)(2,1)} %collective-permute-done.2, bf16[136,2048]{1,0:T(8,128)(2,1)} %collective-permute-done.3, pred[]{:T(512)S(6)} %eq.79, ...), kind=kLoop, calls=%fused_computation.44 | loop fusion | flops 1114111 | bytes 2785284
  50.7 15.4 %collective-permute-done.5 = bf16[256,2048]{1,0:T(8,128)(2,1)S(1)} collective-permute-done((bf16[256,2048]{1,0:T(8,128)(2,1)S(1)}, bf16[256,2048]{1,0:T(8,128)(2,1)S(1)}, u32[]{:S(2)}, u32[]{:S(2)}) %collective-permute-start.5) | collective-permute-done | bytes 1048608 | tf_op jit(solution)/shard_map/ppermute | solution.py:42
  66.1 1.7 %select_dynamic-update-slice_fusion.3 = bf16[1160,2048]{1,0:T(8,128)(2,1)} fusion(bf16[1160,2048]{1,0:T(8,128)(2,1)} %select_dynamic-update-slice_fusion.4, bf16[256,2048]{1,0:T(8,128)(2,1)S(1)} %collective-permute-done.4, bf16[256,2048]{1,0:T(8,128)(2,1)S(1)} %collective-permute-done.5, bf16[256,2048]{1,0:T(8,128)(2,1)S(1)} %collective-permute-done.6, ...), kind=kLoop, calls=%fused_computation.43 | loop fusion | flops 1572864 | bytes 5242883
  67.8 1.7 %select_dynamic-update-slice_fusion.2 = bf16[1160,2048]{1,0:T(8,128)(2,1)} fusion(bf16[1160,2048]{1,0:T(8,128)(2,1)} %select_dynamic-update-slice_fusion.3, bf16[256,2048]{1,0:T(8,128)(2,1)S(1)} %collective-permute-done.4, bf16[256,2048]{1,0:T(8,128)(2,1)S(1)} %collective-permute-done.5, bf16[256,2048]{1,0:T(8,128)(2,1)S(1)} %collective-permute-done.6, ...), kind=kLoop, calls=%fused_computation.42 | loop fusion | flops 1572864 | bytes 5242883
  69.5 1.7 %select_dynamic-update-slice_fusion.1 = bf16[1160,2048]{1,0:T(8,128)(2,1)} fusion(bf16[1160,2048]{1,0:T(8,128)(2,1)} %select_dynamic-update-slice_fusion.2, bf16[256,2048]{1,0:T(8,128)(2,1)S(1)} %collective-permute-done.4, bf16[256,2048]{1,0:T(8,128)(2,1)S(1)} %collective-permute-done.5, bf16[256,2048]{1,0:T(8,128)(2,1)S(1)} %collective-permute-done.6, ...), kind=kLoop, calls=%fused_computation.41 | loop fusion | flops 1572864 | bytes 5242883
  71.2 1.7 %select_dynamic-update-slice_fusion = bf16[1160,2048]{1,0:T(8,128)(2,1)} fusion(bf16[1160,2048]{1,0:T(8,128)(2,1)} %select_dynamic-update-slice_fusion.1, bf16[256,2048]{1,0:T(8,128)(2,1)S(1)} %collective-permute-done.4, bf16[256,2048]{1,0:T(8,128)(2,1)S(1)} %collective-permute-done.5, bf16[256,2048]{1,0:T(8,128)(2,1)S(1)} %collective-permute-done.6, ...), kind=kLoop, calls=%fused_computation.40 | loop fusion | flops 1572864 | bytes 5242883 | tf_op jit(solution)/shard_map/concatenate | solution.py:56
  72.9 7.1 %all-gather.2.cloned.1.call-done = bf16[48,32,2048]{2,1,0:T(8,128)(2,1)} async-done(((bf16[3,32,2048]{2,1,0:T(8,128)(2,1)}), bf16[48,32,2048]{2,1,0:T(8,128)(2,1)}) %all-gather.2.cloned.1.call-update) | async-done | bytes 6291472 | tf_op jit(solution)/shard_map/all_gather | solution.py:67
  80.0 11.2 %convolution_convert_fusion = bf16[1160,1536]{1,0:T(8,128)(2,1)S(1)} fusion(bf16[1160,2048]{1,0:T(8,128)(2,1)} %select_dynamic-update-slice_fusion, bf16[1536,2048]{1,0:T(8,128)(2,1)} %bitcast.79), kind=kOutput, calls=%fused_computation.11 | convolution fusion | flops 7299870720 | bytes 14606336 | tf_op jit(solution)/shard_map/dot_general | solution.py:78
  91.2 10.7 %multiply_add_fusion = f32[1152,1536]{1,0:T(8,128)S(1)} fusion(bf16[1160,1536]{1,0:T(8,128)(2,1)S(1)} %convolution_convert_fusion, f32[1536]{0:T(1024)S(1)} %mul.115, f32[1536]{0:T(1024)S(1)} %mul.112, f32[1536]{0:T(1024)S(1)} %mul.109, f32[1536]{0:T(1024)S(1)} %mul.106, f32[1536]{0:T(1024)S(1)} %mul.103, f32[1536]{0:T(1024)S(1)} %mul.100, ...), kind=kLoop, calls=%fused_computation.12 | loop fusion | flops 47775744 | bytes 31901568 | tf_op jit(solution)/shard_map/add | solution.py:91
  101.9 2.9 %copy-done = f32[1152,1536]{1,0:T(8,128)} copy-done((f32[1152,1536]{1,0:T(8,128)}, f32[1152,1536]{1,0:T(8,128)S(1)}, u32[]{:S(2)}) %copy-start) | copy-done | bytes 7077912
  105.2 1.4 copy.29
  106.6 2.7 %reshape.154 = bf16[32,16,9,128]{3,2,1,0:T(8,128)(2,1)S(1)} reshape(bf16[512,1152]{1,0:T(8,128)(2,1)} %copy.29) | data formatting | bytes 2359296 | tf_op jit(solution)/shard_map/reshape | solution.py:119
  109.8 5.8 %fusion = f32[32,8,128,16]{2,3,1,0:T(8,128)S(1)} fusion(pred[8,128,128]{2,1,0:T(8,128)(4,1)S(1)} %copy-done.3, bf16[32,128,128]{2,1,0:T(8,128)(2,1)} %copy.31, bf16[32,16,8,128]{3,2,1,0:T(8,128)(2,1)S(1)} %get-tuple-element.14), kind=kOutput, calls=%fused_computation.1 | convolution fusion | flops 138412032 | bytes 4325376 | tf_op jit(solution)/shard_map/gcbj,bgij->gcbi/dot_general | solution.py:123
  115.6 4.5 %add_bitcast_fusion = f32[32,16,8,128]{3,1,2,0:T(8,128)S(1)} fusion(f32[32,8,128,16]{2,3,1,0:T(8,128)S(1)} %fusion, pred[8,128,128]{2,1,0:T(8,128)(4,1)S(1)} %get-tuple-element.33, bf16[32,128,128]{2,1,0:T(8,128)(2,1)S(1)} %copy-done.2, bf16[32,16,8,128]{3,2,1,0:T(8,128)(2,1)S(1)} %get-tuple-element.13), kind=kOutput, calls=%fused_computation.27 | convolution fusion | flops 138936320 | bytes 6422528 | tf_op jit(solution)/shard_map/gcbj,bgij->gcbi/dot_general | solution.py:120
  121.0 1.8 %copy.44 = f32[64,8,8,128]{3,1,2,0:T(8,128)} copy(f32[64,8,8,128]{3,2,1,0:T(8,128)S(1)} %bitcast.66) | data formatting | bytes 4194304
  122.7 1.9 %copy.34 = f32[512,1024]{0,1:T(8,128)S(1)} copy(f32[512,1024]{1,0:T(8,128)} %bitcast.67) | data formatting | bytes 4194304 | tf_op jit(solution)/shard_map/reshape | solution.py:126
  124.6 1.9 %fusion.17 = bf16[512,1024]{0,1:T(8,128)(2,1)S(1)} fusion(f32[512,1024]{0,1:T(8,128)S(1)} %copy.34, f32[1152,1536]{1,0:T(8,128)} %copy-done), kind=kLoop, calls=%fused_computation.26 | loop fusion | flops 1048576 | bytes 5242880 | tf_op jit(solution)/shard_map/convert_element_type | solution.py:127
  129.2 6.1 %collective-permute-done.8 = bf16[256,512]{1,0:T(8,128)(2,1)S(1)} collective-permute-done((bf16[256,512]{1,0:T(8,128)(2,1)S(1)}, bf16[256,512]{1,0:T(8,128)(2,1)S(1)}, u32[]{:S(2)}, u32[]{:S(2)}) %collective-permute-start.8) | collective-permute-done | bytes 262176 | tf_op jit(solution)/shard_map/ppermute | solution.py:134
  135.3 5.8 %collective-permute-done.9 = bf16[256,512]{1,0:T(8,128)(2,1)S(1)} collective-permute-done((bf16[256,512]{1,0:T(8,128)(2,1)S(1)}, bf16[256,512]{1,0:T(8,128)(2,1)S(1)}, u32[]{:S(2)}, u32[]{:S(2)}) %collective-permute-start.9) | collective-permute-done | bytes 262176 | tf_op jit(solution)/shard_map/ppermute | solution.py:134
  141.1 6.7 %fusion.14 = bf16[256,2048]{1,0:T(8,128)(2,1)} fusion(bf16[2048,2048]{1,0:T(8,128)(2,1)} %pad_maximum_fusion, bf16[256,2048]{1,0:T(8,128)(2,1)S(1)} %copy-done.1, bf16[256,512]{1,0:T(8,128)(2,1)S(1)} %collective-permute-done.9, bf16[256,512]{1,0:T(8,128)(2,1)S(1)} %collective-permute-done.8, bf16[256,512]{1,0:T(8,128)(2,1)S(1)} %collective-permute-done.7, ...), kind=kOutput, calls=%fused_computation.20 | convolution fusion | flops 2153250816 | bytes 11534336 | tf_op jit(solution)/shard_map/dot_general | solution.py:136
  (50 shorter events, 12.1 us)
Async XLA Ops:
  6.5 8.8 %copy-start.1 = (bf16[256,2048]{1,0:T(8,128)(2,1)S(1)}, bf16[256,2048]{1,0:T(8,128)(2,1)}, u32[]{:S(2)}) copy-start(bf16[256,2048]{1,0:T(8,128)(2,1)} %param.6) | copy-start | bytes 3145732
  6.5 73.5 %all-gather.2.cloned.1.call-start = ((), (), s32[]{:S(2)}) async-start(), calls=%async_computation | async-start | bytes 6684672 | tf_op jit(solution)/shard_map/all_gather | solution.py:67
  10.3 27.8 %collective-permute-start = (bf16[136,2048]{1,0:T(8,128)(2,1)S(1)}, bf16[136,2048]{1,0:T(8,128)(2,1)S(1)}, u32[]{:S(2)}, u32[]{:S(2)}) collective-permute-start(bf16[136,2048]{1,0:T(8,128)(2,1)S(1)} %slice.75), channel_id=1, source_target_pairs={{3,7},{7,11},{11,15},{19,23},{23,27},{27,31},{35,39},{39,43},{43,4... | collective-permute-start | bytes 1671176 | tf_op jit(solution)/shard_map/ppermute | solution.py:54
  11.0 32.7 %collective-permute-start.1 = (bf16[136,2048]{1,0:T(8,128)(2,1)S(1)}, bf16[136,2048]{1,0:T(8,128)(2,1)}, u32[]{:S(2)}, u32[]{:S(2)}) collective-permute-start(bf16[136,2048]{1,0:T(8,128)(2,1)S(1)} %slice.75), channel_id=1, source_target_pairs={{3,6},{7,10},{11,14},{19,22},{23,26},{27,30},{35,38},{39,42},{43,4... | collective-permute-start | bytes 1671176 | tf_op jit(solution)/shard_map/ppermute | solution.py:54
  12.4 36.0 %collective-permute-start.2 = (bf16[136,2048]{1,0:T(8,128)(2,1)S(1)}, bf16[136,2048]{1,0:T(8,128)(2,1)}, u32[]{:S(2)}, u32[]{:S(2)}) collective-permute-start(bf16[136,2048]{1,0:T(8,128)(2,1)S(1)} %slice.75), channel_id=1, source_target_pairs={{3,5},{7,9},{11,13},{19,21},{23,25},{27,29},{35,37},{39,41},{43,45... | collective-permute-start | bytes 1671176 | tf_op jit(solution)/shard_map/ppermute | solution.py:54
  13.9 34.5 %collective-permute-start.3 = (bf16[136,2048]{1,0:T(8,128)(2,1)S(1)}, bf16[136,2048]{1,0:T(8,128)(2,1)}, u32[]{:S(2)}, u32[]{:S(2)}) collective-permute-start(bf16[136,2048]{1,0:T(8,128)(2,1)S(1)} %slice.75), channel_id=1, source_target_pairs={{3,4},{7,8},{11,12},{19,20},{23,24},{27,28},{35,36},{39,40},{43,44... | collective-permute-start | bytes 1671176 | tf_op jit(solution)/shard_map/ppermute | solution.py:54
  15.4 35.4 %collective-permute-start.4 = (bf16[256,2048]{1,0:T(8,128)(2,1)S(1)}, bf16[256,2048]{1,0:T(8,128)(2,1)S(1)}, u32[]{:S(2)}, u32[]{:S(2)}) collective-permute-start(bf16[256,2048]{1,0:T(8,128)(2,1)S(1)} %copy-done.1), channel_id=1, source_target_pairs={{0,3},{1,2},{2,1},{3,0},{4,7},{5,6},{6,5},{7,4},{8,11},{9,10},{10,... | collective-permute-start | bytes 3145736 | tf_op jit(solution)/shard_map/ppermute | solution.py:42
  19.9 12.6 %copy-start.4 = (s32[1,4]{1,0:T(1,128)S(1)}, s32[1,4]{1,0:T(1,128)}, u32[]{:S(2)}) copy-start(s32[1,4]{1,0:T(1,128)} %param.7) | copy-start | bytes 52
  38.1 28.0 %collective-permute-start.5 = (bf16[256,2048]{1,0:T(8,128)(2,1)S(1)}, bf16[256,2048]{1,0:T(8,128)(2,1)S(1)}, u32[]{:S(2)}, u32[]{:S(2)}) collective-permute-start(bf16[256,2048]{1,0:T(8,128)(2,1)S(1)} %copy-done.1), channel_id=1, source_target_pairs={{0,2},{1,3},{2,0},{3,1},{4,6},{5,7},{6,4},{7,5},{8,10},{9,11},{10,... | collective-permute-start | bytes 3145736 | tf_op jit(solution)/shard_map/ppermute | solution.py:42
  43.7 22.5 %collective-permute-start.6 = (bf16[256,2048]{1,0:T(8,128)(2,1)S(1)}, bf16[256,2048]{1,0:T(8,128)(2,1)S(1)}, u32[]{:S(2)}, u32[]{:S(2)}) collective-permute-start(bf16[256,2048]{1,0:T(8,128)(2,1)S(1)} %copy-done.1), channel_id=1, source_target_pairs={{0,1},{1,0},{2,3},{3,2},{4,5},{5,4},{6,7},{7,6},{8,9},{9,8},{10,11... | collective-permute-start | bytes 3145736 | tf_op jit(solution)/shard_map/ppermute | solution.py:42
  101.9 2.9 %copy-start = (f32[1152,1536]{1,0:T(8,128)}, f32[1152,1536]{1,0:T(8,128)S(1)}, u32[]{:S(2)}) copy-start(f32[1152,1536]{1,0:T(8,128)S(1)} %multiply_add_fusion) | copy-start | bytes 21233668
  105.2 4.6 %copy-start.3 = (pred[8,128,128]{2,1,0:T(8,128)(4,1)S(1)}, pred[8,128,128]{2,1,0:T(8,128)(4,1)}, u32[]{:S(2)}) copy-start(pred[8,128,128]{2,1,0:T(8,128)(4,1)} %get-tuple-element.34) | copy-start | bytes 393220
  109.8 5.8 %copy-start.2 = (bf16[32,128,128]{2,1,0:T(8,128)(2,1)S(1)}, bf16[32,128,128]{2,1,0:T(8,128)(2,1)}, u32[]{:S(2)}) copy-start(bf16[32,128,128]{2,1,0:T(8,128)(2,1)} %copy.28) | copy-start | bytes 3145732
  126.7 2.5 %collective-permute-start.7 = (bf16[256,512]{1,0:T(8,128)(2,1)S(1)}, bf16[256,512]{1,0:T(8,128)(2,1)S(1)}, u32[]{:S(2)}, u32[]{:S(2)}) collective-permute-start(bf16[256,512]{1,0:T(8,128)(2,1)S(1)} %get-tuple-element.18), channel_id=1, source_target_pairs={{0,1},{1,0},{2,3},{3,2},{4,5},{5,4},{6,7},{7,6},{8,9},{9,8},{10,11... | collective-permute-start | bytes 786440 | tf_op jit(solution)/shard_map/ppermute | solution.py:134
  127.4 7.9 %collective-permute-start.8 = (bf16[256,512]{1,0:T(8,128)(2,1)S(1)}, bf16[256,512]{1,0:T(8,128)(2,1)S(1)}, u32[]{:S(2)}, u32[]{:S(2)}) collective-permute-start(bf16[256,512]{1,0:T(8,128)(2,1)S(1)} %get-tuple-element.17), channel_id=1, source_target_pairs={{0,2},{1,3},{2,0},{3,1},{4,6},{5,7},{6,4},{7,5},{8,10},{9,11},{10,... | collective-permute-start | bytes 786440 | tf_op jit(solution)/shard_map/ppermute | solution.py:134
  128.7 12.4 %collective-permute-start.9 = (bf16[256,512]{1,0:T(8,128)(2,1)S(1)}, bf16[256,512]{1,0:T(8,128)(2,1)S(1)}, u32[]{:S(2)}, u32[]{:S(2)}) collective-permute-start(bf16[256,512]{1,0:T(8,128)(2,1)S(1)} %get-tuple-element.16), channel_id=1, source_target_pairs={{0,3},{1,2},{2,1},{3,0},{4,7},{5,6},{6,5},{7,4},{8,11},{9,10},{10,... | collective-permute-start | bytes 786440 | tf_op jit(solution)/shard_map/ppermute | solution.py:134
Sparse Core Ops, SparseCore 0:
  9.8 70.1 all-gather.1

commit v13 on v12

--- a/solution.py
+++ b/solution.py
@@ -128,14 +128,13 @@
 
 
     gated = gated.T.reshape(GROUP_DEVS, rows, own)
-    pieces = []
+    result = tokens.astype(jnp.float32)
     for d in range(GROUP_DEVS):
         send = lax.dynamic_index_in_dim(gated, member ^ d, axis=0, keepdims=False)
         got = send if d == 0 else lax.ppermute(send, "seq", swaps[d - 1])
-        pieces.append(got)
-    result = tokens.astype(jnp.float32) + jnp.dot(
-        jnp.concatenate(pieces, axis=1), ow_cat, preferred_element_type=jnp.float32
-    )
+        result = result + jnp.dot(
+            got, ow_cat[d * own : (d + 1) * own], preferred_element_type=jnp.float32
+        )
     return result.astype(jnp.bfloat16)
 
 

time: 155 us -> 157 us (1.013)
  waiting for transfers between devices: 34.4 us -> 28.3 us
  local copies, waits for them, and re-layouts: 25.5 us -> 29.5 us
  other arithmetic: 28.2 us -> 30.2 us
    ppermute x3, waiting for transfers between devices: 11.9 us -> 6.54 us  [local(): got = send if d == 0 else lax.ppermute(send, 'seq', swaps[d - 1])]
    slice x1, local copies, waits for them, and re-layouts: 0.44 us -> 2.3 us  [local(): mi_t[:, :, 1:]]
    unnamed x14 -> x16, local copies, waits for them, and re-layouts: 8.3 us -> 9.24 us
    dot_general x1 -> x4, matrix products: 6.68 us -> 7.4 us  [local(): jnp.dot(got, ow_cat[d * own:(d + 1) * own], preferred_element_type=jnp.fl...]
    unnamed x4 -> x5, other arithmetic: 7.38 us -> 7.53 us
  transfers between devices with their start and end apart: 11 -> 11, of which waited for: 4 -> 4; matrix products, arithmetic and copies ran while one was open for 22% -> 25% of each run, Pallas kernels for 0% -> 0%
where the time goes in v13:
time: 157 us; the launch traced here: 155 us
  matrix products  36.8 us (23%)
  other arithmetic  30.2 us (19%)
  local copies, waits for them, and re-layouts  29.5 us (19%)
  waiting for transfers between devices  28.3 us (18%)
  starting transfers between devices  16.8 us (11%)
  between operations  13.6 us (9%)
    ppermute x3, waiting for transfers between devices, local(): lax.ppermute(tokens, 'seq', perm)  15.4 us
    dot_general x1, matrix products, local(): jnp.dot(ext_tokens, w_all.T, preferred_element_type=jnp.float32)  11.2 us
    add x1, other arithmetic, local(): featured + taps[tap_index] * jnp.where((pos_f >= tap_index)[:, None], shi...  10.7 us
    ppermute x3, starting transfers between devices, local(): lax.ppermute(tokens, 'seq', perm)  9.3 us
    unnamed x16, local copies, waits for them, and re-layouts  9.24 us
    dot_general x2, matrix products, tap_table(): jnp.einsum('ijt,tg->gij', one_hot, long_filter, preferred_element_type=jn...  7.92 us
    unnamed x5, other arithmetic  7.53 us
    dot_general x4, matrix products, local(): jnp.dot(got, ow_cat[d * own:(d + 1) * own], preferred_element_type=jnp.fl...  7.4 us
  transfers between devices with their start and end apart: 11, of which 4 were waited for; matrix products, arithmetic and copies ran while one was open for 25% of the time, Pallas kernels for 0%

profile of v13, /device:TPU:1, one launch (start us, length us, event | category | flops | bytes accessed | tf_op | source)
XLA Modules:
  0.0 155.2 jit_solution(13304042874522965981)
XLA Ops:
  6.5 2.7 %copy.26 = bf16[2048,384]{0,1:T(8,128)(2,1)} copy(bf16[2048,384]{1,0:T(8,128)(2,1)} %param.8) | data formatting | bytes 3145728 | tf_op args[2]
  9.2 1.8 %constant_dynamic-slice_fusion.7 = bf16[3,32,2048]{2,1,0:T(8,128)(2,1)} fusion(bf16[3,128,2048]{2,1,0:T(8,128)(2,1)} %bitcast.79, s32[]{:T(128)S(6)} %select_n.178), kind=kLoop, calls=%fused_computation.73 | loop fusion | bytes 786436 | tf_op jit(solution)/shard_map/dynamic_slice | solution.py:66
  15.8 1.5 collective-permute-start.3
  17.3 3.0 %collective-permute-start.4 = (bf16[256,2048]{1,0:T(8,128)(2,1)S(1)}, bf16[256,2048]{1,0:T(8,128)(2,1)S(1)}, u32[]{:S(2)}, u32[]{:S(2)}) collective-permute-start(bf16[256,2048]{1,0:T(8,128)(2,1)S(1)} %copy-done), channel_id=1, source_target_pairs={{0,3},{1,2},{2,1},{3,0},{4,7},{5,6},{6,5},{7,4},{8,11},{9,10},{10,... | collective-permute-start | bytes 3145736 | tf_op jit(solution)/shard_map/ppermute | solution.py:42
  23.7 4.0 %fusion.28 = bf16[32,128,128]{2,0,1:T(8,128)(2,1)S(1)} fusion(bf16[128,32,1]{0,1,2:T(8,128)(2,1)S(1)} %bitcast.83, s32[128,128]{1,0:T(8,128)S(1)} %get-tuple-element.34), kind=kOutput, calls=%fused_computation.37 | convolution fusion | flops 136839168 | bytes 1122304 | tf_op jit(solution)/shard_map/ijt,tg->gij/dot_general | solution.py:22
  29.1 3.9 %fusion.29 = bf16[32,128,128]{2,0,1:T(8,128)(2,1)S(1)} fusion(bf16[128,32,1]{0,1,2:T(8,128)(2,1)S(1)} %bitcast.84, s32[128,128]{1,0:T(8,128)S(1)} %get-tuple-element.35), kind=kOutput, calls=%fused_computation.38 | convolution fusion | flops 136839168 | bytes 1122304 | tf_op jit(solution)/shard_map/ijt,tg->gij/dot_general | solution.py:22
  35.6 4.4 %constant_dynamic-slice_fusion.11 = (bf16[16,32,2048]{2,1,0:T(8,128)(2,1)S(1)}, bf16[16,32,2048]{2,1,0:T(8,128)(2,1)S(1)}, bf16[16,32,2048]{2,1,0:T(8,128)(2,1)S(1)}, bf16[16,32,2048]{2,1,0:T(8,128)(2,1)S(1)}) fusion(bf16[16,128,2048]{2,1,0:T(8,128)(2,1)} %bitcast.70, s32[]{:T(128)S(6)} %select_n.178, s32[]{:T(128)S(6)} %select_n.215, s32[]{:T(128)S(6)} %select_n.214, ...), kind=kLoop, calls=%fused_computation.77 | loop fusion | bytes 16777232 | tf_op jit(solution)/shard_map/dynamic_slice | solution.py:75
  40.0 5.6 %collective-permute-start.5 = (bf16[256,2048]{1,0:T(8,128)(2,1)S(1)}, bf16[256,2048]{1,0:T(8,128)(2,1)S(1)}, u32[]{:S(2)}, u32[]{:S(2)}) collective-permute-start(bf16[256,2048]{1,0:T(8,128)(2,1)S(1)} %copy-done), channel_id=1, source_target_pairs={{0,2},{1,3},{2,0},{3,1},{4,6},{5,7},{6,4},{7,5},{8,10},{9,11},{10,... | collective-permute-start | bytes 3145736 | tf_op jit(solution)/shard_map/ppermute | solution.py:42
  46.3 4.1 %pad_maximum_fusion = bf16[2048,2048]{1,0:T(8,128)(2,1)} fusion(bf16[512,2048]{1,0:T(8,128)(2,1)S(1)} %bitcast.74, bf16[512,2048]{1,0:T(8,128)(2,1)S(1)} %bitcast.75, bf16[512,2048]{1,0:T(8,128)(2,1)S(1)} %bitcast.76, bf16[512,2048]{1,0:T(8,128)(2,1)S(1)} %bitcast.73), kind=kLoop, calls=%fused_computation | loop fusion | flops 33554432 | bytes 16777216 | tf_op jit(solution)/shard_map/concatenate | solution.py:76
  50.4 2.3 %select_dynamic-update-slice_fusion.4 = bf16[1160,2048]{1,0:T(8,128)(2,1)} fusion(bf16[136,2048]{1,0:T(8,128)(2,1)S(1)} %collective-permute-done, bf16[136,2048]{1,0:T(8,128)(2,1)} %collective-permute-done.1, bf16[136,2048]{1,0:T(8,128)(2,1)} %collective-permute-done.2, bf16[136,2048]{1,0:T(8,128)(2,1)} %collective-permute-done.3, pred[]{:T(512)S(6)} %eq.79, ...), kind=kLoop, calls=%fused_computation.46 | loop fusion | flops 1114111 | bytes 2785284
  52.6 15.4 %collective-permute-done.5 = bf16[256,2048]{1,0:T(8,128)(2,1)S(1)} collective-permute-done((bf16[256,2048]{1,0:T(8,128)(2,1)S(1)}, bf16[256,2048]{1,0:T(8,128)(2,1)S(1)}, u32[]{:S(2)}, u32[]{:S(2)}) %collective-permute-start.5) | collective-permute-done | bytes 1048608 | tf_op jit(solution)/shard_map/ppermute | solution.py:42
  68.1 1.8 %select_dynamic-update-slice_fusion.3 = bf16[1160,2048]{1,0:T(8,128)(2,1)} fusion(bf16[1160,2048]{1,0:T(8,128)(2,1)} %select_dynamic-update-slice_fusion.4, bf16[256,2048]{1,0:T(8,128)(2,1)S(1)} %collective-permute-done.4, bf16[256,2048]{1,0:T(8,128)(2,1)S(1)} %collective-permute-done.5, bf16[256,2048]{1,0:T(8,128)(2,1)S(1)} %collective-permute-done.6, ...), kind=kLoop, calls=%fused_computation.45 | loop fusion | flops 1572864 | bytes 5242883
  69.8 1.7 %select_dynamic-update-slice_fusion.2 = bf16[1160,2048]{1,0:T(8,128)(2,1)} fusion(bf16[1160,2048]{1,0:T(8,128)(2,1)} %select_dynamic-update-slice_fusion.3, bf16[256,2048]{1,0:T(8,128)(2,1)S(1)} %collective-permute-done.4, bf16[256,2048]{1,0:T(8,128)(2,1)S(1)} %collective-permute-done.5, bf16[256,2048]{1,0:T(8,128)(2,1)S(1)} %collective-permute-done.6, ...), kind=kLoop, calls=%fused_computation.44 | loop fusion | flops 1572864 | bytes 5242883
  71.6 1.8 %select_dynamic-update-slice_fusion.1 = bf16[1160,2048]{1,0:T(8,128)(2,1)} fusion(bf16[1160,2048]{1,0:T(8,128)(2,1)} %select_dynamic-update-slice_fusion.2, bf16[256,2048]{1,0:T(8,128)(2,1)S(1)} %collective-permute-done.4, bf16[256,2048]{1,0:T(8,128)(2,1)S(1)} %collective-permute-done.5, bf16[256,2048]{1,0:T(8,128)(2,1)S(1)} %collective-permute-done.6, ...), kind=kLoop, calls=%fused_computation.43 | loop fusion | flops 1572864 | bytes 5242883
  73.3 1.7 %select_dynamic-update-slice_fusion = bf16[1160,2048]{1,0:T(8,128)(2,1)} fusion(bf16[1160,2048]{1,0:T(8,128)(2,1)} %select_dynamic-update-slice_fusion.1, bf16[256,2048]{1,0:T(8,128)(2,1)S(1)} %collective-permute-done.4, bf16[256,2048]{1,0:T(8,128)(2,1)S(1)} %collective-permute-done.5, bf16[256,2048]{1,0:T(8,128)(2,1)S(1)} %collective-permute-done.6, ...), kind=kLoop, calls=%fused_computation.42 | loop fusion | flops 1572864 | bytes 5242883 | tf_op jit(solution)/shard_map/concatenate | solution.py:56
  75.1 6.3 %all-gather.2.cloned.1.call-done = bf16[48,32,2048]{2,1,0:T(8,128)(2,1)} async-done(((bf16[3,32,2048]{2,1,0:T(8,128)(2,1)}), bf16[48,32,2048]{2,1,0:T(8,128)(2,1)}) %all-gather.2.cloned.1.call-update) | async-done | bytes 6291472 | tf_op jit(solution)/shard_map/all_gather | solution.py:67
  81.4 11.2 %convolution_convert_fusion = bf16[1160,1536]{1,0:T(8,128)(2,1)S(1)} fusion(bf16[1160,2048]{1,0:T(8,128)(2,1)} %select_dynamic-update-slice_fusion, bf16[1536,2048]{1,0:T(8,128)(2,1)} %bitcast.85), kind=kOutput, calls=%fused_computation.11 | convolution fusion | flops 7299870720 | bytes 14606336 | tf_op jit(solution)/shard_map/dot_general | solution.py:78
  92.5 10.7 %multiply_add_fusion = f32[1152,1536]{1,0:T(8,128)S(1)} fusion(bf16[1160,1536]{1,0:T(8,128)(2,1)S(1)} %convolution_convert_fusion, f32[1536]{0:T(1024)S(1)} %mul.115, f32[1536]{0:T(1024)S(1)} %mul.112, f32[1536]{0:T(1024)S(1)} %mul.109, f32[1536]{0:T(1024)S(1)} %mul.106, f32[1536]{0:T(1024)S(1)} %mul.103, f32[1536]{0:T(1024)S(1)} %mul.100, ...), kind=kLoop, calls=%fused_computation.12 | loop fusion | flops 47775744 | bytes 31901568 | tf_op jit(solution)/shard_map/add | solution.py:91
  103.2 2.9 %copy-done.1 = f32[1152,1536]{1,0:T(8,128)} copy-done((f32[1152,1536]{1,0:T(8,128)}, f32[1152,1536]{1,0:T(8,128)S(1)}, u32[]{:S(2)}) %copy-start.1) | copy-done | bytes 7077912
  107.6 1.7 %copy.29 = bf16[512,1152]{1,0:T(8,128)(2,1)S(1)} copy(bf16[512,1152]{0,1:T(8,128)(2,1)} %fusion.30) | data formatting | bytes 2359296 | tf_op jit(solution)/shard_map/transpose | solution.py:119
  109.2 1.7 %reshape.154 = bf16[32,16,9,128]{3,2,1,0:T(8,128)(2,1)} reshape(bf16[512,1152]{1,0:T(8,128)(2,1)S(1)} %copy.29) | data formatting | bytes 2359296 | tf_op jit(solution)/shard_map/reshape | solution.py:119
  110.9 2.3 %fusion.39 = (bf16[32,16,8,128]{3,2,1,0:T(8,128)(2,1)S(1)}, bf16[32,16,8,128]{3,2,1,0:T(8,128)(2,1)S(1)}) fusion(bf16[32,16,9,128]{3,2,1,0:T(8,128)(2,1)} %reshape.154), kind=kLoop, calls=%fused_computation.85 | loop fusion | bytes 4194304 | tf_op jit(solution)/shard_map/slice | solution.py:121
  113.2 5.8 %fusion = f32[32,8,128,16]{2,3,1,0:T(8,128)S(1)} fusion(pred[8,128,128]{2,1,0:T(8,128)(4,1)} %get-tuple-element.33, bf16[32,128,128]{2,1,0:T(8,128)(2,1)} %copy.31, bf16[32,16,8,128]{3,2,1,0:T(8,128)(2,1)S(1)} %get-tuple-element.14), kind=kOutput, calls=%fused_computation.1 | convolution fusion | flops 138412032 | bytes 4325376 | tf_op jit(solution)/shard_map/gcbj,bgij->gcbi/dot_general | solution.py:123
  119.1 4.5 %add_bitcast_fusion = f32[32,16,8,128]{3,1,2,0:T(8,128)S(1)} fusion(f32[32,8,128,16]{2,3,1,0:T(8,128)S(1)} %fusion, pred[8,128,128]{2,1,0:T(8,128)(4,1)S(1)} %get-tuple-element.32, bf16[32,128,128]{2,1,0:T(8,128)(2,1)S(1)} %copy-done.2, bf16[32,16,8,128]{3,2,1,0:T(8,128)(2,1)S(1)} %get-tuple-element.13), kind=kOutput, calls=%fused_computation.36 | convolution fusion | flops 138936320 | bytes 6422528 | tf_op jit(solution)/shard_map/gcbj,bgij->gcbi/dot_general | solution.py:120
  124.4 1.8 %copy.44 = f32[64,8,8,128]{3,1,2,0:T(8,128)} copy(f32[64,8,8,128]{3,2,1,0:T(8,128)S(1)} %bitcast.71) | data formatting | bytes 4194304
  126.2 2.9 %copy.34 = f32[512,1024]{0,1:T(8,128)} copy(f32[512,1024]{1,0:T(8,128)} %bitcast.72) | data formatting | bytes 4194304 | tf_op jit(solution)/shard_map/reshape | solution.py:126
  129.1 2.7 %fusion.19 = bf16[512,1024]{0,1:T(8,128)(2,1)S(1)} fusion(f32[512,1024]{0,1:T(8,128)} %copy.34, f32[1152,1536]{1,0:T(8,128)} %copy-done.1), kind=kLoop, calls=%fused_computation.29 | loop fusion | flops 1048576 | bytes 5242880 | tf_op jit(solution)/shard_map/convert_element_type | solution.py:127
  134.3 2.5 %convolution_add_fusion.1 = f32[256,2048]{1,0:T(8,128)S(1)} fusion(bf16[2048,2048]{1,0:T(8,128)(2,1)} %pad_maximum_fusion, bf16[256,2048]{1,0:T(8,128)(2,1)S(1)} %copy-done, bf16[4,256,512]{2,1,0:T(8,128)(2,1)S(1)} %bitcast.78, s32[]{:T(128)S(6)} %select_n.227), kind=kOutput, calls=%fused_computation.21 | convolution fusion | flops 537919488 | bytes 5505028 | tf_op jit(solution)/shard_map/dot_general | solution.py:135
  136.8 2.4 %collective-permute-done.8 = bf16[256,512]{1,0:T(8,128)(2,1)S(1)} collective-permute-done((bf16[256,512]{1,0:T(8,128)(2,1)S(1)}, bf16[256,512]{1,0:T(8,128)(2,1)S(1)}, u32[]{:S(2)}, u32[]{:S(2)}) %collective-permute-start.8) | collective-permute-done | bytes 262176 | tf_op jit(solution)/shard_map/ppermute | solution.py:134
  139.2 2.3 %fusion.22 = f32[256,2048]{1,0:T(8,128)S(1)} fusion(bf16[256,512]{1,0:T(8,128)(2,1)S(1)} %collective-permute-done.8, bf16[2048,2048]{1,0:T(8,128)(2,1)} %pad_maximum_fusion), kind=kOutput, calls=%fused_computation.32 | convolution fusion | flops 536870912 | bytes 4456448 | tf_op jit(solution)/shard_map/dot_general | solution.py:135
  141.5 4.1 %collective-permute-done.9 = bf16[256,512]{1,0:T(8,128)(2,1)S(1)} collective-permute-done((bf16[256,512]{1,0:T(8,128)(2,1)S(1)}, bf16[256,512]{1,0:T(8,128)(2,1)S(1)}, u32[]{:S(2)}, u32[]{:S(2)}) %collective-permute-start.9) | collective-permute-done | bytes 262176 | tf_op jit(solution)/shard_map/ppermute | solution.py:134
  146.4 1.9 %fusion.16 = bf16[256,2048]{1,0:T(8,128)(2,1)} fusion(f32[256,2048]{1,0:T(8,128)S(1)} %fusion.20, f32[256,2048]{1,0:T(8,128)S(1)} %fusion.22, f32[256,2048]{1,0:T(8,128)S(1)} %convolution_add_fusion.1, bf16[256,512]{1,0:T(8,128)(2,1)S(1)} %collective-permute-done.7, bf16[2048,2048]{1,0:T(8,128)(2,1)S(1)} %bitcast.69), kind=kOutput, calls=%fused_computation.23 | convolution fusion | flops 538968064 | bytes 9699328 | tf_op jit(solution)/shard_map/dot_general | solution.py:135
  (56 shorter events, 18.2 us)
Async XLA Ops:
  6.5 10.7 %copy-start = (bf16[256,2048]{1,0:T(8,128)(2,1)S(1)}, bf16[256,2048]{1,0:T(8,128)(2,1)}, u32[]{:S(2)}) copy-start(bf16[256,2048]{1,0:T(8,128)(2,1)} %param.6) | copy-start | bytes 3145732
  6.5 74.8 %all-gather.2.cloned.1.call-start = ((), (), s32[]{:S(2)}) async-start(), calls=%async_computation | async-start | bytes 6684672 | tf_op jit(solution)/shard_map/all_gather | solution.py:67
  12.1 27.9 %collective-permute-start = (bf16[136,2048]{1,0:T(8,128)(2,1)S(1)}, bf16[136,2048]{1,0:T(8,128)(2,1)S(1)}, u32[]{:S(2)}, u32[]{:S(2)}) collective-permute-start(bf16[136,2048]{1,0:T(8,128)(2,1)S(1)} %slice.87), channel_id=1, source_target_pairs={{3,7},{7,11},{11,15},{19,23},{23,27},{27,31},{35,39},{39,43},{43,4... | collective-permute-start | bytes 1671176 | tf_op jit(solution)/shard_map/ppermute | solution.py:54
  12.8 32.8 %collective-permute-start.1 = (bf16[136,2048]{1,0:T(8,128)(2,1)S(1)}, bf16[136,2048]{1,0:T(8,128)(2,1)}, u32[]{:S(2)}, u32[]{:S(2)}) collective-permute-start(bf16[136,2048]{1,0:T(8,128)(2,1)S(1)} %slice.87), channel_id=1, source_target_pairs={{3,6},{7,10},{11,14},{19,22},{23,26},{27,30},{35,38},{39,42},{43,4... | collective-permute-start | bytes 1671176 | tf_op jit(solution)/shard_map/ppermute | solution.py:54
  14.3 36.1 %collective-permute-start.2 = (bf16[136,2048]{1,0:T(8,128)(2,1)S(1)}, bf16[136,2048]{1,0:T(8,128)(2,1)}, u32[]{:S(2)}, u32[]{:S(2)}) collective-permute-start(bf16[136,2048]{1,0:T(8,128)(2,1)S(1)} %slice.87), channel_id=1, source_target_pairs={{3,5},{7,9},{11,13},{19,21},{23,25},{27,29},{35,37},{39,41},{43,45... | collective-permute-start | bytes 1671176 | tf_op jit(solution)/shard_map/ppermute | solution.py:54
  15.8 34.6 %collective-permute-start.3 = (bf16[136,2048]{1,0:T(8,128)(2,1)S(1)}, bf16[136,2048]{1,0:T(8,128)(2,1)}, u32[]{:S(2)}, u32[]{:S(2)}) collective-permute-start(bf16[136,2048]{1,0:T(8,128)(2,1)S(1)} %slice.87), channel_id=1, source_target_pairs={{3,4},{7,8},{11,12},{19,20},{23,24},{27,28},{35,36},{39,40},{43,44... | collective-permute-start | bytes 1671176 | tf_op jit(solution)/shard_map/ppermute | solution.py:54
  17.3 35.4 %collective-permute-start.4 = (bf16[256,2048]{1,0:T(8,128)(2,1)S(1)}, bf16[256,2048]{1,0:T(8,128)(2,1)S(1)}, u32[]{:S(2)}, u32[]{:S(2)}) collective-permute-start(bf16[256,2048]{1,0:T(8,128)(2,1)S(1)} %copy-done), channel_id=1, source_target_pairs={{0,3},{1,2},{2,1},{3,0},{4,7},{5,6},{6,5},{7,4},{8,11},{9,10},{10,... | collective-permute-start | bytes 3145736 | tf_op jit(solution)/shard_map/ppermute | solution.py:42
  21.8 12.6 %copy-start.3 = (s32[1,4]{1,0:T(1,128)S(1)}, s32[1,4]{1,0:T(1,128)}, u32[]{:S(2)}) copy-start(s32[1,4]{1,0:T(1,128)} %param.7) | copy-start | bytes 52
  40.0 28.1 %collective-permute-start.5 = (bf16[256,2048]{1,0:T(8,128)(2,1)S(1)}, bf16[256,2048]{1,0:T(8,128)(2,1)S(1)}, u32[]{:S(2)}, u32[]{:S(2)}) collective-permute-start(bf16[256,2048]{1,0:T(8,128)(2,1)S(1)} %copy-done), channel_id=1, source_target_pairs={{0,2},{1,3},{2,0},{3,1},{4,6},{5,7},{6,4},{7,5},{8,10},{9,11},{10,... | collective-permute-start | bytes 3145736 | tf_op jit(solution)/shard_map/ppermute | solution.py:42
  45.6 22.5 %collective-permute-start.6 = (bf16[256,2048]{1,0:T(8,128)(2,1)S(1)}, bf16[256,2048]{1,0:T(8,128)(2,1)S(1)}, u32[]{:S(2)}, u32[]{:S(2)}) collective-permute-start(bf16[256,2048]{1,0:T(8,128)(2,1)S(1)} %copy-done), channel_id=1, source_target_pairs={{0,1},{1,0},{2,3},{3,2},{4,5},{5,4},{6,7},{7,6},{8,9},{9,8},{10,11... | collective-permute-start | bytes 3145736 | tf_op jit(solution)/shard_map/ppermute | solution.py:42
  103.2 2.9 %copy-start.1 = (f32[1152,1536]{1,0:T(8,128)}, f32[1152,1536]{1,0:T(8,128)S(1)}, u32[]{:S(2)}) copy-start(f32[1152,1536]{1,0:T(8,128)S(1)} %multiply_add_fusion) | copy-start | bytes 21233668
  113.2 5.8 %copy-start.2 = (bf16[32,128,128]{2,1,0:T(8,128)(2,1)S(1)}, bf16[32,128,128]{2,1,0:T(8,128)(2,1)}, u32[]{:S(2)}) copy-start(bf16[32,128,128]{2,1,0:T(8,128)(2,1)} %copy.28) | copy-start | bytes 3145732
  129.1 16.6 %slice-start = ((s8[8388608]{0:T(1024)(128)(4,1)}), s8[4194304]{0:T(1024)(128)(4,1)S(1)}, s32[]{:S(2)}) async-start(s8[8388608]{0:T(1024)(128)(4,1)} %bitcast.68), calls=%async_computation.1 | async-start | bytes 8388608
  131.9 7.3 %collective-permute-start.8 = (bf16[256,512]{1,0:T(8,128)(2,1)S(1)}, bf16[256,512]{1,0:T(8,128)(2,1)S(1)}, u32[]{:S(2)}, u32[]{:S(2)}) collective-permute-start(bf16[256,512]{1,0:T(8,128)(2,1)S(1)} %get-tuple-element.17), channel_id=1, source_target_pairs={{0,2},{1,3},{2,0},{3,1},{4,6},{5,7},{6,4},{7,5},{8,10},{9,11},{10,... | collective-permute-start | bytes 786440 | tf_op jit(solution)/shard_map/ppermute | solution.py:134
  133.3 12.4 %collective-permute-start.9 = (bf16[256,512]{1,0:T(8,128)(2,1)S(1)}, bf16[256,512]{1,0:T(8,128)(2,1)S(1)}, u32[]{:S(2)}, u32[]{:S(2)}) collective-permute-start(bf16[256,512]{1,0:T(8,128)(2,1)S(1)} %get-tuple-element.16), channel_id=1, source_target_pairs={{0,3},{1,2},{2,1},{3,0},{4,7},{5,6},{6,5},{7,4},{8,11},{9,10},{10,... | collective-permute-start | bytes 786440 | tf_op jit(solution)/shard_map/ppermute | solution.py:134
  134.3 11.3 %slice-start.1 = ((s8[8388608]{0:T(1024)(128)(4,1)}), s8[4194304]{0:T(1024)(128)(4,1)S(1)}, s32[]{:S(2)}) async-start(s8[8388608]{0:T(1024)(128)(4,1)} %bitcast.68), calls=%async_computation.2 | async-start | bytes 8388608
  134.3 12.1 %collective-permute-start.7 = (bf16[256,512]{1,0:T(8,128)(2,1)S(1)}, bf16[256,512]{1,0:T(8,128)(2,1)S(1)}, u32[]{:S(2)}, u32[]{:S(2)}) collective-permute-start(bf16[256,512]{1,0:T(8,128)(2,1)S(1)} %get-tuple-element.15), channel_id=1, source_target_pairs={{0,1},{1,0},{2,3},{3,2},{4,5},{5,4},{6,7},{7,6},{8,9},{9,8},{10,11... | collective-permute-start | bytes 786440 | tf_op jit(solution)/shard_map/ppermute | solution.py:134
Sparse Core Ops, SparseCore 0:
  11.2 70.1 all-gather.1

commit v14 on v12

--- a/solution.py
+++ b/solution.py
@@ -39,7 +39,10 @@
     ext_rows = tail + span
 
     swaps = [[(i, i ^ d) for i in range(n_seq)] for d in range(1, GROUP_DEVS)]
-    from_member = [tokens] + [lax.ppermute(tokens, "seq", perm) for perm in swaps]
+    from_member = [tokens, lax.ppermute(tokens, "seq", swaps[0])]
+    for d in range(2, GROUP_DEVS, 2):
+        fetched = lax.ppermute(tokens, "seq", swaps[d - 1])
+        from_member += [fetched, lax.ppermute(fetched, "seq", swaps[0])]
     blocks = []
     for m in range(GROUP_DEVS):
         pick = from_member[0]

time: 155 us -> 155 us (level)
    all_gather x1, waiting for transfers between devices: 7.07 us -> 22.7 us  [local(): w_all = lax.all_gather(w_part, 'fsdp', axis=0, tiled=True)]
    ppermute x3, waiting for transfers between devices: 15.4 us -> 0.28 us  [the longest x1 0.27 us: local(): fetched = lax.ppermute(tokens, 'seq', swaps[d - 1])]
where the time goes in v14:
time: 155 us
  matrix products  36 us (23%)
  waiting for transfers between devices  34.9 us (23%)
  other arithmetic  28.2 us (18%)
  local copies, waits for them, and re-layouts  25.5 us (16%)
  starting transfers between devices  16.5 us (11%)
  between operations  13.6 us (9%)
    all_gather x1, waiting for transfers between devices, local(): w_all = lax.all_gather(w_part, 'fsdp', axis=0, tiled=True)  22.7 us
    ppermute x3, waiting for transfers between devices, local(): got = send if d == 0 else lax.ppermute(send, 'seq', swaps[d - 1])  11.9 us
    dot_general x1, matrix products, local(): jnp.dot(ext_tokens, w_all.T, preferred_element_type=jnp.float32)  11.2 us
    add x1, other arithmetic, local(): featured + taps[tap_index] * jnp.where((pos_f >= tap_index)[:, None], shi...  10.7 us
    ppermute x1, starting transfers between devices, local(): fetched = lax.ppermute(tokens, 'seq', swaps[d - 1])  8.59 us
    unnamed x14, local copies, waits for them, and re-layouts  8.3 us
    dot_general x2, matrix products, tap_table(): jnp.einsum('ijt,tg->gij', one_hot, long_filter, preferred_element_type=jn...  7.92 us
    unnamed x4, other arithmetic  7.39 us
  transfers between devices with their start and end apart: 11, of which 4 were waited for; matrix products, arithmetic and copies ran while one was open for 22% of the time, Pallas kernels for 0%

profile of v14, /device:TPU:1, one launch (start us, length us, event | category | flops | bytes accessed | tf_op | source)
XLA Modules:
  0.0 154.7 jit_solution(10799367417863991124)
XLA Ops:
  6.5 1.8 %copy.26 = bf16[2048,384]{0,1:T(8,128)(2,1)S(1)} copy(bf16[2048,384]{1,0:T(8,128)(2,1)} %param.8) | data formatting | bytes 3145728 | tf_op args[2]
  9.2 1.1 slice.75
  11.0 1.5 collective-permute-start.1
  12.4 1.5 collective-permute-start.2
  13.9 1.5 collective-permute-start.3
  15.4 8.6 %collective-permute-start.4 = (bf16[256,2048]{1,0:T(8,128)(2,1)S(1)}, bf16[256,2048]{1,0:T(8,128)(2,1)S(1)}, u32[]{:S(2)}, u32[]{:S(2)}) collective-permute-start(bf16[256,2048]{1,0:T(8,128)(2,1)S(1)} %copy-done.1), channel_id=1, source_target_pairs={{0,2},{1,3},{2,0},{3,1},{4,6},{5,7},{6,4},{7,5},{8,10},{9,11},{10,... | collective-permute-start | bytes 3145736 | tf_op jit(solution)/shard_map/ppermute | solution.py:44
  27.4 4.0 %fusion.20 = bf16[32,128,128]{2,0,1:T(8,128)(2,1)S(1)} fusion(bf16[128,32,1]{0,1,2:T(8,128)(2,1)S(1)} %bitcast.77, s32[128,128]{1,0:T(8,128)S(1)} %get-tuple-element.35), kind=kOutput, calls=%fused_computation.28 | convolution fusion | flops 136839168 | bytes 1122304 | tf_op jit(solution)/shard_map/ijt,tg->gij/dot_general | solution.py:22
  31.4 1.4 copy.31
  32.8 3.9 %fusion.21 = bf16[32,128,128]{2,0,1:T(8,128)(2,1)S(1)} fusion(bf16[128,32,1]{0,1,2:T(8,128)(2,1)S(1)} %bitcast.78, s32[128,128]{1,0:T(8,128)S(1)} %get-tuple-element.36), kind=kOutput, calls=%fused_computation.29 | convolution fusion | flops 136839168 | bytes 1122304 | tf_op jit(solution)/shard_map/ijt,tg->gij/dot_general | solution.py:22
  36.7 1.4 copy.28
  39.2 4.3 %constant_dynamic-slice_fusion.11 = (bf16[16,32,2048]{2,1,0:T(8,128)(2,1)S(1)}, bf16[16,32,2048]{2,1,0:T(8,128)(2,1)S(1)}, bf16[16,32,2048]{2,1,0:T(8,128)(2,1)S(1)}, bf16[16,32,2048]{2,1,0:T(8,128)(2,1)S(1)}) fusion(bf16[16,128,2048]{2,1,0:T(8,128)(2,1)} %bitcast.65, s32[]{:T(128)S(6)} %select_n.178, s32[]{:T(128)S(6)} %select_n.215, s32[]{:T(128)S(6)} %select_n.214, ...), kind=kLoop, calls=%fused_computation.73 | loop fusion | bytes 16777232 | tf_op jit(solution)/shard_map/dynamic_slice | solution.py:78
  44.2 4.1 %pad_maximum_fusion = bf16[2048,2048]{1,0:T(8,128)(2,1)} fusion(bf16[512,2048]{1,0:T(8,128)(2,1)S(1)} %bitcast.69, bf16[512,2048]{1,0:T(8,128)(2,1)S(1)} %bitcast.70, bf16[512,2048]{1,0:T(8,128)(2,1)S(1)} %bitcast.71, bf16[512,2048]{1,0:T(8,128)(2,1)S(1)} %bitcast.68), kind=kLoop, calls=%fused_computation | loop fusion | flops 33554432 | bytes 16777216 | tf_op jit(solution)/shard_map/concatenate | solution.py:79
  48.3 2.3 %select_dynamic-update-slice_fusion.4 = bf16[1160,2048]{1,0:T(8,128)(2,1)} fusion(bf16[136,2048]{1,0:T(8,128)(2,1)S(1)} %collective-permute-done, bf16[136,2048]{1,0:T(8,128)(2,1)} %collective-permute-done.1, bf16[136,2048]{1,0:T(8,128)(2,1)} %collective-permute-done.2, bf16[136,2048]{1,0:T(8,128)(2,1)} %collective-permute-done.3, pred[]{:T(512)S(6)} %eq.79, ...), kind=kLoop, calls=%fused_computation.44 | loop fusion | flops 1114111 | bytes 2785284
  50.6 1.7 %select_dynamic-update-slice_fusion.3 = bf16[1160,2048]{1,0:T(8,128)(2,1)} fusion(bf16[1160,2048]{1,0:T(8,128)(2,1)} %select_dynamic-update-slice_fusion.4, bf16[256,2048]{1,0:T(8,128)(2,1)S(1)} %collective-permute-done.5, bf16[256,2048]{1,0:T(8,128)(2,1)S(1)} %collective-permute-done.4, bf16[256,2048]{1,0:T(8,128)(2,1)S(1)} %collective-permute-done.6, ...), kind=kLoop, calls=%fused_computation.43 | loop fusion | flops 1572864 | bytes 5242883
  52.3 1.7 %select_dynamic-update-slice_fusion.2 = bf16[1160,2048]{1,0:T(8,128)(2,1)} fusion(bf16[1160,2048]{1,0:T(8,128)(2,1)} %select_dynamic-update-slice_fusion.3, bf16[256,2048]{1,0:T(8,128)(2,1)S(1)} %collective-permute-done.5, bf16[256,2048]{1,0:T(8,128)(2,1)S(1)} %collective-permute-done.4, bf16[256,2048]{1,0:T(8,128)(2,1)S(1)} %collective-permute-done.6, ...), kind=kLoop, calls=%fused_computation.42 | loop fusion | flops 1572864 | bytes 5242883
  54.0 1.7 %select_dynamic-update-slice_fusion.1 = bf16[1160,2048]{1,0:T(8,128)(2,1)} fusion(bf16[1160,2048]{1,0:T(8,128)(2,1)} %select_dynamic-update-slice_fusion.2, bf16[256,2048]{1,0:T(8,128)(2,1)S(1)} %collective-permute-done.5, bf16[256,2048]{1,0:T(8,128)(2,1)S(1)} %collective-permute-done.4, bf16[256,2048]{1,0:T(8,128)(2,1)S(1)} %collective-permute-done.6, ...), kind=kLoop, calls=%fused_computation.41 | loop fusion | flops 1572864 | bytes 5242883
  55.7 1.7 %select_dynamic-update-slice_fusion = bf16[1160,2048]{1,0:T(8,128)(2,1)} fusion(bf16[1160,2048]{1,0:T(8,128)(2,1)} %select_dynamic-update-slice_fusion.1, bf16[256,2048]{1,0:T(8,128)(2,1)S(1)} %collective-permute-done.5, bf16[256,2048]{1,0:T(8,128)(2,1)S(1)} %collective-permute-done.4, bf16[256,2048]{1,0:T(8,128)(2,1)S(1)} %collective-permute-done.6, ...), kind=kLoop, calls=%fused_computation.40 | loop fusion | flops 1572864 | bytes 5242883 | tf_op jit(solution)/shard_map/concatenate | solution.py:59
  57.4 22.7 %all-gather.2.cloned.1.call-done = bf16[48,32,2048]{2,1,0:T(8,128)(2,1)} async-done(((bf16[3,32,2048]{2,1,0:T(8,128)(2,1)}), bf16[48,32,2048]{2,1,0:T(8,128)(2,1)}) %all-gather.2.cloned.1.call-update) | async-done | bytes 6291472 | tf_op jit(solution)/shard_map/all_gather | solution.py:70
  80.1 11.2 %convolution_convert_fusion = bf16[1160,1536]{1,0:T(8,128)(2,1)S(1)} fusion(bf16[1160,2048]{1,0:T(8,128)(2,1)} %select_dynamic-update-slice_fusion, bf16[1536,2048]{1,0:T(8,128)(2,1)} %bitcast.79), kind=kOutput, calls=%fused_computation.11 | convolution fusion | flops 7299870720 | bytes 14606336 | tf_op jit(solution)/shard_map/dot_general | solution.py:81
  91.2 10.7 %multiply_add_fusion = f32[1152,1536]{1,0:T(8,128)S(1)} fusion(bf16[1160,1536]{1,0:T(8,128)(2,1)S(1)} %convolution_convert_fusion, f32[1536]{0:T(1024)S(1)} %mul.115, f32[1536]{0:T(1024)S(1)} %mul.112, f32[1536]{0:T(1024)S(1)} %mul.109, f32[1536]{0:T(1024)S(1)} %mul.106, f32[1536]{0:T(1024)S(1)} %mul.103, f32[1536]{0:T(1024)S(1)} %mul.100, ...), kind=kLoop, calls=%fused_computation.12 | loop fusion | flops 47775744 | bytes 31901568 | tf_op jit(solution)/shard_map/add | solution.py:94
  101.9 2.9 %copy-done = f32[1152,1536]{1,0:T(8,128)} copy-done((f32[1152,1536]{1,0:T(8,128)}, f32[1152,1536]{1,0:T(8,128)S(1)}, u32[]{:S(2)}) %copy-start) | copy-done | bytes 7077912
  105.3 1.4 copy.29
  106.7 2.7 %reshape.154 = bf16[32,16,9,128]{3,2,1,0:T(8,128)(2,1)S(1)} reshape(bf16[512,1152]{1,0:T(8,128)(2,1)} %copy.29) | data formatting | bytes 2359296 | tf_op jit(solution)/shard_map/reshape | solution.py:122
  109.9 5.8 %fusion = f32[32,8,128,16]{2,3,1,0:T(8,128)S(1)} fusion(pred[8,128,128]{2,1,0:T(8,128)(4,1)S(1)} %copy-done.3, bf16[32,128,128]{2,1,0:T(8,128)(2,1)} %copy.31, bf16[32,16,8,128]{3,2,1,0:T(8,128)(2,1)S(1)} %get-tuple-element.14), kind=kOutput, calls=%fused_computation.1 | convolution fusion | flops 138412032 | bytes 4325376 | tf_op jit(solution)/shard_map/gcbj,bgij->gcbi/dot_general | solution.py:126
  115.6 4.5 %add_bitcast_fusion = f32[32,16,8,128]{3,1,2,0:T(8,128)S(1)} fusion(f32[32,8,128,16]{2,3,1,0:T(8,128)S(1)} %fusion, pred[8,128,128]{2,1,0:T(8,128)(4,1)S(1)} %get-tuple-element.33, bf16[32,128,128]{2,1,0:T(8,128)(2,1)S(1)} %copy-done.2, bf16[32,16,8,128]{3,2,1,0:T(8,128)(2,1)S(1)} %get-tuple-element.13), kind=kOutput, calls=%fused_computation.27 | convolution fusion | flops 138936320 | bytes 6422528 | tf_op jit(solution)/shard_map/gcbj,bgij->gcbi/dot_general | solution.py:123
  121.0 1.8 %copy.44 = f32[64,8,8,128]{3,1,2,0:T(8,128)} copy(f32[64,8,8,128]{3,2,1,0:T(8,128)S(1)} %bitcast.66) | data formatting | bytes 4194304
  122.8 1.9 %copy.34 = f32[512,1024]{0,1:T(8,128)S(1)} copy(f32[512,1024]{1,0:T(8,128)} %bitcast.67) | data formatting | bytes 4194304 | tf_op jit(solution)/shard_map/reshape | solution.py:129
  124.7 1.9 %fusion.17 = bf16[512,1024]{0,1:T(8,128)(2,1)S(1)} fusion(f32[512,1024]{0,1:T(8,128)S(1)} %copy.34, f32[1152,1536]{1,0:T(8,128)} %copy-done), kind=kLoop, calls=%fused_computation.26 | loop fusion | flops 1048576 | bytes 5242880 | tf_op jit(solution)/shard_map/convert_element_type | solution.py:130
  127.5 1.3 collective-permute-start.8
  129.2 6.1 %collective-permute-done.8 = bf16[256,512]{1,0:T(8,128)(2,1)S(1)} collective-permute-done((bf16[256,512]{1,0:T(8,128)(2,1)S(1)}, bf16[256,512]{1,0:T(8,128)(2,1)S(1)}, u32[]{:S(2)}, u32[]{:S(2)}) %collective-permute-start.8) | collective-permute-done | bytes 262176 | tf_op jit(solution)/shard_map/ppermute | solution.py:137
  135.4 5.8 %collective-permute-done.9 = bf16[256,512]{1,0:T(8,128)(2,1)S(1)} collective-permute-done((bf16[256,512]{1,0:T(8,128)(2,1)S(1)}, bf16[256,512]{1,0:T(8,128)(2,1)S(1)}, u32[]{:S(2)}, u32[]{:S(2)}) %collective-permute-start.9) | collective-permute-done | bytes 262176 | tf_op jit(solution)/shard_map/ppermute | solution.py:137
  141.2 6.7 %fusion.14 = bf16[256,2048]{1,0:T(8,128)(2,1)} fusion(bf16[2048,2048]{1,0:T(8,128)(2,1)} %pad_maximum_fusion, bf16[256,2048]{1,0:T(8,128)(2,1)S(1)} %copy-done.1, bf16[256,512]{1,0:T(8,128)(2,1)S(1)} %collective-permute-done.9, bf16[256,512]{1,0:T(8,128)(2,1)S(1)} %collective-permute-done.8, bf16[256,512]{1,0:T(8,128)(2,1)S(1)} %collective-permute-done.7, ...), kind=kOutput, calls=%fused_computation.20 | convolution fusion | flops 2153250816 | bytes 11534336 | tf_op jit(solution)/shard_map/dot_general | solution.py:139
  (50 shorter events, 9.7 us)
Async XLA Ops:
  6.5 8.8 %copy-start.1 = (bf16[256,2048]{1,0:T(8,128)(2,1)S(1)}, bf16[256,2048]{1,0:T(8,128)(2,1)}, u32[]{:S(2)}) copy-start(bf16[256,2048]{1,0:T(8,128)(2,1)} %param.6) | copy-start | bytes 3145732
  6.5 73.5 %all-gather.2.cloned.1.call-start = ((), (), s32[]{:S(2)}) async-start(), calls=%async_computation | async-start | bytes 6684672 | tf_op jit(solution)/shard_map/all_gather | solution.py:70
  10.3 33.3 %collective-permute-start = (bf16[136,2048]{1,0:T(8,128)(2,1)S(1)}, bf16[136,2048]{1,0:T(8,128)(2,1)S(1)}, u32[]{:S(2)}, u32[]{:S(2)}) collective-permute-start(bf16[136,2048]{1,0:T(8,128)(2,1)S(1)} %slice.75), channel_id=1, source_target_pairs={{3,7},{7,11},{11,15},{19,23},{23,27},{27,31},{35,39},{39,43},{43,4... | collective-permute-start | bytes 1671176 | tf_op jit(solution)/shard_map/ppermute | solution.py:57
  11.0 37.3 %collective-permute-start.1 = (bf16[136,2048]{1,0:T(8,128)(2,1)S(1)}, bf16[136,2048]{1,0:T(8,128)(2,1)}, u32[]{:S(2)}, u32[]{:S(2)}) collective-permute-start(bf16[136,2048]{1,0:T(8,128)(2,1)S(1)} %slice.75), channel_id=1, source_target_pairs={{3,6},{7,10},{11,14},{19,22},{23,26},{27,30},{35,38},{39,42},{43,4... | collective-permute-start | bytes 1671176 | tf_op jit(solution)/shard_map/ppermute | solution.py:57
  12.4 35.8 %collective-permute-start.2 = (bf16[136,2048]{1,0:T(8,128)(2,1)S(1)}, bf16[136,2048]{1,0:T(8,128)(2,1)}, u32[]{:S(2)}, u32[]{:S(2)}) collective-permute-start(bf16[136,2048]{1,0:T(8,128)(2,1)S(1)} %slice.75), channel_id=1, source_target_pairs={{3,5},{7,9},{11,13},{19,21},{23,25},{27,29},{35,37},{39,41},{43,45... | collective-permute-start | bytes 1671176 | tf_op jit(solution)/shard_map/ppermute | solution.py:57
  13.9 34.4 %collective-permute-start.3 = (bf16[136,2048]{1,0:T(8,128)(2,1)S(1)}, bf16[136,2048]{1,0:T(8,128)(2,1)}, u32[]{:S(2)}, u32[]{:S(2)}) collective-permute-start(bf16[136,2048]{1,0:T(8,128)(2,1)S(1)} %slice.75), channel_id=1, source_target_pairs={{3,4},{7,8},{11,12},{19,20},{23,24},{27,28},{35,36},{39,40},{43,44... | collective-permute-start | bytes 1671176 | tf_op jit(solution)/shard_map/ppermute | solution.py:57
  15.4 28.6 %collective-permute-start.4 = (bf16[256,2048]{1,0:T(8,128)(2,1)S(1)}, bf16[256,2048]{1,0:T(8,128)(2,1)S(1)}, u32[]{:S(2)}, u32[]{:S(2)}) collective-permute-start(bf16[256,2048]{1,0:T(8,128)(2,1)S(1)} %copy-done.1), channel_id=1, source_target_pairs={{0,2},{1,3},{2,0},{3,1},{4,6},{5,7},{6,4},{7,5},{8,10},{9,11},{10,... | collective-permute-start | bytes 3145736 | tf_op jit(solution)/shard_map/ppermute | solution.py:44
  25.5 12.6 %copy-start.4 = (s32[1,4]{1,0:T(1,128)S(1)}, s32[1,4]{1,0:T(1,128)}, u32[]{:S(2)}) copy-start(s32[1,4]{1,0:T(1,128)} %param.7) | copy-start | bytes 52
  43.6 7.0 %collective-permute-start.6 = (bf16[256,2048]{1,0:T(8,128)(2,1)S(1)}, bf16[256,2048]{1,0:T(8,128)(2,1)S(1)}, u32[]{:S(2)}, u32[]{:S(2)}) collective-permute-start(bf16[256,2048]{1,0:T(8,128)(2,1)S(1)} %copy-done.1), channel_id=1, source_target_pairs={{0,1},{1,0},{2,3},{3,2},{4,5},{5,4},{6,7},{7,6},{8,9},{9,8},{10,11... | collective-permute-start | bytes 3145736 | tf_op jit(solution)/shard_map/ppermute | solution.py:42
  44.0 6.6 %collective-permute-start.5 = (bf16[256,2048]{1,0:T(8,128)(2,1)S(1)}, bf16[256,2048]{1,0:T(8,128)(2,1)S(1)}, u32[]{:S(2)}, u32[]{:S(2)}) collective-permute-start(bf16[256,2048]{1,0:T(8,128)(2,1)S(1)} %collective-permute-done.4), channel_id=1, source_target_pairs={{0,1},{1,0},{2,3},{3,2},{4,5},{5,4},{6,7},{7,6},{8,9},{9,8},{10,11... | collective-permute-start | bytes 3145736 | tf_op jit(solution)/shard_map/ppermute | solution.py:45
  101.9 2.9 %copy-start = (f32[1152,1536]{1,0:T(8,128)}, f32[1152,1536]{1,0:T(8,128)S(1)}, u32[]{:S(2)}) copy-start(f32[1152,1536]{1,0:T(8,128)S(1)} %multiply_add_fusion) | copy-start | bytes 21233668
  105.3 4.6 %copy-start.3 = (pred[8,128,128]{2,1,0:T(8,128)(4,1)S(1)}, pred[8,128,128]{2,1,0:T(8,128)(4,1)}, u32[]{:S(2)}) copy-start(pred[8,128,128]{2,1,0:T(8,128)(4,1)} %get-tuple-element.34) | copy-start | bytes 393220
  109.9 5.8 %copy-start.2 = (bf16[32,128,128]{2,1,0:T(8,128)(2,1)S(1)}, bf16[32,128,128]{2,1,0:T(8,128)(2,1)}, u32[]{:S(2)}) copy-start(bf16[32,128,128]{2,1,0:T(8,128)(2,1)} %copy.28) | copy-start | bytes 3145732
  126.7 2.5 %collective-permute-start.7 = (bf16[256,512]{1,0:T(8,128)(2,1)S(1)}, bf16[256,512]{1,0:T(8,128)(2,1)S(1)}, u32[]{:S(2)}, u32[]{:S(2)}) collective-permute-start(bf16[256,512]{1,0:T(8,128)(2,1)S(1)} %get-tuple-element.18), channel_id=1, source_target_pairs={{0,1},{1,0},{2,3},{3,2},{4,5},{5,4},{6,7},{7,6},{8,9},{9,8},{10,11... | collective-permute-start | bytes 786440 | tf_op jit(solution)/shard_map/ppermute | solution.py:137
  127.5 7.9 %collective-permute-start.8 = (bf16[256,512]{1,0:T(8,128)(2,1)S(1)}, bf16[256,512]{1,0:T(8,128)(2,1)S(1)}, u32[]{:S(2)}, u32[]{:S(2)}) collective-permute-start(bf16[256,512]{1,0:T(8,128)(2,1)S(1)} %get-tuple-element.17), channel_id=1, source_target_pairs={{0,2},{1,3},{2,0},{3,1},{4,6},{5,7},{6,4},{7,5},{8,10},{9,11},{10,... | collective-permute-start | bytes 786440 | tf_op jit(solution)/shard_map/ppermute | solution.py:137
  128.8 12.4 %collective-permute-start.9 = (bf16[256,512]{1,0:T(8,128)(2,1)S(1)}, bf16[256,512]{1,0:T(8,128)(2,1)S(1)}, u32[]{:S(2)}, u32[]{:S(2)}) collective-permute-start(bf16[256,512]{1,0:T(8,128)(2,1)S(1)} %get-tuple-element.16), channel_id=1, source_target_pairs={{0,3},{1,2},{2,1},{3,0},{4,7},{5,6},{6,5},{7,4},{8,11},{9,10},{10,... | collective-permute-start | bytes 786440 | tf_op jit(solution)/shard_map/ppermute | solution.py:137
Sparse Core Ops, SparseCore 0:
  9.8 70.1 all-gather.1

commit v15 on v13

--- a/solution.py
+++ b/solution.py
@@ -39,7 +39,10 @@
     ext_rows = tail + span
 
     swaps = [[(i, i ^ d) for i in range(n_seq)] for d in range(1, GROUP_DEVS)]
-    from_member = [tokens] + [lax.ppermute(tokens, "seq", perm) for perm in swaps]
+    from_member = [tokens, lax.ppermute(tokens, "seq", swaps[0])]
+    for d in range(2, GROUP_DEVS, 2):
+        fetched = lax.ppermute(tokens, "seq", swaps[d - 1])
+        from_member += [fetched, lax.ppermute(fetched, "seq", swaps[0])]
     blocks = []
     for m in range(GROUP_DEVS):
         pick = from_member[0]

time: 157 us -> 156 us (level)
    all_gather x1, waiting for transfers between devices: 6.28 us -> 21.9 us  [local(): w_all = lax.all_gather(w_part, 'fsdp', axis=0, tiled=True)]
    ppermute x3, waiting for transfers between devices: 15.4 us -> 0.25 us  [the longest x1 0.24 us: local(): fetched = lax.ppermute(tokens, 'seq', swaps[d - 1])]
where the time goes in v15:
time: 156 us; the launch traced here: 155 us
  matrix products  36.8 us (24%)
  other arithmetic  30.2 us (19%)
  local copies, waits for them, and re-layouts  29.4 us (19%)
  waiting for transfers between devices  28.7 us (18%)
  starting transfers between devices  16.5 us (11%)
  between operations  13.6 us (9%)
    all_gather x1, waiting for transfers between devices, local(): w_all = lax.all_gather(w_part, 'fsdp', axis=0, tiled=True)  21.9 us
    dot_general x1, matrix products, local(): jnp.dot(ext_tokens, w_all.T, preferred_element_type=jnp.float32)  11.2 us
    add x1, other arithmetic, local(): featured + taps[tap_index] * jnp.where((pos_f >= tap_index)[:, None], shi...  10.7 us
    unnamed x16, local copies, waits for them, and re-layouts  9.25 us
    ppermute x1, starting transfers between devices, local(): fetched = lax.ppermute(tokens, 'seq', swaps[d - 1])  8.59 us
    dot_general x2, matrix products, tap_table(): jnp.einsum('ijt,tg->gij', one_hot, long_filter, preferred_element_type=jn...  7.92 us
    unnamed x5, other arithmetic  7.54 us
    dot_general x4, matrix products, local(): jnp.dot(got, ow_cat[d * own:(d + 1) * own], preferred_element_type=jnp.fl...  7.4 us
  transfers between devices with their start and end apart: 11, of which 4 were waited for; matrix products, arithmetic and copies ran while one was open for 25% of the time, Pallas kernels for 0%

profile of v15, /device:TPU:1, one launch (start us, length us, event | category | flops | bytes accessed | tf_op | source)
XLA Modules:
  0.0 155.2 jit_solution(8560500788228618595)
XLA Ops:
  6.5 2.7 %copy.26 = bf16[2048,384]{0,1:T(8,128)(2,1)} copy(bf16[2048,384]{1,0:T(8,128)(2,1)} %param.8) | data formatting | bytes 3145728 | tf_op args[2]
  9.2 1.8 %constant_dynamic-slice_fusion.7 = bf16[3,32,2048]{2,1,0:T(8,128)(2,1)} fusion(bf16[3,128,2048]{2,1,0:T(8,128)(2,1)} %bitcast.79, s32[]{:T(128)S(6)} %select_n.178), kind=kLoop, calls=%fused_computation.73 | loop fusion | bytes 786436 | tf_op jit(solution)/shard_map/dynamic_slice | solution.py:69
  12.8 1.5 collective-permute-start.1
  14.3 1.5 collective-permute-start.2
  15.8 1.5 collective-permute-start.3
  17.3 8.6 %collective-permute-start.4 = (bf16[256,2048]{1,0:T(8,128)(2,1)S(1)}, bf16[256,2048]{1,0:T(8,128)(2,1)S(1)}, u32[]{:S(2)}, u32[]{:S(2)}) collective-permute-start(bf16[256,2048]{1,0:T(8,128)(2,1)S(1)} %copy-done), channel_id=1, source_target_pairs={{0,2},{1,3},{2,0},{3,1},{4,6},{5,7},{6,4},{7,5},{8,10},{9,11},{10,... | collective-permute-start | bytes 3145736 | tf_op jit(solution)/shard_map/ppermute | solution.py:44
  29.3 4.0 %fusion.28 = bf16[32,128,128]{2,0,1:T(8,128)(2,1)S(1)} fusion(bf16[128,32,1]{0,1,2:T(8,128)(2,1)S(1)} %bitcast.83, s32[128,128]{1,0:T(8,128)S(1)} %get-tuple-element.34), kind=kOutput, calls=%fused_computation.37 | convolution fusion | flops 136839168 | bytes 1122304 | tf_op jit(solution)/shard_map/ijt,tg->gij/dot_general | solution.py:22
  34.7 3.9 %fusion.29 = bf16[32,128,128]{2,0,1:T(8,128)(2,1)S(1)} fusion(bf16[128,32,1]{0,1,2:T(8,128)(2,1)S(1)} %bitcast.84, s32[128,128]{1,0:T(8,128)S(1)} %get-tuple-element.35), kind=kOutput, calls=%fused_computation.38 | convolution fusion | flops 136839168 | bytes 1122304 | tf_op jit(solution)/shard_map/ijt,tg->gij/dot_general | solution.py:22
  41.2 4.3 %constant_dynamic-slice_fusion.11 = (bf16[16,32,2048]{2,1,0:T(8,128)(2,1)S(1)}, bf16[16,32,2048]{2,1,0:T(8,128)(2,1)S(1)}, bf16[16,32,2048]{2,1,0:T(8,128)(2,1)S(1)}, bf16[16,32,2048]{2,1,0:T(8,128)(2,1)S(1)}) fusion(bf16[16,128,2048]{2,1,0:T(8,128)(2,1)} %bitcast.70, s32[]{:T(128)S(6)} %select_n.178, s32[]{:T(128)S(6)} %select_n.215, s32[]{:T(128)S(6)} %select_n.214, ...), kind=kLoop, calls=%fused_computation.77 | loop fusion | bytes 16777232 | tf_op jit(solution)/shard_map/dynamic_slice | solution.py:78
  46.1 4.1 %pad_maximum_fusion = bf16[2048,2048]{1,0:T(8,128)(2,1)} fusion(bf16[512,2048]{1,0:T(8,128)(2,1)S(1)} %bitcast.74, bf16[512,2048]{1,0:T(8,128)(2,1)S(1)} %bitcast.75, bf16[512,2048]{1,0:T(8,128)(2,1)S(1)} %bitcast.76, bf16[512,2048]{1,0:T(8,128)(2,1)S(1)} %bitcast.73), kind=kLoop, calls=%fused_computation | loop fusion | flops 33554432 | bytes 16777216 | tf_op jit(solution)/shard_map/concatenate | solution.py:79
  50.2 2.3 %select_dynamic-update-slice_fusion.4 = bf16[1160,2048]{1,0:T(8,128)(2,1)} fusion(bf16[136,2048]{1,0:T(8,128)(2,1)S(1)} %collective-permute-done, bf16[136,2048]{1,0:T(8,128)(2,1)} %collective-permute-done.1, bf16[136,2048]{1,0:T(8,128)(2,1)} %collective-permute-done.2, bf16[136,2048]{1,0:T(8,128)(2,1)} %collective-permute-done.3, pred[]{:T(512)S(6)} %eq.79, ...), kind=kLoop, calls=%fused_computation.46 | loop fusion | flops 1114111 | bytes 2785284
  52.5 1.8 %select_dynamic-update-slice_fusion.3 = bf16[1160,2048]{1,0:T(8,128)(2,1)} fusion(bf16[1160,2048]{1,0:T(8,128)(2,1)} %select_dynamic-update-slice_fusion.4, bf16[256,2048]{1,0:T(8,128)(2,1)S(1)} %collective-permute-done.5, bf16[256,2048]{1,0:T(8,128)(2,1)S(1)} %collective-permute-done.4, bf16[256,2048]{1,0:T(8,128)(2,1)S(1)} %collective-permute-done.6, ...), kind=kLoop, calls=%fused_computation.45 | loop fusion | flops 1572864 | bytes 5242883
  54.2 1.7 %select_dynamic-update-slice_fusion.2 = bf16[1160,2048]{1,0:T(8,128)(2,1)} fusion(bf16[1160,2048]{1,0:T(8,128)(2,1)} %select_dynamic-update-slice_fusion.3, bf16[256,2048]{1,0:T(8,128)(2,1)S(1)} %collective-permute-done.5, bf16[256,2048]{1,0:T(8,128)(2,1)S(1)} %collective-permute-done.4, bf16[256,2048]{1,0:T(8,128)(2,1)S(1)} %collective-permute-done.6, ...), kind=kLoop, calls=%fused_computation.44 | loop fusion | flops 1572864 | bytes 5242883
  56.0 1.8 %select_dynamic-update-slice_fusion.1 = bf16[1160,2048]{1,0:T(8,128)(2,1)} fusion(bf16[1160,2048]{1,0:T(8,128)(2,1)} %select_dynamic-update-slice_fusion.2, bf16[256,2048]{1,0:T(8,128)(2,1)S(1)} %collective-permute-done.5, bf16[256,2048]{1,0:T(8,128)(2,1)S(1)} %collective-permute-done.4, bf16[256,2048]{1,0:T(8,128)(2,1)S(1)} %collective-permute-done.6, ...), kind=kLoop, calls=%fused_computation.43 | loop fusion | flops 1572864 | bytes 5242883
  57.7 1.7 %select_dynamic-update-slice_fusion = bf16[1160,2048]{1,0:T(8,128)(2,1)} fusion(bf16[1160,2048]{1,0:T(8,128)(2,1)} %select_dynamic-update-slice_fusion.1, bf16[256,2048]{1,0:T(8,128)(2,1)S(1)} %collective-permute-done.5, bf16[256,2048]{1,0:T(8,128)(2,1)S(1)} %collective-permute-done.4, bf16[256,2048]{1,0:T(8,128)(2,1)S(1)} %collective-permute-done.6, ...), kind=kLoop, calls=%fused_computation.42 | loop fusion | flops 1572864 | bytes 5242883 | tf_op jit(solution)/shard_map/concatenate | solution.py:59
  59.5 21.9 %all-gather.2.cloned.1.call-done = bf16[48,32,2048]{2,1,0:T(8,128)(2,1)} async-done(((bf16[3,32,2048]{2,1,0:T(8,128)(2,1)}), bf16[48,32,2048]{2,1,0:T(8,128)(2,1)}) %all-gather.2.cloned.1.call-update) | async-done | bytes 6291472 | tf_op jit(solution)/shard_map/all_gather | solution.py:70
  81.4 11.2 %convolution_convert_fusion = bf16[1160,1536]{1,0:T(8,128)(2,1)S(1)} fusion(bf16[1160,2048]{1,0:T(8,128)(2,1)} %select_dynamic-update-slice_fusion, bf16[1536,2048]{1,0:T(8,128)(2,1)} %bitcast.85), kind=kOutput, calls=%fused_computation.11 | convolution fusion | flops 7299870720 | bytes 14606336 | tf_op jit(solution)/shard_map/dot_general | solution.py:81
  92.6 10.7 %multiply_add_fusion = f32[1152,1536]{1,0:T(8,128)S(1)} fusion(bf16[1160,1536]{1,0:T(8,128)(2,1)S(1)} %convolution_convert_fusion, f32[1536]{0:T(1024)S(1)} %mul.115, f32[1536]{0:T(1024)S(1)} %mul.112, f32[1536]{0:T(1024)S(1)} %mul.109, f32[1536]{0:T(1024)S(1)} %mul.106, f32[1536]{0:T(1024)S(1)} %mul.103, f32[1536]{0:T(1024)S(1)} %mul.100, ...), kind=kLoop, calls=%fused_computation.12 | loop fusion | flops 47775744 | bytes 31901568 | tf_op jit(solution)/shard_map/add | solution.py:94
  103.3 2.9 %copy-done.1 = f32[1152,1536]{1,0:T(8,128)} copy-done((f32[1152,1536]{1,0:T(8,128)}, f32[1152,1536]{1,0:T(8,128)S(1)}, u32[]{:S(2)}) %copy-start.1) | copy-done | bytes 7077912
  107.6 1.7 %copy.29 = bf16[512,1152]{1,0:T(8,128)(2,1)S(1)} copy(bf16[512,1152]{0,1:T(8,128)(2,1)} %fusion.30) | data formatting | bytes 2359296 | tf_op jit(solution)/shard_map/transpose | solution.py:122
  109.3 1.7 %reshape.154 = bf16[32,16,9,128]{3,2,1,0:T(8,128)(2,1)} reshape(bf16[512,1152]{1,0:T(8,128)(2,1)S(1)} %copy.29) | data formatting | bytes 2359296 | tf_op jit(solution)/shard_map/reshape | solution.py:122
  110.9 2.3 %fusion.39 = (bf16[32,16,8,128]{3,2,1,0:T(8,128)(2,1)S(1)}, bf16[32,16,8,128]{3,2,1,0:T(8,128)(2,1)S(1)}) fusion(bf16[32,16,9,128]{3,2,1,0:T(8,128)(2,1)} %reshape.154), kind=kLoop, calls=%fused_computation.85 | loop fusion | bytes 4194304 | tf_op jit(solution)/shard_map/slice | solution.py:124
  113.2 5.8 %fusion = f32[32,8,128,16]{2,3,1,0:T(8,128)S(1)} fusion(pred[8,128,128]{2,1,0:T(8,128)(4,1)} %get-tuple-element.33, bf16[32,128,128]{2,1,0:T(8,128)(2,1)} %copy.31, bf16[32,16,8,128]{3,2,1,0:T(8,128)(2,1)S(1)} %get-tuple-element.14), kind=kOutput, calls=%fused_computation.1 | convolution fusion | flops 138412032 | bytes 4325376 | tf_op jit(solution)/shard_map/gcbj,bgij->gcbi/dot_general | solution.py:126
  119.1 4.5 %add_bitcast_fusion = f32[32,16,8,128]{3,1,2,0:T(8,128)S(1)} fusion(f32[32,8,128,16]{2,3,1,0:T(8,128)S(1)} %fusion, pred[8,128,128]{2,1,0:T(8,128)(4,1)S(1)} %get-tuple-element.32, bf16[32,128,128]{2,1,0:T(8,128)(2,1)S(1)} %copy-done.2, bf16[32,16,8,128]{3,2,1,0:T(8,128)(2,1)S(1)} %get-tuple-element.13), kind=kOutput, calls=%fused_computation.36 | convolution fusion | flops 138936320 | bytes 6422528 | tf_op jit(solution)/shard_map/gcbj,bgij->gcbi/dot_general | solution.py:123
  124.5 1.8 %copy.44 = f32[64,8,8,128]{3,1,2,0:T(8,128)} copy(f32[64,8,8,128]{3,2,1,0:T(8,128)S(1)} %bitcast.71) | data formatting | bytes 4194304
  126.3 2.9 %copy.34 = f32[512,1024]{0,1:T(8,128)} copy(f32[512,1024]{1,0:T(8,128)} %bitcast.72) | data formatting | bytes 4194304 | tf_op jit(solution)/shard_map/reshape | solution.py:129
  129.2 2.7 %fusion.19 = bf16[512,1024]{0,1:T(8,128)(2,1)S(1)} fusion(f32[512,1024]{0,1:T(8,128)} %copy.34, f32[1152,1536]{1,0:T(8,128)} %copy-done.1), kind=kLoop, calls=%fused_computation.29 | loop fusion | flops 1048576 | bytes 5242880 | tf_op jit(solution)/shard_map/convert_element_type | solution.py:130
  134.4 2.5 %convolution_add_fusion.1 = f32[256,2048]{1,0:T(8,128)S(1)} fusion(bf16[2048,2048]{1,0:T(8,128)(2,1)} %pad_maximum_fusion, bf16[256,2048]{1,0:T(8,128)(2,1)S(1)} %copy-done, bf16[4,256,512]{2,1,0:T(8,128)(2,1)S(1)} %bitcast.78, s32[]{:T(128)S(6)} %select_n.227), kind=kOutput, calls=%fused_computation.21 | convolution fusion | flops 537919488 | bytes 5505028 | tf_op jit(solution)/shard_map/dot_general | solution.py:138
  136.8 2.4 %collective-permute-done.8 = bf16[256,512]{1,0:T(8,128)(2,1)S(1)} collective-permute-done((bf16[256,512]{1,0:T(8,128)(2,1)S(1)}, bf16[256,512]{1,0:T(8,128)(2,1)S(1)}, u32[]{:S(2)}, u32[]{:S(2)}) %collective-permute-start.8) | collective-permute-done | bytes 262176 | tf_op jit(solution)/shard_map/ppermute | solution.py:137
  139.2 2.3 %fusion.22 = f32[256,2048]{1,0:T(8,128)S(1)} fusion(bf16[256,512]{1,0:T(8,128)(2,1)S(1)} %collective-permute-done.8, bf16[2048,2048]{1,0:T(8,128)(2,1)} %pad_maximum_fusion), kind=kOutput, calls=%fused_computation.32 | convolution fusion | flops 536870912 | bytes 4456448 | tf_op jit(solution)/shard_map/dot_general | solution.py:138
  141.6 4.1 %collective-permute-done.9 = bf16[256,512]{1,0:T(8,128)(2,1)S(1)} collective-permute-done((bf16[256,512]{1,0:T(8,128)(2,1)S(1)}, bf16[256,512]{1,0:T(8,128)(2,1)S(1)}, u32[]{:S(2)}, u32[]{:S(2)}) %collective-permute-start.9) | collective-permute-done | bytes 262176 | tf_op jit(solution)/shard_map/ppermute | solution.py:137
  146.4 1.9 %fusion.16 = bf16[256,2048]{1,0:T(8,128)(2,1)} fusion(f32[256,2048]{1,0:T(8,128)S(1)} %fusion.20, f32[256,2048]{1,0:T(8,128)S(1)} %fusion.22, f32[256,2048]{1,0:T(8,128)S(1)} %convolution_add_fusion.1, bf16[256,512]{1,0:T(8,128)(2,1)S(1)} %collective-permute-done.7, bf16[2048,2048]{1,0:T(8,128)(2,1)S(1)} %bitcast.69), kind=kOutput, calls=%fused_computation.23 | convolution fusion | flops 538968064 | bytes 9699328 | tf_op jit(solution)/shard_map/dot_general | solution.py:138
  (56 shorter events, 15.2 us)
Async XLA Ops:
  6.5 10.7 %copy-start = (bf16[256,2048]{1,0:T(8,128)(2,1)S(1)}, bf16[256,2048]{1,0:T(8,128)(2,1)}, u32[]{:S(2)}) copy-start(bf16[256,2048]{1,0:T(8,128)(2,1)} %param.6) | copy-start | bytes 3145732
  6.5 74.9 %all-gather.2.cloned.1.call-start = ((), (), s32[]{:S(2)}) async-start(), calls=%async_computation | async-start | bytes 6684672 | tf_op jit(solution)/shard_map/all_gather | solution.py:70
  12.1 33.4 %collective-permute-start = (bf16[136,2048]{1,0:T(8,128)(2,1)S(1)}, bf16[136,2048]{1,0:T(8,128)(2,1)S(1)}, u32[]{:S(2)}, u32[]{:S(2)}) collective-permute-start(bf16[136,2048]{1,0:T(8,128)(2,1)S(1)} %slice.87), channel_id=1, source_target_pairs={{3,7},{7,11},{11,15},{19,23},{23,27},{27,31},{35,39},{39,43},{43,4... | collective-permute-start | bytes 1671176 | tf_op jit(solution)/shard_map/ppermute | solution.py:57
  12.8 37.4 %collective-permute-start.1 = (bf16[136,2048]{1,0:T(8,128)(2,1)S(1)}, bf16[136,2048]{1,0:T(8,128)(2,1)}, u32[]{:S(2)}, u32[]{:S(2)}) collective-permute-start(bf16[136,2048]{1,0:T(8,128)(2,1)S(1)} %slice.87), channel_id=1, source_target_pairs={{3,6},{7,10},{11,14},{19,22},{23,26},{27,30},{35,38},{39,42},{43,4... | collective-permute-start | bytes 1671176 | tf_op jit(solution)/shard_map/ppermute | solution.py:57
  14.3 35.9 %collective-permute-start.2 = (bf16[136,2048]{1,0:T(8,128)(2,1)S(1)}, bf16[136,2048]{1,0:T(8,128)(2,1)}, u32[]{:S(2)}, u32[]{:S(2)}) collective-permute-start(bf16[136,2048]{1,0:T(8,128)(2,1)S(1)} %slice.87), channel_id=1, source_target_pairs={{3,5},{7,9},{11,13},{19,21},{23,25},{27,29},{35,37},{39,41},{43,45... | collective-permute-start | bytes 1671176 | tf_op jit(solution)/shard_map/ppermute | solution.py:57
  15.8 34.4 %collective-permute-start.3 = (bf16[136,2048]{1,0:T(8,128)(2,1)S(1)}, bf16[136,2048]{1,0:T(8,128)(2,1)}, u32[]{:S(2)}, u32[]{:S(2)}) collective-permute-start(bf16[136,2048]{1,0:T(8,128)(2,1)S(1)} %slice.87), channel_id=1, source_target_pairs={{3,4},{7,8},{11,12},{19,20},{23,24},{27,28},{35,36},{39,40},{43,44... | collective-permute-start | bytes 1671176 | tf_op jit(solution)/shard_map/ppermute | solution.py:57
  17.3 28.6 %collective-permute-start.4 = (bf16[256,2048]{1,0:T(8,128)(2,1)S(1)}, bf16[256,2048]{1,0:T(8,128)(2,1)S(1)}, u32[]{:S(2)}, u32[]{:S(2)}) collective-permute-start(bf16[256,2048]{1,0:T(8,128)(2,1)S(1)} %copy-done), channel_id=1, source_target_pairs={{0,2},{1,3},{2,0},{3,1},{4,6},{5,7},{6,4},{7,5},{8,10},{9,11},{10,... | collective-permute-start | bytes 3145736 | tf_op jit(solution)/shard_map/ppermute | solution.py:44
  27.4 12.6 %copy-start.3 = (s32[1,4]{1,0:T(1,128)S(1)}, s32[1,4]{1,0:T(1,128)}, u32[]{:S(2)}) copy-start(s32[1,4]{1,0:T(1,128)} %param.7) | copy-start | bytes 52
  45.5 7.0 %collective-permute-start.6 = (bf16[256,2048]{1,0:T(8,128)(2,1)S(1)}, bf16[256,2048]{1,0:T(8,128)(2,1)S(1)}, u32[]{:S(2)}, u32[]{:S(2)}) collective-permute-start(bf16[256,2048]{1,0:T(8,128)(2,1)S(1)} %copy-done), channel_id=1, source_target_pairs={{0,1},{1,0},{2,3},{3,2},{4,5},{5,4},{6,7},{7,6},{8,9},{9,8},{10,11... | collective-permute-start | bytes 3145736 | tf_op jit(solution)/shard_map/ppermute | solution.py:42
  45.9 6.6 %collective-permute-start.5 = (bf16[256,2048]{1,0:T(8,128)(2,1)S(1)}, bf16[256,2048]{1,0:T(8,128)(2,1)S(1)}, u32[]{:S(2)}, u32[]{:S(2)}) collective-permute-start(bf16[256,2048]{1,0:T(8,128)(2,1)S(1)} %collective-permute-done.4), channel_id=1, source_target_pairs={{0,1},{1,0},{2,3},{3,2},{4,5},{5,4},{6,7},{7,6},{8,9},{9,8},{10,11... | collective-permute-start | bytes 3145736 | tf_op jit(solution)/shard_map/ppermute | solution.py:45
  103.3 2.9 %copy-start.1 = (f32[1152,1536]{1,0:T(8,128)}, f32[1152,1536]{1,0:T(8,128)S(1)}, u32[]{:S(2)}) copy-start(f32[1152,1536]{1,0:T(8,128)S(1)} %multiply_add_fusion) | copy-start | bytes 21233668
  113.2 5.8 %copy-start.2 = (bf16[32,128,128]{2,1,0:T(8,128)(2,1)S(1)}, bf16[32,128,128]{2,1,0:T(8,128)(2,1)}, u32[]{:S(2)}) copy-start(bf16[32,128,128]{2,1,0:T(8,128)(2,1)} %copy.28) | copy-start | bytes 3145732
  129.2 16.6 %slice-start = ((s8[8388608]{0:T(1024)(128)(4,1)}), s8[4194304]{0:T(1024)(128)(4,1)S(1)}, s32[]{:S(2)}) async-start(s8[8388608]{0:T(1024)(128)(4,1)} %bitcast.68), calls=%async_computation.1 | async-start | bytes 8388608
  132.0 7.3 %collective-permute-start.8 = (bf16[256,512]{1,0:T(8,128)(2,1)S(1)}, bf16[256,512]{1,0:T(8,128)(2,1)S(1)}, u32[]{:S(2)}, u32[]{:S(2)}) collective-permute-start(bf16[256,512]{1,0:T(8,128)(2,1)S(1)} %get-tuple-element.17), channel_id=1, source_target_pairs={{0,2},{1,3},{2,0},{3,1},{4,6},{5,7},{6,4},{7,5},{8,10},{9,11},{10,... | collective-permute-start | bytes 786440 | tf_op jit(solution)/shard_map/ppermute | solution.py:137
  133.3 12.4 %collective-permute-start.9 = (bf16[256,512]{1,0:T(8,128)(2,1)S(1)}, bf16[256,512]{1,0:T(8,128)(2,1)S(1)}, u32[]{:S(2)}, u32[]{:S(2)}) collective-permute-start(bf16[256,512]{1,0:T(8,128)(2,1)S(1)} %get-tuple-element.16), channel_id=1, source_target_pairs={{0,3},{1,2},{2,1},{3,0},{4,7},{5,6},{6,5},{7,4},{8,11},{9,10},{10,... | collective-permute-start | bytes 786440 | tf_op jit(solution)/shard_map/ppermute | solution.py:137
  134.4 11.3 %slice-start.1 = ((s8[8388608]{0:T(1024)(128)(4,1)}), s8[4194304]{0:T(1024)(128)(4,1)S(1)}, s32[]{:S(2)}) async-start(s8[8388608]{0:T(1024)(128)(4,1)} %bitcast.68), calls=%async_computation.2 | async-start | bytes 8388608
  134.4 12.1 %collective-permute-start.7 = (bf16[256,512]{1,0:T(8,128)(2,1)S(1)}, bf16[256,512]{1,0:T(8,128)(2,1)S(1)}, u32[]{:S(2)}, u32[]{:S(2)}) collective-permute-start(bf16[256,512]{1,0:T(8,128)(2,1)S(1)} %get-tuple-element.15), channel_id=1, source_target_pairs={{0,1},{1,0},{2,3},{3,2},{4,5},{5,4},{6,7},{7,6},{8,9},{9,8},{10,11... | collective-permute-start | bytes 786440 | tf_op jit(solution)/shard_map/ppermute | solution.py:137
Sparse Core Ops, SparseCore 0:
  11.2 70.1 all-gather.1

commit v16 on v14

--- a/solution.py
+++ b/solution.py
@@ -91,9 +91,19 @@
     featured = jnp.zeros((feat_rows, 3 * own), jnp.float32)
     for tap_index in range(width):
         shifted = projected[start - tap_index : ext_rows - tap_index].astype(jnp.float32)
-        featured = featured + taps[tap_index] * jnp.where(
-            (pos_f >= tap_index)[:, None], shifted, 0.0
-        )
+        featured = featured + taps[tap_index] * shifted
+    fix_rows = 8
+    for k in range(seq_starts.shape[0]):
+        first = jnp.clip(seq_starts[k] - (pair_start - tail) - start, 0, feat_rows - fix_rows)
+        src = lax.dynamic_slice_in_dim(
+            projected, first + start - (width - 1), fix_rows + width - 1, axis=0
+        ).astype(jnp.float32)
+        pos_w = lax.dynamic_slice_in_dim(pos_f, first, fix_rows, axis=0)
+        fix = jnp.zeros((fix_rows, 3 * own), jnp.float32)
+        for tap_index in range(width):
+            piece = src[width - 1 - tap_index : width - 1 - tap_index + fix_rows]
+            fix = fix + taps[tap_index] * jnp.where((pos_w >= tap_index)[:, None], piece, 0.0)
+        featured = lax.dynamic_update_slice_in_dim(featured, fix, first, axis=0)
     queries = featured[feat_rows - span :, :own]
     mixed_in = (featured[:, own : 2 * own] * featured[:, 2 * own :]).astype(jnp.bfloat16)
 

time: 155 us -> 163 us (1.052)
  local copies, waits for them, and re-layouts: 25.5 us -> 33.6 us
  waiting for transfers between devices: 34.9 us -> 29.6 us
  between operations: 13.6 us -> 16.3 us
  other arithmetic: 28.2 us -> 30.1 us
    dynamic_update_slice x0 -> x4, local copies, waits for them, and re-layouts: none -> 5.77 us  [local(): featured = lax.dynamic_update_slice_in_dim(featured, fix, first, axis=0)]
    all_gather x1, waiting for transfers between devices: 22.7 us -> 17.6 us  [local(): w_all = lax.all_gather(w_part, 'fsdp', axis=0, tiled=True)]
    transpose x1, other arithmetic: 0.4 us -> 3.81 us  [local(): mi_t = mixed_in.T.reshape(n_groups, per_group, n_blocks + 1, filter_len)]
    add x1 -> x5, other arithmetic: 10.7 us -> 7.99 us  [the longest x1 7.54 us: local(): featured = featured + taps[tap_index] * shifted]
    unnamed x14 -> x18, local copies, waits for them, and re-layouts: 8.3 us -> 6.33 us
    slice x1, local copies, waits for them, and re-layouts: 0.44 us -> 2.3 us  [local(): mi_t[:, :, 1:]]
  transfers between devices with their start and end apart: 11 -> 11, of which waited for: 4 -> 3; matrix products, arithmetic and copies ran while one was open for 22% -> 22% of each run, Pallas kernels for 0% -> 0%
where the time goes in v16:
time: 163 us; the launch traced here: 162 us
  matrix products  36 us (22%)
  local copies, waits for them, and re-layouts  33.6 us (21%)
  other arithmetic  30.1 us (18%)
  waiting for transfers between devices  29.6 us (18%)
  starting transfers between devices  16.8 us (10%)
  between operations  16.3 us (10%)
    all_gather x1, waiting for transfers between devices, local(): w_all = lax.all_gather(w_part, 'fsdp', axis=0, tiled=True)  17.6 us
    ppermute x3, waiting for transfers between devices, local(): got = send if d == 0 else lax.ppermute(send, 'seq', swaps[d - 1])  11.9 us
    dot_general x1, matrix products, local(): jnp.dot(ext_tokens, w_all.T, preferred_element_type=jnp.float32)  11.2 us
    ppermute x1, starting transfers between devices, local(): fetched = lax.ppermute(tokens, 'seq', swaps[d - 1])  8.59 us
    dot_general x2, matrix products, tap_table(): jnp.einsum('ijt,tg->gij', one_hot, long_filter, preferred_element_type=jn...  7.91 us
    unnamed x4, other arithmetic  7.57 us
    add x1, other arithmetic, local(): featured = featured + taps[tap_index] * shifted  7.54 us
    dot_general x1, matrix products, local(): jnp.dot(jnp.concatenate(pieces, axis=1), ow_cat, preferred_element_type=j...  6.68 us
  transfers between devices with their start and end apart: 11, of which 3 were waited for; matrix products, arithmetic and copies ran while one was open for 22% of the time, Pallas kernels for 0%

profile of v16, /device:TPU:1, one launch (start us, length us, event | category | flops | bytes accessed | tf_op | source)
XLA Modules:
  0.0 162.4 jit_solution(74673366965793984)
XLA Ops:
  6.5 2.7 %copy.26 = bf16[2048,384]{0,1:T(8,128)(2,1)} copy(bf16[2048,384]{1,0:T(8,128)(2,1)} %param.8) | data formatting | bytes 3145728 | tf_op args[2]
  9.2 1.8 %constant_dynamic-slice_fusion.7 = bf16[3,32,2048]{2,1,0:T(8,128)(2,1)} fusion(bf16[3,128,2048]{2,1,0:T(8,128)(2,1)} %bitcast.86, s32[]{:T(128)S(6)} %select_n.261), kind=kLoop, calls=%fused_computation.146 | loop fusion | bytes 786436 | tf_op jit(solution)/shard_map/dynamic_slice | solution.py:69
  12.8 1.5 collective-permute-start.1
  14.3 1.5 collective-permute-start.2
  15.8 1.5 collective-permute-start.3
  17.3 8.6 %collective-permute-start.4 = (bf16[256,2048]{1,0:T(8,128)(2,1)S(1)}, bf16[256,2048]{1,0:T(8,128)(2,1)S(1)}, u32[]{:S(2)}, u32[]{:S(2)}) collective-permute-start(bf16[256,2048]{1,0:T(8,128)(2,1)S(1)} %copy-done), channel_id=1, source_target_pairs={{0,2},{1,3},{2,0},{3,1},{4,6},{5,7},{6,4},{7,5},{8,10},{9,11},{10,... | collective-permute-start | bytes 3145736 | tf_op jit(solution)/shard_map/ppermute | solution.py:44
  32.7 4.0 %fusion.20 = bf16[32,128,128]{2,0,1:T(8,128)(2,1)S(1)} fusion(bf16[128,32,1]{0,1,2:T(8,128)(2,1)S(1)} %bitcast.90, s32[128,128]{1,0:T(8,128)S(1)} %get-tuple-element.86), kind=kOutput, calls=%fused_computation.28 | convolution fusion | flops 136839168 | bytes 1122304 | tf_op jit(solution)/shard_map/ijt,tg->gij/dot_general | solution.py:22
  38.0 3.9 %fusion.21 = bf16[32,128,128]{2,0,1:T(8,128)(2,1)S(1)} fusion(bf16[128,32,1]{0,1,2:T(8,128)(2,1)S(1)} %bitcast.91, s32[128,128]{1,0:T(8,128)S(1)} %get-tuple-element.87), kind=kOutput, calls=%fused_computation.29 | convolution fusion | flops 136839168 | bytes 1122304 | tf_op jit(solution)/shard_map/ijt,tg->gij/dot_general | solution.py:22
  45.3 4.3 %constant_dynamic-slice_fusion.11 = (bf16[16,32,2048]{2,1,0:T(8,128)(2,1)S(1)}, bf16[16,32,2048]{2,1,0:T(8,128)(2,1)S(1)}, bf16[16,32,2048]{2,1,0:T(8,128)(2,1)S(1)}, bf16[16,32,2048]{2,1,0:T(8,128)(2,1)S(1)}) fusion(bf16[16,128,2048]{2,1,0:T(8,128)(2,1)} %bitcast.78, s32[]{:T(128)S(6)} %select_n.261, s32[]{:T(128)S(6)} %select_n.296, s32[]{:T(128)S(6)} %select_n.295, ...), kind=kLoop, calls=%fused_computation.150 | loop fusion | bytes 16777232 | tf_op jit(solution)/shard_map/dynamic_slice | solution.py:78
  50.3 4.1 %pad_maximum_fusion = bf16[2048,2048]{1,0:T(8,128)(2,1)} fusion(bf16[512,2048]{1,0:T(8,128)(2,1)S(1)} %bitcast.82, bf16[512,2048]{1,0:T(8,128)(2,1)S(1)} %bitcast.83, bf16[512,2048]{1,0:T(8,128)(2,1)S(1)} %bitcast.84, bf16[512,2048]{1,0:T(8,128)(2,1)S(1)} %bitcast.81), kind=kLoop, calls=%fused_computation | loop fusion | flops 33554432 | bytes 16777216 | tf_op jit(solution)/shard_map/concatenate | solution.py:79
  54.4 2.3 %select_dynamic-update-slice_fusion.4 = bf16[1160,2048]{1,0:T(8,128)(2,1)} fusion(bf16[136,2048]{1,0:T(8,128)(2,1)S(1)} %collective-permute-done, bf16[136,2048]{1,0:T(8,128)(2,1)} %collective-permute-done.1, bf16[136,2048]{1,0:T(8,128)(2,1)} %collective-permute-done.2, bf16[136,2048]{1,0:T(8,128)(2,1)} %collective-permute-done.3, pred[]{:T(512)S(6)} %eq.79, ...), kind=kLoop, calls=%fused_computation.44 | loop fusion | flops 1114111 | bytes 2785284
  56.7 1.8 %select_dynamic-update-slice_fusion.3 = bf16[1160,2048]{1,0:T(8,128)(2,1)} fusion(bf16[1160,2048]{1,0:T(8,128)(2,1)} %select_dynamic-update-slice_fusion.4, bf16[256,2048]{1,0:T(8,128)(2,1)S(1)} %collective-permute-done.5, bf16[256,2048]{1,0:T(8,128)(2,1)S(1)} %collective-permute-done.4, bf16[256,2048]{1,0:T(8,128)(2,1)S(1)} %collective-permute-done.6, ...), kind=kLoop, calls=%fused_computation.43 | loop fusion | flops 1572864 | bytes 5242883
  58.4 1.7 %select_dynamic-update-slice_fusion.2 = bf16[1160,2048]{1,0:T(8,128)(2,1)} fusion(bf16[1160,2048]{1,0:T(8,128)(2,1)} %select_dynamic-update-slice_fusion.3, bf16[256,2048]{1,0:T(8,128)(2,1)S(1)} %collective-permute-done.5, bf16[256,2048]{1,0:T(8,128)(2,1)S(1)} %collective-permute-done.4, bf16[256,2048]{1,0:T(8,128)(2,1)S(1)} %collective-permute-done.6, ...), kind=kLoop, calls=%fused_computation.42 | loop fusion | flops 1572864 | bytes 5242883
  60.2 1.8 %select_dynamic-update-slice_fusion.1 = bf16[1160,2048]{1,0:T(8,128)(2,1)} fusion(bf16[1160,2048]{1,0:T(8,128)(2,1)} %select_dynamic-update-slice_fusion.2, bf16[256,2048]{1,0:T(8,128)(2,1)S(1)} %collective-permute-done.5, bf16[256,2048]{1,0:T(8,128)(2,1)S(1)} %collective-permute-done.4, bf16[256,2048]{1,0:T(8,128)(2,1)S(1)} %collective-permute-done.6, ...), kind=kLoop, calls=%fused_computation.41 | loop fusion | flops 1572864 | bytes 5242883
  62.0 1.8 %select_dynamic-update-slice_fusion = bf16[1160,2048]{1,0:T(8,128)(2,1)} fusion(bf16[1160,2048]{1,0:T(8,128)(2,1)} %select_dynamic-update-slice_fusion.1, bf16[256,2048]{1,0:T(8,128)(2,1)S(1)} %collective-permute-done.5, bf16[256,2048]{1,0:T(8,128)(2,1)S(1)} %collective-permute-done.4, bf16[256,2048]{1,0:T(8,128)(2,1)S(1)} %collective-permute-done.6, ...), kind=kLoop, calls=%fused_computation.40 | loop fusion | flops 1572864 | bytes 5242883 | tf_op jit(solution)/shard_map/concatenate | solution.py:59
  63.7 17.6 %all-gather.2.cloned.1.call-done = bf16[48,32,2048]{2,1,0:T(8,128)(2,1)} async-done(((bf16[3,32,2048]{2,1,0:T(8,128)(2,1)}), bf16[48,32,2048]{2,1,0:T(8,128)(2,1)}) %all-gather.2.cloned.1.call-update) | async-done | bytes 6291472 | tf_op jit(solution)/shard_map/all_gather | solution.py:70
  81.4 11.2 %convolution_convert_fusion = bf16[1160,1536]{1,0:T(8,128)(2,1)S(1)} fusion(bf16[1160,2048]{1,0:T(8,128)(2,1)} %select_dynamic-update-slice_fusion, bf16[1536,2048]{1,0:T(8,128)(2,1)} %bitcast.92), kind=kOutput, calls=%fused_computation.11 | convolution fusion | flops 7299870720 | bytes 14606336 | tf_op jit(solution)/shard_map/dot_general | solution.py:81
  92.6 7.5 %multiply_add_fusion = f32[1152,1536]{1,0:T(8,128)} fusion(bf16[1160,1536]{1,0:T(8,128)(2,1)S(1)} %convolution_convert_fusion, f32[1536]{0:T(1024)S(1)} %mul.296, f32[1536]{0:T(1024)S(1)} %mul.145, f32[1536]{0:T(1024)S(1)} %mul.142, f32[1536]{0:T(1024)S(1)} %mul.139, f32[1536]{0:T(1024)S(1)} %mul.136, f32[1536]{0:T(1024)S(1)} %mul.133, f32[1536]{0:T(1024)S(1)} %mul.127), kind=kLoop, calls=%fused_computation.12 | loop fusion | flops 35389440 | bytes 31893504 | tf_op jit(solution)/shard_map/add | solution.py:94
  100.3 1.5 dynamic_update_slice.12
  105.0 1.4 dynamic_update_slice.15
  106.4 3.8 %fusion.22 = bf16[512,1152]{0,1:T(8,128)(2,1)} fusion(f32[1152,1536]{1,0:T(8,128)} %dynamic_update_slice.15), kind=kLoop, calls=%fused_computation.30 | loop fusion | flops 1179648 | bytes 5898240 | tf_op jit(solution)/shard_map/transpose | solution.py:132
  110.2 1.7 %copy.29 = bf16[512,1152]{1,0:T(8,128)(2,1)S(1)} copy(bf16[512,1152]{0,1:T(8,128)(2,1)} %fusion.22) | data formatting | bytes 2359296 | tf_op jit(solution)/shard_map/transpose | solution.py:132
  111.9 1.7 %reshape.182 = bf16[32,16,9,128]{3,2,1,0:T(8,128)(2,1)} reshape(bf16[512,1152]{1,0:T(8,128)(2,1)S(1)} %copy.29) | data formatting | bytes 2359296 | tf_op jit(solution)/shard_map/reshape | solution.py:132
  113.6 2.3 %fusion.89 = (bf16[32,16,8,128]{3,2,1,0:T(8,128)(2,1)S(1)}, bf16[32,16,8,128]{3,2,1,0:T(8,128)(2,1)S(1)}) fusion(bf16[32,16,9,128]{3,2,1,0:T(8,128)(2,1)} %reshape.182), kind=kLoop, calls=%fused_computation.189 | loop fusion | bytes 4194304 | tf_op jit(solution)/shard_map/slice | solution.py:134
  115.9 5.8 %fusion = f32[32,8,128,16]{2,3,1,0:T(8,128)S(1)} fusion(pred[8,128,128]{2,1,0:T(8,128)(4,1)S(1)} %copy-done.3, bf16[32,128,128]{2,1,0:T(8,128)(2,1)} %copy.31, bf16[32,16,8,128]{3,2,1,0:T(8,128)(2,1)S(1)} %get-tuple-element.26), kind=kOutput, calls=%fused_computation.1 | convolution fusion | flops 138412032 | bytes 4325376 | tf_op jit(solution)/shard_map/gcbj,bgij->gcbi/dot_general | solution.py:136
  121.7 4.5 %add_bitcast_fusion = f32[32,16,8,128]{3,1,2,0:T(8,128)S(1)} fusion(f32[32,8,128,16]{2,3,1,0:T(8,128)S(1)} %fusion, pred[8,128,128]{2,1,0:T(8,128)(4,1)S(1)} %copy-done.2, bf16[32,128,128]{2,1,0:T(8,128)(2,1)S(1)} %copy-done.1, bf16[32,16,8,128]{3,2,1,0:T(8,128)(2,1)S(1)} %get-tuple-element.25), kind=kOutput, calls=%fused_computation.27 | convolution fusion | flops 138936320 | bytes 6422528 | tf_op jit(solution)/shard_map/gcbj,bgij->gcbi/dot_general | solution.py:133
  127.1 1.8 %copy.44 = f32[64,8,8,128]{3,1,2,0:T(8,128)} copy(f32[64,8,8,128]{3,2,1,0:T(8,128)S(1)} %bitcast.79) | data formatting | bytes 4194304
  128.9 2.9 %copy.34 = f32[512,1024]{0,1:T(8,128)} copy(f32[512,1024]{1,0:T(8,128)} %bitcast.80) | data formatting | bytes 4194304 | tf_op jit(solution)/shard_map/reshape | solution.py:139
  131.8 2.6 %fusion.17 = bf16[512,1024]{0,1:T(8,128)(2,1)S(1)} fusion(f32[512,1024]{0,1:T(8,128)} %copy.34, f32[1152,1536]{1,0:T(8,128)} %dynamic_update_slice.15), kind=kLoop, calls=%fused_computation.26 | loop fusion | flops 1048576 | bytes 5242880 | tf_op jit(solution)/shard_map/convert_element_type | solution.py:140
  136.9 6.1 %collective-permute-done.8 = bf16[256,512]{1,0:T(8,128)(2,1)S(1)} collective-permute-done((bf16[256,512]{1,0:T(8,128)(2,1)S(1)}, bf16[256,512]{1,0:T(8,128)(2,1)S(1)}, u32[]{:S(2)}, u32[]{:S(2)}) %collective-permute-start.8) | collective-permute-done | bytes 262176 | tf_op jit(solution)/shard_map/ppermute | solution.py:147
  143.0 5.8 %collective-permute-done.9 = bf16[256,512]{1,0:T(8,128)(2,1)S(1)} collective-permute-done((bf16[256,512]{1,0:T(8,128)(2,1)S(1)}, bf16[256,512]{1,0:T(8,128)(2,1)S(1)}, u32[]{:S(2)}, u32[]{:S(2)}) %collective-permute-start.9) | collective-permute-done | bytes 262176 | tf_op jit(solution)/shard_map/ppermute | solution.py:147
  148.8 6.7 %fusion.14 = bf16[256,2048]{1,0:T(8,128)(2,1)} fusion(bf16[2048,2048]{1,0:T(8,128)(2,1)} %pad_maximum_fusion, bf16[256,2048]{1,0:T(8,128)(2,1)S(1)} %copy-done, bf16[256,512]{1,0:T(8,128)(2,1)S(1)} %collective-permute-done.9, bf16[256,512]{1,0:T(8,128)(2,1)S(1)} %collective-permute-done.8, bf16[256,512]{1,0:T(8,128)(2,1)S(1)} %collective-permute-done.7, ...), kind=kOutput, calls=%fused_computation.20 | convolution fusion | flops 2153250816 | bytes 11534336 | tf_op jit(solution)/shard_map/dot_general | solution.py:149
  (68 shorter events, 18.1 us)
Async XLA Ops:
  6.5 10.7 %copy-start = (bf16[256,2048]{1,0:T(8,128)(2,1)S(1)}, bf16[256,2048]{1,0:T(8,128)(2,1)}, u32[]{:S(2)}) copy-start(bf16[256,2048]{1,0:T(8,128)(2,1)} %param.6) | copy-start | bytes 3145732
  6.5 19.3 %copy-start.6 = (s32[1,4]{1,0:T(1,128)S(1)}, s32[1,4]{1,0:T(1,128)}, u32[]{:S(2)}) copy-start(s32[1,4]{1,0:T(1,128)} %param.7) | copy-start | bytes 52
  6.5 74.8 %all-gather.2.cloned.1.call-start = ((), (), s32[]{:S(2)}) async-start(), calls=%async_computation | async-start | bytes 6684672 | tf_op jit(solution)/shard_map/all_gather | solution.py:70
  12.1 37.6 %collective-permute-start = (bf16[136,2048]{1,0:T(8,128)(2,1)S(1)}, bf16[136,2048]{1,0:T(8,128)(2,1)S(1)}, u32[]{:S(2)}, u32[]{:S(2)}) collective-permute-start(bf16[136,2048]{1,0:T(8,128)(2,1)S(1)} %slice.198), channel_id=1, source_target_pairs={{3,7},{7,11},{11,15},{19,23},{23,27},{27,31},{35,39},{39,43},{43,4... | collective-permute-start | bytes 1671176 | tf_op jit(solution)/shard_map/ppermute | solution.py:57
  12.8 41.6 %collective-permute-start.1 = (bf16[136,2048]{1,0:T(8,128)(2,1)S(1)}, bf16[136,2048]{1,0:T(8,128)(2,1)}, u32[]{:S(2)}, u32[]{:S(2)}) collective-permute-start(bf16[136,2048]{1,0:T(8,128)(2,1)S(1)} %slice.198), channel_id=1, source_target_pairs={{3,6},{7,10},{11,14},{19,22},{23,26},{27,30},{35,38},{39,42},{43,4... | collective-permute-start | bytes 1671176 | tf_op jit(solution)/shard_map/ppermute | solution.py:57
  14.3 40.1 %collective-permute-start.2 = (bf16[136,2048]{1,0:T(8,128)(2,1)S(1)}, bf16[136,2048]{1,0:T(8,128)(2,1)}, u32[]{:S(2)}, u32[]{:S(2)}) collective-permute-start(bf16[136,2048]{1,0:T(8,128)(2,1)S(1)} %slice.198), channel_id=1, source_target_pairs={{3,5},{7,9},{11,13},{19,21},{23,25},{27,29},{35,37},{39,41},{43,45... | collective-permute-start | bytes 1671176 | tf_op jit(solution)/shard_map/ppermute | solution.py:57
  15.8 38.6 %collective-permute-start.3 = (bf16[136,2048]{1,0:T(8,128)(2,1)S(1)}, bf16[136,2048]{1,0:T(8,128)(2,1)}, u32[]{:S(2)}, u32[]{:S(2)}) collective-permute-start(bf16[136,2048]{1,0:T(8,128)(2,1)S(1)} %slice.198), channel_id=1, source_target_pairs={{3,4},{7,8},{11,12},{19,20},{23,24},{27,28},{35,36},{39,40},{43,44... | collective-permute-start | bytes 1671176 | tf_op jit(solution)/shard_map/ppermute | solution.py:57
  17.3 32.5 %collective-permute-start.4 = (bf16[256,2048]{1,0:T(8,128)(2,1)S(1)}, bf16[256,2048]{1,0:T(8,128)(2,1)S(1)}, u32[]{:S(2)}, u32[]{:S(2)}) collective-permute-start(bf16[256,2048]{1,0:T(8,128)(2,1)S(1)} %copy-done), channel_id=1, source_target_pairs={{0,2},{1,3},{2,0},{3,1},{4,6},{5,7},{6,4},{7,5},{8,10},{9,11},{10,... | collective-permute-start | bytes 3145736 | tf_op jit(solution)/shard_map/ppermute | solution.py:44
  29.4 0.7 copy-start.4
  31.6 12.7 %copy-start.5 = (s32[1160]{0:T(1024)S(1)}, s32[1160]{0:T(1024)}, u32[]{:S(2)}) copy-start(s32[1160]{0:T(1024)} %copy-done.4) | copy-start | bytes 13924
  49.7 7.0 %collective-permute-start.6 = (bf16[256,2048]{1,0:T(8,128)(2,1)S(1)}, bf16[256,2048]{1,0:T(8,128)(2,1)S(1)}, u32[]{:S(2)}, u32[]{:S(2)}) collective-permute-start(bf16[256,2048]{1,0:T(8,128)(2,1)S(1)} %copy-done), channel_id=1, source_target_pairs={{0,1},{1,0},{2,3},{3,2},{4,5},{5,4},{6,7},{7,6},{8,9},{9,8},{10,11... | collective-permute-start | bytes 3145736 | tf_op jit(solution)/shard_map/ppermute | solution.py:42
  49.8 6.9 %collective-permute-start.5 = (bf16[256,2048]{1,0:T(8,128)(2,1)S(1)}, bf16[256,2048]{1,0:T(8,128)(2,1)S(1)}, u32[]{:S(2)}, u32[]{:S(2)}) collective-permute-start(bf16[256,2048]{1,0:T(8,128)(2,1)S(1)} %collective-permute-done.4), channel_id=1, source_target_pairs={{0,1},{1,0},{2,3},{3,2},{4,5},{5,4},{6,7},{7,6},{8,9},{9,8},{10,11... | collective-permute-start | bytes 3145736 | tf_op jit(solution)/shard_map/ppermute | solution.py:45
  110.2 5.7 %copy-start.3 = (pred[8,128,128]{2,1,0:T(8,128)(4,1)S(1)}, pred[8,128,128]{2,1,0:T(8,128)(4,1)}, u32[]{:S(2)}) copy-start(pred[8,128,128]{2,1,0:T(8,128)(4,1)} %get-tuple-element.45) | copy-start | bytes 393220
  115.9 5.8 %copy-start.1 = (bf16[32,128,128]{2,1,0:T(8,128)(2,1)S(1)}, bf16[32,128,128]{2,1,0:T(8,128)(2,1)}, u32[]{:S(2)}) copy-start(bf16[32,128,128]{2,1,0:T(8,128)(2,1)} %copy.28) | copy-start | bytes 3145732
  115.9 5.8 %copy-start.2 = (pred[8,128,128]{2,1,0:T(8,128)(4,1)S(1)}, pred[8,128,128]{2,1,0:T(8,128)(4,1)}, u32[]{:S(2)}) copy-start(pred[8,128,128]{2,1,0:T(8,128)(4,1)} %get-tuple-element.44) | copy-start | bytes 393220
  134.4 2.5 %collective-permute-start.7 = (bf16[256,512]{1,0:T(8,128)(2,1)S(1)}, bf16[256,512]{1,0:T(8,128)(2,1)S(1)}, u32[]{:S(2)}, u32[]{:S(2)}) collective-permute-start(bf16[256,512]{1,0:T(8,128)(2,1)S(1)} %get-tuple-element.30), channel_id=1, source_target_pairs={{0,1},{1,0},{2,3},{3,2},{4,5},{5,4},{6,7},{7,6},{8,9},{9,8},{10,11... | collective-permute-start | bytes 786440 | tf_op jit(solution)/shard_map/ppermute | solution.py:147
  135.2 7.9 %collective-permute-start.8 = (bf16[256,512]{1,0:T(8,128)(2,1)S(1)}, bf16[256,512]{1,0:T(8,128)(2,1)S(1)}, u32[]{:S(2)}, u32[]{:S(2)}) collective-permute-start(bf16[256,512]{1,0:T(8,128)(2,1)S(1)} %get-tuple-element.29), channel_id=1, source_target_pairs={{0,2},{1,3},{2,0},{3,1},{4,6},{5,7},{6,4},{7,5},{8,10},{9,11},{10,... | collective-permute-start | bytes 786440 | tf_op jit(solution)/shard_map/ppermute | solution.py:147
  136.5 12.4 %collective-permute-start.9 = (bf16[256,512]{1,0:T(8,128)(2,1)S(1)}, bf16[256,512]{1,0:T(8,128)(2,1)S(1)}, u32[]{:S(2)}, u32[]{:S(2)}) collective-permute-start(bf16[256,512]{1,0:T(8,128)(2,1)S(1)} %get-tuple-element.28), channel_id=1, source_target_pairs={{0,3},{1,2},{2,1},{3,0},{4,7},{5,6},{6,5},{7,4},{8,11},{9,10},{10,... | collective-permute-start | bytes 786440 | tf_op jit(solution)/shard_map/ppermute | solution.py:147
Sparse Core Ops, SparseCore 0:
  11.1 70.1 all-gather.1
